TPU v7x, 32 devices: a whole 2x2x4 slice. The times are simulated.
32 devices in a mesh: prow: 4 (over y, x), pcol: 4 (over z), cuts: 2 (over core).
Axes of the slice: x: 2, y: 2, z: 4, core: 2. Of those that a mesh axis runs over, the one named last changes fastest.
Arguments:
- amplitudes: bfloat16 [6144, 6400], P('prow', 'cuts'), may hold values from -6 to 6
- integrals: bfloat16 [6400, 1600], P(('cuts', 'prow'), 'pcol'), may hold values from -0.21875 to 0.21875
- irrep_rows: int32 [6400], replicated, may hold values from 0 to 7, as said below
- irrep_cols: int32 [1600], P('pcol'), may hold values from 0 to 7, as said below
- mirror_row: int32 [6144], replicated, may hold values from 0 to 6143, as said below
Outputs:
- residual: float32 [6144, 1600], P(('prow', 'cuts'), 'pcol')
Inputs may be any that keep to these rules, and one draw needn't show every extreme that they name: irrep_rows is non-decreasing along the contraction pairs (pairs sorted by irrep, tiles of uneven size), and every one of the 8 irreps holds at least one pair. Some aligned run of 800 pairs carries a single irrep, and that irrep also covers some whole aligned run of 400 columns, so the mask of that tile is all ones. irrep_cols is non-decreasing along the columns (tiles of uneven size), and every one of the 8 irreps holds at least one column. Some aligned run of 400 columns carries a single irrep. mirror_row is an involution without fixed points. Rows are grouped into 8 aligned blocks of 768 rows, block b = r * 2 + c; the partner of every row of block (r, c) lies in block (r XOR (2), c).
All inputs are finite; a program needn't handle non-finite values.
Results may differ from a plain program's by a relative error of at most 0.0003.
Values may be sent and summed in bfloat16 or wider, within the bound.
No kernel may reach another device: no remote copies, remote signals or barrier semaphores. Data moves between devices by JAX's collectives and lax.ppermute only.
A program may use at most 64 MiB of HBM per device.

v0:
```python
import jax
import jax.numpy as jnp
from jax import lax
from jax.sharding import PartitionSpec as P


def partner(value, axis, stride):
    return lax.ppermute(value, axis, [(i, i ^ 1 << stride) for i in range(lax.axis_size(axis))])


def shards(amplitudes, integrals, irrep_rows, irrep_cols, mirror_row):
    prow_count = lax.axis_size("prow")
    top_bit = prow_count.bit_length() - 2
    row_count = amplitudes.shape[0]
    slice_width = amplitudes.shape[1]
    prow_idx = lax.axis_index("prow")
    cuts_idx = lax.axis_index("cuts")
    partner_idx = jnp.bitwise_xor(prow_idx, prow_count // 2)
    piece = lax.all_gather(integrals, "prow", axis=0, tiled=True)
    count = piece.shape[0]
    base = cuts_idx * slice_width
    labels = lax.dynamic_slice(irrep_rows, (base,), (count,))
    same = labels[:, None] == irrep_cols[None, :]
    blocked = jnp.where(same, piece, jnp.zeros_like(piece))
    terms = jnp.dot(amplitudes, blocked, preferred_element_type=jnp.float32)
    mine = lax.dynamic_slice(mirror_row, (prow_idx * row_count,), (row_count,))
    local = mine - partner_idx * row_count
    fetched = partner(terms, "prow", top_bit)
    antisym = terms - jnp.take(fetched, local, axis=0)
    residual = lax.psum_scatter(antisym, "cuts", scatter_dimension=0, tiled=True)
    return residual


def solution(mesh):
    placed = (P("prow", "cuts"), P(("cuts", "prow"), "pcol"), P(), P("pcol"), P())
    return jax.shard_map(
        shards, mesh=mesh, in_specs=placed, out_specs=P(("prow", "cuts"), "pcol"), check_vma=False
    )
```

profile of v0, /device:TPU:0, one launch (start us, length us, event | category | flops | bytes accessed | tf_op | source)
XLA Modules:
  0.0 153.7 jit_solution(17844110228926920546)
XLA Ops:
  6.5 0.0 all-gather.3.cloned.1.call-start
  6.5 0.7 all-gather.3.cloned.1.call-update
  7.3 0.0 reduce-scatter.2.cloned.1.call-start
  7.3 0.8 dynamic_slice.6
  8.1 45.5 %all-gather.3.cloned.1.call-done = bf16[4,800,400]{1,2,0:T(8,128)(2,1)} async-done(((bf16[1,800,400]{1,2,0:T(8,128)(2,1)}), bf16[4,800,400]{1,2,0:T(8,128)(2,1)}) %all-gather.3.cloned.1.call-update) | async-done | bytes 2560016 | tf_op jit(solution)/shard_map/all_gather | solution.py:19
  53.6 2.9 %copy.11 = bf16[4,800,400]{1,0,2:T(4,128)(2,1)S(1)} copy(bf16[4,800,400]{1,2,0:T(8,128)(2,1)} %all-gather.3.cloned.1.call-done) | data formatting | bytes 5120000 | tf_op jit(solution)/shard_map/all_gather | solution.py:19
  56.5 0.0 copy-start.1
  56.5 3.7 %reshape.17 = bf16[3200,400]{0,1:T(8,128)(2,1)} reshape(bf16[4,800,400]{1,0,2:T(4,128)(2,1)S(1)} %copy.11) | data formatting | bytes 5120000
  60.2 0.0 copy-done.1
  60.2 8.0 %convolution_bitcast_fusion = f32[1536,400]{0,1:T(8,128)S(1)} fusion(bf16[1536,3200]{1,0:T(8,128)(2,1)} %param.5, bf16[3200,400]{0,1:T(8,128)(2,1)} %reshape.17, s32[3200]{0:T(1024)S(1)} %dynamic_slice.6, s32[400]{0:T(512)S(1)} %copy-done.1), kind=kOutput, calls=%fused_computation.2 | convolution fusion | flops 3934720000 | bytes 14862400 | tf_op jit(solution)/shard_map/dot_general | solution.py:25
  68.3 0.0 copy-start
  68.3 1.5 collective-permute-start
  69.8 0.8 compare_and_fusion
  70.6 0.0 copy-done
  70.6 52.9 %collective-permute-done = f32[1536,400]{0,1:T(8,128)} collective-permute-done((f32[1536,400]{0,1:T(8,128)S(1)}, f32[1536,400]{0,1:T(8,128)}, u32[]{:S(2)}, u32[]{:S(2)}) %collective-permute-start) | collective-permute-done | bytes 2457632 | tf_op jit(solution)/shard_map/ppermute | solution.py:8
  123.5 2.3 %copy.12 = f32[1536,400]{1,0:T(8,128)S(1)} copy(f32[1536,400]{0,1:T(8,128)} %collective-permute-done) | data formatting | bytes 4915200 | tf_op jit(solution)/shard_map/ppermute | solution.py:8
  125.8 4.9 %gather_fusion = f32[1536,400]{1,0:T(8,128)} fusion(f32[1536,400]{1,0:T(8,128)S(1)} %copy.12, s32[2048]{0:T(1024)S(1)} %pad_clamp_fusion), kind=kCustom, calls=%fused_computation | custom fusion | bytes 4921344 | tf_op jit(solution)/shard_map/jit(_take)/gather | solution.py:29
  130.7 2.3 %copy.13 = f32[1536,400]{0,1:T(8,128)S(1)} copy(f32[1536,400]{1,0:T(8,128)} %gather_fusion) | data formatting | bytes 4915200 | tf_op jit(solution)/shard_map/jit(_take)/gather | solution.py:29
  133.1 3.6 %select_subtract_fusion = f32[1536,400]{0,1:T(8,128)} fusion(f32[1536,400]{0,1:T(8,128)} %copy-done, f32[1536,400]{0,1:T(8,128)S(1)} %copy.13, pred[1536]{0:T(1024)(128)(4,1)S(1)} %get-tuple-element.5), kind=kLoop, calls=%fused_computation.5 | loop fusion | flops 1228800 | bytes 7374336 | tf_op jit(solution)/shard_map/sub | solution.py:29
  136.7 0.0 reduce-scatter.2.cloned.1.call-update
  136.7 10.2 %reduce-scatter.2.cloned.1.call-done = f32[768,400]{0,1:T(8,128)} async-done(((f32[1536,400]{0,1:T(8,128)}), f32[768,400]{0,1:T(8,128)}) %reduce-scatter.2.cloned.1.call-update) | async-done | bytes 1228816 | tf_op jit(solution)/shard_map/reduce_scatter | solution.py:30
  (1 shorter events, 0.0 us)
Async XLA Ops:
  6.5 47.1 %all-gather.3.cloned.1.call-start = ((), (), s32[]{:S(2)}) async-start(), calls=%async_computation.2 | async-start | bytes 3584000 | tf_op jit(solution)/shard_map/all_gather | solution.py:19
  7.3 139.6 %reduce-scatter.2.cloned.1.call-start = ((), (), s32[]{:S(2)}) async-start(), calls=%async_computation.1 | async-start | bytes 3686400 | tf_op jit(solution)/shard_map/reduce_scatter | solution.py:30
  56.5 3.7 %copy-start.1 = (s32[400]{0:T(512)S(1)}, s32[400]{0:T(512)}, u32[]{:S(2)}) copy-start(s32[400]{0:T(512)} %param.8) | copy-start | bytes 4804
  68.3 2.3 %copy-start = (f32[1536,400]{0,1:T(8,128)}, f32[1536,400]{0,1:T(8,128)S(1)}, u32[]{:S(2)}) copy-start(f32[1536,400]{0,1:T(8,128)S(1)} %convolution_bitcast_fusion) | copy-start | bytes 7372804
  68.3 55.3 %collective-permute-start = (f32[1536,400]{0,1:T(8,128)S(1)}, f32[1536,400]{0,1:T(8,128)}, u32[]{:S(2)}, u32[]{:S(2)}) collective-permute-start(f32[1536,400]{0,1:T(8,128)S(1)} %convolution_bitcast_fusion), channel_id=1, source_target_pairs={{0,16},{8,24},{16,0},{24,8},{1,17},{9,25},{17,1},{25,9},{2,18},{10... | collective-permute-start | bytes 7372808 | tf_op jit(solution)/shard_map/ppermute | solution.py:8
Sparse Core Ops, SparseCore 0:
  9.2 44.3 all-gather.2
  136.8 9.9 reduce-scatter.1
where the time goes:
time: 154 us
  waiting for transfers between devices  109 us (71%)
  local copies, waits for them, and re-layouts  16.9 us (11%)
  between operations  13.5 us (9%)
  matrix products  8.04 us (5%)
  other arithmetic  4.4 us (3%)
  starting transfers between devices  1.57 us (1%)
    ppermute x1, waiting for transfers between devices, partner(): lax.ppermute(value, axis, [(i, i ^ 1 << stride) for i in range(lax.axis_s...  52.9 us
    all_gather x1, waiting for transfers between devices, shards(): piece = lax.all_gather(integrals, 'prow', axis=0, tiled=True)  45.5 us
    reduce_scatter x1, waiting for transfers between devices, shards(): lax.psum_scatter(antisym, 'cuts', scatter_dimension=0, tiled=True)  10.2 us
    dot_general x1, matrix products, shards(): terms = jnp.dot(amplitudes, blocked, preferred_element_type=jnp.float32)  8.04 us
    gather x2, local copies, waits for them, and re-layouts, shards(): antisym = terms - jnp.take(fetched, local, axis=0)  7.26 us
    unnamed x5, local copies, waits for them, and re-layouts  3.68 us
    sub x1, other arithmetic, shards(): antisym = terms - jnp.take(fetched, local, axis=0)  3.61 us
  transfers between devices with their start and end apart: 3, of which 3 were waited for; matrix products, arithmetic and copies ran while one was open for 1% of the time, Pallas kernels for 0%

commit v1 on v0

v1 whole, which is shorter than its diff:
```python
import jax
import jax.numpy as jnp
from jax import lax
from jax.sharding import PartitionSpec as P


def swap(value, axis, mask):
    return lax.ppermute(value, axis, [(i, i ^ mask) for i in range(lax.axis_size(axis))])


def gather_prow(own, prow_idx, prow_count):
    count = own.shape[0]
    blocks = {0: own}
    if prow_count == 4:
        blocks[1] = swap(own, "prow", 1)
        blocks[2] = swap(own, "prow", 2)
        blocks[3] = swap(blocks[2], "prow", 1)
    else:
        for s in range(1, prow_count):
            blocks[s] = swap(own, "prow", s)
    piece = jnp.zeros((prow_count * count,) + own.shape[1:], own.dtype)
    for s, block in blocks.items():
        piece = lax.dynamic_update_slice(piece, block, (jnp.bitwise_xor(prow_idx, s) * count, 0))
    return piece


def reduce_cuts(terms, cuts_idx, cuts_count):
    rows = terms.shape[0] // cuts_count
    total = lax.dynamic_slice_in_dim(terms, cuts_idx * rows, rows, axis=0)
    for s in range(1, cuts_count):
        part = lax.dynamic_slice_in_dim(terms, jnp.bitwise_xor(cuts_idx, s) * rows, rows, axis=0)
        total = total + swap(part, "cuts", s)
    return total


def shards(amplitudes, integrals, irrep_rows, irrep_cols, mirror_row):
    prow_count = lax.axis_size("prow")
    cuts_count = lax.axis_size("cuts")
    slice_width = amplitudes.shape[1]
    prow_idx = lax.axis_index("prow")
    cuts_idx = lax.axis_index("cuts")
    piece = gather_prow(integrals, prow_idx, prow_count)
    count = piece.shape[0]
    labels = lax.dynamic_slice(irrep_rows, (cuts_idx * slice_width,), (count,))
    same = labels[:, None] == irrep_cols[None, :]
    blocked = jnp.where(same, piece, jnp.zeros_like(piece))
    terms = jnp.dot(amplitudes, blocked, preferred_element_type=jnp.float32)
    cycle = reduce_cuts(terms, cuts_idx, cuts_count)
    block_rows = cycle.shape[0]
    half = prow_count // 2
    own_block = prow_idx * cuts_count + cuts_idx
    partner_block = jnp.bitwise_xor(prow_idx, half) * cuts_count + cuts_idx
    mine = lax.dynamic_slice(mirror_row, (own_block * block_rows,), (block_rows,))
    local = mine - partner_block * block_rows
    fetched = swap(cycle, "prow", half)
    return cycle - jnp.take(fetched, local, axis=0)


def solution(mesh):
    placed = (P("prow", "cuts"), P(("cuts", "prow"), "pcol"), P(), P("pcol"), P())
    return jax.shard_map(
        shards, mesh=mesh, in_specs=placed, out_specs=P(("prow", "cuts"), "pcol"), check_vma=False
    )
```

time: 154 us -> 105 us (0.68)
  waiting for transfers between devices: 109 us -> 44.4 us
  local copies, waits for them, and re-layouts: 16.9 us -> 40.2 us
  between operations: 13.5 us -> 0.18 us
  starting transfers between devices: 1.57 us -> 8.08 us
    all_gather x1 -> x0, waiting for transfers between devices: 45.5 us -> none  [shards(): piece = lax.all_gather(integrals, 'prow', axis=0, tiled=True)]
    dynamic_update_slice x0 -> x4, local copies, waits for them, and re-layouts: none -> 34.2 us  [gather_prow(): lax.dynamic_update_slice(piece, block, (jnp.bitwise_xor(prow_idx, s) * co...]
    reduce_scatter x1 -> x0, waiting for transfers between devices: 10.2 us -> none  [shards(): lax.psum_scatter(antisym, 'cuts', scatter_dimension=0, tiled=True)]
    ppermute x1 -> x5, waiting for transfers between devices: 52.9 us -> 44.4 us  [swap(): lax.ppermute(value, axis, [(i, i ^ mask) for i in range(lax.axis_size(axi...]
    ppermute x1 -> x5, starting transfers between devices: 1.53 us -> 8.08 us  [swap(): lax.ppermute(value, axis, [(i, i ^ mask) for i in range(lax.axis_size(axi...]
    gather x2, local copies, waits for them, and re-layouts: 7.26 us -> 3.65 us  [shards(): return cycle - jnp.take(fetched, local, axis=0)]
    all_gather x1 -> x0, local copies, waits for them, and re-layouts: 2.92 us -> none  [shards(): piece = lax.all_gather(integrals, 'prow', axis=0, tiled=True)]
    unnamed x5 -> x12, local copies, waits for them, and re-layouts: 3.68 us -> 1.48 us
  transfers between devices with their start and end apart: 3 -> 5, of which waited for: 3 -> 3; matrix products, arithmetic and copies ran while one was open for 1% -> 25% of each run, Pallas kernels for 0% -> 0%
where the time goes in v1:
time: 105 us
  waiting for transfers between devices  44.4 us (42%)
  local copies, waits for them, and re-layouts  40.2 us (38%)
  starting transfers between devices  8.08 us (8%)
  matrix products  7.25 us (7%)
  other arithmetic  4.67 us (4%)
    ppermute x5, waiting for transfers between devices, swap(): lax.ppermute(value, axis, [(i, i ^ mask) for i in range(lax.axis_size(axi...  44.4 us
    dynamic_update_slice x4, local copies, waits for them, and re-layouts, gather_prow(): lax.dynamic_update_slice(piece, block, (jnp.bitwise_xor(prow_idx, s) * co...  34.2 us
    ppermute x5, starting transfers between devices, swap(): lax.ppermute(value, axis, [(i, i ^ mask) for i in range(lax.axis_size(axi...  8.08 us
    dot_general x1, matrix products, shards(): terms = jnp.dot(amplitudes, blocked, preferred_element_type=jnp.float32)  7.25 us
    gather x2, local copies, waits for them, and re-layouts, shards(): return cycle - jnp.take(fetched, local, axis=0)  3.65 us
    sub x1, other arithmetic, shards(): return cycle - jnp.take(fetched, local, axis=0)  2.46 us
  transfers between devices with their start and end apart: 5, of which 3 were waited for; matrix products, arithmetic and copies ran while one was open for 25% of the time, Pallas kernels for 0%

profile of v1, /device:TPU:0, one launch (start us, length us, event | category | flops | bytes accessed | tf_op | source)
XLA Modules:
  0.0 104.7 jit_solution(4293564452855566279)
XLA Ops:
  0.0 3.0 %collective-permute-start.1 = (bf16[800,400]{0,1:T(8,128)(2,1)}, bf16[800,400]{0,1:T(8,128)(2,1)}, u32[]{:S(2)}, u32[]{:S(2)}) collective-permute-start(bf16[800,400]{0,1:T(8,128)(2,1)} %param.6), channel_id=1, source_target_pairs={{0,16},{8,24},{16,0},{24,8},{1,17},{9,25},{17,1},{25,9},{2,18},{10... | collective-permute-start | bytes 1920008 | tf_op jit(solution)/shard_map/ppermute | solution.py:8
  3.0 1.5 %collective-permute-start = (bf16[800,400]{0,1:T(8,128)(2,1)}, bf16[800,400]{0,1:T(8,128)(2,1)}, u32[]{:S(2)}, u32[]{:S(2)}) collective-permute-start(bf16[800,400]{0,1:T(8,128)(2,1)} %param.6), channel_id=1, source_target_pairs={{0,8},{8,0},{16,24},{24,16},{1,9},{9,1},{17,25},{25,17},{2,10},{10... | collective-permute-start | bytes 1920008 | tf_op jit(solution)/shard_map/ppermute | solution.py:8
  4.5 14.9 %collective-permute-done.1 = bf16[800,400]{0,1:T(8,128)(2,1)} collective-permute-done((bf16[800,400]{0,1:T(8,128)(2,1)}, bf16[800,400]{0,1:T(8,128)(2,1)}, u32[]{:S(2)}, u32[]{:S(2)}) %collective-permute-start.1) | collective-permute-done | bytes 640032 | tf_op jit(solution)/shard_map/ppermute | solution.py:8
  19.4 1.6 %collective-permute-start.2 = (bf16[800,400]{0,1:T(8,128)(2,1)}, bf16[800,400]{0,1:T(8,128)(2,1)}, u32[]{:S(2)}, u32[]{:S(2)}) collective-permute-start(bf16[800,400]{0,1:T(8,128)(2,1)} %collective-permute-done.1), channel_id=1, source_target_pairs={{0,8},{8,0},{16,24},{24,16},{1,9},{9,1},{17,25},{25,17},{2,10},{10... | collective-permute-start | bytes 1920008 | tf_op jit(solution)/shard_map/ppermute | solution.py:8
  21.0 0.2 broadcast.8
  21.2 0.0 copy-done.3
  21.2 6.9 %dynamic_update_slice.12 = bf16[3200,400]{0,1:T(8,128)(2,1)S(1)} dynamic-update-slice(bf16[3200,400]{0,1:T(8,128)(2,1)S(1)} %broadcast.8, bf16[800,400]{0,1:T(8,128)(2,1)S(1)} %copy-done.3, s32[]{:T(128)S(6)} %select_n.38, s32[]{:T(128)} %constant.17.clone.1) | dynamic-update-slice | bytes 1280004 | tf_op jit(solution)/shard_map/dynamic_update_slice | solution.py:23
  28.2 0.1 dynamic_slice.12
  28.3 0.0 collective-permute-done
  28.3 9.2 %dynamic_update_slice.13 = bf16[3200,400]{0,1:T(8,128)(2,1)S(1)} dynamic-update-slice(bf16[3200,400]{0,1:T(8,128)(2,1)S(1)} %dynamic_update_slice.12, bf16[800,400]{0,1:T(8,128)(2,1)} %collective-permute-done, s32[]{:T(128)S(6)} %select_n.39, s32[]{:T(128)} %constant.17.clone.1) | dynamic-update-slice | bytes 1280004 | tf_op jit(solution)/shard_map/dynamic_update_slice | solution.py:23
  37.5 0.0 copy-start.5
  37.5 9.2 %dynamic_update_slice.14 = bf16[3200,400]{0,1:T(8,128)(2,1)S(1)} dynamic-update-slice(bf16[3200,400]{0,1:T(8,128)(2,1)S(1)} %dynamic_update_slice.13, bf16[800,400]{0,1:T(8,128)(2,1)} %collective-permute-done.1, s32[]{:T(128)S(6)} %select_n.40, s32[]{:T(128)} %constant.17.clone.1) | dynamic-update-slice | bytes 1280004 | tf_op jit(solution)/shard_map/dynamic_update_slice | solution.py:23
  46.7 0.0 collective-permute-done.2
  46.7 8.9 %dynamic_update_slice.15 = bf16[3200,400]{0,1:T(8,128)(2,1)S(1)} dynamic-update-slice(bf16[3200,400]{0,1:T(8,128)(2,1)S(1)} %dynamic_update_slice.14, bf16[800,400]{0,1:T(8,128)(2,1)} %collective-permute-done.2, s32[]{:T(128)S(6)} %select_n.41, s32[]{:T(128)} %constant.17.clone.1) | dynamic-update-slice | bytes 1280004 | tf_op jit(solution)/shard_map/dynamic_update_slice | solution.py:23
  55.6 0.0 copy-done.5
  55.6 7.2 %fusion = f32[400,1536]{1,0:T(8,128)S(1)} fusion(bf16[1536,3200]{1,0:T(8,128)(2,1)} %param.5, bf16[3200,400]{0,1:T(8,128)(2,1)S(1)} %dynamic_update_slice.15, s32[3200]{0:T(1024)S(1)} %dynamic_slice.12, s32[400]{0:T(512)S(1)} %copy-done.5), kind=kOutput, calls=%fused_computation.2 | convolution fusion | flops 3934720000 | bytes 14862400 | tf_op jit(solution)/shard_map/dot_general | solution.py:47
  62.9 0.0 copy-start.2
  62.9 1.5 %copy-done.2 = f32[400,1536]{1,0:T(8,128)} copy-done((f32[400,1536]{1,0:T(8,128)}, f32[400,1536]{1,0:T(8,128)S(1)}, u32[]{:S(2)}) %copy-start.2) | copy-done | bytes 2457624
  64.4 0.1 dynamic-slice_bitcast_fusion
  64.4 0.1 collective-permute-start.3
  64.5 2.9 %collective-permute-done.3 = f32[768,400]{0,1:T(8,128)S(1)} collective-permute-done((f32[768,400]{0,1:T(8,128)S(1)}, f32[768,400]{0,1:T(8,128)S(1)}, u32[]{:S(2)}, u32[]{:S(2)}) %collective-permute-start.3) | collective-permute-done | bytes 1228832 | tf_op jit(solution)/shard_map/ppermute | solution.py:8
  67.4 1.4 %bitcast_add_fusion = f32[768,400]{0,1:T(8,128)S(1)} fusion(f32[768,400]{0,1:T(8,128)S(1)} %collective-permute-done.3, f32[400,1536]{1,0:T(8,128)} %copy-done.2, s32[]{:T(128)S(6)} %select_n.43), kind=kLoop, calls=%fused_computation.6 | loop fusion | flops 307200 | bytes 3686404 | tf_op jit(solution)/shard_map/add | solution.py:32
  68.9 0.0 copy-start
  68.9 1.9 %collective-permute-start.4 = (f32[768,400]{0,1:T(8,128)S(1)}, f32[768,400]{0,1:T(8,128)S(1)}, u32[]{:S(2)}, u32[]{:S(2)}) collective-permute-start(f32[768,400]{0,1:T(8,128)S(1)} %bitcast_add_fusion), channel_id=1, source_target_pairs={{0,16},{8,24},{16,0},{24,8},{1,17},{9,25},{17,1},{25,9},{2,18},{10... | collective-permute-start | bytes 3686408 | tf_op jit(solution)/shard_map/ppermute | solution.py:8
  70.8 0.8 compare_and_fusion
  71.6 26.5 %collective-permute-done.4 = f32[768,400]{0,1:T(8,128)S(1)} collective-permute-done((f32[768,400]{0,1:T(8,128)S(1)}, f32[768,400]{0,1:T(8,128)S(1)}, u32[]{:S(2)}, u32[]{:S(2)}) %collective-permute-start.4) | collective-permute-done | bytes 1228832 | tf_op jit(solution)/shard_map/ppermute | solution.py:8
  98.1 0.5 copy.6
  98.6 2.2 %gather_fusion = f32[768,400]{1,0:T(8,128)S(1)} fusion(f32[768,400]{1,0:T(8,128)S(1)} %copy.6, s32[1024]{0:T(1024)S(1)} %pad_clamp_fusion), kind=kCustom, calls=%fused_computation | custom fusion | bytes 2460672 | tf_op jit(solution)/shard_map/jit(_take)/gather | solution.py:56
  100.7 0.0 copy-start.1
  100.7 1.5 %copy.7 = f32[768,400]{0,1:T(8,128)} copy(f32[768,400]{1,0:T(8,128)S(1)} %gather_fusion) | data formatting | bytes 2457600 | tf_op jit(solution)/shard_map/jit(_take)/gather | solution.py:56
  102.2 0.0 copy-done.1
  102.2 2.5 %select_subtract_fusion = f32[768,400]{0,1:T(8,128)} fusion(f32[768,400]{0,1:T(8,128)S(1)} %copy-done.1, f32[768,400]{0,1:T(8,128)} %copy.7, pred[768]{0:T(1024)(128)(4,1)S(1)} %get-tuple-element.5), kind=kLoop, calls=%fused_computation.7 | loop fusion | flops 614400 | bytes 3687168 | tf_op jit(solution)/shard_map/sub | solution.py:56
  (5 shorter events, 0.0 us)
Async XLA Ops:
  0.0 21.2 %copy-start.3 = (bf16[800,400]{0,1:T(8,128)(2,1)S(1)}, bf16[800,400]{0,1:T(8,128)(2,1)}, u32[]{:S(2)}) copy-start(bf16[800,400]{0,1:T(8,128)(2,1)} %param.6) | copy-start | bytes 1920004
  0.0 19.4 %collective-permute-start.1 = (bf16[800,400]{0,1:T(8,128)(2,1)}, bf16[800,400]{0,1:T(8,128)(2,1)}, u32[]{:S(2)}, u32[]{:S(2)}) collective-permute-start(bf16[800,400]{0,1:T(8,128)(2,1)} %param.6), channel_id=1, source_target_pairs={{0,16},{8,24},{16,0},{24,8},{1,17},{9,25},{17,1},{25,9},{2,18},{10... | collective-permute-start | bytes 1920008 | tf_op jit(solution)/shard_map/ppermute | solution.py:8
  3.0 25.3 %collective-permute-start = (bf16[800,400]{0,1:T(8,128)(2,1)}, bf16[800,400]{0,1:T(8,128)(2,1)}, u32[]{:S(2)}, u32[]{:S(2)}) collective-permute-start(bf16[800,400]{0,1:T(8,128)(2,1)} %param.6), channel_id=1, source_target_pairs={{0,8},{8,0},{16,24},{24,16},{1,9},{9,1},{17,25},{25,17},{2,10},{10... | collective-permute-start | bytes 1920008 | tf_op jit(solution)/shard_map/ppermute | solution.py:8
  19.4 27.3 %collective-permute-start.2 = (bf16[800,400]{0,1:T(8,128)(2,1)}, bf16[800,400]{0,1:T(8,128)(2,1)}, u32[]{:S(2)}, u32[]{:S(2)}) collective-permute-start(bf16[800,400]{0,1:T(8,128)(2,1)} %collective-permute-done.1), channel_id=1, source_target_pairs={{0,8},{8,0},{16,24},{24,16},{1,9},{9,1},{17,25},{25,17},{2,10},{10... | collective-permute-start | bytes 1920008 | tf_op jit(solution)/shard_map/ppermute | solution.py:8
  21.0 7.1 %copy-start.4 = (s32[6400]{0:T(1024)S(1)}, s32[6400]{0:T(1024)}, u32[]{:S(2)}) copy-start(s32[6400]{0:T(1024)} %param.7) | copy-start | bytes 76804
  37.5 18.1 %copy-start.5 = (s32[400]{0:T(512)S(1)}, s32[400]{0:T(512)}, u32[]{:S(2)}) copy-start(s32[400]{0:T(512)} %param.8) | copy-start | bytes 4804
  62.9 1.5 %copy-start.2 = (f32[400,1536]{1,0:T(8,128)}, f32[400,1536]{1,0:T(8,128)S(1)}, u32[]{:S(2)}) copy-start(f32[400,1536]{1,0:T(8,128)S(1)} %fusion) | copy-start | bytes 7372804
  64.4 3.0 %collective-permute-start.3 = (f32[768,400]{0,1:T(8,128)S(1)}, f32[768,400]{0,1:T(8,128)S(1)}, u32[]{:S(2)}, u32[]{:S(2)}) collective-permute-start(f32[768,400]{0,1:T(8,128)S(1)} %dynamic-slice_bitcast_fusion), channel_id=1, source_target_pairs={{0,1},{1,0},{2,3},{3,2},{4,5},{5,4},{6,7},{7,6},{8,9},{9,8},{10,11... | collective-permute-start | bytes 3686408 | tf_op jit(solution)/shard_map/ppermute | solution.py:8
  68.9 2.7 %copy-start = (f32[768,400]{0,1:T(8,128)}, f32[768,400]{0,1:T(8,128)S(1)}, u32[]{:S(2)}) copy-start(f32[768,400]{0,1:T(8,128)S(1)} %bitcast_add_fusion) | copy-start | bytes 3686404
  68.9 29.2 %collective-permute-start.4 = (f32[768,400]{0,1:T(8,128)S(1)}, f32[768,400]{0,1:T(8,128)S(1)}, u32[]{:S(2)}, u32[]{:S(2)}) collective-permute-start(f32[768,400]{0,1:T(8,128)S(1)} %bitcast_add_fusion), channel_id=1, source_target_pairs={{0,16},{8,24},{16,0},{24,8},{1,17},{9,25},{17,1},{25,9},{2,18},{10... | collective-permute-start | bytes 3686408 | tf_op jit(solution)/shard_map/ppermute | solution.py:8
  100.7 1.5 %copy-start.1 = (f32[768,400]{0,1:T(8,128)S(1)}, f32[768,400]{0,1:T(8,128)}, u32[]{:S(2)}) copy-start(f32[768,400]{0,1:T(8,128)} %copy-done) | copy-start | bytes 3686404

commit v2 on v1

v2 whole, which is shorter than its diff:
```python
import jax
import jax.numpy as jnp
from jax import lax
from jax.experimental import pallas as pl
from jax.experimental.pallas import tpu as pltpu
from jax.sharding import PartitionSpec as P


def swap(value, axis, mask):
    return lax.ppermute(value, axis, [(i, i ^ mask) for i in range(lax.axis_size(axis))])


def gather_prow(own, prow_idx, prow_count):
    count = own.shape[0]
    if prow_count == 4 and count % 32 == 0:
        half = count // 2
        from_x = swap(own, "prow", 1)
        from_y = swap(own, "prow", 2)
        diag_a = swap(from_y[:half], "prow", 1)
        diag_b = swap(from_x[half:], "prow", 2)
        base = jnp.bitwise_xor(prow_idx, 3) * count
        return [(own, prow_idx * count), (from_x, jnp.bitwise_xor(prow_idx, 1) * count),
                (from_y, jnp.bitwise_xor(prow_idx, 2) * count), (diag_a, base), (diag_b, base + half)]
    blocks = [(own, prow_idx * count)]
    for s in range(1, prow_count):
        blocks.append((swap(own, "prow", s), jnp.bitwise_xor(prow_idx, s) * count))
    return blocks


def contract(amplitudes, blocks):
    rows, width = amplitudes.shape
    cols = blocks[0][0].shape[1]
    n = len(blocks)
    counts = [b.shape[0] for b, _ in blocks]
    if any(c % 16 for c in counts):
        piece = jnp.zeros((width, cols), blocks[0][0].dtype)
        for b, o in blocks:
            piece = lax.dynamic_update_slice(piece, b, (o, 0))
        return jnp.dot(amplitudes, piece, preferred_element_type=jnp.float32)
    offsets = jnp.stack([o for _, o in blocks]).astype(jnp.int32)
    tm = rows // 4 if rows % 32 == 0 else rows

    def kernel(off_ref, a_ref, *refs):
        w_refs = refs[:n]
        o_ref, wbuf, sem = refs[n:]

        @pl.when(pl.program_id(0) == 0)
        def _():
            copies = [pltpu.make_async_copy(w_refs[s], wbuf.at[pl.ds(pl.multiple_of(off_ref[s], 16), counts[s])], sem.at[s])
                      for s in range(n)]
            for c in copies:
                c.start()
            for c in copies:
                c.wait()

        o_ref[...] = jnp.dot(a_ref[...], wbuf[...], preferred_element_type=jnp.float32)

    grid_spec = pltpu.PrefetchScalarGridSpec(
        num_scalar_prefetch=1,
        grid=(rows // tm,),
        in_specs=[pl.BlockSpec((tm, width), lambda i, o: (i, 0))] + [pl.BlockSpec(memory_space=pl.ANY)] * n,
        out_specs=pl.BlockSpec((tm, cols), lambda i, o: (i, 0)),
        scratch_shapes=[pltpu.VMEM((width, cols), blocks[0][0].dtype), pltpu.SemaphoreType.DMA((n,))],
    )
    return pl.pallas_call(
        kernel,
        grid_spec=grid_spec,
        out_shape=jax.ShapeDtypeStruct((rows, cols), jnp.float32),
        compiler_params=pltpu.CompilerParams(dimension_semantics=("arbitrary",)),
    )(offsets, amplitudes, *[b for b, _ in blocks])


def reduce_cuts(terms, cuts_idx, cuts_count):
    rows = terms.shape[0] // cuts_count
    total = lax.dynamic_slice_in_dim(terms, cuts_idx * rows, rows, axis=0)
    for s in range(1, cuts_count):
        part = lax.dynamic_slice_in_dim(terms, jnp.bitwise_xor(cuts_idx, s) * rows, rows, axis=0)
        total = total + swap(part, "cuts", s)
    return total


def shards(amplitudes, integrals, irrep_rows, irrep_cols, mirror_row):
    prow_count = lax.axis_size("prow")
    cuts_count = lax.axis_size("cuts")
    prow_idx = lax.axis_index("prow")
    cuts_idx = lax.axis_index("cuts")
    count = integrals.shape[0]
    labels = lax.dynamic_slice(irrep_rows, ((cuts_idx * prow_count + prow_idx) * count,), (count,))
    same = labels[:, None] == irrep_cols[None, :]
    blocked = jnp.where(same, integrals, jnp.zeros_like(integrals))
    terms = contract(amplitudes, gather_prow(blocked, prow_idx, prow_count))
    cycle = reduce_cuts(terms, cuts_idx, cuts_count)
    block_rows = cycle.shape[0]
    half = prow_count // 2
    own_block = prow_idx * cuts_count + cuts_idx
    partner_block = jnp.bitwise_xor(prow_idx, half) * cuts_count + cuts_idx
    mine = lax.dynamic_slice(mirror_row, (own_block * block_rows,), (block_rows,))
    local = mine - partner_block * block_rows
    fetched = swap(cycle, "prow", half)
    return cycle - jnp.take(fetched, local, axis=0)


def solution(mesh):
    placed = (P("prow", "cuts"), P(("cuts", "prow"), "pcol"), P(), P("pcol"), P())
    return jax.shard_map(
        shards, mesh=mesh, in_specs=placed, out_specs=P(("prow", "cuts"), "pcol"), check_vma=False
    )
```

time: 105 us -> 95.1 us (0.906)
  local copies, waits for them, and re-layouts: 40.2 us -> 15.8 us
  Pallas kernels: 0 us -> 11.9 us
  waiting for transfers between devices: 44.4 us -> 52.3 us
  matrix products: 7.25 us -> 0 us
  starting transfers between devices: 8.08 us -> 9.41 us
    dynamic_update_slice x4 -> x0, local copies, waits for them, and re-layouts: 34.2 us -> none  [gather_prow(): lax.dynamic_update_slice(piece, block, (jnp.bitwise_xor(prow_idx, s) * co...]
    pallas_call x0 -> x1, Pallas kernels: none -> 11.9 us  [contract(): pl.pallas_call(kernel, grid_spec=grid_spec, out_shape=jax.ShapeDtypeStruc...]
    ppermute x5 -> x6, waiting for transfers between devices: 44.4 us -> 52.3 us  [swap(): lax.ppermute(value, axis, [(i, i ^ mask) for i in range(lax.axis_size(axi...]
    dot_general x1 -> x0, matrix products: 7.25 us -> none  [shards(): terms = jnp.dot(amplitudes, blocked, preferred_element_type=jnp.float32)]
    ppermute x1 -> x4, local copies, waits for them, and re-layouts: 0.46 us -> 3.9 us  [swap(): lax.ppermute(value, axis, [(i, i ^ mask) for i in range(lax.axis_size(axi...]
    dynamic_slice x1 -> x2, local copies, waits for them, and re-layouts: 0.08 us -> 1.97 us  [reduce_cuts(): lax.dynamic_slice_in_dim(terms, jnp.bitwise_xor(cuts_idx, s) * rows, rows...]
    sub x0 -> x1, local copies, waits for them, and re-layouts: none -> 1.47 us  [shards(): return cycle - jnp.take(fetched, local, axis=0)]
    ppermute x5 -> x6, starting transfers between devices: 8.08 us -> 9.41 us  [swap(): lax.ppermute(value, axis, [(i, i ^ mask) for i in range(lax.axis_size(axi...]
  transfers between devices with their start and end apart: 5 -> 6, of which waited for: 3 -> 5; matrix products, arithmetic and copies ran while one was open for 25% -> 4% of each run, Pallas kernels for 0% -> 0%
where the time goes in v2:
time: 95.1 us; the launch traced here: 94.6 us
  waiting for transfers between devices  52.3 us (55%)
  local copies, waits for them, and re-layouts  15.8 us (17%)
  Pallas kernels  11.9 us (13%)
  starting transfers between devices  9.41 us (10%)
  other arithmetic  5.09 us (5%)
    ppermute x6, waiting for transfers between devices, swap(): lax.ppermute(value, axis, [(i, i ^ mask) for i in range(lax.axis_size(axi...  52.3 us
    pallas_call x1, Pallas kernels, contract(): pl.pallas_call(kernel, grid_spec=grid_spec, out_shape=jax.ShapeDtypeStruc...  11.9 us
    ppermute x6, starting transfers between devices, swap(): lax.ppermute(value, axis, [(i, i ^ mask) for i in range(lax.axis_size(axi...  9.41 us
    ppermute x4, local copies, waits for them, and re-layouts, swap(): lax.ppermute(value, axis, [(i, i ^ mask) for i in range(lax.axis_size(axi...  3.9 us
    gather x1, local copies, waits for them, and re-layouts, shards(): return cycle - jnp.take(fetched, local, axis=0)  3.12 us
    unnamed x11, local copies, waits for them, and re-layouts  2.18 us
    dynamic_slice x2, local copies, waits for them, and re-layouts, reduce_cuts(): lax.dynamic_slice_in_dim(terms, jnp.bitwise_xor(cuts_idx, s) * rows, rows...  1.97 us
  transfers between devices with their start and end apart: 6, of which 5 were waited for; matrix products, arithmetic and copies ran while one was open for 4% of the time, Pallas kernels for 0%

profile of v2, /device:TPU:0, one launch (start us, length us, event | category | flops | bytes accessed | tf_op | source)
XLA Modules:
  0.0 94.6 jit_solution(15825900181242357029)
XLA Ops:
  0.0 1.4 %copy.20 = bf16[800,400]{1,0:T(8,128)(2,1)S(1)} copy(bf16[800,400]{0,1:T(8,128)(2,1)} %param.6) | data formatting | bytes 1280000 | tf_op args[1]
  1.4 0.8 dynamic_slice.12
  2.2 0.9 compare_select_fusion.refs_0_
  3.1 0.0 copy-start
  3.1 0.4 copy.21
  3.5 3.0 %collective-permute-start.1 = (bf16[800,400]{0,1:T(8,128)(2,1)S(1)}, bf16[800,400]{0,1:T(8,128)(2,1)}, u32[]{:S(2)}, u32[]{:S(2)}) collective-permute-start(bf16[800,400]{0,1:T(8,128)(2,1)S(1)} %copy.21), channel_id=1, source_target_pairs={{0,16},{8,24},{16,0},{24,8},{1,17},{9,25},{17,1},{25,9},{2,18},{10... | collective-permute-start | bytes 1920008 | tf_op jit(solution)/shard_map/ppermute | solution.py:10
  6.5 1.5 %collective-permute-start = (bf16[800,400]{0,1:T(8,128)(2,1)S(1)}, bf16[800,400]{0,1:T(8,128)(2,1)S(1)}, u32[]{:S(2)}, u32[]{:S(2)}) collective-permute-start(bf16[800,400]{0,1:T(8,128)(2,1)S(1)} %copy.21), channel_id=1, source_target_pairs={{0,8},{8,0},{16,24},{24,16},{1,9},{9,1},{17,25},{25,17},{2,10},{10... | collective-permute-start | bytes 1920008 | tf_op jit(solution)/shard_map/ppermute | solution.py:10
  8.0 14.7 %collective-permute-done.1 = bf16[800,400]{0,1:T(8,128)(2,1)} collective-permute-done((bf16[800,400]{0,1:T(8,128)(2,1)S(1)}, bf16[800,400]{0,1:T(8,128)(2,1)}, u32[]{:S(2)}, u32[]{:S(2)}) %collective-permute-start.1) | collective-permute-done | bytes 640032 | tf_op jit(solution)/shard_map/ppermute | solution.py:10
  22.7 1.4 %copy.26.refs_2_ = bf16[800,400]{1,0:T(8,128)(2,1)S(1)} copy(bf16[800,400]{0,1:T(8,128)(2,1)} %collective-permute-done.1) | data formatting | bytes 1280000 | tf_op jit(solution)/shard_map/ppermute | solution.py:10
  24.1 0.8 slice.10
  24.9 1.7 %collective-permute-start.2 = (bf16[400,400]{1,0:T(8,128)(2,1)}, bf16[400,400]{1,0:T(8,128)(2,1)S(1)}, u32[]{:S(2)}, u32[]{:S(2)}) collective-permute-start(bf16[400,400]{1,0:T(8,128)(2,1)} %slice.10), channel_id=1, source_target_pairs={{0,8},{8,0},{16,24},{24,16},{1,9},{9,1},{17,25},{25,17},{2,10},{10... | collective-permute-start | bytes 960008 | tf_op jit(solution)/shard_map/ppermute | solution.py:10
  26.6 0.3 copy.25.refs_1_
  27.0 1.6 %collective-permute-start.3 = (bf16[400,400]{1,0:T(8,128)(2,1)S(1)}, bf16[400,400]{1,0:T(8,128)(2,1)S(1)}, u32[]{:S(2)}, u32[]{:S(2)}) collective-permute-start(bf16[400,400]{1,0:T(8,128)(2,1)S(1)} %slice.11), channel_id=1, source_target_pairs={{0,16},{8,24},{16,0},{24,8},{1,17},{9,25},{17,1},{25,9},{2,18},{10... | collective-permute-start | bytes 960008 | tf_op jit(solution)/shard_map/ppermute | solution.py:10
  28.6 0.7 stack.23.off_ref
  29.2 6.5 %collective-permute-done.2.refs_3_ = bf16[400,400]{1,0:T(8,128)(2,1)S(1)} collective-permute-done((bf16[400,400]{1,0:T(8,128)(2,1)}, bf16[400,400]{1,0:T(8,128)(2,1)S(1)}, u32[]{:S(2)}, u32[]{:S(2)}) %collective-permute-start.2) | collective-permute-done | bytes 320032 | tf_op jit(solution)/shard_map/ppermute | solution.py:10
  35.8 1.3 %collective-permute-done.3.refs_4_ = bf16[400,400]{1,0:T(8,128)(2,1)S(1)} collective-permute-done((bf16[400,400]{1,0:T(8,128)(2,1)S(1)}, bf16[400,400]{1,0:T(8,128)(2,1)S(1)}, u32[]{:S(2)}, u32[]{:S(2)}) %collective-permute-start.3) | collective-permute-done | bytes 320032 | tf_op jit(solution)/shard_map/ppermute | solution.py:10
  37.1 0.8 copy-done.4
  37.9 11.9 %shard_map.55 = f32[1536,400]{1,0:T(8,128)} custom-call(s32[5]{0:T(128)} %stack.23.off_ref, bf16[1536,3200]{1,0:T(8,128)(2,1)} %a_ref.1, bf16[800,400]{1,0:T(8,128)(2,1)} %copy-done, bf16[800,400]{1,0:T(8,128)(2,1)} %copy-done.2, bf16[800,400]{1,0:T(8,128)(2,1)} %copy-done.1, bf16[400,400]{1,0:T(8,128)(2,1)} %copy-done.3, bf16[400,400]{1,0:T(8,128)(2,1)} %copy-done.4), custom_call_target="tpu_custom_call" | custom-call | tf_op jit(solution)/shard_map/pallas_call | solution.py:65
  49.8 1.5 %constant_dynamic-slice_fusion = f32[768,400]{1,0:T(8,128)S(1)} fusion(f32[1536,400]{1,0:T(8,128)} %shard_map.55, s32[]{:T(128)S(6)} %select_n.28), kind=kLoop, calls=%fused_computation.7 | loop fusion | bytes 2457604 | tf_op jit(solution)/shard_map/dynamic_slice | solution.py:77
  51.4 0.4 copy.27
  51.8 0.1 collective-permute-start.4
  51.9 2.9 %collective-permute-done.4 = f32[768,400]{0,1:T(8,128)S(1)} collective-permute-done((f32[768,400]{0,1:T(8,128)S(1)}, f32[768,400]{0,1:T(8,128)S(1)}, u32[]{:S(2)}, u32[]{:S(2)}) %collective-permute-start.4) | collective-permute-done | bytes 1228832 | tf_op jit(solution)/shard_map/ppermute | solution.py:10
  54.8 0.5 copy.28
  55.2 1.8 %dynamic-slice_add_fusion = f32[768,400]{1,0:T(8,128)S(1)} fusion(f32[768,400]{1,0:T(8,128)S(1)} %copy.28, f32[1536,400]{1,0:T(8,128)} %shard_map.55, s32[]{:T(128)S(6)} %select_n.27), kind=kLoop, calls=%fused_computation.3 | loop fusion | flops 307200 | bytes 3686404 | tf_op jit(solution)/shard_map/add | solution.py:78
  57.0 0.4 copy.29
  57.4 1.6 %collective-permute-start.5 = (f32[768,400]{0,1:T(8,128)S(1)}, f32[768,400]{0,1:T(8,128)}, u32[]{:S(2)}, u32[]{:S(2)}) collective-permute-start(f32[768,400]{0,1:T(8,128)S(1)} %copy.29), channel_id=1, source_target_pairs={{0,16},{8,24},{16,0},{24,8},{1,17},{9,25},{17,1},{25,9},{2,18},{10... | collective-permute-start | bytes 3686408 | tf_op jit(solution)/shard_map/ppermute | solution.py:10
  59.0 0.8 compare_and_fusion
  59.8 26.9 %collective-permute-done.5 = f32[768,400]{0,1:T(8,128)} collective-permute-done((f32[768,400]{0,1:T(8,128)S(1)}, f32[768,400]{0,1:T(8,128)}, u32[]{:S(2)}, u32[]{:S(2)}) %collective-permute-start.5) | collective-permute-done | bytes 1228832 | tf_op jit(solution)/shard_map/ppermute | solution.py:10
  86.6 1.8 %copy.30 = f32[768,400]{1,0:T(8,128)S(1)} copy(f32[768,400]{0,1:T(8,128)} %collective-permute-done.5) | data formatting | bytes 2457600 | tf_op jit(solution)/shard_map/ppermute | solution.py:10
  88.4 3.1 %gather_fusion = f32[768,400]{1,0:T(8,128)} fusion(f32[768,400]{1,0:T(8,128)S(1)} %copy.30, s32[1024]{0:T(1024)S(1)} %pad_clamp_fusion), kind=kCustom, calls=%fused_computation | custom fusion | bytes 2460672 | tf_op jit(solution)/shard_map/jit(_take)/gather | solution.py:100
  91.5 1.6 %select_subtract_fusion = f32[768,400]{1,0:T(8,128)S(1)} fusion(f32[768,400]{1,0:T(8,128)S(1)} %dynamic-slice_add_fusion, f32[768,400]{1,0:T(8,128)} %gather_fusion, pred[768]{0:T(1024)(128)(4,1)S(1)} %get-tuple-element.5), kind=kLoop, calls=%fused_computation.2 | loop fusion | flops 614400 | bytes 3687168 | tf_op jit(solution)/shard_map/sub | solution.py:100
  93.1 1.5 %copy.31 = f32[768,400]{0,1:T(8,128)} copy(f32[768,400]{1,0:T(8,128)S(1)} %select_subtract_fusion) | data formatting | bytes 2457600 | tf_op jit(solution)/shard_map/sub | solution.py:100
  (11 shorter events, 0.1 us)
Async XLA Ops:
  3.1 21.8 %copy-start = (bf16[800,400]{1,0:T(8,128)(2,1)}, bf16[800,400]{1,0:T(8,128)(2,1)S(1)}, u32[]{:S(2)}) copy-start(bf16[800,400]{1,0:T(8,128)(2,1)S(1)} %compare_select_fusion.refs_0_) | copy-start | bytes 1920004
  3.5 19.2 %collective-permute-start.1 = (bf16[800,400]{0,1:T(8,128)(2,1)S(1)}, bf16[800,400]{0,1:T(8,128)(2,1)}, u32[]{:S(2)}, u32[]{:S(2)}) collective-permute-start(bf16[800,400]{0,1:T(8,128)(2,1)S(1)} %copy.21), channel_id=1, source_target_pairs={{0,16},{8,24},{16,0},{24,8},{1,17},{9,25},{17,1},{25,9},{2,18},{10... | collective-permute-start | bytes 1920008 | tf_op jit(solution)/shard_map/ppermute | solution.py:10
  6.5 20.1 %collective-permute-start = (bf16[800,400]{0,1:T(8,128)(2,1)S(1)}, bf16[800,400]{0,1:T(8,128)(2,1)S(1)}, u32[]{:S(2)}, u32[]{:S(2)}) collective-permute-start(bf16[800,400]{0,1:T(8,128)(2,1)S(1)} %copy.21), channel_id=1, source_target_pairs={{0,8},{8,0},{16,24},{24,16},{1,9},{9,1},{17,25},{25,17},{2,10},{10... | collective-permute-start | bytes 1920008 | tf_op jit(solution)/shard_map/ppermute | solution.py:10
  24.1 2.9 %copy-start.1 = (bf16[800,400]{1,0:T(8,128)(2,1)}, bf16[800,400]{1,0:T(8,128)(2,1)S(1)}, u32[]{:S(2)}) copy-start(bf16[800,400]{1,0:T(8,128)(2,1)S(1)} %copy.26.refs_2_) | copy-start | bytes 1920004
  24.9 10.9 %collective-permute-start.2 = (bf16[400,400]{1,0:T(8,128)(2,1)}, bf16[400,400]{1,0:T(8,128)(2,1)S(1)}, u32[]{:S(2)}, u32[]{:S(2)}) collective-permute-start(bf16[400,400]{1,0:T(8,128)(2,1)} %slice.10), channel_id=1, source_target_pairs={{0,8},{8,0},{16,24},{24,16},{1,9},{9,1},{17,25},{25,17},{2,10},{10... | collective-permute-start | bytes 960008 | tf_op jit(solution)/shard_map/ppermute | solution.py:10
  26.9 10.2 %copy-start.2 = (bf16[800,400]{1,0:T(8,128)(2,1)}, bf16[800,400]{1,0:T(8,128)(2,1)S(1)}, u32[]{:S(2)}) copy-start(bf16[800,400]{1,0:T(8,128)(2,1)S(1)} %copy.25.refs_1_) | copy-start | bytes 1920004
  27.0 10.1 %collective-permute-start.3 = (bf16[400,400]{1,0:T(8,128)(2,1)S(1)}, bf16[400,400]{1,0:T(8,128)(2,1)S(1)}, u32[]{:S(2)}, u32[]{:S(2)}) collective-permute-start(bf16[400,400]{1,0:T(8,128)(2,1)S(1)} %slice.11), channel_id=1, source_target_pairs={{0,16},{8,24},{16,0},{24,8},{1,17},{9,25},{17,1},{25,9},{2,18},{10... | collective-permute-start | bytes 960008 | tf_op jit(solution)/shard_map/ppermute | solution.py:10
  35.8 1.3 %copy-start.3 = (bf16[400,400]{1,0:T(8,128)(2,1)}, bf16[400,400]{1,0:T(8,128)(2,1)S(1)}, u32[]{:S(2)}) copy-start(bf16[400,400]{1,0:T(8,128)(2,1)S(1)} %collective-permute-done.2.refs_3_) | copy-start | bytes 960004
  37.1 0.8 copy-start.4
  51.8 3.0 %collective-permute-start.4 = (f32[768,400]{0,1:T(8,128)S(1)}, f32[768,400]{0,1:T(8,128)S(1)}, u32[]{:S(2)}, u32[]{:S(2)}) collective-permute-start(f32[768,400]{0,1:T(8,128)S(1)} %copy.27), channel_id=1, source_target_pairs={{0,1},{1,0},{2,3},{3,2},{4,5},{5,4},{6,7},{7,6},{8,9},{9,8},{10,11... | collective-permute-start | bytes 3686408 | tf_op jit(solution)/shard_map/ppermute | solution.py:10
  57.4 29.2 %collective-permute-start.5 = (f32[768,400]{0,1:T(8,128)S(1)}, f32[768,400]{0,1:T(8,128)}, u32[]{:S(2)}, u32[]{:S(2)}) collective-permute-start(f32[768,400]{0,1:T(8,128)S(1)} %copy.29), channel_id=1, source_target_pairs={{0,16},{8,24},{16,0},{24,8},{1,17},{9,25},{17,1},{25,9},{2,18},{10... | collective-permute-start | bytes 3686408 | tf_op jit(solution)/shard_map/ppermute | solution.py:10

commit v3 on v2

--- a/solution.py
+++ b/solution.py
@@ -84,20 +84,26 @@
     cuts_count = lax.axis_size("cuts")
     prow_idx = lax.axis_index("prow")
     cuts_idx = lax.axis_index("cuts")
-    count = integrals.shape[0]
+    count, cols = integrals.shape
     labels = lax.dynamic_slice(irrep_rows, ((cuts_idx * prow_count + prow_idx) * count,), (count,))
     same = labels[:, None] == irrep_cols[None, :]
     blocked = jnp.where(same, integrals, jnp.zeros_like(integrals))
-    terms = contract(amplitudes, gather_prow(blocked, prow_idx, prow_count))
-    cycle = reduce_cuts(terms, cuts_idx, cuts_count)
-    block_rows = cycle.shape[0]
+    block_rows = amplitudes.shape[0] // cuts_count
     half = prow_count // 2
     own_block = prow_idx * cuts_count + cuts_idx
     partner_block = jnp.bitwise_xor(prow_idx, half) * cuts_count + cuts_idx
     mine = lax.dynamic_slice(mirror_row, (own_block * block_rows,), (block_rows,))
     local = mine - partner_block * block_rows
-    fetched = swap(cycle, "prow", half)
-    return cycle - jnp.take(fetched, local, axis=0)
+    chunks = 2 if cols % 16 == 0 else 1
+    width = cols // chunks
+    results = []
+    for j in range(chunks):
+        part = blocked[:, j * width:(j + 1) * width]
+        terms = contract(amplitudes, gather_prow(part, prow_idx, prow_count))
+        cycle = reduce_cuts(terms, cuts_idx, cuts_count)
+        fetched = swap(cycle, "prow", half)
+        results.append(cycle - jnp.take(fetched, local, axis=0))
+    return jnp.concatenate(results, axis=1) if chunks > 1 else results[0]
 
 
 def solution(mesh):

time: 95.1 us -> 97.6 us (1.026)
  waiting for transfers between devices: 52.3 us -> 31.2 us
  local copies, waits for them, and re-layouts: 15.8 us -> 27.3 us
  Pallas kernels: 11.9 us -> 18.6 us
  starting transfers between devices: 9.41 us -> 14.8 us
    ppermute x6 -> x12, waiting for transfers between devices: 52.3 us -> 31.2 us  [swap(): lax.ppermute(value, axis, [(i, i ^ mask) for i in range(lax.axis_size(axi...]
    pallas_call x1 -> x2, Pallas kernels: 11.9 us -> 18.6 us  [contract(): pl.pallas_call(kernel, grid_spec=grid_spec, out_shape=jax.ShapeDtypeStruc...]
    ppermute x6 -> x12, starting transfers between devices: 9.41 us -> 14.8 us  [swap(): lax.ppermute(value, axis, [(i, i ^ mask) for i in range(lax.axis_size(axi...]
    ppermute x4, local copies, waits for them, and re-layouts: 3.9 us -> 6.23 us  [swap(): lax.ppermute(value, axis, [(i, i ^ mask) for i in range(lax.axis_size(axi...]
    gather x1 -> x2, local copies, waits for them, and re-layouts: 3.12 us -> 5.03 us  [shards(): results.append(cycle - jnp.take(fetched, local, axis=0))]
    unnamed x11 -> x25, local copies, waits for them, and re-layouts: 2.18 us -> 4.09 us
    dynamic_slice x2 -> x4, local copies, waits for them, and re-layouts: 1.97 us -> 3.71 us  [reduce_cuts(): lax.dynamic_slice_in_dim(terms, jnp.bitwise_xor(cuts_idx, s) * rows, rows...]
    add x1 -> x2, local copies, waits for them, and re-layouts: 0.43 us -> 2.17 us  [reduce_cuts(): total = total + swap(part, 'cuts', s)]
  transfers between devices with their start and end apart: 6 -> 12, of which waited for: 5 -> 5; matrix products, arithmetic and copies ran while one was open for 4% -> 19% of each run, Pallas kernels for 0% -> 19%
where the time goes in v3:
time: 97.6 us; the launch traced here: 96.9 us
  waiting for transfers between devices  31.2 us (32%)
  local copies, waits for them, and re-layouts  27.3 us (28%)
  Pallas kernels  18.6 us (19%)
  starting transfers between devices  14.8 us (15%)
  other arithmetic  4.78 us (5%)
    ppermute x12, waiting for transfers between devices, swap(): lax.ppermute(value, axis, [(i, i ^ mask) for i in range(lax.axis_size(axi...  31.2 us
    pallas_call x2, Pallas kernels, contract(): pl.pallas_call(kernel, grid_spec=grid_spec, out_shape=jax.ShapeDtypeStruc...  18.6 us
    ppermute x12, starting transfers between devices, swap(): lax.ppermute(value, axis, [(i, i ^ mask) for i in range(lax.axis_size(axi...  14.8 us
    ppermute x4, local copies, waits for them, and re-layouts, swap(): lax.ppermute(value, axis, [(i, i ^ mask) for i in range(lax.axis_size(axi...  6.23 us
    gather x2, local copies, waits for them, and re-layouts, shards(): results.append(cycle - jnp.take(fetched, local, axis=0))  5.03 us
    unnamed x25, local copies, waits for them, and re-layouts  4.09 us
    dynamic_slice x4, local copies, waits for them, and re-layouts, reduce_cuts(): lax.dynamic_slice_in_dim(terms, jnp.bitwise_xor(cuts_idx, s) * rows, rows...  3.71 us
    add x2, local copies, waits for them, and re-layouts, reduce_cuts(): total = total + swap(part, 'cuts', s)  2.17 us
  transfers between devices with their start and end apart: 12, of which 5 were waited for; matrix products, arithmetic and copies ran while one was open for 19% of the time, Pallas kernels for 19%

profile of v3, /device:TPU:0, one launch (start us, length us, event | category | flops | bytes accessed | tf_op | source)
XLA Modules:
  0.0 96.9 jit_solution(9666538540347343526)
XLA Ops:
  0.0 1.4 %copy.8 = bf16[800,400]{1,0:T(8,128)(2,1)S(1)} copy(bf16[800,400]{0,1:T(8,128)(2,1)} %param.8) | data formatting | bytes 1280000 | tf_op args[1]
  1.4 0.8 dynamic_slice.18
  2.2 0.9 compare_select_fusion
  3.3 3.0 %collective-permute-start.7 = (bf16[800,200]{1,0:T(8,128)(2,1)S(1)}, bf16[800,200]{1,0:T(8,128)(2,1)S(1)}, u32[]{:S(2)}, u32[]{:S(2)}) collective-permute-start(bf16[800,200]{1,0:T(8,128)(2,1)S(1)} %get-tuple-element.9.refs_0_), channel_id=1, source_target_pairs={{0,16},{8,24},{16,0},{24,8},{1,17},{9,25},{17,1},{25,9},{2,18},{10... | collective-permute-start | bytes 960008 | tf_op jit(solution)/shard_map/ppermute | solution.py:10
  6.4 1.5 %collective-permute-start.6 = (bf16[800,200]{1,0:T(8,128)(2,1)S(1)}, bf16[800,200]{1,0:T(8,128)(2,1)S(1)}, u32[]{:S(2)}, u32[]{:S(2)}) collective-permute-start(bf16[800,200]{1,0:T(8,128)(2,1)S(1)} %get-tuple-element.9.refs_0_), channel_id=1, source_target_pairs={{0,8},{8,0},{16,24},{24,16},{1,9},{9,1},{17,25},{25,17},{2,10},{10... | collective-permute-start | bytes 960008 | tf_op jit(solution)/shard_map/ppermute | solution.py:10
  8.5 8.2 %collective-permute-done.7.refs_2_ = bf16[800,200]{1,0:T(8,128)(2,1)S(1)} collective-permute-done((bf16[800,200]{1,0:T(8,128)(2,1)S(1)}, bf16[800,200]{1,0:T(8,128)(2,1)S(1)}, u32[]{:S(2)}, u32[]{:S(2)}) %collective-permute-start.7) | collective-permute-done | bytes 320032 | tf_op jit(solution)/shard_map/ppermute | solution.py:10
  17.4 2.0 %collective-permute-start.8 = (bf16[400,200]{1,0:T(8,128)(2,1)}, bf16[400,200]{1,0:T(8,128)(2,1)S(1)}, u32[]{:S(2)}, u32[]{:S(2)}) collective-permute-start(bf16[400,200]{1,0:T(8,128)(2,1)} %slice.32), channel_id=1, source_target_pairs={{0,8},{8,0},{16,24},{24,16},{1,9},{9,1},{17,25},{25,17},{2,10},{10... | collective-permute-start | bytes 480008 | tf_op jit(solution)/shard_map/ppermute | solution.py:10
  20.2 1.5 %collective-permute-start.9 = (bf16[400,200]{1,0:T(8,128)(2,1)}, bf16[400,200]{1,0:T(8,128)(2,1)S(1)}, u32[]{:S(2)}, u32[]{:S(2)}) collective-permute-start(bf16[400,200]{1,0:T(8,128)(2,1)} %slice.33), channel_id=1, source_target_pairs={{0,16},{8,24},{16,0},{24,8},{1,17},{9,25},{17,1},{25,9},{2,18},{10... | collective-permute-start | bytes 480008 | tf_op jit(solution)/shard_map/ppermute | solution.py:10
  22.3 3.1 %collective-permute-done.1.refs_2_ = bf16[800,200]{1,0:T(8,128)(2,1)S(1)} collective-permute-done((bf16[800,200]{1,0:T(8,128)(2,1)S(1)}, bf16[800,200]{1,0:T(8,128)(2,1)S(1)}, u32[]{:S(2)}, u32[]{:S(2)}) %collective-permute-start.1) | collective-permute-done | bytes 320032 | tf_op jit(solution)/shard_map/ppermute | solution.py:10
  26.2 2.0 %collective-permute-start.2 = (bf16[400,200]{1,0:T(8,128)(2,1)}, bf16[400,200]{1,0:T(8,128)(2,1)S(1)}, u32[]{:S(2)}, u32[]{:S(2)}) collective-permute-start(bf16[400,200]{1,0:T(8,128)(2,1)} %slice.29), channel_id=1, source_target_pairs={{0,8},{8,0},{16,24},{24,16},{1,9},{9,1},{17,25},{25,17},{2,10},{10... | collective-permute-start | bytes 480008 | tf_op jit(solution)/shard_map/ppermute | solution.py:10
  29.0 1.5 %collective-permute-start.3 = (bf16[400,200]{1,0:T(8,128)(2,1)}, bf16[400,200]{1,0:T(8,128)(2,1)S(1)}, u32[]{:S(2)}, u32[]{:S(2)}) collective-permute-start(bf16[400,200]{1,0:T(8,128)(2,1)} %slice.30), channel_id=1, source_target_pairs={{0,16},{8,24},{16,0},{24,8},{1,17},{9,25},{17,1},{25,9},{2,18},{10... | collective-permute-start | bytes 480008 | tf_op jit(solution)/shard_map/ppermute | solution.py:10
  30.5 1.4 %collective-permute-done.8.refs_3_ = bf16[400,200]{1,0:T(8,128)(2,1)S(1)} collective-permute-done((bf16[400,200]{1,0:T(8,128)(2,1)}, bf16[400,200]{1,0:T(8,128)(2,1)S(1)}, u32[]{:S(2)}, u32[]{:S(2)}) %collective-permute-start.8) | collective-permute-done | bytes 160032 | tf_op jit(solution)/shard_map/ppermute | solution.py:10
  33.3 9.3 %shard_map.56 = f32[1536,200]{1,0:T(8,128)} custom-call(s32[5]{0:T(128)} %stack.29.off_ref, bf16[1536,3200]{1,0:T(8,128)(2,1)} %a_ref.3, bf16[800,200]{1,0:T(8,128)(2,1)} %copy-done.3, bf16[800,200]{1,0:T(8,128)(2,1)} %copy-done.7, bf16[800,200]{1,0:T(8,128)(2,1)} %copy-done.6, bf16[400,200]{1,0:T(8,128)(2,1)} %copy-done.8, bf16[400,200]{1,0:T(8,128)(2,1)} %copy-done.9), custom_call_target="tpu_custom_call" | custom-call | tf_op jit(solution)/shard_map/pallas_call | solution.py:65
  42.6 1.2 %constant_dynamic-slice_fusion = f32[768,200]{1,0:T(8,128)S(1)} fusion(f32[1536,200]{1,0:T(8,128)} %shard_map.56, s32[]{:T(128)S(6)} %select_n.28), kind=kLoop, calls=%fused_computation.11 | loop fusion | bytes 1228804 | tf_op jit(solution)/shard_map/dynamic_slice | solution.py:77
  45.5 9.3 %shard_map.55 = f32[1536,200]{1,0:T(8,128)} custom-call(s32[5]{0:T(128)} %stack.29.off_ref, bf16[1536,3200]{1,0:T(8,128)(2,1)} %a_ref.3, bf16[800,200]{1,0:T(8,128)(2,1)} %copy-done.2, bf16[800,200]{1,0:T(8,128)(2,1)} %copy-done.5, bf16[800,200]{1,0:T(8,128)(2,1)} %copy-done.4, bf16[400,200]{1,0:T(8,128)(2,1)} %copy-done.10, bf16[400,200]{1,0:T(8,128)(2,1)} %copy-done.11), custom_call_target="tpu_custom_call" | custom-call | tf_op jit(solution)/shard_map/pallas_call | solution.py:65
  54.8 1.2 %constant_dynamic-slice_fusion.1 = f32[768,200]{1,0:T(8,128)S(1)} fusion(f32[1536,200]{1,0:T(8,128)} %shard_map.55, s32[]{:T(128)S(6)} %select_n.28), kind=kLoop, calls=%fused_computation.12 | loop fusion | bytes 1228804 | tf_op jit(solution)/shard_map/dynamic_slice | solution.py:77
  56.0 1.1 %copy.9 = f32[768,200]{0,1:T(8,128)} copy(f32[768,200]{1,0:T(8,128)S(1)} %constant_dynamic-slice_fusion.1) | data formatting | bytes 1228800 | tf_op jit(solution)/shard_map/dynamic_slice | solution.py:77
  57.5 1.3 %copy.14 = f32[768,200]{1,0:T(8,128)S(1)} copy(f32[768,200]{0,1:T(8,128)} %collective-permute-done.10) | data formatting | bytes 1228800 | tf_op jit(solution)/shard_map/ppermute | solution.py:10
  59.0 1.1 %copy.15 = f32[768,200]{0,1:T(8,128)} copy(f32[768,200]{1,0:T(8,128)S(1)} %dynamic-slice_add_fusion) | data formatting | bytes 1228800 | tf_op jit(solution)/shard_map/add | solution.py:78
  60.2 2.2 %copy.10 = f32[768,200]{1,0:T(8,128)} copy(f32[768,200]{0,1:T(8,128)} %collective-permute-done.4) | data formatting | bytes 1228800 | tf_op jit(solution)/shard_map/ppermute | solution.py:10
  62.4 1.2 %dynamic-slice_add_fusion.1 = f32[768,200]{1,0:T(8,128)S(1)} fusion(f32[768,200]{1,0:T(8,128)} %copy.10, f32[1536,200]{1,0:T(8,128)S(1)} %copy-done.1, s32[]{:T(128)S(6)} %select_n.27), kind=kLoop, calls=%fused_computation.7 | loop fusion | flops 153600 | bytes 1843204 | tf_op jit(solution)/shard_map/add | solution.py:78
  63.6 1.1 %copy.11 = f32[768,200]{0,1:T(8,128)} copy(f32[768,200]{1,0:T(8,128)S(1)} %dynamic-slice_add_fusion.1) | data formatting | bytes 1228800 | tf_op jit(solution)/shard_map/add | solution.py:78
  64.7 2.0 %collective-permute-start.5 = (f32[768,200]{0,1:T(8,128)}, f32[768,200]{0,1:T(8,128)}, u32[]{:S(2)}, u32[]{:S(2)}) collective-permute-start(f32[768,200]{0,1:T(8,128)} %copy.11), channel_id=1, source_target_pairs={{0,16},{8,24},{16,0},{24,8},{1,17},{9,25},{17,1},{25,9},{2,18},{10... | collective-permute-start | bytes 1843208 | tf_op jit(solution)/shard_map/ppermute | solution.py:10
  66.7 0.8 compare_and_fusion
  67.5 9.7 %collective-permute-done.11 = f32[768,200]{0,1:T(8,128)} collective-permute-done((f32[768,200]{0,1:T(8,128)}, f32[768,200]{0,1:T(8,128)}, u32[]{:S(2)}, u32[]{:S(2)}) %collective-permute-start.11) | collective-permute-done | bytes 614432 | tf_op jit(solution)/shard_map/ppermute | solution.py:10
  77.1 1.3 %copy.16 = f32[768,200]{1,0:T(8,128)S(1)} copy(f32[768,200]{0,1:T(8,128)} %collective-permute-done.11) | data formatting | bytes 1228800 | tf_op jit(solution)/shard_map/ppermute | solution.py:10
  78.5 2.1 %gather_fusion.1 = f32[768,200]{1,0:T(8,128)S(1)} fusion(f32[768,200]{1,0:T(8,128)S(1)} %copy.16, s32[1024]{0:T(1024)S(1)} %pad_clamp_fusion), kind=kCustom, calls=%fused_computation.1.clone | custom fusion | bytes 1231872 | tf_op jit(solution)/shard_map/jit(_take)/gather | solution.py:105
  80.6 8.8 %collective-permute-done.5 = f32[768,200]{0,1:T(8,128)} collective-permute-done((f32[768,200]{0,1:T(8,128)}, f32[768,200]{0,1:T(8,128)}, u32[]{:S(2)}, u32[]{:S(2)}) %collective-permute-start.5) | collective-permute-done | bytes 614432 | tf_op jit(solution)/shard_map/ppermute | solution.py:10
  89.4 1.3 %copy.12 = f32[768,200]{1,0:T(8,128)S(1)} copy(f32[768,200]{0,1:T(8,128)} %collective-permute-done.5) | data formatting | bytes 1228800 | tf_op jit(solution)/shard_map/ppermute | solution.py:10
  90.7 2.9 %gather_fusion = f32[768,200]{1,0:T(8,128)} fusion(f32[768,200]{1,0:T(8,128)S(1)} %copy.12, s32[1024]{0:T(1024)S(1)} %pad_clamp_fusion), kind=kCustom, calls=%fused_computation.clone | custom fusion | bytes 1231872 | tf_op jit(solution)/shard_map/jit(_take)/gather | solution.py:105
  93.6 1.3 %select_subtract_fusion.1 = (f32[768,200]{1,0:T(8,128)S(1)}, f32[768,200]{1,0:T(8,128)S(1)}) fusion(f32[768,200]{1,0:T(8,128)S(1)} %dynamic-slice_add_fusion.1, f32[768,200]{1,0:T(8,128)} %gather_fusion, pred[768]{0:T(1024)(128)(4,1)S(1)} %get-tuple-element.6, f32[768,200]{1,0:T(8,128)S(1)} %dynamic-slice_add_fusion, f32[768,200]{1,0:T(8,128)S(1)} %gather_fusion.1), kind=kLoop, calls=%fused_computation.5 | loop fusion | flops 614400 | bytes 3687168 | tf_op jit(solution)/shard_map/sub | solution.py:105
  95.4 1.5 %copy.17 = f32[768,400]{0,1:T(8,128)} copy(f32[768,400]{1,0:T(8,128)S(1)} %pad_maximum_fusion) | data formatting | bytes 2457600 | tf_op jit(solution)/shard_map/concatenate | solution.py:106
  (46 shorter events, 8.4 us)
Async XLA Ops:
  3.3 28.6 %copy-start.3 = (bf16[800,200]{1,0:T(8,128)(2,1)}, bf16[800,200]{1,0:T(8,128)(2,1)S(1)}, u32[]{:S(2)}) copy-start(bf16[800,200]{1,0:T(8,128)(2,1)S(1)} %get-tuple-element.9.refs_0_) | copy-start | bytes 960004
  3.3 39.3 %copy-start.2 = (bf16[800,200]{1,0:T(8,128)(2,1)}, bf16[800,200]{1,0:T(8,128)(2,1)S(1)}, u32[]{:S(2)}) copy-start(bf16[800,200]{1,0:T(8,128)(2,1)S(1)} %get-tuple-element.8.refs_0_) | copy-start | bytes 960004
  3.3 13.3 %collective-permute-start.7 = (bf16[800,200]{1,0:T(8,128)(2,1)S(1)}, bf16[800,200]{1,0:T(8,128)(2,1)S(1)}, u32[]{:S(2)}, u32[]{:S(2)}) collective-permute-start(bf16[800,200]{1,0:T(8,128)(2,1)S(1)} %get-tuple-element.9.refs_0_), channel_id=1, source_target_pairs={{0,16},{8,24},{16,0},{24,8},{1,17},{9,25},{17,1},{25,9},{2,18},{10... | collective-permute-start | bytes 960008 | tf_op jit(solution)/shard_map/ppermute | solution.py:10
  6.4 13.1 %collective-permute-start.6 = (bf16[800,200]{1,0:T(8,128)(2,1)S(1)}, bf16[800,200]{1,0:T(8,128)(2,1)S(1)}, u32[]{:S(2)}, u32[]{:S(2)}) collective-permute-start(bf16[800,200]{1,0:T(8,128)(2,1)S(1)} %get-tuple-element.9.refs_0_), channel_id=1, source_target_pairs={{0,8},{8,0},{16,24},{24,16},{1,9},{9,1},{17,25},{25,17},{2,10},{10... | collective-permute-start | bytes 960008 | tf_op jit(solution)/shard_map/ppermute | solution.py:10
  7.8 17.6 %collective-permute-start.1 = (bf16[800,200]{1,0:T(8,128)(2,1)S(1)}, bf16[800,200]{1,0:T(8,128)(2,1)S(1)}, u32[]{:S(2)}, u32[]{:S(2)}) collective-permute-start(bf16[800,200]{1,0:T(8,128)(2,1)S(1)} %get-tuple-element.8.refs_0_), channel_id=1, source_target_pairs={{0,16},{8,24},{16,0},{24,8},{1,17},{9,25},{17,1},{25,9},{2,18},{10... | collective-permute-start | bytes 960008 | tf_op jit(solution)/shard_map/ppermute | solution.py:10
  8.4 19.9 %collective-permute-start = (bf16[800,200]{1,0:T(8,128)(2,1)S(1)}, bf16[800,200]{1,0:T(8,128)(2,1)S(1)}, u32[]{:S(2)}, u32[]{:S(2)}) collective-permute-start(bf16[800,200]{1,0:T(8,128)(2,1)S(1)} %get-tuple-element.8.refs_0_), channel_id=1, source_target_pairs={{0,8},{8,0},{16,24},{24,16},{1,9},{9,1},{17,25},{25,17},{2,10},{10... | collective-permute-start | bytes 960008 | tf_op jit(solution)/shard_map/ppermute | solution.py:10
  16.7 15.3 %copy-start.6 = (bf16[800,200]{1,0:T(8,128)(2,1)}, bf16[800,200]{1,0:T(8,128)(2,1)S(1)}, u32[]{:S(2)}) copy-start(bf16[800,200]{1,0:T(8,128)(2,1)S(1)} %collective-permute-done.7.refs_2_) | copy-start | bytes 960004
  17.4 14.5 %collective-permute-start.8 = (bf16[400,200]{1,0:T(8,128)(2,1)}, bf16[400,200]{1,0:T(8,128)(2,1)S(1)}, u32[]{:S(2)}, u32[]{:S(2)}) collective-permute-start(bf16[400,200]{1,0:T(8,128)(2,1)} %slice.32), channel_id=1, source_target_pairs={{0,8},{8,0},{16,24},{24,16},{1,9},{9,1},{17,25},{25,17},{2,10},{10... | collective-permute-start | bytes 480008 | tf_op jit(solution)/shard_map/ppermute | solution.py:10
  19.4 12.5 %copy-start.7 = (bf16[800,200]{1,0:T(8,128)(2,1)}, bf16[800,200]{1,0:T(8,128)(2,1)S(1)}, u32[]{:S(2)}) copy-start(bf16[800,200]{1,0:T(8,128)(2,1)S(1)} %collective-permute-done.6.refs_1_) | copy-start | bytes 960004
  20.2 11.8 %collective-permute-start.9 = (bf16[400,200]{1,0:T(8,128)(2,1)}, bf16[400,200]{1,0:T(8,128)(2,1)S(1)}, u32[]{:S(2)}, u32[]{:S(2)}) collective-permute-start(bf16[400,200]{1,0:T(8,128)(2,1)} %slice.33), channel_id=1, source_target_pairs={{0,16},{8,24},{16,0},{24,8},{1,17},{9,25},{17,1},{25,9},{2,18},{10... | collective-permute-start | bytes 480008 | tf_op jit(solution)/shard_map/ppermute | solution.py:10
  25.4 17.2 %copy-start.4 = (bf16[800,200]{1,0:T(8,128)(2,1)}, bf16[800,200]{1,0:T(8,128)(2,1)S(1)}, u32[]{:S(2)}) copy-start(bf16[800,200]{1,0:T(8,128)(2,1)S(1)} %collective-permute-done.1.refs_2_) | copy-start | bytes 960004
  26.2 17.9 %collective-permute-start.2 = (bf16[400,200]{1,0:T(8,128)(2,1)}, bf16[400,200]{1,0:T(8,128)(2,1)S(1)}, u32[]{:S(2)}, u32[]{:S(2)}) collective-permute-start(bf16[400,200]{1,0:T(8,128)(2,1)} %slice.29), channel_id=1, source_target_pairs={{0,8},{8,0},{16,24},{24,16},{1,9},{9,1},{17,25},{25,17},{2,10},{10... | collective-permute-start | bytes 480008 | tf_op jit(solution)/shard_map/ppermute | solution.py:10
  28.2 14.4 %copy-start.5 = (bf16[800,200]{1,0:T(8,128)(2,1)}, bf16[800,200]{1,0:T(8,128)(2,1)S(1)}, u32[]{:S(2)}) copy-start(bf16[800,200]{1,0:T(8,128)(2,1)S(1)} %collective-permute-done.refs_1_) | copy-start | bytes 960004
  29.0 15.2 %collective-permute-start.3 = (bf16[400,200]{1,0:T(8,128)(2,1)}, bf16[400,200]{1,0:T(8,128)(2,1)S(1)}, u32[]{:S(2)}, u32[]{:S(2)}) collective-permute-start(bf16[400,200]{1,0:T(8,128)(2,1)} %slice.30), channel_id=1, source_target_pairs={{0,16},{8,24},{16,0},{24,8},{1,17},{9,25},{17,1},{25,9},{2,18},{10... | collective-permute-start | bytes 480008 | tf_op jit(solution)/shard_map/ppermute | solution.py:10
  31.9 0.7 copy-start.8
  32.6 0.7 copy-start.9
  44.1 13.5 %collective-permute-start.10 = (f32[768,200]{0,1:T(8,128)S(1)}, f32[768,200]{0,1:T(8,128)}, u32[]{:S(2)}, u32[]{:S(2)}) collective-permute-start(f32[768,200]{0,1:T(8,128)S(1)} %copy.13), channel_id=1, source_target_pairs={{0,1},{1,0},{2,3},{3,2},{4,5},{5,4},{6,7},{7,6},{8,9},{9,8},{10,11... | collective-permute-start | bytes 1843208 | tf_op jit(solution)/shard_map/ppermute | solution.py:10
  44.1 0.7 copy-start.10
  44.8 0.7 copy-start.11
  56.0 2.9 %copy-start = (f32[1536,200]{1,0:T(8,128)S(1)}, f32[1536,200]{1,0:T(8,128)}, u32[]{:S(2)}) copy-start(f32[1536,200]{1,0:T(8,128)} %shard_map.56) | copy-start | bytes 3686404
  57.1 3.1 %collective-permute-start.4 = (f32[768,200]{0,1:T(8,128)}, f32[768,200]{0,1:T(8,128)}, u32[]{:S(2)}, u32[]{:S(2)}) collective-permute-start(f32[768,200]{0,1:T(8,128)} %copy.9), channel_id=1, source_target_pairs={{0,1},{1,0},{2,3},{3,2},{4,5},{5,4},{6,7},{7,6},{8,9},{9,8},{10,11... | collective-permute-start | bytes 1843208 | tf_op jit(solution)/shard_map/ppermute | solution.py:10
  59.0 3.4 %copy-start.1 = (f32[1536,200]{1,0:T(8,128)S(1)}, f32[1536,200]{1,0:T(8,128)}, u32[]{:S(2)}) copy-start(f32[1536,200]{1,0:T(8,128)} %shard_map.55) | copy-start | bytes 3686404
  60.1 17.0 %collective-permute-start.11 = (f32[768,200]{0,1:T(8,128)}, f32[768,200]{0,1:T(8,128)}, u32[]{:S(2)}, u32[]{:S(2)}) collective-permute-start(f32[768,200]{0,1:T(8,128)} %copy.15), channel_id=1, source_target_pairs={{0,16},{8,24},{16,0},{24,8},{1,17},{9,25},{17,1},{25,9},{2,18},{10... | collective-permute-start | bytes 1843208 | tf_op jit(solution)/shard_map/ppermute | solution.py:10
  64.7 24.7 %collective-permute-start.5 = (f32[768,200]{0,1:T(8,128)}, f32[768,200]{0,1:T(8,128)}, u32[]{:S(2)}, u32[]{:S(2)}) collective-permute-start(f32[768,200]{0,1:T(8,128)} %copy.11), channel_id=1, source_target_pairs={{0,16},{8,24},{16,0},{24,8},{1,17},{9,25},{17,1},{25,9},{2,18},{10... | collective-permute-start | bytes 1843208 | tf_op jit(solution)/shard_map/ppermute | solution.py:10

commit v4 on v3

--- a/solution.py
+++ b/solution.py
@@ -27,47 +27,43 @@
     return blocks
 
 
-def contract(amplitudes, blocks):
-    rows, width = amplitudes.shape
+def assemble(blocks, width):
     cols = blocks[0][0].shape[1]
+    dtype = blocks[0][0].dtype
     n = len(blocks)
     counts = [b.shape[0] for b, _ in blocks]
     if any(c % 16 for c in counts):
-        piece = jnp.zeros((width, cols), blocks[0][0].dtype)
+        piece = jnp.zeros((width, cols), dtype)
         for b, o in blocks:
             piece = lax.dynamic_update_slice(piece, b, (o, 0))
-        return jnp.dot(amplitudes, piece, preferred_element_type=jnp.float32)
+        return piece
     offsets = jnp.stack([o for _, o in blocks]).astype(jnp.int32)
-    tm = rows // 4 if rows % 32 == 0 else rows
 
-    def kernel(off_ref, a_ref, *refs):
+    def kernel(off_ref, *refs):
         w_refs = refs[:n]
-        o_ref, wbuf, sem = refs[n:]
-
-        @pl.when(pl.program_id(0) == 0)
-        def _():
-            copies = [pltpu.make_async_copy(w_refs[s], wbuf.at[pl.ds(pl.multiple_of(off_ref[s], 16), counts[s])], sem.at[s])
-                      for s in range(n)]
-            for c in copies:
-                c.start()
-            for c in copies:
-                c.wait()
-
-        o_ref[...] = jnp.dot(a_ref[...], wbuf[...], preferred_element_type=jnp.float32)
+        o_ref, sem = refs[n:]
+        copies = [pltpu.make_async_copy(w_refs[s], o_ref.at[pl.ds(pl.multiple_of(off_ref[s], 16), counts[s])], sem.at[s])
+                  for s in range(n)]
+        for c in copies:
+            c.start()
+        for c in copies:
+            c.wait()
 
     grid_spec = pltpu.PrefetchScalarGridSpec(
         num_scalar_prefetch=1,
-        grid=(rows // tm,),
-        in_specs=[pl.BlockSpec((tm, width), lambda i, o: (i, 0))] + [pl.BlockSpec(memory_space=pl.ANY)] * n,
-        out_specs=pl.BlockSpec((tm, cols), lambda i, o: (i, 0)),
-        scratch_shapes=[pltpu.VMEM((width, cols), blocks[0][0].dtype), pltpu.SemaphoreType.DMA((n,))],
+        grid=(1,),
+        in_specs=[pl.BlockSpec(memory_space=pl.ANY)] * n,
+        out_specs=pl.BlockSpec(memory_space=pl.ANY),
+        scratch_shapes=[pltpu.SemaphoreType.DMA((n,))],
     )
     return pl.pallas_call(
-        kernel,
-        grid_spec=grid_spec,
-        out_shape=jax.ShapeDtypeStruct((rows, cols), jnp.float32),
-        compiler_params=pltpu.CompilerParams(dimension_semantics=("arbitrary",)),
-    )(offsets, amplitudes, *[b for b, _ in blocks])
+        kernel, grid_spec=grid_spec, out_shape=jax.ShapeDtypeStruct((width, cols), dtype)
+    )(offsets, *[b for b, _ in blocks])
+
+
+def contract(amplitudes, blocks):
+    piece = assemble(blocks, amplitudes.shape[1])
+    return jnp.dot(amplitudes, piece, preferred_element_type=jnp.float32)
 
 
 def reduce_cuts(terms, cuts_idx, cuts_count):

time: 97.6 us -> 187 us (1.92)
  Pallas kernels: 18.6 us -> 103 us
  local copies, waits for them, and re-layouts: 27.3 us -> 11 us
  matrix products: 0 us -> 15.5 us
  waiting for transfers between devices: 31.2 us -> 37.2 us
    pallas_call x2, Pallas kernels: 18.6 us -> 103 us  [assemble(): pl.pallas_call(kernel, grid_spec=grid_spec, out_shape=jax.ShapeDtypeStruc...]
    dot_general x0 -> x2, matrix products: none -> 15.5 us  [contract(): return jnp.dot(amplitudes, piece, preferred_element_type=jnp.float32)]
    ppermute x12, waiting for transfers between devices: 31.2 us -> 37.2 us  [swap(): lax.ppermute(value, axis, [(i, i ^ mask) for i in range(lax.axis_size(axi...]
    ppermute x4 -> x2, local copies, waits for them, and re-layouts: 6.23 us -> 1.6 us  [swap(): lax.ppermute(value, axis, [(i, i ^ mask) for i in range(lax.axis_size(axi...]
    dynamic_slice x4 -> x2, local copies, waits for them, and re-layouts: 3.71 us -> 0.92 us  [reduce_cuts(): lax.dynamic_slice_in_dim(terms, jnp.bitwise_xor(cuts_idx, s) * rows, rows...]
    add x2 -> x0, local copies, waits for them, and re-layouts: 2.17 us -> none  [reduce_cuts(): total = total + swap(part, 'cuts', s)]
    unnamed x25 -> x15, local copies, waits for them, and re-layouts: 4.09 us -> 2.07 us
    gather x2 -> x4, local copies, waits for them, and re-layouts: 5.03 us -> 4.72 us  [shards(): results.append(cycle - jnp.take(fetched, local, axis=0))]
  transfers between devices with their start and end apart: 12 -> 12, of which waited for: 5 -> 6; matrix products, arithmetic and copies ran while one was open for 19% -> 13% of each run, Pallas kernels for 19% -> 55%
where the time goes in v4:
time: 187 us
  Pallas kernels  103 us (55%)
  waiting for transfers between devices  37.2 us (20%)
  matrix products  15.5 us (8%)
  starting transfers between devices  14.5 us (8%)
  local copies, waits for them, and re-layouts  11 us (6%)
  other arithmetic  5.37 us (3%)
    pallas_call x2, Pallas kernels, assemble(): pl.pallas_call(kernel, grid_spec=grid_spec, out_shape=jax.ShapeDtypeStruc...  103 us
    ppermute x12, waiting for transfers between devices, swap(): lax.ppermute(value, axis, [(i, i ^ mask) for i in range(lax.axis_size(axi...  37.2 us
    dot_general x2, matrix products, contract(): return jnp.dot(amplitudes, piece, preferred_element_type=jnp.float32)  15.5 us
    ppermute x12, starting transfers between devices, swap(): lax.ppermute(value, axis, [(i, i ^ mask) for i in range(lax.axis_size(axi...  14.5 us
    gather x4, local copies, waits for them, and re-layouts, shards(): results.append(cycle - jnp.take(fetched, local, axis=0))  4.72 us
  transfers between devices with their start and end apart: 12, of which 6 were waited for; matrix products, arithmetic and copies ran while one was open for 13% of the time, Pallas kernels for 55%

profile of v4, /device:TPU:0, one launch (start us, length us, event | category | flops | bytes accessed | tf_op | source)
XLA Modules:
  0.0 186.7 jit_solution(2048709658419179952)
XLA Ops:
  0.0 1.4 copy.6
  1.4 0.8 dynamic_slice.18
  2.2 0.9 compare_select_fusion
  3.3 3.0 %collective-permute-start.1 = (bf16[800,200]{1,0:T(8,128)(2,1)S(1)}, bf16[800,200]{1,0:T(8,128)(2,1)S(1)}, u32[]{:S(2)}, u32[]{:S(2)}) collective-permute-start(bf16[800,200]{1,0:T(8,128)(2,1)S(1)} %get-tuple-element.8.refs_0_), channel_id=1, source_target_pairs={{0,16},{8,24},{16,0},{24,8},{1,17},{9,25},{17,1},{25,9},{2,18},{10... | collective-permute-start | bytes 960008 | tf_op jit(solution)/shard_map/ppermute | solution.py:10
  6.4 1.5 collective-permute-start
  7.8 0.5 collective-permute-start.7
  8.5 8.2 %collective-permute-done.1.refs_2_ = bf16[800,200]{1,0:T(8,128)(2,1)S(1)} collective-permute-done((bf16[800,200]{1,0:T(8,128)(2,1)S(1)}, bf16[800,200]{1,0:T(8,128)(2,1)S(1)}, u32[]{:S(2)}, u32[]{:S(2)}) %collective-permute-start.1) | collective-permute-done | bytes 320032 | tf_op jit(solution)/shard_map/ppermute | solution.py:10
  16.7 2.1 %collective-permute-start.2 = (bf16[400,200]{1,0:T(8,128)(2,1)S(1)}, bf16[400,200]{1,0:T(8,128)(2,1)S(1)}, u32[]{:S(2)}, u32[]{:S(2)}) collective-permute-start(bf16[400,200]{1,0:T(8,128)(2,1)S(1)} %slice.29), channel_id=1, source_target_pairs={{0,8},{8,0},{16,24},{24,16},{1,9},{9,1},{17,25},{25,17},{2,10},{10... | collective-permute-start | bytes 480008 | tf_op jit(solution)/shard_map/ppermute | solution.py:10
  18.8 1.6 collective-permute-start.3
  20.4 0.7 stack.29.off_ref
  21.0 4.4 %collective-permute-done.7.refs_2_ = bf16[800,200]{1,0:T(8,128)(2,1)S(1)} collective-permute-done((bf16[800,200]{1,0:T(8,128)(2,1)S(1)}, bf16[800,200]{1,0:T(8,128)(2,1)S(1)}, u32[]{:S(2)}, u32[]{:S(2)}) %collective-permute-start.7) | collective-permute-done | bytes 320032 | tf_op jit(solution)/shard_map/ppermute | solution.py:10
  25.4 2.1 %collective-permute-start.8 = (bf16[400,200]{1,0:T(8,128)(2,1)S(1)}, bf16[400,200]{1,0:T(8,128)(2,1)}, u32[]{:S(2)}, u32[]{:S(2)}) collective-permute-start(bf16[400,200]{1,0:T(8,128)(2,1)S(1)} %slice.32), channel_id=1, source_target_pairs={{0,8},{8,0},{16,24},{24,16},{1,9},{9,1},{17,25},{25,17},{2,10},{10... | collective-permute-start | bytes 480008 | tf_op jit(solution)/shard_map/ppermute | solution.py:10
  27.6 1.6 collective-permute-start.9
  29.2 2.8 %collective-permute-done.2.refs_3_ = bf16[400,200]{1,0:T(8,128)(2,1)S(1)} collective-permute-done((bf16[400,200]{1,0:T(8,128)(2,1)S(1)}, bf16[400,200]{1,0:T(8,128)(2,1)S(1)}, u32[]{:S(2)}, u32[]{:S(2)}) %collective-permute-start.2) | collective-permute-done | bytes 160032 | tf_op jit(solution)/shard_map/ppermute | solution.py:10
  31.9 0.7 copy-done.6
  32.6 51.4 %shard_map.55 = bf16[3200,200]{1,0:T(8,128)(2,1)} custom-call(s32[5]{0:T(128)} %stack.29.off_ref, bf16[800,200]{1,0:T(8,128)(2,1)} %copy-done.1, bf16[800,200]{1,0:T(8,128)(2,1)} %copy-done.5, bf16[800,200]{1,0:T(8,128)(2,1)} %copy-done.4, bf16[400,200]{1,0:T(8,128)(2,1)} %copy-done.6, bf16[400,200]{1,0:T(8,128)(2,1)} %collective-permute-done.3.refs_4_), custom_call_target="tpu_custom_call" | custom-call | tf_op jit(solution)/shard_map/pallas_call | solution.py:59
  84.1 7.7 %fusion.1 = f32[200,1536]{1,0:T(8,128)S(1)} fusion(bf16[3200,200]{1,0:T(8,128)(2,1)} %shard_map.55, bf16[1536,3200]{1,0:T(8,128)(2,1)} %param.7), kind=kOutput, calls=%fused_computation.14 | convolution fusion | flops 1966080000 | bytes 12339200 | tf_op jit(solution)/shard_map/dot_general | solution.py:66
  92.0 51.4 %shard_map.56 = bf16[3200,200]{1,0:T(8,128)(2,1)} custom-call(s32[5]{0:T(128)} %stack.29.off_ref, bf16[800,200]{1,0:T(8,128)(2,1)} %copy-done, bf16[800,200]{1,0:T(8,128)(2,1)} %copy-done.3, bf16[800,200]{1,0:T(8,128)(2,1)} %copy-done.2, bf16[400,200]{1,0:T(8,128)(2,1)} %collective-permute-done.8.refs_3_, bf16[400,200]{1,0:T(8,128)(2,1)} %collective-permute-done.9.refs_4_), custom_call_target="tpu_custom_call" | custom-call | tf_op jit(solution)/shard_map/pallas_call | solution.py:59
  143.4 7.7 %fusion.2 = f32[200,1536]{1,0:T(8,128)S(1)} fusion(bf16[3200,200]{1,0:T(8,128)(2,1)} %shard_map.56, bf16[1536,3200]{1,0:T(8,128)(2,1)} %param.7), kind=kOutput, calls=%fused_computation.15 | convolution fusion | flops 1966080000 | bytes 12339200 | tf_op jit(solution)/shard_map/dot_general | solution.py:66
  151.2 0.9 dynamic-slice_bitcast_fusion
  152.0 0.5 collective-permute-start.10
  152.5 1.2 bitcast_add_fusion.1
  153.8 0.7 collective-permute-done.10
  154.5 1.2 bitcast_add_fusion
  155.7 1.3 collective-permute-start.11
  157.0 0.8 compare_and_fusion
  157.8 12.8 %collective-permute-done.5 = f32[768,200]{0,1:T(8,128)} collective-permute-done((f32[768,200]{0,1:T(8,128)S(1)}, f32[768,200]{0,1:T(8,128)}, u32[]{:S(2)}, u32[]{:S(2)}) %collective-permute-start.5) | collective-permute-done | bytes 614432 | tf_op jit(solution)/shard_map/ppermute | solution.py:10
  170.6 1.3 copy.7
  171.9 2.1 %gather_fusion = f32[768,200]{1,0:T(8,128)S(1)} fusion(f32[768,200]{1,0:T(8,128)S(1)} %copy.7, s32[1024]{0:T(1024)S(1)} %pad_clamp_fusion), kind=kCustom, calls=%fused_computation.clone | custom fusion | bytes 1231872 | tf_op jit(solution)/shard_map/jit(_take)/gather | solution.py:101
  174.3 8.4 %collective-permute-done.11 = f32[768,200]{0,1:T(8,128)S(1)} collective-permute-done((f32[768,200]{0,1:T(8,128)S(1)}, f32[768,200]{0,1:T(8,128)S(1)}, u32[]{:S(2)}, u32[]{:S(2)}) %collective-permute-start.11) | collective-permute-done | bytes 614432 | tf_op jit(solution)/shard_map/ppermute | solution.py:10
  183.0 2.1 %gather_fusion.1 = f32[768,200]{1,0:T(8,128)S(1)} fusion(f32[768,200]{1,0:T(8,128)S(1)} %copy.9, s32[1024]{0:T(1024)S(1)} %pad_clamp_fusion), kind=kCustom, calls=%fused_computation.1.clone | custom fusion | bytes 1231872 | tf_op jit(solution)/shard_map/jit(_take)/gather | solution.py:101
  185.6 1.1 pad_maximum_fusion
  (33 shorter events, 1.6 us)
Async XLA Ops:
  3.3 28.6 %copy-start.1 = (bf16[800,200]{1,0:T(8,128)(2,1)}, bf16[800,200]{1,0:T(8,128)(2,1)S(1)}, u32[]{:S(2)}) copy-start(bf16[800,200]{1,0:T(8,128)(2,1)S(1)} %get-tuple-element.8.refs_0_) | copy-start | bytes 960004
  3.3 80.7 %copy-start = (bf16[800,200]{1,0:T(8,128)(2,1)}, bf16[800,200]{1,0:T(8,128)(2,1)S(1)}, u32[]{:S(2)}) copy-start(bf16[800,200]{1,0:T(8,128)(2,1)S(1)} %get-tuple-element.9.refs_0_) | copy-start | bytes 960004
  3.3 13.3 %collective-permute-start.1 = (bf16[800,200]{1,0:T(8,128)(2,1)S(1)}, bf16[800,200]{1,0:T(8,128)(2,1)S(1)}, u32[]{:S(2)}, u32[]{:S(2)}) collective-permute-start(bf16[800,200]{1,0:T(8,128)(2,1)S(1)} %get-tuple-element.8.refs_0_), channel_id=1, source_target_pairs={{0,16},{8,24},{16,0},{24,8},{1,17},{9,25},{17,1},{25,9},{2,18},{10... | collective-permute-start | bytes 960008 | tf_op jit(solution)/shard_map/ppermute | solution.py:10
  6.4 12.4 %collective-permute-start = (bf16[800,200]{1,0:T(8,128)(2,1)S(1)}, bf16[800,200]{1,0:T(8,128)(2,1)S(1)}, u32[]{:S(2)}, u32[]{:S(2)}) collective-permute-start(bf16[800,200]{1,0:T(8,128)(2,1)S(1)} %get-tuple-element.8.refs_0_), channel_id=1, source_target_pairs={{0,8},{8,0},{16,24},{24,16},{1,9},{9,1},{17,25},{25,17},{2,10},{10... | collective-permute-start | bytes 960008 | tf_op jit(solution)/shard_map/ppermute | solution.py:10
  7.8 17.6 %collective-permute-start.7 = (bf16[800,200]{1,0:T(8,128)(2,1)S(1)}, bf16[800,200]{1,0:T(8,128)(2,1)S(1)}, u32[]{:S(2)}, u32[]{:S(2)}) collective-permute-start(bf16[800,200]{1,0:T(8,128)(2,1)S(1)} %get-tuple-element.9.refs_0_), channel_id=1, source_target_pairs={{0,16},{8,24},{16,0},{24,8},{1,17},{9,25},{17,1},{25,9},{2,18},{10... | collective-permute-start | bytes 960008 | tf_op jit(solution)/shard_map/ppermute | solution.py:10
  8.4 19.2 %collective-permute-start.6 = (bf16[800,200]{1,0:T(8,128)(2,1)S(1)}, bf16[800,200]{1,0:T(8,128)(2,1)S(1)}, u32[]{:S(2)}, u32[]{:S(2)}) collective-permute-start(bf16[800,200]{1,0:T(8,128)(2,1)S(1)} %get-tuple-element.9.refs_0_), channel_id=1, source_target_pairs={{0,8},{8,0},{16,24},{24,16},{1,9},{9,1},{17,25},{25,17},{2,10},{10... | collective-permute-start | bytes 960008 | tf_op jit(solution)/shard_map/ppermute | solution.py:10
  16.7 15.3 %copy-start.4 = (bf16[800,200]{1,0:T(8,128)(2,1)}, bf16[800,200]{1,0:T(8,128)(2,1)S(1)}, u32[]{:S(2)}) copy-start(bf16[800,200]{1,0:T(8,128)(2,1)S(1)} %collective-permute-done.1.refs_2_) | copy-start | bytes 960004
  16.7 15.2 %collective-permute-start.2 = (bf16[400,200]{1,0:T(8,128)(2,1)S(1)}, bf16[400,200]{1,0:T(8,128)(2,1)S(1)}, u32[]{:S(2)}, u32[]{:S(2)}) collective-permute-start(bf16[400,200]{1,0:T(8,128)(2,1)S(1)} %slice.29), channel_id=1, source_target_pairs={{0,8},{8,0},{16,24},{24,16},{1,9},{9,1},{17,25},{25,17},{2,10},{10... | collective-permute-start | bytes 480008 | tf_op jit(solution)/shard_map/ppermute | solution.py:10
  18.8 13.2 %copy-start.5 = (bf16[800,200]{1,0:T(8,128)(2,1)}, bf16[800,200]{1,0:T(8,128)(2,1)S(1)}, u32[]{:S(2)}) copy-start(bf16[800,200]{1,0:T(8,128)(2,1)S(1)} %collective-permute-done.refs_1_) | copy-start | bytes 960004
  18.8 13.1 %collective-permute-start.3 = (bf16[400,200]{1,0:T(8,128)(2,1)S(1)}, bf16[400,200]{1,0:T(8,128)(2,1)}, u32[]{:S(2)}, u32[]{:S(2)}) collective-permute-start(bf16[400,200]{1,0:T(8,128)(2,1)S(1)} %slice.30), channel_id=1, source_target_pairs={{0,16},{8,24},{16,0},{24,8},{1,17},{9,25},{17,1},{25,9},{2,18},{10... | collective-permute-start | bytes 480008 | tf_op jit(solution)/shard_map/ppermute | solution.py:10
  25.4 58.6 %copy-start.2 = (bf16[800,200]{1,0:T(8,128)(2,1)}, bf16[800,200]{1,0:T(8,128)(2,1)S(1)}, u32[]{:S(2)}) copy-start(bf16[800,200]{1,0:T(8,128)(2,1)S(1)} %collective-permute-done.7.refs_2_) | copy-start | bytes 960004
  25.4 66.5 %collective-permute-start.8 = (bf16[400,200]{1,0:T(8,128)(2,1)S(1)}, bf16[400,200]{1,0:T(8,128)(2,1)}, u32[]{:S(2)}, u32[]{:S(2)}) collective-permute-start(bf16[400,200]{1,0:T(8,128)(2,1)S(1)} %slice.32), channel_id=1, source_target_pairs={{0,8},{8,0},{16,24},{24,16},{1,9},{9,1},{17,25},{25,17},{2,10},{10... | collective-permute-start | bytes 480008 | tf_op jit(solution)/shard_map/ppermute | solution.py:10
  27.5 56.5 %copy-start.3 = (bf16[800,200]{1,0:T(8,128)(2,1)}, bf16[800,200]{1,0:T(8,128)(2,1)S(1)}, u32[]{:S(2)}) copy-start(bf16[800,200]{1,0:T(8,128)(2,1)S(1)} %collective-permute-done.6.refs_1_) | copy-start | bytes 960004
  27.6 64.4 %collective-permute-start.9 = (bf16[400,200]{1,0:T(8,128)(2,1)S(1)}, bf16[400,200]{1,0:T(8,128)(2,1)}, u32[]{:S(2)}, u32[]{:S(2)}) collective-permute-start(bf16[400,200]{1,0:T(8,128)(2,1)S(1)} %slice.33), channel_id=1, source_target_pairs={{0,16},{8,24},{16,0},{24,8},{1,17},{9,25},{17,1},{25,9},{2,18},{10... | collective-permute-start | bytes 480008 | tf_op jit(solution)/shard_map/ppermute | solution.py:10
  31.9 0.7 copy-start.6
  91.9 60.7 %collective-permute-start.4 = (f32[768,200]{0,1:T(8,128)S(1)}, f32[768,200]{0,1:T(8,128)}, u32[]{:S(2)}, u32[]{:S(2)}) collective-permute-start(f32[768,200]{0,1:T(8,128)S(1)} %dynamic-slice_bitcast_fusion.1), channel_id=1, source_target_pairs={{0,1},{1,0},{2,3},{3,2},{4,5},{5,4},{6,7},{7,6},{8,9},{9,8},{10,11... | collective-permute-start | bytes 1843208 | tf_op jit(solution)/shard_map/ppermute | solution.py:10
  152.0 2.5 %collective-permute-start.10 = (f32[768,200]{0,1:T(8,128)}, f32[768,200]{0,1:T(8,128)}, u32[]{:S(2)}, u32[]{:S(2)}) collective-permute-start(f32[768,200]{0,1:T(8,128)} %dynamic-slice_bitcast_fusion), channel_id=1, source_target_pairs={{0,1},{1,0},{2,3},{3,2},{4,5},{5,4},{6,7},{7,6},{8,9},{9,8},{10,11... | collective-permute-start | bytes 1843208 | tf_op jit(solution)/shard_map/ppermute | solution.py:10
  153.7 16.9 %collective-permute-start.5 = (f32[768,200]{0,1:T(8,128)S(1)}, f32[768,200]{0,1:T(8,128)}, u32[]{:S(2)}, u32[]{:S(2)}) collective-permute-start(f32[768,200]{0,1:T(8,128)S(1)} %bitcast_add_fusion.1), channel_id=1, source_target_pairs={{0,16},{8,24},{16,0},{24,8},{1,17},{9,25},{17,1},{25,9},{2,18},{10... | collective-permute-start | bytes 1843208 | tf_op jit(solution)/shard_map/ppermute | solution.py:10
  155.7 27.0 %collective-permute-start.11 = (f32[768,200]{0,1:T(8,128)S(1)}, f32[768,200]{0,1:T(8,128)S(1)}, u32[]{:S(2)}, u32[]{:S(2)}) collective-permute-start(f32[768,200]{0,1:T(8,128)S(1)} %bitcast_add_fusion), channel_id=1, source_target_pairs={{0,16},{8,24},{16,0},{24,8},{1,17},{9,25},{17,1},{25,9},{2,18},{10... | collective-permute-start | bytes 1843208 | tf_op jit(solution)/shard_map/ppermute | solution.py:10

commit v5 on v1

v5 whole, which is shorter than its diff:
```python
import jax
import jax.numpy as jnp
from jax import lax
from jax.experimental import pallas as pl
from jax.experimental.pallas import tpu as pltpu
from jax.sharding import PartitionSpec as P


def swap(value, axis, mask):
    return lax.ppermute(value, axis, [(i, i ^ mask) for i in range(lax.axis_size(axis))])


def gather_prow(own, prow_idx, prow_count):
    count = own.shape[0]
    if prow_count == 4 and count % 32 == 0:
        half = count // 2
        from_x = swap(own, "prow", 1)
        from_y = swap(own, "prow", 2)
        diag_a = swap(from_y[:half], "prow", 1)
        diag_b = swap(from_x[half:], "prow", 2)
        base = jnp.bitwise_xor(prow_idx, 3) * count
        return [[(own, prow_idx * count)], [(from_y, jnp.bitwise_xor(prow_idx, 2) * count)],
                [(from_x, jnp.bitwise_xor(prow_idx, 1) * count)], [(diag_a, base), (diag_b, base + half)]]
    groups = [[(own, prow_idx * count)]]
    for s in range(1, prow_count):
        groups.append([(swap(own, "prow", s), jnp.bitwise_xor(prow_idx, s) * count)])
    return groups


def window(count, width, prow_count):
    lane = 128
    if width % lane or count % 16:
        return None
    span = max(-(-((j * count) % lane + count) // lane) * lane for j in range(prow_count))
    if any((j * count) // lane * lane + span > width for j in range(prow_count)):
        return None
    return span


def partial_product(amplitudes, group, first, span, acc):
    rows, width = amplitudes.shape
    cols = group[0][0].shape[1]
    lane = 128
    n = len(group)
    counts = [b.shape[0] for b, _ in group]
    offsets = jnp.stack([first] + [o - first // lane * lane for _, o in group]).astype(jnp.int32)

    def kernel(off_ref, a_hbm, *refs):
        w_refs = refs[:n]
        rest = refs[n:]
        if acc is None:
            o_ref, a_buf, w_buf, sem = rest
        else:
            acc_ref, o_ref, a_buf, w_buf, sem = rest
        start = pl.multiple_of(off_ref[0] // lane * lane, lane)
        copy = pltpu.make_async_copy(a_hbm.at[:, pl.ds(start, span)], a_buf, sem.at[0])
        copy.start()
        w_buf[...] = jnp.zeros(w_buf.shape, w_buf.dtype)
        for s in range(n):
            w_buf[pl.ds(pl.multiple_of(off_ref[s + 1], 16), counts[s]), :] = w_refs[s][...]
        copy.wait()
        product = jnp.dot(a_buf[...], w_buf[...], preferred_element_type=jnp.float32)
        o_ref[...] = product if acc is None else acc_ref[...] + product

    vmem = pl.BlockSpec(memory_space=pltpu.MemorySpace.VMEM)
    smem = pl.BlockSpec(memory_space=pltpu.MemorySpace.SMEM)
    operands = [offsets, amplitudes] + [b for b, _ in group] + ([] if acc is None else [acc])
    return pl.pallas_call(
        kernel,
        in_specs=[smem, pl.BlockSpec(memory_space=pl.ANY)] + [vmem] * (len(operands) - 2),
        out_specs=vmem,
        out_shape=jax.ShapeDtypeStruct((rows, cols), jnp.float32),
        scratch_shapes=[pltpu.VMEM((rows, span), amplitudes.dtype), pltpu.VMEM((span, cols), group[0][0].dtype),
                        pltpu.SemaphoreType.DMA((1,))],
        input_output_aliases={} if acc is None else {len(operands) - 1: 0},
    )(*operands)


def contract(amplitudes, groups, prow_idx, prow_count):
    rows, width = amplitudes.shape
    count, cols = groups[0][0][0].shape
    span = window(count, width, prow_count)
    if span is None:
        piece = jnp.zeros((width, cols), groups[0][0][0].dtype)
        for group in groups:
            for b, o in group:
                piece = lax.dynamic_update_slice(piece, b, (o, 0))
        return jnp.dot(amplitudes, piece, preferred_element_type=jnp.float32)
    acc = None
    for group in groups:
        acc = partial_product(amplitudes, group, group[0][1], span, acc)
    return acc


def reduce_cuts(terms, cuts_idx, cuts_count):
    rows = terms.shape[0] // cuts_count
    total = lax.dynamic_slice_in_dim(terms, cuts_idx * rows, rows, axis=0)
    for s in range(1, cuts_count):
        part = lax.dynamic_slice_in_dim(terms, jnp.bitwise_xor(cuts_idx, s) * rows, rows, axis=0)
        total = total + swap(part, "cuts", s)
    return total


def shards(amplitudes, integrals, irrep_rows, irrep_cols, mirror_row):
    prow_count = lax.axis_size("prow")
    cuts_count = lax.axis_size("cuts")
    prow_idx = lax.axis_index("prow")
    cuts_idx = lax.axis_index("cuts")
    count = integrals.shape[0]
    labels = lax.dynamic_slice(irrep_rows, ((cuts_idx * prow_count + prow_idx) * count,), (count,))
    same = labels[:, None] == irrep_cols[None, :]
    blocked = jnp.where(same, integrals, jnp.zeros_like(integrals))
    terms = contract(amplitudes, gather_prow(blocked, prow_idx, prow_count), prow_idx, prow_count)
    cycle = reduce_cuts(terms, cuts_idx, cuts_count)
    block_rows = cycle.shape[0]
    half = prow_count // 2
    own_block = prow_idx * cuts_count + cuts_idx
    partner_block = jnp.bitwise_xor(prow_idx, half) * cuts_count + cuts_idx
    mine = lax.dynamic_slice(mirror_row, (own_block * block_rows,), (block_rows,))
    local = mine - partner_block * block_rows
    fetched = swap(cycle, "prow", half)
    return cycle - jnp.take(fetched, local, axis=0)


def solution(mesh):
    placed = (P("prow", "cuts"), P(("cuts", "prow"), "pcol"), P(), P("pcol"), P())
    return jax.shard_map(
        shards, mesh=mesh, in_specs=placed, out_specs=P(("prow", "cuts"), "pcol"), check_vma=False
    )
```

time: 105 us -> 106 us (level)
  Pallas kernels: 0 us -> 28.5 us
  local copies, waits for them, and re-layouts: 40.2 us -> 21.1 us
  matrix products: 7.25 us -> 0 us
  waiting for transfers between devices: 44.4 us -> 38.6 us
  other arithmetic: 4.67 us -> 8.6 us
    dynamic_update_slice x4 -> x0, local copies, waits for them, and re-layouts: 34.2 us -> none  [gather_prow(): lax.dynamic_update_slice(piece, block, (jnp.bitwise_xor(prow_idx, s) * co...]
    pallas_call x0 -> x4, Pallas kernels: none -> 28.5 us  [partial_product(): pl.pallas_call(kernel, in_specs=[smem, pl.BlockSpec(memory_space=pl.ANY)]...]
    dot_general x1 -> x0, matrix products: 7.25 us -> none  [shards(): terms = jnp.dot(amplitudes, blocked, preferred_element_type=jnp.float32)]
    ppermute x5 -> x6, waiting for transfers between devices: 44.4 us -> 38.6 us  [swap(): lax.ppermute(value, axis, [(i, i ^ mask) for i in range(lax.axis_size(axi...]
    dynamic_slice x1 -> x2, local copies, waits for them, and re-layouts: 0.08 us -> 5.72 us  [reduce_cuts(): lax.dynamic_slice_in_dim(terms, jnp.bitwise_xor(cuts_idx, s) * rows, rows...]
    ppermute x1 -> x4, local copies, waits for them, and re-layouts: 0.46 us -> 3.97 us  [swap(): lax.ppermute(value, axis, [(i, i ^ mask) for i in range(lax.axis_size(axi...]
    another operation x0 -> x4, other arithmetic: none -> 2.36 us  [partial_product(): jnp.stack([first] + [o - first // lane * lane for _, o in group])]
    add x0 -> x1, local copies, waits for them, and re-layouts: none -> 1.84 us  [reduce_cuts(): total = total + swap(part, 'cuts', s)]
  transfers between devices with their start and end apart: 5 -> 6, of which waited for: 3 -> 3; matrix products, arithmetic and copies ran while one was open for 25% -> 4% of each run, Pallas kernels for 0% -> 20%
where the time goes in v5:
time: 106 us; the launch traced here: 105 us
  waiting for transfers between devices  38.6 us (36%)
  Pallas kernels  28.5 us (27%)
  local copies, waits for them, and re-layouts  21.1 us (20%)
  other arithmetic  8.6 us (8%)
  starting transfers between devices  8.36 us (8%)
    ppermute x6, waiting for transfers between devices, swap(): lax.ppermute(value, axis, [(i, i ^ mask) for i in range(lax.axis_size(axi...  38.6 us
    pallas_call x4, Pallas kernels, partial_product(): pl.pallas_call(kernel, in_specs=[smem, pl.BlockSpec(memory_space=pl.ANY)]...  28.5 us
    ppermute x6, starting transfers between devices, swap(): lax.ppermute(value, axis, [(i, i ^ mask) for i in range(lax.axis_size(axi...  8.36 us
    dynamic_slice x2, local copies, waits for them, and re-layouts, reduce_cuts(): lax.dynamic_slice_in_dim(terms, jnp.bitwise_xor(cuts_idx, s) * rows, rows...  5.72 us
    ppermute x4, local copies, waits for them, and re-layouts, swap(): lax.ppermute(value, axis, [(i, i ^ mask) for i in range(lax.axis_size(axi...  3.97 us
    gather x1, local copies, waits for them, and re-layouts, shards(): return cycle - jnp.take(fetched, local, axis=0)  3.14 us
    add x1, other arithmetic, reduce_cuts(): total = total + swap(part, 'cuts', s)  2.91 us
    unnamed x15, local copies, waits for them, and re-layouts  2.9 us
  transfers between devices with their start and end apart: 6, of which 3 were waited for; matrix products, arithmetic and copies ran while one was open for 4% of the time, Pallas kernels for 20%

profile of v5, /device:TPU:0, one launch (start us, length us, event | category | flops | bytes accessed | tf_op | source)
XLA Modules:
  0.0 105.3 jit_solution(15354633264838346438)
XLA Ops:
  0.0 1.4 %copy.23 = bf16[800,400]{1,0:T(8,128)(2,1)S(1)} copy(bf16[800,400]{0,1:T(8,128)(2,1)} %param.6) | data formatting | bytes 1280000 | tf_op args[1]
  1.4 0.8 dynamic_slice.12
  2.2 0.9 compare_select_fusion.refs_0_
  3.5 3.0 %collective-permute-start = (bf16[800,400]{0,1:T(8,128)(2,1)S(1)}, bf16[800,400]{0,1:T(8,128)(2,1)S(1)}, u32[]{:S(2)}, u32[]{:S(2)}) collective-permute-start(bf16[800,400]{0,1:T(8,128)(2,1)S(1)} %copy.24), channel_id=1, source_target_pairs={{0,16},{8,24},{16,0},{24,8},{1,17},{9,25},{17,1},{25,9},{2,18},{10... | collective-permute-start | bytes 1920008 | tf_op jit(solution)/shard_map/ppermute | solution.py:10
  6.5 1.5 %collective-permute-start.2 = (bf16[800,400]{0,1:T(8,128)(2,1)S(1)}, bf16[800,400]{0,1:T(8,128)(2,1)S(1)}, u32[]{:S(2)}, u32[]{:S(2)}) collective-permute-start(bf16[800,400]{0,1:T(8,128)(2,1)S(1)} %copy.24), channel_id=1, source_target_pairs={{0,8},{8,0},{16,24},{24,16},{1,9},{9,1},{17,25},{25,17},{2,10},{10... | collective-permute-start | bytes 1920008 | tf_op jit(solution)/shard_map/ppermute | solution.py:10
  8.0 0.6 pad_add_fusion.3.off_ref
  8.6 6.4 %shard_map.55.refs_1_ = f32[1536,400]{1,0:T(8,128)} custom-call(s32[2]{0:T(128)} %pad_add_fusion.3.off_ref, bf16[1536,3200]{1,0:T(8,128)(2,1)} %a_hbm.7, bf16[800,400]{1,0:T(8,128)(2,1)} %copy-done.2), custom_call_target="tpu_custom_call" | custom-call | tf_op jit(solution)/shard_map/pallas_call | solution.py:68
  15.0 7.6 %collective-permute-done = bf16[800,400]{0,1:T(8,128)(2,1)S(1)} collective-permute-done((bf16[800,400]{0,1:T(8,128)(2,1)S(1)}, bf16[800,400]{0,1:T(8,128)(2,1)S(1)}, u32[]{:S(2)}, u32[]{:S(2)}) %collective-permute-start) | collective-permute-done | bytes 640032 | tf_op jit(solution)/shard_map/ppermute | solution.py:10
  22.9 1.8 %collective-permute-start.1 = (bf16[400,400]{1,0:T(8,128)(2,1)S(1)}, bf16[400,400]{1,0:T(8,128)(2,1)S(1)}, u32[]{:S(2)}, u32[]{:S(2)}) collective-permute-start(bf16[400,400]{1,0:T(8,128)(2,1)S(1)} %slice.10), channel_id=1, source_target_pairs={{0,8},{8,0},{16,24},{24,16},{1,9},{9,1},{17,25},{25,17},{2,10},{10... | collective-permute-start | bytes 960008 | tf_op jit(solution)/shard_map/ppermute | solution.py:10
  25.0 0.8 slice.11
  25.8 1.5 %collective-permute-start.3 = (bf16[400,400]{1,0:T(8,128)(2,1)}, bf16[400,400]{1,0:T(8,128)(2,1)S(1)}, u32[]{:S(2)}, u32[]{:S(2)}) collective-permute-start(bf16[400,400]{1,0:T(8,128)(2,1)} %slice.11), channel_id=1, source_target_pairs={{0,16},{8,24},{16,0},{24,8},{1,17},{9,25},{17,1},{25,9},{2,18},{10... | collective-permute-start | bytes 960008 | tf_op jit(solution)/shard_map/ppermute | solution.py:10
  27.4 0.6 pad_add_fusion.2.off_ref
  27.9 0.6 pad_add_fusion.1.off_ref
  28.5 0.6 pad_add_fusion.off_ref
  29.1 7.4 %shard_map.56.refs_1_ = f32[1536,400]{1,0:T(8,128)} custom-call(s32[2]{0:T(128)} %pad_add_fusion.2.off_ref, bf16[1536,3200]{1,0:T(8,128)(2,1)} %a_hbm.7, bf16[800,400]{1,0:T(8,128)(2,1)} %copy-done.3, f32[1536,400]{1,0:T(8,128)} %shard_map.55.refs_1_), custom_call_target="tpu_custom_call", output_to_operand_aliasing={{}: (3, {})} | custom-call | tf_op jit(solution)/shard_map/pallas_call | solution.py:68
  36.5 7.4 %shard_map.57.refs_2_ = f32[1536,400]{1,0:T(8,128)} custom-call(s32[2]{0:T(128)} %pad_add_fusion.1.off_ref, bf16[1536,3200]{1,0:T(8,128)(2,1)} %a_hbm.7, bf16[800,400]{1,0:T(8,128)(2,1)} %copy-done.4, f32[1536,400]{1,0:T(8,128)} %shard_map.56.refs_1_), custom_call_target="tpu_custom_call", output_to_operand_aliasing={{}: (3, {})} | custom-call | tf_op jit(solution)/shard_map/pallas_call | solution.py:68
  43.9 0.7 copy-done.5
  44.7 0.8 copy-done.6
  45.4 7.4 %shard_map.58 = f32[1536,400]{1,0:T(8,128)} custom-call(s32[3]{0:T(128)} %pad_add_fusion.off_ref, bf16[1536,3200]{1,0:T(8,128)(2,1)} %a_hbm.7, bf16[400,400]{1,0:T(8,128)(2,1)} %copy-done.5, bf16[400,400]{1,0:T(8,128)(2,1)} %copy-done.6, f32[1536,400]{1,0:T(8,128)} %shard_map.57.refs_2_), custom_call_target="tpu_custom_call", output_to_operand_aliasing={{}: (4, {})} | custom-call | tf_op jit(solution)/shard_map/pallas_call | solution.py:68
  52.8 2.7 %constant_dynamic-slice_fusion = f32[768,400]{1,0:T(8,128)} fusion(f32[1536,400]{1,0:T(8,128)} %shard_map.58, s32[]{:T(128)S(6)} %select_n.47), kind=kLoop, calls=%fused_computation.11 | loop fusion | bytes 2457604 | tf_op jit(solution)/shard_map/dynamic_slice | solution.py:99
  55.5 3.0 %copy.30 = f32[768,400]{0,1:T(8,128)} copy(f32[768,400]{1,0:T(8,128)} %constant_dynamic-slice_fusion) | data formatting | bytes 2457600 | tf_op jit(solution)/shard_map/dynamic_slice | solution.py:99
  58.6 3.3 %collective-permute-done.4 = f32[768,400]{0,1:T(8,128)} collective-permute-done((f32[768,400]{0,1:T(8,128)}, f32[768,400]{0,1:T(8,128)}, u32[]{:S(2)}, u32[]{:S(2)}) %collective-permute-start.4) | collective-permute-done | bytes 1228832 | tf_op jit(solution)/shard_map/ppermute | solution.py:10
  61.8 2.9 %copy.31 = f32[768,400]{1,0:T(8,128)} copy(f32[768,400]{0,1:T(8,128)} %collective-permute-done.4) | data formatting | bytes 2457600 | tf_op jit(solution)/shard_map/ppermute | solution.py:10
  64.7 2.9 %dynamic-slice_add_fusion = f32[768,400]{1,0:T(8,128)} fusion(f32[768,400]{1,0:T(8,128)} %copy.31, f32[1536,400]{1,0:T(8,128)S(1)} %copy-done, s32[]{:T(128)S(6)} %select_n.46), kind=kLoop, calls=%fused_computation.3 | loop fusion | flops 307200 | bytes 3686404 | tf_op jit(solution)/shard_map/add | solution.py:100
  67.7 1.8 %copy.32 = f32[768,400]{0,1:T(8,128)S(1)} copy(f32[768,400]{1,0:T(8,128)} %dynamic-slice_add_fusion) | data formatting | bytes 2457600 | tf_op jit(solution)/shard_map/add | solution.py:100
  69.5 0.6 collective-permute-start.5
  70.1 0.8 compare_and_fusion
  70.8 27.8 %collective-permute-done.5 = f32[768,400]{0,1:T(8,128)S(1)} collective-permute-done((f32[768,400]{0,1:T(8,128)S(1)}, f32[768,400]{0,1:T(8,128)S(1)}, u32[]{:S(2)}, u32[]{:S(2)}) %collective-permute-start.5) | collective-permute-done | bytes 1228832 | tf_op jit(solution)/shard_map/ppermute | solution.py:10
  98.6 0.5 copy.33
  99.1 3.1 %gather_fusion = f32[768,400]{1,0:T(8,128)} fusion(f32[768,400]{1,0:T(8,128)S(1)} %copy.33, s32[1024]{0:T(1024)S(1)} %pad_clamp_fusion), kind=kCustom, calls=%fused_computation | custom fusion | bytes 2460672 | tf_op jit(solution)/shard_map/jit(_take)/gather | solution.py:122
  102.2 1.6 %select_subtract_fusion = f32[768,400]{1,0:T(8,128)S(1)} fusion(f32[768,400]{1,0:T(8,128)S(1)} %copy-done.1, f32[768,400]{1,0:T(8,128)} %gather_fusion, pred[768]{0:T(1024)(128)(4,1)S(1)} %get-tuple-element.5), kind=kLoop, calls=%fused_computation.2 | loop fusion | flops 614400 | bytes 3687168 | tf_op jit(solution)/shard_map/sub | solution.py:122
  103.9 1.5 %copy.34 = f32[768,400]{0,1:T(8,128)} copy(f32[768,400]{1,0:T(8,128)S(1)} %select_subtract_fusion) | data formatting | bytes 2457600 | tf_op jit(solution)/shard_map/sub | solution.py:122
  (21 shorter events, 1.0 us)
Async XLA Ops:
  3.1 5.5 %copy-start.2 = (bf16[800,400]{1,0:T(8,128)(2,1)}, bf16[800,400]{1,0:T(8,128)(2,1)S(1)}, u32[]{:S(2)}) copy-start(bf16[800,400]{1,0:T(8,128)(2,1)S(1)} %compare_select_fusion.refs_0_) | copy-start | bytes 1920004
  3.5 19.1 %collective-permute-start = (bf16[800,400]{0,1:T(8,128)(2,1)S(1)}, bf16[800,400]{0,1:T(8,128)(2,1)S(1)}, u32[]{:S(2)}, u32[]{:S(2)}) collective-permute-start(bf16[800,400]{0,1:T(8,128)(2,1)S(1)} %copy.24), channel_id=1, source_target_pairs={{0,16},{8,24},{16,0},{24,8},{1,17},{9,25},{17,1},{25,9},{2,18},{10... | collective-permute-start | bytes 1920008 | tf_op jit(solution)/shard_map/ppermute | solution.py:10
  6.5 18.2 %collective-permute-start.2 = (bf16[800,400]{0,1:T(8,128)(2,1)S(1)}, bf16[800,400]{0,1:T(8,128)(2,1)S(1)}, u32[]{:S(2)}, u32[]{:S(2)}) collective-permute-start(bf16[800,400]{0,1:T(8,128)(2,1)S(1)} %copy.24), channel_id=1, source_target_pairs={{0,8},{8,0},{16,24},{24,16},{1,9},{9,1},{17,25},{25,17},{2,10},{10... | collective-permute-start | bytes 1920008 | tf_op jit(solution)/shard_map/ppermute | solution.py:10
  22.9 3.0 %copy-start.3 = (bf16[800,400]{1,0:T(8,128)(2,1)}, bf16[800,400]{1,0:T(8,128)(2,1)S(1)}, u32[]{:S(2)}) copy-start(bf16[800,400]{1,0:T(8,128)(2,1)S(1)} %copy.25.refs_0_) | copy-start | bytes 1920004
  22.9 21.0 %collective-permute-start.1 = (bf16[400,400]{1,0:T(8,128)(2,1)S(1)}, bf16[400,400]{1,0:T(8,128)(2,1)S(1)}, u32[]{:S(2)}, u32[]{:S(2)}) collective-permute-start(bf16[400,400]{1,0:T(8,128)(2,1)S(1)} %slice.10), channel_id=1, source_target_pairs={{0,8},{8,0},{16,24},{24,16},{1,9},{9,1},{17,25},{25,17},{2,10},{10... | collective-permute-start | bytes 960008 | tf_op jit(solution)/shard_map/ppermute | solution.py:10
  25.0 11.5 %copy-start.4 = (bf16[800,400]{1,0:T(8,128)(2,1)}, bf16[800,400]{1,0:T(8,128)(2,1)S(1)}, u32[]{:S(2)}) copy-start(bf16[800,400]{1,0:T(8,128)(2,1)S(1)} %copy.27.refs_0_) | copy-start | bytes 1920004
  25.8 18.1 %collective-permute-start.3 = (bf16[400,400]{1,0:T(8,128)(2,1)}, bf16[400,400]{1,0:T(8,128)(2,1)S(1)}, u32[]{:S(2)}, u32[]{:S(2)}) collective-permute-start(bf16[400,400]{1,0:T(8,128)(2,1)} %slice.11), channel_id=1, source_target_pairs={{0,16},{8,24},{16,0},{24,8},{1,17},{9,25},{17,1},{25,9},{2,18},{10... | collective-permute-start | bytes 960008 | tf_op jit(solution)/shard_map/ppermute | solution.py:10
  43.9 0.8 copy-start.5
  44.7 0.8 copy-start.6
  55.5 9.2 %copy-start = (f32[1536,400]{1,0:T(8,128)S(1)}, f32[1536,400]{1,0:T(8,128)}, u32[]{:S(2)}) copy-start(f32[1536,400]{1,0:T(8,128)} %shard_map.58) | copy-start | bytes 7372804
  58.6 3.3 %collective-permute-start.4 = (f32[768,400]{0,1:T(8,128)}, f32[768,400]{0,1:T(8,128)}, u32[]{:S(2)}, u32[]{:S(2)}) collective-permute-start(f32[768,400]{0,1:T(8,128)} %copy.30), channel_id=1, source_target_pairs={{0,1},{1,0},{2,3},{3,2},{4,5},{5,4},{6,7},{7,6},{8,9},{9,8},{10,11... | collective-permute-start | bytes 3686408 | tf_op jit(solution)/shard_map/ppermute | solution.py:10
  69.5 29.1 %collective-permute-start.5 = (f32[768,400]{0,1:T(8,128)S(1)}, f32[768,400]{0,1:T(8,128)S(1)}, u32[]{:S(2)}, u32[]{:S(2)}) collective-permute-start(f32[768,400]{0,1:T(8,128)S(1)} %copy.32), channel_id=1, source_target_pairs={{0,16},{8,24},{16,0},{24,8},{1,17},{9,25},{17,1},{25,9},{2,18},{10... | collective-permute-start | bytes 3686408 | tf_op jit(solution)/shard_map/ppermute | solution.py:10
  99.1 3.2 %copy-start.1 = (f32[768,400]{1,0:T(8,128)S(1)}, f32[768,400]{1,0:T(8,128)}, u32[]{:S(2)}) copy-start(f32[768,400]{1,0:T(8,128)} %dynamic-slice_add_fusion) | copy-start | bytes 3686404

commit v6 on v1

--- a/solution.py
+++ b/solution.py
@@ -1,6 +1,8 @@
 import jax
 import jax.numpy as jnp
 from jax import lax
+from jax.experimental import pallas as pl
+from jax.experimental.pallas import tpu as pltpu
 from jax.sharding import PartitionSpec as P
 
 
@@ -10,18 +12,29 @@
 
 def gather_prow(own, prow_idx, prow_count):
     count = own.shape[0]
-    blocks = {0: own}
-    if prow_count == 4:
-        blocks[1] = swap(own, "prow", 1)
-        blocks[2] = swap(own, "prow", 2)
-        blocks[3] = swap(blocks[2], "prow", 1)
-    else:
-        for s in range(1, prow_count):
-            blocks[s] = swap(own, "prow", s)
-    piece = jnp.zeros((prow_count * count,) + own.shape[1:], own.dtype)
-    for s, block in blocks.items():
-        piece = lax.dynamic_update_slice(piece, block, (jnp.bitwise_xor(prow_idx, s) * count, 0))
-    return piece
+    if prow_count == 4 and count % 32 == 0:
+        half = count // 2
+        from_x = swap(own, "prow", 1)
+        from_y = swap(own, "prow", 2)
+        diag_a = swap(from_y[:half], "prow", 1)
+        diag_b = swap(from_x[half:], "prow", 2)
+        base = jnp.bitwise_xor(prow_idx, 3) * count
+        return [[(own, prow_idx * count)], [(from_y, jnp.bitwise_xor(prow_idx, 2) * count)],
+                [(from_x, jnp.bitwise_xor(prow_idx, 1) * count)], [(diag_a, base), (diag_b, base + half)]]
+    groups = [[(own, prow_idx * count)]]
+    for s in range(1, prow_count):
+        groups.append([(swap(own, "prow", s), jnp.bitwise_xor(prow_idx, s) * count)])
+    return groups
+
+
+def contract(amplitudes, groups, prow_idx, prow_count):
+    terms = None
+    for group in groups:
+        for b, o in group:
+            window = lax.dynamic_slice_in_dim(amplitudes, o, b.shape[0], axis=1)
+            product = jnp.dot(window, b, preferred_element_type=jnp.float32)
+            terms = product if terms is None else terms + product
+    return terms
 
 
 def reduce_cuts(terms, cuts_idx, cuts_count):
@@ -36,15 +49,13 @@
 def shards(amplitudes, integrals, irrep_rows, irrep_cols, mirror_row):
     prow_count = lax.axis_size("prow")
     cuts_count = lax.axis_size("cuts")
-    slice_width = amplitudes.shape[1]
     prow_idx = lax.axis_index("prow")
     cuts_idx = lax.axis_index("cuts")
-    piece = gather_prow(integrals, prow_idx, prow_count)
-    count = piece.shape[0]
-    labels = lax.dynamic_slice(irrep_rows, (cuts_idx * slice_width,), (count,))
+    count = integrals.shape[0]
+    labels = lax.dynamic_slice(irrep_rows, ((cuts_idx * prow_count + prow_idx) * count,), (count,))
     same = labels[:, None] == irrep_cols[None, :]
-    blocked = jnp.where(same, piece, jnp.zeros_like(piece))
-    terms = jnp.dot(amplitudes, blocked, preferred_element_type=jnp.float32)
+    blocked = jnp.where(same, integrals, jnp.zeros_like(integrals))
+    terms = contract(amplitudes, gather_prow(blocked, prow_idx, prow_count), prow_idx, prow_count)
     cycle = reduce_cuts(terms, cuts_idx, cuts_count)
     block_rows = cycle.shape[0]
     half = prow_count // 2

time: 105 us -> 79.3 us (0.76)
  local copies, waits for them, and re-layouts: 40.2 us -> 6.18 us
  matrix products: 7.25 us -> 9.93 us
  other arithmetic: 4.67 us -> 7.1 us
  waiting for transfers between devices: 44.4 us -> 46.8 us
    dynamic_update_slice x4 -> x0, local copies, waits for them, and re-layouts: 34.2 us -> none  [gather_prow(): lax.dynamic_update_slice(piece, block, (jnp.bitwise_xor(prow_idx, s) * co...]
    dot_general x1 -> x5, matrix products: 7.25 us -> 9.93 us  [contract(): product = jnp.dot(window, b, preferred_element_type=jnp.float32)]
    ppermute x5 -> x6, waiting for transfers between devices: 44.4 us -> 46.8 us  [swap(): lax.ppermute(value, axis, [(i, i ^ mask) for i in range(lax.axis_size(axi...]
    unnamed x12 -> x2, local copies, waits for them, and re-layouts: 1.48 us -> 0.01 us
    select_n x0 -> x1, other arithmetic: none -> 1.38 us  [shards(): blocked = jnp.where(same, integrals, jnp.zeros_like(integrals))]
    slice x0 -> x2, local copies, waits for them, and re-layouts: none -> 1.23 us  [the longest x1 1.03 us: gather_prow(): diag_a = swap(from_y[:half], 'prow', 1)]
    gather x2, local copies, waits for them, and re-layouts: 3.65 us -> 2.59 us  [shards(): return cycle - jnp.take(fetched, local, axis=0)]
    ppermute x5 -> x6, starting transfers between devices: 8.08 us -> 8.78 us  [swap(): lax.ppermute(value, axis, [(i, i ^ mask) for i in range(lax.axis_size(axi...]
  transfers between devices with their start and end apart: 5 -> 6, of which waited for: 3 -> 5; matrix products, arithmetic and copies ran while one was open for 25% -> 12% of each run, Pallas kernels for 0% -> 0%
where the time goes in v6:
time: 79.3 us; the launch traced here: 78.9 us
  waiting for transfers between devices  46.8 us (59%)
  matrix products  9.93 us (13%)
  starting transfers between devices  8.78 us (11%)
  other arithmetic  7.1 us (9%)
  local copies, waits for them, and re-layouts  6.18 us (8%)
    ppermute x6, waiting for transfers between devices, swap(): lax.ppermute(value, axis, [(i, i ^ mask) for i in range(lax.axis_size(axi...  46.8 us
    dot_general x5, matrix products, contract(): product = jnp.dot(window, b, preferred_element_type=jnp.float32)  9.93 us
    ppermute x6, starting transfers between devices, swap(): lax.ppermute(value, axis, [(i, i ^ mask) for i in range(lax.axis_size(axi...  8.78 us
    gather x2, local copies, waits for them, and re-layouts, shards(): return cycle - jnp.take(fetched, local, axis=0)  2.59 us
    add x1, other arithmetic, reduce_cuts(): total = total + swap(part, 'cuts', s)  2.47 us
    sub x1, other arithmetic, shards(): return cycle - jnp.take(fetched, local, axis=0)  2.47 us
  transfers between devices with their start and end apart: 6, of which 5 were waited for; matrix products, arithmetic and copies ran while one was open for 12% of the time, Pallas kernels for 0%

profile of v6, /device:TPU:0, one launch (start us, length us, event | category | flops | bytes accessed | tf_op | source)
XLA Modules:
  0.0 78.9 jit_solution(7105536229171460406)
XLA Ops:
  0.0 0.8 dynamic_slice.28
  0.8 1.4 %compare_select_fusion = bf16[800,400]{0,1:T(8,128)(2,1)S(1)} fusion(bf16[800,400]{0,1:T(8,128)(2,1)} %param.6, s32[800]{0:T(1024)S(1)} %dynamic_slice.28, s32[400]{0:T(512)} %param.8), kind=kLoop, calls=%fused_computation.13 | loop fusion | flops 640000 | bytes 1284800 | tf_op jit(solution)/shard_map/jit(_where)/select_n | solution.py:57
  2.2 3.0 %collective-permute-start.1 = (bf16[800,400]{0,1:T(8,128)(2,1)S(1)}, bf16[800,400]{0,1:T(8,128)(2,1)S(1)}, u32[]{:S(2)}, u32[]{:S(2)}) collective-permute-start(bf16[800,400]{0,1:T(8,128)(2,1)S(1)} %compare_select_fusion), channel_id=1, source_target_pairs={{0,8},{8,0},{16,24},{24,16},{1,9},{9,1},{17,25},{25,17},{2,10},{10... | collective-permute-start | bytes 1920008 | tf_op jit(solution)/shard_map/ppermute | solution.py:10
  5.2 1.5 %collective-permute-start = (bf16[800,400]{0,1:T(8,128)(2,1)S(1)}, bf16[800,400]{0,1:T(8,128)(2,1)}, u32[]{:S(2)}, u32[]{:S(2)}) collective-permute-start(bf16[800,400]{0,1:T(8,128)(2,1)S(1)} %compare_select_fusion), channel_id=1, source_target_pairs={{0,16},{8,24},{16,0},{24,8},{1,17},{9,25},{17,1},{25,9},{2,18},{10... | collective-permute-start | bytes 1920008 | tf_op jit(solution)/shard_map/ppermute | solution.py:10
  6.7 0.0 copy-start
  6.7 3.6 %fusion.4 = f32[1536,400]{0,1:T(8,128)S(1)} fusion(bf16[800,400]{0,1:T(8,128)(2,1)S(1)} %compare_select_fusion, bf16[1536,3200]{1,0:T(8,128)(2,1)} %param.5, s32[]{:T(128)S(6)} %select_n.40), kind=kOutput, calls=%fused_computation.7 | convolution fusion | flops 983040000 | bytes 5850116 | tf_op jit(solution)/shard_map/dot_general | solution.py:35
  10.3 10.9 %collective-permute-done.1 = bf16[800,400]{0,1:T(8,128)(2,1)S(1)} collective-permute-done((bf16[800,400]{0,1:T(8,128)(2,1)S(1)}, bf16[800,400]{0,1:T(8,128)(2,1)S(1)}, u32[]{:S(2)}, u32[]{:S(2)}) %collective-permute-start.1) | collective-permute-done | bytes 640032 | tf_op jit(solution)/shard_map/ppermute | solution.py:10
  21.2 0.2 slice.11
  21.4 1.8 %collective-permute-start.3 = (bf16[400,400]{0,1:T(8,128)(2,1)S(1)}, bf16[400,400]{0,1:T(8,128)(2,1)S(1)}, u32[]{:S(2)}, u32[]{:S(2)}) collective-permute-start(bf16[400,400]{0,1:T(8,128)(2,1)S(1)} %slice.11), channel_id=1, source_target_pairs={{0,16},{8,24},{16,0},{24,8},{1,17},{9,25},{17,1},{25,9},{2,18},{10... | collective-permute-start | bytes 960008 | tf_op jit(solution)/shard_map/ppermute | solution.py:10
  23.2 0.0 collective-permute-done
  23.3 1.0 %slice.10 = bf16[400,400]{0,1:T(8,128)(2,1)S(1)} slice(bf16[800,400]{0,1:T(8,128)(2,1)} %collective-permute-done), slice={[0:400], [0:400]} | slice | bytes 640000 | tf_op jit(solution)/shard_map/slice | solution.py:19
  24.3 1.6 %collective-permute-start.2 = (bf16[400,400]{0,1:T(8,128)(2,1)S(1)}, bf16[400,400]{0,1:T(8,128)(2,1)S(1)}, u32[]{:S(2)}, u32[]{:S(2)}) collective-permute-start(bf16[400,400]{0,1:T(8,128)(2,1)S(1)} %slice.10), channel_id=1, source_target_pairs={{0,8},{8,0},{16,24},{24,16},{1,9},{9,1},{17,25},{25,17},{2,10},{10... | collective-permute-start | bytes 960008 | tf_op jit(solution)/shard_map/ppermute | solution.py:10
  25.8 0.0 copy-done
  25.8 2.8 %convolution_add_fusion.1 = f32[1536,400]{0,1:T(8,128)S(1)} fusion(f32[1536,400]{0,1:T(8,128)S(1)} %fusion.4, bf16[800,400]{0,1:T(8,128)(2,1)} %collective-permute-done, bf16[1536,3200]{1,0:T(8,128)(2,1)S(1)} %copy-done, s32[]{:T(128)S(6)} %select_n.43), kind=kOutput, calls=%fused_computation.3 | convolution fusion | flops 983654400 | bytes 8307716 | tf_op jit(solution)/shard_map/dot_general | solution.py:35
  28.6 3.6 %collective-permute-done.3 = bf16[400,400]{0,1:T(8,128)(2,1)S(1)} collective-permute-done((bf16[400,400]{0,1:T(8,128)(2,1)S(1)}, bf16[400,400]{0,1:T(8,128)(2,1)S(1)}, u32[]{:S(2)}, u32[]{:S(2)}) %collective-permute-start.3) | collective-permute-done | bytes 320032 | tf_op jit(solution)/shard_map/ppermute | solution.py:10
  32.2 0.9 %fusion.6 = f32[1536,400]{0,1:T(8,128)S(1)} fusion(bf16[400,400]{0,1:T(8,128)(2,1)S(1)} %collective-permute-done.3, bf16[1536,3200]{1,0:T(8,128)(2,1)S(1)} %copy-done, s32[]{:T(128)S(6)} %select_n.46), kind=kOutput, calls=%fused_computation.9 | convolution fusion | flops 491520000 | bytes 4440068 | tf_op jit(solution)/shard_map/dot_general | solution.py:35
  33.2 1.3 %collective-permute-done.2 = bf16[400,400]{0,1:T(8,128)(2,1)S(1)} collective-permute-done((bf16[400,400]{0,1:T(8,128)(2,1)S(1)}, bf16[400,400]{0,1:T(8,128)(2,1)S(1)}, u32[]{:S(2)}, u32[]{:S(2)}) %collective-permute-start.2) | collective-permute-done | bytes 320032 | tf_op jit(solution)/shard_map/ppermute | solution.py:10
  34.5 0.9 %fusion.8 = f32[1536,400]{0,1:T(8,128)S(1)} fusion(bf16[400,400]{0,1:T(8,128)(2,1)S(1)} %collective-permute-done.2, bf16[1536,3200]{1,0:T(8,128)(2,1)S(1)} %copy-done, s32[]{:T(128)S(6)} %select_n.45), kind=kOutput, calls=%fused_computation.11 | convolution fusion | flops 491520000 | bytes 4440068 | tf_op jit(solution)/shard_map/dot_general | solution.py:35
  35.5 1.7 %fusion.1 = f32[1536,400]{0,1:T(8,128)S(1)} fusion(f32[1536,400]{0,1:T(8,128)S(1)} %fusion.6, f32[1536,400]{0,1:T(8,128)S(1)} %fusion.8, f32[1536,400]{0,1:T(8,128)S(1)} %convolution_add_fusion.1, bf16[800,400]{0,1:T(8,128)(2,1)S(1)} %collective-permute-done.1, bf16[1536,3200]{1,0:T(8,128)(2,1)S(1)} %copy-done, s32[]{:T(128)S(6)} %select_n.44), kind=kOutput, calls=%fused_computation.4 | convolution fusion | flops 984883200 | bytes 13299716 | tf_op jit(solution)/shard_map/dot_general | solution.py:35
  37.2 1.1 %constant_dynamic-slice_fusion = f32[768,400]{0,1:T(8,128)} fusion(f32[1536,400]{0,1:T(8,128)S(1)} %fusion.1, s32[]{:T(128)S(6)} %select_n.48), kind=kLoop, calls=%fused_computation.19 | loop fusion | bytes 2457604 | tf_op jit(solution)/shard_map/dynamic_slice | solution.py:44
  38.3 0.0 collective-permute-start.4
  38.3 3.3 %collective-permute-done.4 = f32[768,400]{0,1:T(8,128)} collective-permute-done((f32[768,400]{0,1:T(8,128)}, f32[768,400]{0,1:T(8,128)}, u32[]{:S(2)}, u32[]{:S(2)}) %collective-permute-start.4) | collective-permute-done | bytes 1228832 | tf_op jit(solution)/shard_map/ppermute | solution.py:10
  41.6 2.5 %dynamic-slice_add_fusion = f32[768,400]{0,1:T(8,128)} fusion(f32[768,400]{0,1:T(8,128)} %collective-permute-done.4, f32[1536,400]{0,1:T(8,128)S(1)} %fusion.1, s32[]{:T(128)S(6)} %select_n.47), kind=kLoop, calls=%fused_computation.15 | loop fusion | flops 307200 | bytes 3686404 | tf_op jit(solution)/shard_map/add | solution.py:45
  44.0 0.9 %collective-permute-start.5 = (f32[768,400]{0,1:T(8,128)}, f32[768,400]{0,1:T(8,128)S(1)}, u32[]{:S(2)}, u32[]{:S(2)}) collective-permute-start(f32[768,400]{0,1:T(8,128)} %dynamic-slice_add_fusion), channel_id=1, source_target_pairs={{0,16},{8,24},{16,0},{24,8},{1,17},{9,25},{17,1},{25,9},{2,18},{10... | collective-permute-start | bytes 3686408 | tf_op jit(solution)/shard_map/ppermute | solution.py:10
  44.9 0.8 compare_and_fusion
  45.7 27.7 %collective-permute-done.5 = f32[768,400]{0,1:T(8,128)S(1)} collective-permute-done((f32[768,400]{0,1:T(8,128)}, f32[768,400]{0,1:T(8,128)S(1)}, u32[]{:S(2)}, u32[]{:S(2)}) %collective-permute-start.5) | collective-permute-done | bytes 1228832 | tf_op jit(solution)/shard_map/ppermute | solution.py:10
  73.4 0.5 copy.6
  73.8 2.2 %gather_fusion = f32[768,400]{1,0:T(8,128)S(1)} fusion(f32[768,400]{1,0:T(8,128)S(1)} %copy.6, s32[1024]{0:T(1024)S(1)} %pad_clamp_fusion), kind=kCustom, calls=%fused_computation | custom fusion | bytes 2460672 | tf_op jit(solution)/shard_map/jit(_take)/gather | solution.py:67
  76.0 0.4 copy.7
  76.4 2.5 %select_subtract_fusion = f32[768,400]{0,1:T(8,128)} fusion(f32[768,400]{0,1:T(8,128)} %dynamic-slice_add_fusion, f32[768,400]{0,1:T(8,128)S(1)} %copy.7, pred[768]{0:T(1024)(128)(4,1)S(1)} %get-tuple-element.5), kind=kLoop, calls=%fused_computation.14 | loop fusion | flops 614400 | bytes 3687168 | tf_op jit(solution)/shard_map/sub | solution.py:67
  (1 shorter events, 0.0 us)
Async XLA Ops:
  2.2 19.1 %collective-permute-start.1 = (bf16[800,400]{0,1:T(8,128)(2,1)S(1)}, bf16[800,400]{0,1:T(8,128)(2,1)S(1)}, u32[]{:S(2)}, u32[]{:S(2)}) collective-permute-start(bf16[800,400]{0,1:T(8,128)(2,1)S(1)} %compare_select_fusion), channel_id=1, source_target_pairs={{0,8},{8,0},{16,24},{24,16},{1,9},{9,1},{17,25},{25,17},{2,10},{10... | collective-permute-start | bytes 1920008 | tf_op jit(solution)/shard_map/ppermute | solution.py:10
  5.2 18.1 %collective-permute-start = (bf16[800,400]{0,1:T(8,128)(2,1)S(1)}, bf16[800,400]{0,1:T(8,128)(2,1)}, u32[]{:S(2)}, u32[]{:S(2)}) collective-permute-start(bf16[800,400]{0,1:T(8,128)(2,1)S(1)} %compare_select_fusion), channel_id=1, source_target_pairs={{0,16},{8,24},{16,0},{24,8},{1,17},{9,25},{17,1},{25,9},{2,18},{10... | collective-permute-start | bytes 1920008 | tf_op jit(solution)/shard_map/ppermute | solution.py:10
  6.7 19.2 %copy-start = (bf16[1536,3200]{1,0:T(8,128)(2,1)S(1)}, bf16[1536,3200]{1,0:T(8,128)(2,1)}, u32[]{:S(2)}) copy-start(bf16[1536,3200]{1,0:T(8,128)(2,1)} %param.5) | copy-start | bytes 29491204
  21.4 10.8 %collective-permute-start.3 = (bf16[400,400]{0,1:T(8,128)(2,1)S(1)}, bf16[400,400]{0,1:T(8,128)(2,1)S(1)}, u32[]{:S(2)}, u32[]{:S(2)}) collective-permute-start(bf16[400,400]{0,1:T(8,128)(2,1)S(1)} %slice.11), channel_id=1, source_target_pairs={{0,16},{8,24},{16,0},{24,8},{1,17},{9,25},{17,1},{25,9},{2,18},{10... | collective-permute-start | bytes 960008 | tf_op jit(solution)/shard_map/ppermute | solution.py:10
  24.3 10.2 %collective-permute-start.2 = (bf16[400,400]{0,1:T(8,128)(2,1)S(1)}, bf16[400,400]{0,1:T(8,128)(2,1)S(1)}, u32[]{:S(2)}, u32[]{:S(2)}) collective-permute-start(bf16[400,400]{0,1:T(8,128)(2,1)S(1)} %slice.10), channel_id=1, source_target_pairs={{0,8},{8,0},{16,24},{24,16},{1,9},{9,1},{17,25},{25,17},{2,10},{10... | collective-permute-start | bytes 960008 | tf_op jit(solution)/shard_map/ppermute | solution.py:10
  38.3 3.3 %collective-permute-start.4 = (f32[768,400]{0,1:T(8,128)}, f32[768,400]{0,1:T(8,128)}, u32[]{:S(2)}, u32[]{:S(2)}) collective-permute-start(f32[768,400]{0,1:T(8,128)} %constant_dynamic-slice_fusion), channel_id=1, source_target_pairs={{0,1},{1,0},{2,3},{3,2},{4,5},{5,4},{6,7},{7,6},{8,9},{9,8},{10,11... | collective-permute-start | bytes 3686408 | tf_op jit(solution)/shard_map/ppermute | solution.py:10
  44.0 29.3 %collective-permute-start.5 = (f32[768,400]{0,1:T(8,128)}, f32[768,400]{0,1:T(8,128)S(1)}, u32[]{:S(2)}, u32[]{:S(2)}) collective-permute-start(f32[768,400]{0,1:T(8,128)} %dynamic-slice_add_fusion), channel_id=1, source_target_pairs={{0,16},{8,24},{16,0},{24,8},{1,17},{9,25},{17,1},{25,9},{2,18},{10... | collective-permute-start | bytes 3686408 | tf_op jit(solution)/shard_map/ppermute | solution.py:10

commit v7 on v6

--- a/solution.py
+++ b/solution.py
@@ -27,23 +27,15 @@
     return groups
 
 
-def contract(amplitudes, groups, prow_idx, prow_count):
+def contract(amplitudes, groups, first, rows):
+    band = lax.dynamic_slice_in_dim(amplitudes, first, rows, axis=0)
     terms = None
     for group in groups:
         for b, o in group:
-            window = lax.dynamic_slice_in_dim(amplitudes, o, b.shape[0], axis=1)
+            window = lax.dynamic_slice_in_dim(band, o, b.shape[0], axis=1)
             product = jnp.dot(window, b, preferred_element_type=jnp.float32)
             terms = product if terms is None else terms + product
     return terms
-
-
-def reduce_cuts(terms, cuts_idx, cuts_count):
-    rows = terms.shape[0] // cuts_count
-    total = lax.dynamic_slice_in_dim(terms, cuts_idx * rows, rows, axis=0)
-    for s in range(1, cuts_count):
-        part = lax.dynamic_slice_in_dim(terms, jnp.bitwise_xor(cuts_idx, s) * rows, rows, axis=0)
-        total = total + swap(part, "cuts", s)
-    return total
 
 
 def shards(amplitudes, integrals, irrep_rows, irrep_cols, mirror_row):
@@ -55,16 +47,31 @@
     labels = lax.dynamic_slice(irrep_rows, ((cuts_idx * prow_count + prow_idx) * count,), (count,))
     same = labels[:, None] == irrep_cols[None, :]
     blocked = jnp.where(same, integrals, jnp.zeros_like(integrals))
-    terms = contract(amplitudes, gather_prow(blocked, prow_idx, prow_count), prow_idx, prow_count)
-    cycle = reduce_cuts(terms, cuts_idx, cuts_count)
-    block_rows = cycle.shape[0]
+    groups = gather_prow(blocked, prow_idx, prow_count)
+    block_rows = amplitudes.shape[0] // cuts_count
+    sent = []
+    for s in range(1, cuts_count):
+        other = jnp.bitwise_xor(cuts_idx, s)
+        sent.append((s, contract(amplitudes, groups, other * block_rows, block_rows)))
+    kept = contract(amplitudes, groups, cuts_idx * block_rows, block_rows)
+    pieces = 2 if block_rows % 16 == 0 else 1
+    step = block_rows // pieces
     half = prow_count // 2
+    fetched = []
+    cycle = []
+    for h in range(pieces):
+        total = kept[h * step:(h + 1) * step]
+        for s, part in sent:
+            total = total + swap(part[h * step:(h + 1) * step], "cuts", s)
+        cycle.append(total)
+        fetched.append(swap(total, "prow", half))
+    cycle = jnp.concatenate(cycle, axis=0) if pieces > 1 else cycle[0]
+    fetched = jnp.concatenate(fetched, axis=0) if pieces > 1 else fetched[0]
     own_block = prow_idx * cuts_count + cuts_idx
     partner_block = jnp.bitwise_xor(prow_idx, half) * cuts_count + cuts_idx
     mine = lax.dynamic_slice(mirror_row, (own_block * block_rows,), (block_rows,))
     local = mine - partner_block * block_rows
-    fetched = swap(cycle, "prow", half)
-    return cycle - jnp.take(fetched, local, axis=0)
+    return cycle - jnp.take(fetched, local, axis=0, mode="clip")
 
 
 def solution(mesh):

time: 79.3 us -> 74.6 us (0.941)
  waiting for transfers between devices: 46.8 us -> 39.7 us
  matrix products: 9.93 us -> 13.9 us
  local copies, waits for them, and re-layouts: 6.18 us -> 4.14 us
  starting transfers between devices: 8.78 us -> 10.5 us
  other arithmetic: 7.1 us -> 5.85 us
    ppermute x6 -> x8, waiting for transfers between devices: 46.8 us -> 39.7 us  [swap(): lax.ppermute(value, axis, [(i, i ^ mask) for i in range(lax.axis_size(axi...]
    dot_general x5 -> x10, matrix products: 9.93 us -> 13.9 us  [contract(): product = jnp.dot(window, b, preferred_element_type=jnp.float32)]
    ppermute x6 -> x8, starting transfers between devices: 8.78 us -> 10.5 us  [swap(): lax.ppermute(value, axis, [(i, i ^ mask) for i in range(lax.axis_size(axi...]
    add x1, other arithmetic: 2.47 us -> 1.18 us  [shards(): total = total + swap(part[h * step:(h + 1) * step], 'cuts', s)]
    dynamic_slice x1 -> x0, local copies, waits for them, and re-layouts: 1.12 us -> none  [reduce_cuts(): lax.dynamic_slice_in_dim(terms, jnp.bitwise_xor(cuts_idx, s) * rows, rows...]
    slice x1, local copies, waits for them, and re-layouts: 1.03 us -> 0.03 us  [gather_prow(): diag_a = swap(from_y[:half], 'prow', 1)]
    sub x1 -> x2, other arithmetic: 2.47 us -> 3.2 us  [the longest x1 2.43 us: shards(): return cycle - jnp.take(fetched, local, axis=0, mode='clip')]
  transfers between devices with their start and end apart: 6 -> 8, of which waited for: 5 -> 5; matrix products, arithmetic and copies ran while one was open for 12% -> 18% of each run, Pallas kernels for 0% -> 0%
where the time goes in v7:
time: 74.6 us; the launch traced here: 74.3 us
  waiting for transfers between devices  39.7 us (53%)
  matrix products  13.9 us (19%)
  starting transfers between devices  10.5 us (14%)
  other arithmetic  5.85 us (8%)
  local copies, waits for them, and re-layouts  4.14 us (6%)
    ppermute x8, waiting for transfers between devices, swap(): lax.ppermute(value, axis, [(i, i ^ mask) for i in range(lax.axis_size(axi...  39.7 us
    dot_general x10, matrix products, contract(): product = jnp.dot(window, b, preferred_element_type=jnp.float32)  13.9 us
    ppermute x8, starting transfers between devices, swap(): lax.ppermute(value, axis, [(i, i ^ mask) for i in range(lax.axis_size(axi...  10.5 us
    gather x2, local copies, waits for them, and re-layouts, shards(): return cycle - jnp.take(fetched, local, axis=0, mode='clip')  2.59 us
    sub x1, other arithmetic, shards(): return cycle - jnp.take(fetched, local, axis=0, mode='clip')  2.43 us
  transfers between devices with their start and end apart: 8, of which 5 were waited for; matrix products, arithmetic and copies ran while one was open for 18% of the time, Pallas kernels for 0%

profile of v7, /device:TPU:0, one launch (start us, length us, event | category | flops | bytes accessed | tf_op | source)
XLA Modules:
  0.0 74.3 jit_solution(10078192549785927875)
XLA Ops:
  0.0 0.8 %dynamic_slice.39 = s32[800]{0:T(1024)S(1)} dynamic-slice(s32[6400]{0:T(1024)} %param.7, s32[]{:T(128)S(6)} %select_n.54), dynamic_slice_sizes={800} | dynamic-slice | bytes 6404 | tf_op jit(solution)/shard_map/dynamic_slice | solution.py:47
  0.8 1.4 %compare_select_fusion = bf16[800,400]{0,1:T(8,128)(2,1)S(1)} fusion(bf16[800,400]{0,1:T(8,128)(2,1)} %param.6, s32[800]{0:T(1024)S(1)} %dynamic_slice.39, s32[400]{0:T(512)} %param.8), kind=kLoop, calls=%fused_computation.1 | loop fusion | flops 640000 | bytes 1284800 | tf_op jit(solution)/shard_map/jit(_where)/select_n | solution.py:49
  2.2 3.0 %collective-permute-start.1 = (bf16[800,400]{0,1:T(8,128)(2,1)S(1)}, bf16[800,400]{0,1:T(8,128)(2,1)S(1)}, u32[]{:S(2)}, u32[]{:S(2)}) collective-permute-start(bf16[800,400]{0,1:T(8,128)(2,1)S(1)} %compare_select_fusion), channel_id=1, source_target_pairs={{0,8},{8,0},{16,24},{24,16},{1,9},{9,1},{17,25},{25,17},{2,10},{10... | collective-permute-start | bytes 1920008 | tf_op jit(solution)/shard_map/ppermute | solution.py:10
  5.2 1.5 %collective-permute-start = (bf16[800,400]{0,1:T(8,128)(2,1)S(1)}, bf16[800,400]{0,1:T(8,128)(2,1)S(1)}, u32[]{:S(2)}, u32[]{:S(2)}) collective-permute-start(bf16[800,400]{0,1:T(8,128)(2,1)S(1)} %compare_select_fusion), channel_id=1, source_target_pairs={{0,16},{8,24},{16,0},{24,8},{1,17},{9,25},{17,1},{25,9},{2,18},{10... | collective-permute-start | bytes 1920008 | tf_op jit(solution)/shard_map/ppermute | solution.py:10
  6.7 2.6 %fusion.10 = f32[768,400]{0,1:T(8,128)S(1)} fusion(bf16[800,400]{0,1:T(8,128)(2,1)S(1)} %compare_select_fusion, bf16[1536,3200]{1,0:T(8,128)(2,1)} %param.5, s32[]{:T(128)S(6)} %select_n.51, s32[]{:T(128)S(6)} %select_n.53), kind=kOutput, calls=%fused_computation.16 | convolution fusion | flops 491520000 | bytes 3245064 | tf_op jit(solution)/shard_map/dot_general | solution.py:36
  9.2 3.1 %fusion.6 = f32[768,400]{0,1:T(8,128)S(1)} fusion(bf16[800,400]{0,1:T(8,128)(2,1)S(1)} %compare_select_fusion, bf16[1536,3200]{1,0:T(8,128)(2,1)} %param.5, s32[]{:T(128)S(6)} %select_n.65, s32[]{:T(128)S(6)} %select_n.53), kind=kOutput, calls=%fused_computation.12 | convolution fusion | flops 491520000 | bytes 3245064 | tf_op jit(solution)/shard_map/dot_general | solution.py:36
  12.3 8.9 %collective-permute-done.1 = bf16[800,400]{0,1:T(8,128)(2,1)S(1)} collective-permute-done((bf16[800,400]{0,1:T(8,128)(2,1)S(1)}, bf16[800,400]{0,1:T(8,128)(2,1)S(1)}, u32[]{:S(2)}, u32[]{:S(2)}) %collective-permute-start.1) | collective-permute-done | bytes 640032 | tf_op jit(solution)/shard_map/ppermute | solution.py:10
  21.2 0.2 slice.27
  21.4 1.8 %collective-permute-start.3 = (bf16[400,400]{0,1:T(8,128)(2,1)S(1)}, bf16[400,400]{0,1:T(8,128)(2,1)S(1)}, u32[]{:S(2)}, u32[]{:S(2)}) collective-permute-start(bf16[400,400]{0,1:T(8,128)(2,1)S(1)} %slice.27), channel_id=1, source_target_pairs={{0,16},{8,24},{16,0},{24,8},{1,17},{9,25},{17,1},{25,9},{2,18},{10... | collective-permute-start | bytes 960008 | tf_op jit(solution)/shard_map/ppermute | solution.py:10
  23.3 1.6 %collective-permute-start.2 = (bf16[400,400]{0,1:T(8,128)(2,1)S(1)}, bf16[400,400]{0,1:T(8,128)(2,1)S(1)}, u32[]{:S(2)}, u32[]{:S(2)}) collective-permute-start(bf16[400,400]{0,1:T(8,128)(2,1)S(1)} %slice.26), channel_id=1, source_target_pairs={{0,8},{8,0},{16,24},{24,16},{1,9},{9,1},{17,25},{25,17},{2,10},{10... | collective-permute-start | bytes 960008 | tf_op jit(solution)/shard_map/ppermute | solution.py:10
  24.8 2.4 %convolution_add_fusion.3 = f32[768,400]{0,1:T(8,128)S(1)} fusion(f32[768,400]{0,1:T(8,128)S(1)} %fusion.10, bf16[800,400]{0,1:T(8,128)(2,1)S(1)} %collective-permute-done, bf16[1536,3200]{1,0:T(8,128)(2,1)} %param.5, s32[]{:T(128)S(6)} %select_n.51, s32[]{:T(128)S(6)} %select_n.57), kind=kOutput, calls=%fused_computation.9 | convolution fusion | flops 491827200 | bytes 4473864 | tf_op jit(solution)/shard_map/dot_general | solution.py:36
  27.3 1.0 %convolution_add_fusion.1 = f32[768,400]{0,1:T(8,128)S(1)} fusion(f32[768,400]{0,1:T(8,128)S(1)} %fusion.6, bf16[800,400]{0,1:T(8,128)(2,1)S(1)} %collective-permute-done, bf16[1536,3200]{1,0:T(8,128)(2,1)S(1)} %copy-done, s32[]{:T(128)S(6)} %select_n.65, s32[]{:T(128)S(6)} %select_n.57), kind=kOutput, calls=%fused_computation.5 | convolution fusion | flops 491827200 | bytes 4550664 | tf_op jit(solution)/shard_map/dot_general | solution.py:36
  28.3 3.8 %collective-permute-done.3 = bf16[400,400]{0,1:T(8,128)(2,1)S(1)} collective-permute-done((bf16[400,400]{0,1:T(8,128)(2,1)S(1)}, bf16[400,400]{0,1:T(8,128)(2,1)S(1)}, u32[]{:S(2)}, u32[]{:S(2)}) %collective-permute-start.3) | collective-permute-done | bytes 320032 | tf_op jit(solution)/shard_map/ppermute | solution.py:10
  32.1 0.7 fusion.12
  32.8 0.6 collective-permute-done.2
  33.4 0.7 fusion.14
  34.1 1.1 %fusion.1 = f32[768,400]{0,1:T(8,128)S(1)} fusion(f32[768,400]{0,1:T(8,128)S(1)} %fusion.12, f32[768,400]{0,1:T(8,128)S(1)} %fusion.14, f32[768,400]{0,1:T(8,128)S(1)} %convolution_add_fusion.1, bf16[800,400]{0,1:T(8,128)(2,1)S(1)} %collective-permute-done.1, bf16[1536,3200]{1,0:T(8,128)(2,1)S(1)} %copy-done, s32[]{:T(128)S(6)} %select_n.65, s32[]{:T(128)S(6)} %select_n.59), kind=kOutput, calls=%fused_computation.4 | convolution fusion | flops 492441600 | bytes 7008264 | tf_op jit(solution)/shard_map/dot_general | solution.py:36
  35.4 0.5 collective-permute-start.5
  35.9 0.7 fusion.16
  36.5 0.7 fusion.18
  37.2 1.1 %fusion.3 = f32[768,400]{0,1:T(8,128)S(1)} fusion(f32[768,400]{0,1:T(8,128)S(1)} %fusion.16, f32[768,400]{0,1:T(8,128)S(1)} %fusion.18, f32[768,400]{0,1:T(8,128)S(1)} %convolution_add_fusion.3, bf16[800,400]{0,1:T(8,128)(2,1)S(1)} %collective-permute-done.1, bf16[1536,3200]{1,0:T(8,128)(2,1)S(1)} %copy-done, s32[]{:T(128)S(6)} %select_n.51, s32[]{:T(128)S(6)} %select_n.59), kind=kOutput, calls=%fused_computation.8 | convolution fusion | flops 492441600 | bytes 7008264 | tf_op jit(solution)/shard_map/dot_general | solution.py:36
  38.3 1.2 %slice_add_fusion.1 = (f32[384,400]{0,1:T(8,128)}, f32[384,400]{0,1:T(8,128)}) fusion(f32[384,400]{0,1:T(8,128)S(1)} %collective-permute-done.4, f32[768,400]{0,1:T(8,128)S(1)} %fusion.3, f32[384,400]{0,1:T(8,128)S(1)} %collective-permute-done.5), kind=kLoop, calls=%fused_computation.29 | loop fusion | flops 307200 | bytes 3686400 | tf_op jit(solution)/shard_map/add | solution.py:65
  39.5 0.9 %collective-permute-start.6 = (f32[384,400]{0,1:T(8,128)}, f32[384,400]{0,1:T(8,128)S(1)}, u32[]{:S(2)}, u32[]{:S(2)}) collective-permute-start(f32[384,400]{0,1:T(8,128)} %get-tuple-element.5), channel_id=1, source_target_pairs={{0,16},{8,24},{16,0},{24,8},{1,17},{9,25},{17,1},{25,9},{2,18},{10... | collective-permute-start | bytes 1843208 | tf_op jit(solution)/shard_map/ppermute | solution.py:10
  40.4 1.1 %collective-permute-start.7 = (f32[384,400]{0,1:T(8,128)}, f32[384,400]{0,1:T(8,128)S(1)}, u32[]{:S(2)}, u32[]{:S(2)}) collective-permute-start(f32[384,400]{0,1:T(8,128)} %get-tuple-element.6), channel_id=1, source_target_pairs={{0,16},{8,24},{16,0},{24,8},{1,17},{9,25},{17,1},{25,9},{2,18},{10... | collective-permute-start | bytes 1843208 | tf_op jit(solution)/shard_map/ppermute | solution.py:10
  41.5 0.8 %dynamic-slice_subtract_fusion = s32[768]{0:T(1024)S(1)} fusion(s32[6144]{0:T(1024)} %param.9, s32[]{:T(128)S(6)} %select_n.66, s32[]{:T(128)S(6)} %mul.47), kind=kLoop, calls=%fused_computation.31 | loop fusion | flops 768 | bytes 6152 | tf_op jit(solution)/shard_map/sub | solution.py:73
  42.3 14.1 %collective-permute-done.6 = f32[384,400]{0,1:T(8,128)S(1)} collective-permute-done((f32[384,400]{0,1:T(8,128)}, f32[384,400]{0,1:T(8,128)S(1)}, u32[]{:S(2)}, u32[]{:S(2)}) %collective-permute-start.6) | collective-permute-done | bytes 614432 | tf_op jit(solution)/shard_map/ppermute | solution.py:10
  56.4 12.3 %collective-permute-done.7 = f32[384,400]{0,1:T(8,128)S(1)} collective-permute-done((f32[384,400]{0,1:T(8,128)}, f32[384,400]{0,1:T(8,128)S(1)}, u32[]{:S(2)}, u32[]{:S(2)}) %collective-permute-start.7) | collective-permute-done | bytes 614432 | tf_op jit(solution)/shard_map/ppermute | solution.py:10
  68.7 0.1 pad_maximum_fusion
  68.8 0.5 copy.6
  69.3 2.2 %gather_fusion = f32[768,400]{1,0:T(8,128)S(1)} fusion(f32[768,400]{1,0:T(8,128)S(1)} %copy.6, s32[1024]{0:T(1024)S(1)} %pad_clamp_fusion), kind=kCustom, calls=%fused_computation | custom fusion | bytes 2460672 | tf_op jit(solution)/shard_map/jit(_take)/gather | solution.py:74
  71.5 0.4 copy.7
  71.9 2.4 %maximum_subtract_fusion = f32[768,400]{0,1:T(8,128)} fusion(f32[768,400]{0,1:T(8,128)S(1)} %copy.7, f32[384,400]{0,1:T(8,128)} %get-tuple-element.6, f32[384,400]{0,1:T(8,128)} %get-tuple-element.5), kind=kLoop, calls=%fused_computation.18 | loop fusion | flops 614400 | bytes 3686400 | tf_op jit(solution)/shard_map/sub | solution.py:74
  (9 shorter events, 0.2 us)
Async XLA Ops:
  2.2 19.1 %collective-permute-start.1 = (bf16[800,400]{0,1:T(8,128)(2,1)S(1)}, bf16[800,400]{0,1:T(8,128)(2,1)S(1)}, u32[]{:S(2)}, u32[]{:S(2)}) collective-permute-start(bf16[800,400]{0,1:T(8,128)(2,1)S(1)} %compare_select_fusion), channel_id=1, source_target_pairs={{0,8},{8,0},{16,24},{24,16},{1,9},{9,1},{17,25},{25,17},{2,10},{10... | collective-permute-start | bytes 1920008 | tf_op jit(solution)/shard_map/ppermute | solution.py:10
  5.2 18.1 %collective-permute-start = (bf16[800,400]{0,1:T(8,128)(2,1)S(1)}, bf16[800,400]{0,1:T(8,128)(2,1)S(1)}, u32[]{:S(2)}, u32[]{:S(2)}) collective-permute-start(bf16[800,400]{0,1:T(8,128)(2,1)S(1)} %compare_select_fusion), channel_id=1, source_target_pairs={{0,16},{8,24},{16,0},{24,8},{1,17},{9,25},{17,1},{25,9},{2,18},{10... | collective-permute-start | bytes 1920008 | tf_op jit(solution)/shard_map/ppermute | solution.py:10
  6.7 20.6 %copy-start = (bf16[1536,3200]{1,0:T(8,128)(2,1)S(1)}, bf16[1536,3200]{1,0:T(8,128)(2,1)}, u32[]{:S(2)}) copy-start(bf16[1536,3200]{1,0:T(8,128)(2,1)} %param.5) | copy-start | bytes 29491204
  21.4 10.7 %collective-permute-start.3 = (bf16[400,400]{0,1:T(8,128)(2,1)S(1)}, bf16[400,400]{0,1:T(8,128)(2,1)S(1)}, u32[]{:S(2)}, u32[]{:S(2)}) collective-permute-start(bf16[400,400]{0,1:T(8,128)(2,1)S(1)} %slice.27), channel_id=1, source_target_pairs={{0,16},{8,24},{16,0},{24,8},{1,17},{9,25},{17,1},{25,9},{2,18},{10... | collective-permute-start | bytes 960008 | tf_op jit(solution)/shard_map/ppermute | solution.py:10
  23.3 10.1 %collective-permute-start.2 = (bf16[400,400]{0,1:T(8,128)(2,1)S(1)}, bf16[400,400]{0,1:T(8,128)(2,1)S(1)}, u32[]{:S(2)}, u32[]{:S(2)}) collective-permute-start(bf16[400,400]{0,1:T(8,128)(2,1)S(1)} %slice.26), channel_id=1, source_target_pairs={{0,8},{8,0},{16,24},{24,16},{1,9},{9,1},{17,25},{25,17},{2,10},{10... | collective-permute-start | bytes 960008 | tf_op jit(solution)/shard_map/ppermute | solution.py:10
  35.3 3.0 %collective-permute-start.4 = (f32[384,400]{0,1:T(8,128)S(1)}, f32[384,400]{0,1:T(8,128)S(1)}, u32[]{:S(2)}, u32[]{:S(2)}) collective-permute-start(f32[384,400]{0,1:T(8,128)S(1)} %get-tuple-element.7), channel_id=1, source_target_pairs={{0,1},{1,0},{2,3},{3,2},{4,5},{5,4},{6,7},{7,6},{8,9},{9,8},{10,11... | collective-permute-start | bytes 1843208 | tf_op jit(solution)/shard_map/ppermute | solution.py:10
  35.4 3.0 %collective-permute-start.5 = (f32[384,400]{0,1:T(8,128)S(1)}, f32[384,400]{0,1:T(8,128)S(1)}, u32[]{:S(2)}, u32[]{:S(2)}) collective-permute-start(f32[384,400]{0,1:T(8,128)S(1)} %get-tuple-element.8), channel_id=1, source_target_pairs={{0,1},{1,0},{2,3},{3,2},{4,5},{5,4},{6,7},{7,6},{8,9},{9,8},{10,11... | collective-permute-start | bytes 1843208 | tf_op jit(solution)/shard_map/ppermute | solution.py:10
  39.5 16.9 %collective-permute-start.6 = (f32[384,400]{0,1:T(8,128)}, f32[384,400]{0,1:T(8,128)S(1)}, u32[]{:S(2)}, u32[]{:S(2)}) collective-permute-start(f32[384,400]{0,1:T(8,128)} %get-tuple-element.5), channel_id=1, source_target_pairs={{0,16},{8,24},{16,0},{24,8},{1,17},{9,25},{17,1},{25,9},{2,18},{10... | collective-permute-start | bytes 1843208 | tf_op jit(solution)/shard_map/ppermute | solution.py:10
  40.4 28.3 %collective-permute-start.7 = (f32[384,400]{0,1:T(8,128)}, f32[384,400]{0,1:T(8,128)S(1)}, u32[]{:S(2)}, u32[]{:S(2)}) collective-permute-start(f32[384,400]{0,1:T(8,128)} %get-tuple-element.6), channel_id=1, source_target_pairs={{0,16},{8,24},{16,0},{24,8},{1,17},{9,25},{17,1},{25,9},{2,18},{10... | collective-permute-start | bytes 1843208 | tf_op jit(solution)/shard_map/ppermute | solution.py:10

commit v8 on v7

--- a/solution.py
+++ b/solution.py
@@ -27,13 +27,15 @@
     return groups
 
 
-def contract(amplitudes, groups, first, rows):
+def contract(amplitudes, groups, first, rows, labels, irrep_cols):
     band = lax.dynamic_slice_in_dim(amplitudes, first, rows, axis=0)
     terms = None
     for group in groups:
         for b, o in group:
             window = lax.dynamic_slice_in_dim(band, o, b.shape[0], axis=1)
-            product = jnp.dot(window, b, preferred_element_type=jnp.float32)
+            same = lax.dynamic_slice_in_dim(labels, o, b.shape[0])[:, None] == irrep_cols[None, :]
+            blocked = jnp.where(same, b, jnp.zeros_like(b))
+            product = jnp.dot(window, blocked, preferred_element_type=jnp.float32)
             terms = product if terms is None else terms + product
     return terms
 
@@ -43,17 +45,15 @@
     cuts_count = lax.axis_size("cuts")
     prow_idx = lax.axis_index("prow")
     cuts_idx = lax.axis_index("cuts")
-    count = integrals.shape[0]
-    labels = lax.dynamic_slice(irrep_rows, ((cuts_idx * prow_count + prow_idx) * count,), (count,))
-    same = labels[:, None] == irrep_cols[None, :]
-    blocked = jnp.where(same, integrals, jnp.zeros_like(integrals))
-    groups = gather_prow(blocked, prow_idx, prow_count)
+    width = amplitudes.shape[1]
+    labels = lax.dynamic_slice_in_dim(irrep_rows, cuts_idx * width, width)
+    groups = gather_prow(integrals, prow_idx, prow_count)
     block_rows = amplitudes.shape[0] // cuts_count
     sent = []
     for s in range(1, cuts_count):
         other = jnp.bitwise_xor(cuts_idx, s)
-        sent.append((s, contract(amplitudes, groups, other * block_rows, block_rows)))
-    kept = contract(amplitudes, groups, cuts_idx * block_rows, block_rows)
+        sent.append((s, contract(amplitudes, groups, other * block_rows, block_rows, labels, irrep_cols)))
+    kept = contract(amplitudes, groups, cuts_idx * block_rows, block_rows, labels, irrep_cols)
     pieces = 2 if block_rows % 16 == 0 else 1
     step = block_rows // pieces
     half = prow_count // 2

time: 74.6 us -> 73.5 us (0.985)
  other arithmetic: 5.85 us -> 4.49 us
  waiting for transfers between devices: 39.7 us -> 38.4 us
  local copies, waits for them, and re-layouts: 4.14 us -> 5.1 us
    select_n x1 -> x0, other arithmetic: 1.38 us -> none  [shards(): blocked = jnp.where(same, integrals, jnp.zeros_like(integrals))]
    ppermute x8, waiting for transfers between devices: 39.7 us -> 38.4 us  [swap(): lax.ppermute(value, axis, [(i, i ^ mask) for i in range(lax.axis_size(axi...]
    dynamic_slice x1 -> x2, local copies, waits for them, and re-layouts: 0.77 us -> 1.73 us  [contract(): lax.dynamic_slice_in_dim(labels, o, b.shape[0])[:, None]]
  transfers between devices with their start and end apart: 8 -> 8, of which waited for: 5 -> 5; matrix products, arithmetic and copies ran while one was open for 18% -> 21% of each run, Pallas kernels for 0% -> 0%
where the time goes in v8:
time: 73.5 us; the launch traced here: 73.1 us
  waiting for transfers between devices  38.4 us (52%)
  matrix products  14.5 us (20%)
  starting transfers between devices  10.4 us (14%)
  local copies, waits for them, and re-layouts  5.1 us (7%)
  other arithmetic  4.49 us (6%)
    ppermute x8, waiting for transfers between devices, swap(): lax.ppermute(value, axis, [(i, i ^ mask) for i in range(lax.axis_size(axi...  38.4 us
    dot_general x10, matrix products, contract(): product = jnp.dot(window, blocked, preferred_element_type=jnp.float32)  14.5 us
    ppermute x8, starting transfers between devices, swap(): lax.ppermute(value, axis, [(i, i ^ mask) for i in range(lax.axis_size(axi...  10.4 us
    gather x2, local copies, waits for them, and re-layouts, shards(): return cycle - jnp.take(fetched, local, axis=0, mode='clip')  2.59 us
    sub x1, other arithmetic, shards(): return cycle - jnp.take(fetched, local, axis=0, mode='clip')  2.43 us
    dynamic_slice x2, local copies, waits for them, and re-layouts, contract(): lax.dynamic_slice_in_dim(labels, o, b.shape[0])[:, None]  1.73 us
  transfers between devices with their start and end apart: 8, of which 5 were waited for; matrix products, arithmetic and copies ran while one was open for 21% of the time, Pallas kernels for 0%

profile of v8, /device:TPU:0, one launch (start us, length us, event | category | flops | bytes accessed | tf_op | source)
XLA Modules:
  0.0 73.1 jit_solution(4541053201446481172)
XLA Ops:
  0.0 3.0 %collective-permute-start = (bf16[800,400]{0,1:T(8,128)(2,1)}, bf16[800,400]{0,1:T(8,128)(2,1)S(1)}, u32[]{:S(2)}, u32[]{:S(2)}) collective-permute-start(bf16[800,400]{0,1:T(8,128)(2,1)} %param.6), channel_id=1, source_target_pairs={{0,16},{8,24},{16,0},{24,8},{1,17},{9,25},{17,1},{25,9},{2,18},{10... | collective-permute-start | bytes 1920008 | tf_op jit(solution)/shard_map/ppermute | solution.py:10
  3.0 1.5 %collective-permute-start.1 = (bf16[800,400]{0,1:T(8,128)(2,1)}, bf16[800,400]{0,1:T(8,128)(2,1)S(1)}, u32[]{:S(2)}, u32[]{:S(2)}) collective-permute-start(bf16[800,400]{0,1:T(8,128)(2,1)} %param.6), channel_id=1, source_target_pairs={{0,8},{8,0},{16,24},{24,16},{1,9},{9,1},{17,25},{25,17},{2,10},{10... | collective-permute-start | bytes 1920008 | tf_op jit(solution)/shard_map/ppermute | solution.py:10
  4.5 0.9 %fusion.31 = (s32[800]{0:T(1024)S(1)}, s32[800]{0:T(1024)S(1)}, s32[800]{0:T(1024)S(1)}) fusion(s32[6400]{0:T(1024)} %param.7, s32[]{:T(128)S(6)} %dynamic_slice.73, s32[]{:T(128)S(6)} %dynamic_slice.70, s32[]{:T(128)S(6)} %dynamic_slice.67), kind=kLoop, calls=%fused_computation.47 | loop fusion | bytes 19212 | tf_op jit(solution)/shard_map/dynamic_slice | solution.py:36
  5.3 0.8 %fusion.32 = (s32[400]{0:T(512)S(1)}, s32[400]{0:T(512)S(1)}) fusion(s32[6400]{0:T(1024)} %param.7, s32[]{:T(128)S(6)} %dynamic_slice.76, s32[]{:T(128)S(6)} %dynamic_slice.79), kind=kLoop, calls=%fused_computation.48 | loop fusion | bytes 6408 | tf_op jit(solution)/shard_map/dynamic_slice | solution.py:36
  6.2 3.0 %fusion.6 = f32[768,400]{0,1:T(8,128)S(1)} fusion(bf16[1536,3200]{1,0:T(8,128)(2,1)} %param.5, s32[]{:T(128)S(6)} %select_n.100, s32[]{:T(128)S(6)} %select_n.83, bf16[800,400]{0,1:T(8,128)(2,1)} %param.6, s32[800]{0:T(1024)S(1)} %get-tuple-element.11, s32[400]{0:T(512)} %param.8), kind=kOutput, calls=%fused_computation.14 | convolution fusion | flops 492160000 | bytes 3327112 | tf_op jit(solution)/shard_map/dot_general | solution.py:38
  9.2 3.3 %fusion.10 = f32[768,400]{0,1:T(8,128)S(1)} fusion(bf16[1536,3200]{1,0:T(8,128)(2,1)} %param.5, s32[]{:T(128)S(6)} %select_n.81, s32[]{:T(128)S(6)} %select_n.83, bf16[800,400]{0,1:T(8,128)(2,1)} %param.6, s32[800]{0:T(1024)S(1)} %get-tuple-element.11, s32[400]{0:T(512)S(1)} %copy-done.1), kind=kOutput, calls=%fused_computation.18 | convolution fusion | flops 492160000 | bytes 3326664 | tf_op jit(solution)/shard_map/dot_general | solution.py:38
  12.5 6.7 %collective-permute-done = bf16[800,400]{0,1:T(8,128)(2,1)S(1)} collective-permute-done((bf16[800,400]{0,1:T(8,128)(2,1)}, bf16[800,400]{0,1:T(8,128)(2,1)S(1)}, u32[]{:S(2)}, u32[]{:S(2)}) %collective-permute-start) | collective-permute-done | bytes 640032 | tf_op jit(solution)/shard_map/ppermute | solution.py:10
  19.3 1.8 %collective-permute-start.2 = (bf16[400,400]{0,1:T(8,128)(2,1)S(1)}, bf16[400,400]{0,1:T(8,128)(2,1)S(1)}, u32[]{:S(2)}, u32[]{:S(2)}) collective-permute-start(bf16[400,400]{0,1:T(8,128)(2,1)S(1)} %slice.26), channel_id=1, source_target_pairs={{0,8},{8,0},{16,24},{24,16},{1,9},{9,1},{17,25},{25,17},{2,10},{10... | collective-permute-start | bytes 960008 | tf_op jit(solution)/shard_map/ppermute | solution.py:10
  21.0 0.2 slice.27
  21.3 1.6 %collective-permute-start.3 = (bf16[400,400]{0,1:T(8,128)(2,1)S(1)}, bf16[400,400]{0,1:T(8,128)(2,1)S(1)}, u32[]{:S(2)}, u32[]{:S(2)}) collective-permute-start(bf16[400,400]{0,1:T(8,128)(2,1)S(1)} %slice.27), channel_id=1, source_target_pairs={{0,16},{8,24},{16,0},{24,8},{1,17},{9,25},{17,1},{25,9},{2,18},{10... | collective-permute-start | bytes 960008 | tf_op jit(solution)/shard_map/ppermute | solution.py:10
  22.8 1.2 %convolution_add_fusion.1 = f32[768,400]{0,1:T(8,128)S(1)} fusion(f32[768,400]{0,1:T(8,128)S(1)} %fusion.6, bf16[1536,3200]{1,0:T(8,128)(2,1)S(1)} %copy-done, s32[]{:T(128)S(6)} %select_n.100, s32[]{:T(128)S(6)} %select_n.88, bf16[800,400]{0,1:T(8,128)(2,1)S(1)} %collective-permute-done, s32[800]{0:T(1024)S(1)} %get-tuple-element.10, s32[400]{0:T(512)S(1)} %copy-done.1), kind=kOutput, calls=%fused_computation.7 | convolution fusion | flops 492467200 | bytes 4556808 | tf_op jit(solution)/shard_map/dot_general | solution.py:38
  24.1 1.3 %convolution_add_fusion.3 = f32[768,400]{0,1:T(8,128)S(1)} fusion(f32[768,400]{0,1:T(8,128)S(1)} %fusion.10, bf16[1536,3200]{1,0:T(8,128)(2,1)S(1)} %copy-done, s32[]{:T(128)S(6)} %select_n.81, s32[]{:T(128)S(6)} %select_n.88, bf16[800,400]{0,1:T(8,128)(2,1)S(1)} %collective-permute-done, s32[800]{0:T(1024)S(1)} %get-tuple-element.10, s32[400]{0:T(512)S(1)} %copy-done.1), kind=kOutput, calls=%fused_computation.11 | convolution fusion | flops 492467200 | bytes 4556808 | tf_op jit(solution)/shard_map/dot_general | solution.py:38
  25.4 4.6 %collective-permute-done.2 = bf16[400,400]{0,1:T(8,128)(2,1)S(1)} collective-permute-done((bf16[400,400]{0,1:T(8,128)(2,1)S(1)}, bf16[400,400]{0,1:T(8,128)(2,1)S(1)}, u32[]{:S(2)}, u32[]{:S(2)}) %collective-permute-start.2) | collective-permute-done | bytes 320032 | tf_op jit(solution)/shard_map/ppermute | solution.py:10
  30.0 0.8 %fusion.14 = f32[768,400]{0,1:T(8,128)S(1)} fusion(bf16[1536,3200]{1,0:T(8,128)(2,1)S(1)} %copy-done, s32[]{:T(128)S(6)} %select_n.100, s32[]{:T(128)S(6)} %select_n.94, bf16[400,400]{0,1:T(8,128)(2,1)S(1)} %collective-permute-done.2, s32[400]{0:T(512)S(1)} %get-tuple-element.12, s32[400]{0:T(512)S(1)} %copy-done.1), kind=kOutput, calls=%fused_computation.26 | convolution fusion | flops 246080000 | bytes 2428936 | tf_op jit(solution)/shard_map/dot_general | solution.py:38
  30.8 0.6 collective-permute-done.3
  31.4 0.8 %fusion.12 = f32[768,400]{0,1:T(8,128)S(1)} fusion(bf16[1536,3200]{1,0:T(8,128)(2,1)S(1)} %copy-done, s32[]{:T(128)S(6)} %select_n.100, s32[]{:T(128)S(6)} %select_n.97, bf16[400,400]{0,1:T(8,128)(2,1)S(1)} %collective-permute-done.3, s32[400]{0:T(512)S(1)} %get-tuple-element.13, s32[400]{0:T(512)S(1)} %copy-done.1), kind=kOutput, calls=%fused_computation.24 | convolution fusion | flops 246080000 | bytes 2428936 | tf_op jit(solution)/shard_map/dot_general | solution.py:38
  32.2 1.3 %fusion.1 = f32[768,400]{0,1:T(8,128)S(1)} fusion(f32[768,400]{0,1:T(8,128)S(1)} %fusion.12, f32[768,400]{0,1:T(8,128)S(1)} %fusion.14, f32[768,400]{0,1:T(8,128)S(1)} %convolution_add_fusion.1, bf16[1536,3200]{1,0:T(8,128)(2,1)S(1)} %copy-done, s32[]{:T(128)S(6)} %select_n.100, s32[]{:T(128)S(6)} %select_n.91, ...), kind=kOutput, calls=%fused_computation.6 | convolution fusion | flops 493081600 | bytes 7014408 | tf_op jit(solution)/shard_map/dot_general | solution.py:38
  33.7 0.5 collective-permute-start.5
  34.2 0.8 %fusion.18 = f32[768,400]{0,1:T(8,128)S(1)} fusion(bf16[1536,3200]{1,0:T(8,128)(2,1)S(1)} %copy-done, s32[]{:T(128)S(6)} %select_n.81, s32[]{:T(128)S(6)} %select_n.94, bf16[400,400]{0,1:T(8,128)(2,1)S(1)} %collective-permute-done.2, s32[400]{0:T(512)S(1)} %get-tuple-element.12, s32[400]{0:T(512)S(1)} %copy-done.1), kind=kOutput, calls=%fused_computation.30 | convolution fusion | flops 246080000 | bytes 2428936 | tf_op jit(solution)/shard_map/dot_general | solution.py:38
  34.9 0.8 %fusion.16 = f32[768,400]{0,1:T(8,128)S(1)} fusion(bf16[1536,3200]{1,0:T(8,128)(2,1)S(1)} %copy-done, s32[]{:T(128)S(6)} %select_n.81, s32[]{:T(128)S(6)} %select_n.97, bf16[400,400]{0,1:T(8,128)(2,1)S(1)} %collective-permute-done.3, s32[400]{0:T(512)S(1)} %get-tuple-element.13, s32[400]{0:T(512)S(1)} %copy-done.1), kind=kOutput, calls=%fused_computation.28 | convolution fusion | flops 246080000 | bytes 2428936 | tf_op jit(solution)/shard_map/dot_general | solution.py:38
  35.7 1.3 %fusion.3 = f32[768,400]{0,1:T(8,128)S(1)} fusion(f32[768,400]{0,1:T(8,128)S(1)} %fusion.16, f32[768,400]{0,1:T(8,128)S(1)} %fusion.18, f32[768,400]{0,1:T(8,128)S(1)} %convolution_add_fusion.3, bf16[1536,3200]{1,0:T(8,128)(2,1)S(1)} %copy-done, s32[]{:T(128)S(6)} %select_n.81, s32[]{:T(128)S(6)} %select_n.91, ...), kind=kOutput, calls=%fused_computation.10 | convolution fusion | flops 493081600 | bytes 7014408 | tf_op jit(solution)/shard_map/dot_general | solution.py:38
  37.1 1.2 %slice_add_fusion.1 = (f32[384,400]{0,1:T(8,128)}, f32[384,400]{0,1:T(8,128)}) fusion(f32[384,400]{0,1:T(8,128)S(1)} %collective-permute-done.4, f32[768,400]{0,1:T(8,128)S(1)} %fusion.3, f32[384,400]{0,1:T(8,128)S(1)} %collective-permute-done.5), kind=kLoop, calls=%fused_computation.33 | loop fusion | flops 307200 | bytes 3686400 | tf_op jit(solution)/shard_map/add | solution.py:65
  38.3 1.5 %collective-permute-start.6 = (f32[384,400]{0,1:T(8,128)}, f32[384,400]{0,1:T(8,128)S(1)}, u32[]{:S(2)}, u32[]{:S(2)}) collective-permute-start(f32[384,400]{0,1:T(8,128)} %get-tuple-element.5), channel_id=1, source_target_pairs={{0,16},{8,24},{16,0},{24,8},{1,17},{9,25},{17,1},{25,9},{2,18},{10... | collective-permute-start | bytes 1843208 | tf_op jit(solution)/shard_map/ppermute | solution.py:10
  39.8 0.5 collective-permute-start.7
  40.3 0.8 %dynamic-slice_subtract_fusion = s32[768]{0:T(1024)S(1)} fusion(s32[6144]{0:T(1024)} %param.9, s32[]{:T(128)S(6)} %select_n.101, s32[]{:T(128)S(6)} %mul.43), kind=kLoop, calls=%fused_computation.35 | loop fusion | flops 768 | bytes 6152 | tf_op jit(solution)/shard_map/sub | solution.py:73
  41.1 14.1 %collective-permute-done.6 = f32[384,400]{0,1:T(8,128)S(1)} collective-permute-done((f32[384,400]{0,1:T(8,128)}, f32[384,400]{0,1:T(8,128)S(1)}, u32[]{:S(2)}, u32[]{:S(2)}) %collective-permute-start.6) | collective-permute-done | bytes 614432 | tf_op jit(solution)/shard_map/ppermute | solution.py:10
  55.2 12.3 %collective-permute-done.7 = f32[384,400]{0,1:T(8,128)S(1)} collective-permute-done((f32[384,400]{0,1:T(8,128)}, f32[384,400]{0,1:T(8,128)S(1)}, u32[]{:S(2)}, u32[]{:S(2)}) %collective-permute-start.7) | collective-permute-done | bytes 614432 | tf_op jit(solution)/shard_map/ppermute | solution.py:10
  67.5 0.1 pad_maximum_fusion
  67.6 0.5 copy.6
  68.1 2.2 %gather_fusion = f32[768,400]{1,0:T(8,128)S(1)} fusion(f32[768,400]{1,0:T(8,128)S(1)} %copy.6, s32[1024]{0:T(1024)S(1)} %pad_clamp_fusion), kind=kCustom, calls=%fused_computation | custom fusion | bytes 2460672 | tf_op jit(solution)/shard_map/jit(_take)/gather | solution.py:74
  70.2 0.4 copy.7
  70.7 2.4 %maximum_subtract_fusion = f32[768,400]{0,1:T(8,128)} fusion(f32[768,400]{0,1:T(8,128)S(1)} %copy.7, f32[384,400]{0,1:T(8,128)} %get-tuple-element.6, f32[384,400]{0,1:T(8,128)} %get-tuple-element.5), kind=kLoop, calls=%fused_computation.20 | loop fusion | flops 614400 | bytes 3686400 | tf_op jit(solution)/shard_map/sub | solution.py:74
  (11 shorter events, 0.2 us)
Async XLA Ops:
  0.0 19.2 %collective-permute-start = (bf16[800,400]{0,1:T(8,128)(2,1)}, bf16[800,400]{0,1:T(8,128)(2,1)S(1)}, u32[]{:S(2)}, u32[]{:S(2)}) collective-permute-start(bf16[800,400]{0,1:T(8,128)(2,1)} %param.6), channel_id=1, source_target_pairs={{0,16},{8,24},{16,0},{24,8},{1,17},{9,25},{17,1},{25,9},{2,18},{10... | collective-permute-start | bytes 1920008 | tf_op jit(solution)/shard_map/ppermute | solution.py:10
  3.0 18.1 %collective-permute-start.1 = (bf16[800,400]{0,1:T(8,128)(2,1)}, bf16[800,400]{0,1:T(8,128)(2,1)S(1)}, u32[]{:S(2)}, u32[]{:S(2)}) collective-permute-start(bf16[800,400]{0,1:T(8,128)(2,1)} %param.6), channel_id=1, source_target_pairs={{0,8},{8,0},{16,24},{24,16},{1,9},{9,1},{17,25},{25,17},{2,10},{10... | collective-permute-start | bytes 1920008 | tf_op jit(solution)/shard_map/ppermute | solution.py:10
  4.5 4.7 %copy-start.1 = (s32[400]{0:T(512)S(1)}, s32[400]{0:T(512)}, u32[]{:S(2)}) copy-start(s32[400]{0:T(512)} %param.8) | copy-start | bytes 4804
  6.2 16.6 %copy-start = (bf16[1536,3200]{1,0:T(8,128)(2,1)S(1)}, bf16[1536,3200]{1,0:T(8,128)(2,1)}, u32[]{:S(2)}) copy-start(bf16[1536,3200]{1,0:T(8,128)(2,1)} %param.5) | copy-start | bytes 29491204
  19.3 10.7 %collective-permute-start.2 = (bf16[400,400]{0,1:T(8,128)(2,1)S(1)}, bf16[400,400]{0,1:T(8,128)(2,1)S(1)}, u32[]{:S(2)}, u32[]{:S(2)}) collective-permute-start(bf16[400,400]{0,1:T(8,128)(2,1)S(1)} %slice.26), channel_id=1, source_target_pairs={{0,8},{8,0},{16,24},{24,16},{1,9},{9,1},{17,25},{25,17},{2,10},{10... | collective-permute-start | bytes 960008 | tf_op jit(solution)/shard_map/ppermute | solution.py:10
  21.3 10.1 %collective-permute-start.3 = (bf16[400,400]{0,1:T(8,128)(2,1)S(1)}, bf16[400,400]{0,1:T(8,128)(2,1)S(1)}, u32[]{:S(2)}, u32[]{:S(2)}) collective-permute-start(bf16[400,400]{0,1:T(8,128)(2,1)S(1)} %slice.27), channel_id=1, source_target_pairs={{0,16},{8,24},{16,0},{24,8},{1,17},{9,25},{17,1},{25,9},{2,18},{10... | collective-permute-start | bytes 960008 | tf_op jit(solution)/shard_map/ppermute | solution.py:10
  33.6 3.5 %collective-permute-start.4 = (f32[384,400]{0,1:T(8,128)S(1)}, f32[384,400]{0,1:T(8,128)S(1)}, u32[]{:S(2)}, u32[]{:S(2)}) collective-permute-start(f32[384,400]{0,1:T(8,128)S(1)} %get-tuple-element.7), channel_id=1, source_target_pairs={{0,1},{1,0},{2,3},{3,2},{4,5},{5,4},{6,7},{7,6},{8,9},{9,8},{10,11... | collective-permute-start | bytes 1843208 | tf_op jit(solution)/shard_map/ppermute | solution.py:10
  33.7 3.4 %collective-permute-start.5 = (f32[384,400]{0,1:T(8,128)S(1)}, f32[384,400]{0,1:T(8,128)S(1)}, u32[]{:S(2)}, u32[]{:S(2)}) collective-permute-start(f32[384,400]{0,1:T(8,128)S(1)} %get-tuple-element.8), channel_id=1, source_target_pairs={{0,1},{1,0},{2,3},{3,2},{4,5},{5,4},{6,7},{7,6},{8,9},{9,8},{10,11... | collective-permute-start | bytes 1843208 | tf_op jit(solution)/shard_map/ppermute | solution.py:10
  38.3 16.9 %collective-permute-start.6 = (f32[384,400]{0,1:T(8,128)}, f32[384,400]{0,1:T(8,128)S(1)}, u32[]{:S(2)}, u32[]{:S(2)}) collective-permute-start(f32[384,400]{0,1:T(8,128)} %get-tuple-element.5), channel_id=1, source_target_pairs={{0,16},{8,24},{16,0},{24,8},{1,17},{9,25},{17,1},{25,9},{2,18},{10... | collective-permute-start | bytes 1843208 | tf_op jit(solution)/shard_map/ppermute | solution.py:10
  39.8 27.7 %collective-permute-start.7 = (f32[384,400]{0,1:T(8,128)}, f32[384,400]{0,1:T(8,128)S(1)}, u32[]{:S(2)}, u32[]{:S(2)}) collective-permute-start(f32[384,400]{0,1:T(8,128)} %get-tuple-element.6), channel_id=1, source_target_pairs={{0,16},{8,24},{16,0},{24,8},{1,17},{9,25},{17,1},{25,9},{2,18},{10... | collective-permute-start | bytes 1843208 | tf_op jit(solution)/shard_map/ppermute | solution.py:10

commit v9 on v8

--- a/solution.py
+++ b/solution.py
@@ -10,12 +10,18 @@
     return lax.ppermute(value, axis, [(i, i ^ mask) for i in range(lax.axis_size(axis))])
 
 
-def gather_prow(own, prow_idx, prow_count):
+def gather_prow(own, prow_idx, prow_count, via_x=False, hold=None):
     count = own.shape[0]
     if prow_count == 4 and count % 32 == 0:
         half = count // 2
         from_x = swap(own, "prow", 1)
         from_y = swap(own, "prow", 2)
+        if hold is not None:
+            from_x, from_y, _ = lax.optimization_barrier((from_x, from_y, hold))
+        if via_x:
+            return [[(own, prow_idx * count)], [(from_y, jnp.bitwise_xor(prow_idx, 2) * count)],
+                    [(from_x, jnp.bitwise_xor(prow_idx, 1) * count)],
+                    [(swap(from_y, "prow", 1), jnp.bitwise_xor(prow_idx, 3) * count)]]
         diag_a = swap(from_y[:half], "prow", 1)
         diag_b = swap(from_x[half:], "prow", 2)
         base = jnp.bitwise_xor(prow_idx, 3) * count
@@ -40,21 +46,21 @@
     return terms
 
 
-def shards(amplitudes, integrals, irrep_rows, irrep_cols, mirror_row):
+def antisym(amplitudes, integrals, labels, irrep_cols, local, via_x, pieces, after, hold):
     prow_count = lax.axis_size("prow")
     cuts_count = lax.axis_size("cuts")
     prow_idx = lax.axis_index("prow")
     cuts_idx = lax.axis_index("cuts")
-    width = amplitudes.shape[1]
-    labels = lax.dynamic_slice_in_dim(irrep_rows, cuts_idx * width, width)
-    groups = gather_prow(integrals, prow_idx, prow_count)
+    if after is not None:
+        integrals, _ = lax.optimization_barrier((integrals, after))
+    groups = gather_prow(integrals, prow_idx, prow_count, via_x, hold)
     block_rows = amplitudes.shape[0] // cuts_count
     sent = []
     for s in range(1, cuts_count):
         other = jnp.bitwise_xor(cuts_idx, s)
         sent.append((s, contract(amplitudes, groups, other * block_rows, block_rows, labels, irrep_cols)))
     kept = contract(amplitudes, groups, cuts_idx * block_rows, block_rows, labels, irrep_cols)
-    pieces = 2 if block_rows % 16 == 0 else 1
+    pieces = pieces if block_rows % (8 * pieces) == 0 else 1
     step = block_rows // pieces
     half = prow_count // 2
     fetched = []
@@ -67,11 +73,34 @@
         fetched.append(swap(total, "prow", half))
     cycle = jnp.concatenate(cycle, axis=0) if pieces > 1 else cycle[0]
     fetched = jnp.concatenate(fetched, axis=0) if pieces > 1 else fetched[0]
+    return cycle - jnp.take(fetched, local, axis=0, mode="clip"), groups[1][0][0], cycle
+
+
+def shards(amplitudes, integrals, irrep_rows, irrep_cols, mirror_row):
+    prow_count = lax.axis_size("prow")
+    cuts_count = lax.axis_size("cuts")
+    prow_idx = lax.axis_index("prow")
+    cuts_idx = lax.axis_index("cuts")
+    width = amplitudes.shape[1]
+    cols = integrals.shape[1]
+    labels = lax.dynamic_slice_in_dim(irrep_rows, cuts_idx * width, width)
+    block_rows = amplitudes.shape[0] // cuts_count
+    half = prow_count // 2
     own_block = prow_idx * cuts_count + cuts_idx
     partner_block = jnp.bitwise_xor(prow_idx, half) * cuts_count + cuts_idx
     mine = lax.dynamic_slice(mirror_row, (own_block * block_rows,), (block_rows,))
     local = mine - partner_block * block_rows
-    return cycle - jnp.take(fetched, local, axis=0, mode="clip")
+    chunks = 2 if cols % 16 == 0 else 1
+    step = cols // chunks
+    results = []
+    after = None
+    hold = None
+    for j in range(chunks):
+        result, after, hold = antisym(amplitudes, integrals[:, j * step:(j + 1) * step], labels,
+                                      irrep_cols[j * step:(j + 1) * step], local, False, 1 if chunks > 1 else 2,
+                                      after, hold)
+        results.append(result)
+    return jnp.concatenate(results, axis=1) if chunks > 1 else results[0]
 
 
 def solution(mesh):

time: 73.5 us -> 82.9 us (1.13)
  matrix products: 14.5 us -> 24.7 us
  waiting for transfers between devices: 38.4 us -> 33 us
  local copies, waits for them, and re-layouts: 5.1 us -> 10.4 us
  other arithmetic: 4.49 us -> 2.02 us
  starting transfers between devices: 10.4 us -> 12 us
    dot_general x10 -> x20, matrix products: 14.5 us -> 24.7 us  [contract(): product = jnp.dot(window, blocked, preferred_element_type=jnp.float32)]
    ppermute x8 -> x12, waiting for transfers between devices: 38.4 us -> 33 us  [swap(): lax.ppermute(value, axis, [(i, i ^ mask) for i in range(lax.axis_size(axi...]
    sub x1 -> x2, other arithmetic: 2.43 us -> 0.13 us  [antisym(): cycle - jnp.take(fetched, local, axis=0, mode='clip')]
    gather x2 -> x4, local copies, waits for them, and re-layouts: 2.59 us -> 4.72 us  [antisym(): jnp.take(fetched, local, axis=0, mode='clip')]
    slice x1 -> x2, local copies, waits for them, and re-layouts: 0.08 us -> 1.98 us  [the longest x1 1.15 us: shards(): integrals[:, j * step:(j + 1) * step]]
    ppermute x8 -> x12, starting transfers between devices: 10.4 us -> 12 us  [swap(): lax.ppermute(value, axis, [(i, i ^ mask) for i in range(lax.axis_size(axi...]
    ppermute x0 -> x2, local copies, waits for them, and re-layouts: none -> 1.6 us  [swap(): lax.ppermute(value, axis, [(i, i ^ mask) for i in range(lax.axis_size(axi...]
    add x1 -> x0, other arithmetic: 1.19 us -> none  [shards(): total = total + swap(part[h * step:(h + 1) * step], 'cuts', s)]
  transfers between devices with their start and end apart: 8 -> 12, of which waited for: 5 -> 3; matrix products, arithmetic and copies ran while one was open for 21% -> 38% of each run, Pallas kernels for 0% -> 0%
where the time goes in v9:
time: 82.9 us; the launch traced here: 82.5 us
  waiting for transfers between devices  33 us (40%)
  matrix products  24.7 us (30%)
  starting transfers between devices  12 us (14%)
  local copies, waits for them, and re-layouts  10.4 us (13%)
  other arithmetic  2.02 us (2%)
    ppermute x12, waiting for transfers between devices, swap(): lax.ppermute(value, axis, [(i, i ^ mask) for i in range(lax.axis_size(axi...  33 us
    dot_general x20, matrix products, contract(): product = jnp.dot(window, blocked, preferred_element_type=jnp.float32)  24.7 us
    ppermute x12, starting transfers between devices, swap(): lax.ppermute(value, axis, [(i, i ^ mask) for i in range(lax.axis_size(axi...  12 us
    gather x4, local copies, waits for them, and re-layouts, antisym(): jnp.take(fetched, local, axis=0, mode='clip')  4.72 us
    dynamic_slice x2, local copies, waits for them, and re-layouts, contract(): lax.dynamic_slice_in_dim(labels, o, b.shape[0])[:, None]  1.81 us
  transfers between devices with their start and end apart: 12, of which 3 were waited for; matrix products, arithmetic and copies ran while one was open for 38% of the time, Pallas kernels for 0%

profile of v9, /device:TPU:0, one launch (start us, length us, event | category | flops | bytes accessed | tf_op | source)
XLA Modules:
  0.0 82.5 jit_solution(17573006892975531558)
XLA Ops:
  0.0 1.1 %fusion.60 = (bf16[800,200]{0,1:T(8,128)(2,1)S(1)}, bf16[800,200]{0,1:T(8,128)(2,1)S(1)}) fusion(bf16[800,400]{0,1:T(8,128)(2,1)} %param.6), kind=kLoop, calls=%fused_computation.85 | loop fusion | bytes 1280000 | tf_op jit(solution)/shard_map/slice | solution.py:99
  1.2 3.0 %collective-permute-start = (bf16[800,200]{0,1:T(8,128)(2,1)S(1)}, bf16[800,200]{0,1:T(8,128)(2,1)S(1)}, u32[]{:S(2)}, u32[]{:S(2)}) collective-permute-start(bf16[800,200]{0,1:T(8,128)(2,1)S(1)} %get-tuple-element.11), channel_id=1, source_target_pairs={{0,16},{8,24},{16,0},{24,8},{1,17},{9,25},{17,1},{25,9},{2,18},{10... | collective-permute-start | bytes 960008 | tf_op jit(solution)/shard_map/ppermute | solution.py:10
  4.2 1.5 %collective-permute-start.1 = (bf16[800,200]{0,1:T(8,128)(2,1)S(1)}, bf16[800,200]{0,1:T(8,128)(2,1)S(1)}, u32[]{:S(2)}, u32[]{:S(2)}) collective-permute-start(bf16[800,200]{0,1:T(8,128)(2,1)S(1)} %get-tuple-element.11), channel_id=1, source_target_pairs={{0,8},{8,0},{16,24},{24,16},{1,9},{9,1},{17,25},{25,17},{2,10},{10... | collective-permute-start | bytes 960008 | tf_op jit(solution)/shard_map/ppermute | solution.py:10
  5.7 0.8 %fusion.63 = (s32[200]{0:T(256)S(1)}, s32[200]{0:T(256)S(1)}) fusion(s32[400]{0:T(512)} %param.8), kind=kLoop, calls=%fused_computation.88 | loop fusion | bytes 3200 | tf_op jit(solution)/shard_map/slice | solution.py:100
  6.5 1.0 %fusion.61 = (s32[800]{0:T(1024)S(1)}, s32[800]{0:T(1024)S(1)}, s32[800]{0:T(1024)S(1)}) fusion(s32[6400]{0:T(1024)} %param.7, s32[]{:T(128)S(6)} %dynamic_slice.95, s32[]{:T(128)S(6)} %dynamic_slice.92, s32[]{:T(128)S(6)} %dynamic_slice.43), kind=kLoop, calls=%fused_computation.86 | loop fusion | bytes 19212 | tf_op jit(solution)/shard_map/dynamic_slice | solution.py:42
  7.5 2.7 %fusion.14 = f32[768,200]{0,1:T(8,128)S(1)} fusion(bf16[1536,3200]{1,0:T(8,128)(2,1)} %param.5, s32[]{:T(128)S(6)} %select_n.142, s32[]{:T(128)S(6)} %select_n.125, s32[800]{0:T(1024)S(1)} %get-tuple-element.15, s32[200]{0:T(256)S(1)} %get-tuple-element.19, bf16[800,400]{0,1:T(8,128)(2,1)} %param.6), kind=kOutput, calls=%fused_computation.27 | convolution fusion | flops 246080000 | bytes 2353064 | tf_op jit(solution)/shard_map/dot_general | solution.py:44
  10.1 0.9 %fusion.62 = (s32[400]{0:T(512)S(1)}, s32[400]{0:T(512)S(1)}) fusion(s32[6400]{0:T(1024)} %param.7, s32[]{:T(128)S(6)} %dynamic_slice.98, s32[]{:T(128)S(6)} %dynamic_slice.101), kind=kLoop, calls=%fused_computation.87 | loop fusion | bytes 6408 | tf_op jit(solution)/shard_map/dynamic_slice | solution.py:42
  11.0 2.5 %fusion.22 = f32[768,200]{0,1:T(8,128)S(1)} fusion(bf16[1536,3200]{1,0:T(8,128)(2,1)} %param.5, s32[]{:T(128)S(6)} %select_n.123, s32[]{:T(128)S(6)} %select_n.125, s32[800]{0:T(1024)S(1)} %get-tuple-element.15, s32[200]{0:T(256)S(1)} %get-tuple-element.19, bf16[800,400]{0,1:T(8,128)(2,1)} %param.6), kind=kOutput, calls=%fused_computation.35 | convolution fusion | flops 246080000 | bytes 2353064 | tf_op jit(solution)/shard_map/dot_general | solution.py:44
  13.5 0.7 collective-permute-start.6
  14.3 1.5 %collective-permute-start.7 = (bf16[800,200]{0,1:T(8,128)(2,1)S(1)}, bf16[800,200]{0,1:T(8,128)(2,1)S(1)}, u32[]{:S(2)}, u32[]{:S(2)}) collective-permute-start(bf16[800,200]{0,1:T(8,128)(2,1)S(1)} %get-tuple-element.8), channel_id=1, source_target_pairs={{0,16},{8,24},{16,0},{24,8},{1,17},{9,25},{17,1},{25,9},{2,18},{10... | collective-permute-start | bytes 960008 | tf_op jit(solution)/shard_map/ppermute | solution.py:10
  16.5 1.4 %collective-permute-start.3 = (bf16[400,200]{0,1:T(8,128)(2,1)S(1)}, bf16[400,200]{0,1:T(8,128)(2,1)S(1)}, u32[]{:S(2)}, u32[]{:S(2)}) collective-permute-start(bf16[400,200]{0,1:T(8,128)(2,1)S(1)} %slice.37), channel_id=1, source_target_pairs={{0,16},{8,24},{16,0},{24,8},{1,17},{9,25},{17,1},{25,9},{2,18},{10... | collective-permute-start | bytes 480008 | tf_op jit(solution)/shard_map/ppermute | solution.py:10
  17.9 2.5 %convolution_add_fusion.7 = f32[768,200]{0,1:T(8,128)S(1)} fusion(f32[768,200]{0,1:T(8,128)S(1)} %fusion.14, bf16[1536,3200]{1,0:T(8,128)(2,1)} %param.5, s32[]{:T(128)S(6)} %select_n.142, s32[]{:T(128)S(6)} %select_n.130, bf16[800,200]{0,1:T(8,128)(2,1)S(1)} %collective-permute-done, s32[800]{0:T(1024)S(1)} %get-tuple-element.14, s32[200]{0:T(256)S(1)} %get-tuple-element.19), kind=kOutput, calls=%fused_computation.14 | convolution fusion | flops 246233600 | bytes 2929064 | tf_op jit(solution)/shard_map/dot_general | solution.py:44
  20.4 7.1 %collective-permute-done.2 = bf16[400,200]{0,1:T(8,128)(2,1)S(1)} collective-permute-done((bf16[400,200]{0,1:T(8,128)(2,1)S(1)}, bf16[400,200]{0,1:T(8,128)(2,1)S(1)}, u32[]{:S(2)}, u32[]{:S(2)}) %collective-permute-start.2) | collective-permute-done | bytes 160032 | tf_op jit(solution)/shard_map/ppermute | solution.py:10
  27.5 1.9 %fusion.29 = f32[768,200]{0,1:T(8,128)S(1)} fusion(bf16[1536,3200]{1,0:T(8,128)(2,1)} %param.5, s32[]{:T(128)S(6)} %select_n.142, s32[]{:T(128)S(6)} %select_n.136, bf16[400,200]{0,1:T(8,128)(2,1)S(1)} %collective-permute-done.2, s32[400]{0:T(512)S(1)} %get-tuple-element.16, s32[200]{0:T(256)S(1)} %get-tuple-element.19), kind=kOutput, calls=%fused_computation.48 | convolution fusion | flops 123040000 | bytes 1563240 | tf_op jit(solution)/shard_map/dot_general | solution.py:44
  30.2 1.1 %fusion.4 = f32[768,200]{0,1:T(8,128)S(1)} fusion(f32[768,200]{0,1:T(8,128)S(1)} %fusion.26, f32[768,200]{0,1:T(8,128)S(1)} %fusion.29, f32[768,200]{0,1:T(8,128)S(1)} %convolution_add_fusion.7, bf16[1536,3200]{1,0:T(8,128)(2,1)S(1)} %copy-done, s32[]{:T(128)S(6)} %select_n.142, s32[]{:T(128)S(6)} %select_n.133, ...), kind=kOutput, calls=%fused_computation.13 | convolution fusion | flops 246540800 | bytes 4197384 | tf_op jit(solution)/shard_map/dot_general | solution.py:44
  31.4 1.1 %convolution_add_fusion.9 = f32[768,200]{0,1:T(8,128)S(1)} fusion(f32[768,200]{0,1:T(8,128)S(1)} %fusion.22, bf16[1536,3200]{1,0:T(8,128)(2,1)S(1)} %copy-done, s32[]{:T(128)S(6)} %select_n.123, s32[]{:T(128)S(6)} %select_n.130, bf16[800,200]{0,1:T(8,128)(2,1)S(1)} %collective-permute-done, s32[800]{0:T(1024)S(1)} %get-tuple-element.14, ...), kind=kOutput, calls=%fused_computation.19 | convolution fusion | flops 246233600 | bytes 2968584 | tf_op jit(solution)/shard_map/dot_general | solution.py:44
  34.0 1.2 %fusion.7 = f32[768,200]{0,1:T(8,128)S(1)} fusion(f32[768,200]{0,1:T(8,128)S(1)} %collective-permute-done.4, f32[768,200]{0,1:T(8,128)S(1)} %fusion.33, f32[768,200]{0,1:T(8,128)S(1)} %fusion.36, f32[768,200]{0,1:T(8,128)S(1)} %convolution_add_fusion.9, bf16[1536,3200]{1,0:T(8,128)(2,1)S(1)} %copy-done, s32[]{:T(128)S(6)} %select_n.123, s32[]{:T(128)S(6)} %select_n.133, ...), kind=kOutput, calls=%fused_computation.18 | convolution fusion | flops 246694400 | bytes 4811784 | tf_op jit(solution)/shard_map/dot_general | solution.py:44
  35.7 1.1 %fusion.10 = f32[768,200]{0,1:T(8,128)S(1)} fusion(bf16[1536,3200]{1,0:T(8,128)(2,1)S(1)} %copy-done, s32[]{:T(128)S(6)} %select_n.142, s32[]{:T(128)S(6)} %select_n.130, bf16[800,200]{0,1:T(8,128)(2,1)S(1)} %collective-permute-done.7, s32[800]{0:T(1024)S(1)} %get-tuple-element.14, s32[200]{0:T(256)S(1)} %get-tuple-element.18), kind=kOutput, calls=%fused_computation.23 | convolution fusion | flops 246080000 | bytes 2354184 | tf_op jit(solution)/shard_map/dot_general | solution.py:44
  36.8 1.1 %convolution_add_fusion.3 = f32[768,200]{0,1:T(8,128)S(1)} fusion(f32[768,200]{0,1:T(8,128)S(1)} %fusion.10, bf16[1536,3200]{1,0:T(8,128)(2,1)S(1)} %copy-done, s32[]{:T(128)S(6)} %select_n.142, s32[]{:T(128)S(6)} %select_n.125, bf16[800,200]{0,1:T(8,128)(2,1)S(1)} %get-tuple-element.8, s32[800]{0:T(1024)S(1)} %get-tuple-element.15, ...), kind=kOutput, calls=%fused_computation.8 | convolution fusion | flops 246233600 | bytes 2968584 | tf_op jit(solution)/shard_map/dot_general | solution.py:44
  38.1 1.1 %convolution_add_fusion.2 = f32[768,200]{0,1:T(8,128)S(1)} fusion(f32[768,200]{0,1:T(8,128)S(1)} %convolution_add_fusion.3, bf16[1536,3200]{1,0:T(8,128)(2,1)S(1)} %copy-done, s32[]{:T(128)S(6)} %select_n.142, s32[]{:T(128)S(6)} %select_n.133, bf16[800,200]{0,1:T(8,128)(2,1)S(1)} %collective-permute-done.6, s32[800]{0:T(1024)S(1)} %get-tuple-element.13, ...), kind=kOutput, calls=%fused_computation.7 | convolution fusion | flops 246233600 | bytes 2968584 | tf_op jit(solution)/shard_map/dot_general | solution.py:44
  39.2 1.6 %collective-permute-start.9 = (bf16[400,200]{0,1:T(8,128)(2,1)S(1)}, bf16[400,200]{0,1:T(8,128)(2,1)S(1)}, u32[]{:S(2)}, u32[]{:S(2)}) collective-permute-start(bf16[400,200]{0,1:T(8,128)(2,1)S(1)} %slice.31), channel_id=1, source_target_pairs={{0,16},{8,24},{16,0},{24,8},{1,17},{9,25},{17,1},{25,9},{2,18},{10... | collective-permute-start | bytes 480008 | tf_op jit(solution)/shard_map/ppermute | solution.py:10
  41.3 1.1 %fusion.18 = f32[768,200]{0,1:T(8,128)S(1)} fusion(bf16[1536,3200]{1,0:T(8,128)(2,1)S(1)} %copy-done, s32[]{:T(128)S(6)} %select_n.123, s32[]{:T(128)S(6)} %select_n.130, bf16[800,200]{0,1:T(8,128)(2,1)S(1)} %collective-permute-done.7, s32[800]{0:T(1024)S(1)} %get-tuple-element.14, s32[200]{0:T(256)S(1)} %get-tuple-element.18), kind=kOutput, calls=%fused_computation.31 | convolution fusion | flops 246080000 | bytes 2354184 | tf_op jit(solution)/shard_map/dot_general | solution.py:44
  42.4 13.5 %collective-permute-done.9 = bf16[400,200]{0,1:T(8,128)(2,1)S(1)} collective-permute-done((bf16[400,200]{0,1:T(8,128)(2,1)S(1)}, bf16[400,200]{0,1:T(8,128)(2,1)S(1)}, u32[]{:S(2)}, u32[]{:S(2)}) %collective-permute-start.9) | collective-permute-done | bytes 160032 | tf_op jit(solution)/shard_map/ppermute | solution.py:10
  57.4 1.1 %convolution_add_fusion.5 = f32[768,200]{0,1:T(8,128)S(1)} fusion(f32[768,200]{0,1:T(8,128)S(1)} %fusion.18, bf16[1536,3200]{1,0:T(8,128)(2,1)S(1)} %copy-done, s32[]{:T(128)S(6)} %select_n.123, s32[]{:T(128)S(6)} %select_n.125, bf16[800,200]{0,1:T(8,128)(2,1)S(1)} %get-tuple-element.8, s32[800]{0:T(1024)S(1)} %get-tuple-element.15, ...), kind=kOutput, calls=%fused_computation.10 | convolution fusion | flops 246233600 | bytes 2968584 | tf_op jit(solution)/shard_map/dot_general | solution.py:44
  58.5 1.1 %convolution_add_fusion.4 = f32[768,200]{0,1:T(8,128)S(1)} fusion(f32[768,200]{0,1:T(8,128)S(1)} %convolution_add_fusion.5, bf16[1536,3200]{1,0:T(8,128)(2,1)S(1)} %copy-done, s32[]{:T(128)S(6)} %select_n.123, s32[]{:T(128)S(6)} %select_n.133, bf16[800,200]{0,1:T(8,128)(2,1)S(1)} %collective-permute-done.6, s32[800]{0:T(1024)S(1)} %get-tuple-element.13, ...), kind=kOutput, calls=%fused_computation.9 | convolution fusion | flops 246233600 | bytes 2968584 | tf_op jit(solution)/shard_map/dot_general | solution.py:44
  60.4 0.7 fusion.1
  61.6 0.8 dynamic-slice_subtract_fusion
  62.7 2.1 %gather_fusion = f32[768,200]{1,0:T(8,128)S(1)} fusion(f32[768,200]{1,0:T(8,128)S(1)} %copy.6, s32[1024]{0:T(1024)S(1)} %pad_clamp_fusion), kind=kCustom, calls=%fused_computation | custom fusion | bytes 1231872 | tf_op jit(solution)/shard_map/jit(_take)/gather | solution.py:76
  65.1 12.4 %collective-permute-done.11 = f32[768,200]{0,1:T(8,128)} collective-permute-done((f32[768,200]{0,1:T(8,128)S(1)}, f32[768,200]{0,1:T(8,128)}, u32[]{:S(2)}, u32[]{:S(2)}) %collective-permute-start.11) | collective-permute-done | bytes 614432 | tf_op jit(solution)/shard_map/ppermute | solution.py:10
  77.6 1.3 %copy.8 = f32[768,200]{1,0:T(8,128)S(1)} copy(f32[768,200]{0,1:T(8,128)} %collective-permute-done.11) | data formatting | bytes 1228800 | tf_op jit(solution)/shard_map/ppermute | solution.py:10
  78.9 2.1 %gather_fusion.1 = f32[768,200]{1,0:T(8,128)S(1)} fusion(f32[768,200]{1,0:T(8,128)S(1)} %copy.8, s32[1024]{0:T(1024)S(1)} %pad_clamp_fusion), kind=kCustom, calls=%fused_computation.1 | custom fusion | bytes 1231872 | tf_op jit(solution)/shard_map/jit(_take)/gather | solution.py:76
  81.3 1.1 %pad_maximum_fusion = f32[768,400]{0,1:T(8,128)} fusion(f32[768,200]{0,1:T(8,128)S(1)} %sub.15, f32[768,200]{0,1:T(8,128)S(1)} %sub.14), kind=kLoop, calls=%fused_computation.20 | loop fusion | flops 307200 | bytes 2457600 | tf_op jit(solution)/shard_map/concatenate | solution.py:103
  (33 shorter events, 7.7 us)
Async XLA Ops:
  1.2 12.4 %collective-permute-start = (bf16[800,200]{0,1:T(8,128)(2,1)S(1)}, bf16[800,200]{0,1:T(8,128)(2,1)S(1)}, u32[]{:S(2)}, u32[]{:S(2)}) collective-permute-start(bf16[800,200]{0,1:T(8,128)(2,1)S(1)} %get-tuple-element.11), channel_id=1, source_target_pairs={{0,16},{8,24},{16,0},{24,8},{1,17},{9,25},{17,1},{25,9},{2,18},{10... | collective-permute-start | bytes 960008 | tf_op jit(solution)/shard_map/ppermute | solution.py:10
  4.2 12.2 %collective-permute-start.1 = (bf16[800,200]{0,1:T(8,128)(2,1)S(1)}, bf16[800,200]{0,1:T(8,128)(2,1)S(1)}, u32[]{:S(2)}, u32[]{:S(2)}) collective-permute-start(bf16[800,200]{0,1:T(8,128)(2,1)S(1)} %get-tuple-element.11), channel_id=1, source_target_pairs={{0,8},{8,0},{16,24},{24,16},{1,9},{9,1},{17,25},{25,17},{2,10},{10... | collective-permute-start | bytes 960008 | tf_op jit(solution)/shard_map/ppermute | solution.py:10
  6.5 22.9 %copy-start = (bf16[1536,3200]{1,0:T(8,128)(2,1)S(1)}, bf16[1536,3200]{1,0:T(8,128)(2,1)}, u32[]{:S(2)}) copy-start(bf16[1536,3200]{1,0:T(8,128)(2,1)} %param.5) | copy-start | bytes 29491204
  13.5 22.2 %collective-permute-start.6 = (bf16[800,200]{0,1:T(8,128)(2,1)S(1)}, bf16[800,200]{0,1:T(8,128)(2,1)S(1)}, u32[]{:S(2)}, u32[]{:S(2)}) collective-permute-start(bf16[800,200]{0,1:T(8,128)(2,1)S(1)} %get-tuple-element.8), channel_id=1, source_target_pairs={{0,8},{8,0},{16,24},{24,16},{1,9},{9,1},{17,25},{25,17},{2,10},{10... | collective-permute-start | bytes 960008 | tf_op jit(solution)/shard_map/ppermute | solution.py:10
  14.3 21.4 %collective-permute-start.7 = (bf16[800,200]{0,1:T(8,128)(2,1)S(1)}, bf16[800,200]{0,1:T(8,128)(2,1)S(1)}, u32[]{:S(2)}, u32[]{:S(2)}) collective-permute-start(bf16[800,200]{0,1:T(8,128)(2,1)S(1)} %get-tuple-element.8), channel_id=1, source_target_pairs={{0,16},{8,24},{16,0},{24,8},{1,17},{9,25},{17,1},{25,9},{2,18},{10... | collective-permute-start | bytes 960008 | tf_op jit(solution)/shard_map/ppermute | solution.py:10
  15.8 11.7 %collective-permute-start.2 = (bf16[400,200]{0,1:T(8,128)(2,1)S(1)}, bf16[400,200]{0,1:T(8,128)(2,1)S(1)}, u32[]{:S(2)}, u32[]{:S(2)}) collective-permute-start(bf16[400,200]{0,1:T(8,128)(2,1)S(1)} %slice.36), channel_id=1, source_target_pairs={{0,8},{8,0},{16,24},{24,16},{1,9},{9,1},{17,25},{25,17},{2,10},{10... | collective-permute-start | bytes 480008 | tf_op jit(solution)/shard_map/ppermute | solution.py:10
  16.5 12.9 %collective-permute-start.3 = (bf16[400,200]{0,1:T(8,128)(2,1)S(1)}, bf16[400,200]{0,1:T(8,128)(2,1)S(1)}, u32[]{:S(2)}, u32[]{:S(2)}) collective-permute-start(bf16[400,200]{0,1:T(8,128)(2,1)S(1)} %slice.37), channel_id=1, source_target_pairs={{0,16},{8,24},{16,0},{24,8},{1,17},{9,25},{17,1},{25,9},{2,18},{10... | collective-permute-start | bytes 480008 | tf_op jit(solution)/shard_map/ppermute | solution.py:10
  31.3 2.6 %collective-permute-start.4 = (f32[768,200]{0,1:T(8,128)S(1)}, f32[768,200]{0,1:T(8,128)S(1)}, u32[]{:S(2)}, u32[]{:S(2)}) collective-permute-start(f32[768,200]{0,1:T(8,128)S(1)} %fusion.4), channel_id=1, source_target_pairs={{0,1},{1,0},{2,3},{3,2},{4,5},{5,4},{6,7},{7,6},{8,9},{9,8},{10,11... | collective-permute-start | bytes 1843208 | tf_op jit(solution)/shard_map/ppermute | solution.py:10
  35.2 27.2 %collective-permute-start.5 = (f32[768,200]{0,1:T(8,128)S(1)}, f32[768,200]{0,1:T(8,128)S(1)}, u32[]{:S(2)}, u32[]{:S(2)}) collective-permute-start(f32[768,200]{0,1:T(8,128)S(1)} %fusion.7), channel_id=1, source_target_pairs={{0,16},{8,24},{16,0},{24,8},{1,17},{9,25},{17,1},{25,9},{2,18},{10... | collective-permute-start | bytes 1843208 | tf_op jit(solution)/shard_map/ppermute | solution.py:10
  39.2 16.6 %collective-permute-start.9 = (bf16[400,200]{0,1:T(8,128)(2,1)S(1)}, bf16[400,200]{0,1:T(8,128)(2,1)S(1)}, u32[]{:S(2)}, u32[]{:S(2)}) collective-permute-start(bf16[400,200]{0,1:T(8,128)(2,1)S(1)} %slice.31), channel_id=1, source_target_pairs={{0,16},{8,24},{16,0},{24,8},{1,17},{9,25},{17,1},{25,9},{2,18},{10... | collective-permute-start | bytes 480008 | tf_op jit(solution)/shard_map/ppermute | solution.py:10
  40.8 15.7 %collective-permute-start.8 = (bf16[400,200]{0,1:T(8,128)(2,1)S(1)}, bf16[400,200]{0,1:T(8,128)(2,1)S(1)}, u32[]{:S(2)}, u32[]{:S(2)}) collective-permute-start(bf16[400,200]{0,1:T(8,128)(2,1)S(1)} %slice.30), channel_id=1, source_target_pairs={{0,8},{8,0},{16,24},{24,16},{1,9},{9,1},{17,25},{25,17},{2,10},{10... | collective-permute-start | bytes 480008 | tf_op jit(solution)/shard_map/ppermute | solution.py:10
  57.3 3.1 %collective-permute-start.10 = (f32[768,200]{0,1:T(8,128)S(1)}, f32[768,200]{0,1:T(8,128)S(1)}, u32[]{:S(2)}, u32[]{:S(2)}) collective-permute-start(f32[768,200]{0,1:T(8,128)S(1)} %fusion.2), channel_id=1, source_target_pairs={{0,1},{1,0},{2,3},{3,2},{4,5},{5,4},{6,7},{7,6},{8,9},{9,8},{10,11... | collective-permute-start | bytes 1843208 | tf_op jit(solution)/shard_map/ppermute | solution.py:10
  61.1 16.4 %collective-permute-start.11 = (f32[768,200]{0,1:T(8,128)S(1)}, f32[768,200]{0,1:T(8,128)}, u32[]{:S(2)}, u32[]{:S(2)}) collective-permute-start(f32[768,200]{0,1:T(8,128)S(1)} %fusion.1), channel_id=1, source_target_pairs={{0,16},{8,24},{16,0},{24,8},{1,17},{9,25},{17,1},{25,9},{2,18},{10... | collective-permute-start | bytes 1843208 | tf_op jit(solution)/shard_map/ppermute | solution.py:10

commit v10 on v9

--- a/solution.py
+++ b/solution.py
@@ -97,7 +97,7 @@
     hold = None
     for j in range(chunks):
         result, after, hold = antisym(amplitudes, integrals[:, j * step:(j + 1) * step], labels,
-                                      irrep_cols[j * step:(j + 1) * step], local, False, 1 if chunks > 1 else 2,
+                                      irrep_cols[j * step:(j + 1) * step], local, chunks > 1, 1 if chunks > 1 else 2,
                                       after, hold)
         results.append(result)
     return jnp.concatenate(results, axis=1) if chunks > 1 else results[0]

time: 82.9 us -> 76.4 us (0.922)
  waiting for transfers between devices: 33 us -> 28.4 us
  local copies, waits for them, and re-layouts: 10.4 us -> 7.71 us
  matrix products: 24.7 us -> 25.6 us
    ppermute x12 -> x10, waiting for transfers between devices: 33 us -> 28.4 us  [swap(): lax.ppermute(value, axis, [(i, i ^ mask) for i in range(lax.axis_size(axi...]
    dynamic_slice x2 -> x1, local copies, waits for them, and re-layouts: 1.81 us -> 0.09 us  [contract(): lax.dynamic_slice_in_dim(labels, o, b.shape[0])[:, None]]
    dot_general x20 -> x16, matrix products: 24.7 us -> 25.6 us  [contract(): product = jnp.dot(window, blocked, preferred_element_type=jnp.float32)]
    ppermute x12 -> x10, starting transfers between devices: 12 us -> 12.1 us  [swap(): lax.ppermute(value, axis, [(i, i ^ mask) for i in range(lax.axis_size(axi...]
  transfers between devices with their start and end apart: 12 -> 10, of which waited for: 3 -> 6; matrix products, arithmetic and copies ran while one was open for 38% -> 35% of each run, Pallas kernels for 0% -> 0%
where the time goes in v10:
time: 76.4 us; the launch traced here: 76.1 us
  waiting for transfers between devices  28.4 us (37%)
  matrix products  25.6 us (34%)
  starting transfers between devices  12.1 us (16%)
  local copies, waits for them, and re-layouts  7.71 us (10%)
  other arithmetic  2.06 us (3%)
    ppermute x10, waiting for transfers between devices, swap(): lax.ppermute(value, axis, [(i, i ^ mask) for i in range(lax.axis_size(axi...  28.4 us
    dot_general x16, matrix products, contract(): product = jnp.dot(window, blocked, preferred_element_type=jnp.float32)  25.6 us
    ppermute x10, starting transfers between devices, swap(): lax.ppermute(value, axis, [(i, i ^ mask) for i in range(lax.axis_size(axi...  12.1 us
    gather x4, local copies, waits for them, and re-layouts, antisym(): jnp.take(fetched, local, axis=0, mode='clip')  4.72 us
    ppermute x2, local copies, waits for them, and re-layouts, swap(): lax.ppermute(value, axis, [(i, i ^ mask) for i in range(lax.axis_size(axi...  1.6 us
  transfers between devices with their start and end apart: 10, of which 6 were waited for; matrix products, arithmetic and copies ran while one was open for 35% of the time, Pallas kernels for 0%

profile of v10, /device:TPU:0, one launch (start us, length us, event | category | flops | bytes accessed | tf_op | source)
XLA Modules:
  0.0 76.1 jit_solution(13809763766918839389)
XLA Ops:
  0.0 1.2 %fusion.40 = (bf16[800,200]{0,1:T(8,128)(2,1)S(1)}, bf16[800,200]{0,1:T(8,128)(2,1)S(1)}) fusion(bf16[800,400]{0,1:T(8,128)(2,1)} %param.6), kind=kLoop, calls=%fused_computation.65 | loop fusion | bytes 1280000 | tf_op jit(solution)/shard_map/slice | solution.py:99
  1.2 3.0 %collective-permute-start = (bf16[800,200]{0,1:T(8,128)(2,1)S(1)}, bf16[800,200]{0,1:T(8,128)(2,1)S(1)}, u32[]{:S(2)}, u32[]{:S(2)}) collective-permute-start(bf16[800,200]{0,1:T(8,128)(2,1)S(1)} %get-tuple-element.11), channel_id=1, source_target_pairs={{0,16},{8,24},{16,0},{24,8},{1,17},{9,25},{17,1},{25,9},{2,18},{10... | collective-permute-start | bytes 960008 | tf_op jit(solution)/shard_map/ppermute | solution.py:10
  4.3 1.5 %collective-permute-start.1 = (bf16[800,200]{0,1:T(8,128)(2,1)S(1)}, bf16[800,200]{0,1:T(8,128)(2,1)S(1)}, u32[]{:S(2)}, u32[]{:S(2)}) collective-permute-start(bf16[800,200]{0,1:T(8,128)(2,1)S(1)} %get-tuple-element.11), channel_id=1, source_target_pairs={{0,8},{8,0},{16,24},{24,16},{1,9},{9,1},{17,25},{25,17},{2,10},{10... | collective-permute-start | bytes 960008 | tf_op jit(solution)/shard_map/ppermute | solution.py:10
  5.9 2.5 %fusion.10 = f32[768,200]{0,1:T(8,128)S(1)} fusion(bf16[1536,3200]{1,0:T(8,128)(2,1)} %param.5, s32[]{:T(128)S(6)} %select_n.118, s32[]{:T(128)S(6)} %select_n.104, s32[800]{0:T(1024)S(1)} %get-tuple-element.15, s32[200]{0:T(256)S(1)} %get-tuple-element.18, bf16[800,400]{0,1:T(8,128)(2,1)S(1)} %copy-done.1), kind=kOutput, calls=%fused_computation.25 | convolution fusion | flops 246080000 | bytes 2354184 | tf_op jit(solution)/shard_map/dot_general | solution.py:44
  8.4 4.2 %collective-permute-done = bf16[800,200]{0,1:T(8,128)(2,1)S(1)} collective-permute-done((bf16[800,200]{0,1:T(8,128)(2,1)S(1)}, bf16[800,200]{0,1:T(8,128)(2,1)S(1)}, u32[]{:S(2)}, u32[]{:S(2)}) %collective-permute-start) | collective-permute-done | bytes 320032 | tf_op jit(solution)/shard_map/ppermute | solution.py:10
  12.6 1.7 %collective-permute-start.2 = (bf16[800,200]{0,1:T(8,128)(2,1)S(1)}, bf16[800,200]{0,1:T(8,128)(2,1)S(1)}, u32[]{:S(2)}, u32[]{:S(2)}) collective-permute-start(bf16[800,200]{0,1:T(8,128)(2,1)S(1)} %collective-permute-done), channel_id=1, source_target_pairs={{0,8},{8,0},{16,24},{24,16},{1,9},{9,1},{17,25},{25,17},{2,10},{10... | collective-permute-start | bytes 960008 | tf_op jit(solution)/shard_map/ppermute | solution.py:10
  14.3 2.7 %convolution_add_fusion.8 = f32[768,200]{0,1:T(8,128)S(1)} fusion(f32[768,200]{0,1:T(8,128)S(1)} %fusion.10, bf16[1536,3200]{1,0:T(8,128)(2,1)} %param.5, s32[]{:T(128)S(6)} %select_n.118, s32[]{:T(128)S(6)} %select_n.109, bf16[800,200]{0,1:T(8,128)(2,1)S(1)} %collective-permute-done, s32[800]{0:T(1024)S(1)} %get-tuple-element.14, s32[200]{0:T(256)S(1)} %get-tuple-element.18), kind=kOutput, calls=%fused_computation.11 | convolution fusion | flops 246233600 | bytes 2929064 | tf_op jit(solution)/shard_map/dot_general | solution.py:44
  17.0 3.1 %convolution_add_fusion.7 = f32[768,200]{0,1:T(8,128)S(1)} fusion(f32[768,200]{0,1:T(8,128)S(1)} %convolution_add_fusion.8, bf16[1536,3200]{1,0:T(8,128)(2,1)} %param.5, s32[]{:T(128)S(6)} %select_n.118, s32[]{:T(128)S(6)} %select_n.112, bf16[800,200]{0,1:T(8,128)(2,1)S(1)} %collective-permute-done.1, s32[800]{0:T(1024)S(1)} %get-tuple-element.16, ...), kind=kOutput, calls=%fused_computation.10 | convolution fusion | flops 246233600 | bytes 2929064 | tf_op jit(solution)/shard_map/dot_general | solution.py:44
  20.1 2.1 %collective-permute-done.2 = bf16[800,200]{0,1:T(8,128)(2,1)S(1)} collective-permute-done((bf16[800,200]{0,1:T(8,128)(2,1)S(1)}, bf16[800,200]{0,1:T(8,128)(2,1)S(1)}, u32[]{:S(2)}, u32[]{:S(2)}) %collective-permute-start.2) | collective-permute-done | bytes 320032 | tf_op jit(solution)/shard_map/ppermute | solution.py:10
  22.2 2.5 %convolution_add_fusion.6 = f32[768,200]{0,1:T(8,128)S(1)} fusion(f32[768,200]{0,1:T(8,128)S(1)} %convolution_add_fusion.7, bf16[1536,3200]{1,0:T(8,128)(2,1)} %param.5, s32[]{:T(128)S(6)} %select_n.118, s32[]{:T(128)S(6)} %select_n.115, bf16[800,200]{0,1:T(8,128)(2,1)S(1)} %collective-permute-done.2, s32[800]{0:T(1024)S(1)} %get-tuple-element.13, ...), kind=kOutput, calls=%fused_computation.9 | convolution fusion | flops 246233600 | bytes 2929064 | tf_op jit(solution)/shard_map/dot_general | solution.py:44
  24.7 2.5 %fusion.20 = f32[768,200]{0,1:T(8,128)S(1)} fusion(bf16[1536,3200]{1,0:T(8,128)(2,1)} %param.5, s32[]{:T(128)S(6)} %select_n.102, s32[]{:T(128)S(6)} %select_n.104, s32[800]{0:T(1024)S(1)} %get-tuple-element.15, s32[200]{0:T(256)S(1)} %get-tuple-element.18, bf16[800,400]{0,1:T(8,128)(2,1)S(1)} %copy-done.1), kind=kOutput, calls=%fused_computation.35 | convolution fusion | flops 246080000 | bytes 2354184 | tf_op jit(solution)/shard_map/dot_general | solution.py:44
  27.2 1.5 %collective-permute-start.5 = (bf16[800,200]{0,1:T(8,128)(2,1)S(1)}, bf16[800,200]{0,1:T(8,128)(2,1)S(1)}, u32[]{:S(2)}, u32[]{:S(2)}) collective-permute-start(bf16[800,200]{0,1:T(8,128)(2,1)S(1)} %get-tuple-element.8), channel_id=1, source_target_pairs={{0,8},{8,0},{16,24},{24,16},{1,9},{9,1},{17,25},{25,17},{2,10},{10... | collective-permute-start | bytes 960008 | tf_op jit(solution)/shard_map/ppermute | solution.py:10
  28.7 1.4 %collective-permute-start.6 = (bf16[800,200]{0,1:T(8,128)(2,1)S(1)}, bf16[800,200]{0,1:T(8,128)(2,1)S(1)}, u32[]{:S(2)}, u32[]{:S(2)}) collective-permute-start(bf16[800,200]{0,1:T(8,128)(2,1)S(1)} %get-tuple-element.8), channel_id=1, source_target_pairs={{0,16},{8,24},{16,0},{24,8},{1,17},{9,25},{17,1},{25,9},{2,18},{10... | collective-permute-start | bytes 960008 | tf_op jit(solution)/shard_map/ppermute | solution.py:10
  30.2 1.1 %convolution_add_fusion.11 = f32[768,200]{0,1:T(8,128)S(1)} fusion(f32[768,200]{0,1:T(8,128)S(1)} %fusion.20, bf16[1536,3200]{1,0:T(8,128)(2,1)S(1)} %copy-done, s32[]{:T(128)S(6)} %select_n.102, s32[]{:T(128)S(6)} %select_n.109, bf16[800,200]{0,1:T(8,128)(2,1)S(1)} %collective-permute-done, s32[800]{0:T(1024)S(1)} %get-tuple-element.14, ...), kind=kOutput, calls=%fused_computation.15 | convolution fusion | flops 246233600 | bytes 2968584 | tf_op jit(solution)/shard_map/dot_general | solution.py:44
  31.3 1.1 %convolution_add_fusion.10 = f32[768,200]{0,1:T(8,128)S(1)} fusion(f32[768,200]{0,1:T(8,128)S(1)} %convolution_add_fusion.11, bf16[1536,3200]{1,0:T(8,128)(2,1)S(1)} %copy-done, s32[]{:T(128)S(6)} %select_n.102, s32[]{:T(128)S(6)} %select_n.112, bf16[800,200]{0,1:T(8,128)(2,1)S(1)} %collective-permute-done.1, s32[800]{0:T(1024)S(1)} %get-tuple-element.16, ...), kind=kOutput, calls=%fused_computation.14 | convolution fusion | flops 246233600 | bytes 2968584 | tf_op jit(solution)/shard_map/dot_general | solution.py:44
  32.5 1.1 %fusion.1 = f32[768,200]{0,1:T(8,128)S(1)} fusion(f32[768,200]{0,1:T(8,128)S(1)} %collective-permute-done.3, f32[768,200]{0,1:T(8,128)S(1)} %convolution_add_fusion.10, bf16[1536,3200]{1,0:T(8,128)(2,1)S(1)} %copy-done, s32[]{:T(128)S(6)} %select_n.102, s32[]{:T(128)S(6)} %select_n.115, bf16[800,200]{0,1:T(8,128)(2,1)S(1)} %collective-permute-done.2, ...), kind=kOutput, calls=%fused_computation.13 | convolution fusion | flops 246387200 | bytes 3582984 | tf_op jit(solution)/shard_map/dot_general | solution.py:44
  34.2 3.8 %collective-permute-done.5 = bf16[800,200]{0,1:T(8,128)(2,1)S(1)} collective-permute-done((bf16[800,200]{0,1:T(8,128)(2,1)S(1)}, bf16[800,200]{0,1:T(8,128)(2,1)S(1)}, u32[]{:S(2)}, u32[]{:S(2)}) %collective-permute-start.5) | collective-permute-done | bytes 320032 | tf_op jit(solution)/shard_map/ppermute | solution.py:10
  38.0 1.9 %collective-permute-done.6 = bf16[800,200]{0,1:T(8,128)(2,1)S(1)} collective-permute-done((bf16[800,200]{0,1:T(8,128)(2,1)S(1)}, bf16[800,200]{0,1:T(8,128)(2,1)S(1)}, u32[]{:S(2)}, u32[]{:S(2)}) %collective-permute-start.6) | collective-permute-done | bytes 320032 | tf_op jit(solution)/shard_map/ppermute | solution.py:10
  41.6 1.1 %convolution_add_fusion.2 = f32[768,200]{0,1:T(8,128)S(1)} fusion(f32[768,200]{0,1:T(8,128)S(1)} %fusion.6, bf16[1536,3200]{1,0:T(8,128)(2,1)S(1)} %copy-done, s32[]{:T(128)S(6)} %select_n.118, s32[]{:T(128)S(6)} %select_n.104, bf16[800,200]{0,1:T(8,128)(2,1)S(1)} %get-tuple-element.8, s32[800]{0:T(1024)S(1)} %get-tuple-element.15, s32[200]{0:T(256)S(1)} %get-tuple-element.17), kind=kOutput, calls=%fused_computation.4 | convolution fusion | flops 246233600 | bytes 2968584 | tf_op jit(solution)/shard_map/dot_general | solution.py:44
  42.7 1.1 %convolution_add_fusion.1 = f32[768,200]{0,1:T(8,128)S(1)} fusion(f32[768,200]{0,1:T(8,128)S(1)} %convolution_add_fusion.2, bf16[1536,3200]{1,0:T(8,128)(2,1)S(1)} %copy-done, s32[]{:T(128)S(6)} %select_n.118, s32[]{:T(128)S(6)} %select_n.112, bf16[800,200]{0,1:T(8,128)(2,1)S(1)} %collective-permute-done.5, s32[800]{0:T(1024)S(1)} %get-tuple-element.16, ...), kind=kOutput, calls=%fused_computation.3 | convolution fusion | flops 246233600 | bytes 2968584 | tf_op jit(solution)/shard_map/dot_general | solution.py:44
  43.9 5.0 %collective-permute-done.7 = bf16[800,200]{0,1:T(8,128)(2,1)S(1)} collective-permute-done((bf16[800,200]{0,1:T(8,128)(2,1)S(1)}, bf16[800,200]{0,1:T(8,128)(2,1)S(1)}, u32[]{:S(2)}, u32[]{:S(2)}) %collective-permute-start.7) | collective-permute-done | bytes 320032 | tf_op jit(solution)/shard_map/ppermute | solution.py:10
  48.9 1.3 %convolution_add_fusion = f32[768,200]{0,1:T(8,128)S(1)} fusion(f32[768,200]{0,1:T(8,128)S(1)} %convolution_add_fusion.1, bf16[1536,3200]{1,0:T(8,128)(2,1)S(1)} %copy-done, s32[]{:T(128)S(6)} %select_n.118, s32[]{:T(128)S(6)} %select_n.115, bf16[800,200]{0,1:T(8,128)(2,1)S(1)} %collective-permute-done.7, s32[800]{0:T(1024)S(1)} %get-tuple-element.13, ...), kind=kOutput, calls=%fused_computation.2 | convolution fusion | flops 246233600 | bytes 2968584 | tf_op jit(solution)/shard_map/dot_general | solution.py:44
  50.2 1.1 %fusion.16 = f32[768,200]{0,1:T(8,128)S(1)} fusion(bf16[1536,3200]{1,0:T(8,128)(2,1)S(1)} %copy-done, s32[]{:T(128)S(6)} %select_n.102, s32[]{:T(128)S(6)} %select_n.109, bf16[800,200]{0,1:T(8,128)(2,1)S(1)} %collective-permute-done.6, s32[800]{0:T(1024)S(1)} %get-tuple-element.14, s32[200]{0:T(256)S(1)} %get-tuple-element.17), kind=kOutput, calls=%fused_computation.31 | convolution fusion | flops 246080000 | bytes 2354184 | tf_op jit(solution)/shard_map/dot_general | solution.py:44
  51.3 1.1 %convolution_add_fusion.5 = f32[768,200]{0,1:T(8,128)S(1)} fusion(f32[768,200]{0,1:T(8,128)S(1)} %fusion.16, bf16[1536,3200]{1,0:T(8,128)(2,1)S(1)} %copy-done, s32[]{:T(128)S(6)} %select_n.102, s32[]{:T(128)S(6)} %select_n.104, bf16[800,200]{0,1:T(8,128)(2,1)S(1)} %get-tuple-element.8, s32[800]{0:T(1024)S(1)} %get-tuple-element.15, ...), kind=kOutput, calls=%fused_computation.8 | convolution fusion | flops 246233600 | bytes 2968584 | tf_op jit(solution)/shard_map/dot_general | solution.py:44
  52.4 1.1 %convolution_add_fusion.4 = f32[768,200]{0,1:T(8,128)S(1)} fusion(f32[768,200]{0,1:T(8,128)S(1)} %convolution_add_fusion.5, bf16[1536,3200]{1,0:T(8,128)(2,1)S(1)} %copy-done, s32[]{:T(128)S(6)} %select_n.102, s32[]{:T(128)S(6)} %select_n.112, bf16[800,200]{0,1:T(8,128)(2,1)S(1)} %collective-permute-done.5, s32[800]{0:T(1024)S(1)} %get-tuple-element.16, ...), kind=kOutput, calls=%fused_computation.7 | convolution fusion | flops 246233600 | bytes 2968584 | tf_op jit(solution)/shard_map/dot_general | solution.py:44
  53.6 1.1 %fusion = f32[768,200]{0,1:T(8,128)S(1)} fusion(f32[768,200]{0,1:T(8,128)S(1)} %collective-permute-done.8, f32[768,200]{0,1:T(8,128)S(1)} %convolution_add_fusion.4, bf16[1536,3200]{1,0:T(8,128)(2,1)S(1)} %copy-done, s32[]{:T(128)S(6)} %select_n.102, s32[]{:T(128)S(6)} %select_n.115, bf16[800,200]{0,1:T(8,128)(2,1)S(1)} %collective-permute-done.7, ...), kind=kOutput, calls=%fused_computation.6 | convolution fusion | flops 246387200 | bytes 3582984 | tf_op jit(solution)/shard_map/dot_general | solution.py:44
  54.7 1.5 %collective-permute-start.9 = (f32[768,200]{0,1:T(8,128)S(1)}, f32[768,200]{0,1:T(8,128)}, u32[]{:S(2)}, u32[]{:S(2)}) collective-permute-start(f32[768,200]{0,1:T(8,128)S(1)} %fusion), channel_id=1, source_target_pairs={{0,16},{8,24},{16,0},{24,8},{1,17},{9,25},{17,1},{25,9},{2,18},{10... | collective-permute-start | bytes 1843208 | tf_op jit(solution)/shard_map/ppermute | solution.py:10
  57.3 2.1 %gather_fusion = f32[768,200]{1,0:T(8,128)S(1)} fusion(f32[768,200]{1,0:T(8,128)S(1)} %copy.6, s32[1024]{0:T(1024)S(1)} %pad_clamp_fusion), kind=kCustom, calls=%fused_computation | custom fusion | bytes 1231872 | tf_op jit(solution)/shard_map/jit(_take)/gather | solution.py:76
  59.7 11.4 %collective-permute-done.9 = f32[768,200]{0,1:T(8,128)} collective-permute-done((f32[768,200]{0,1:T(8,128)S(1)}, f32[768,200]{0,1:T(8,128)}, u32[]{:S(2)}, u32[]{:S(2)}) %collective-permute-start.9) | collective-permute-done | bytes 614432 | tf_op jit(solution)/shard_map/ppermute | solution.py:10
  71.1 1.3 %copy.8 = f32[768,200]{1,0:T(8,128)S(1)} copy(f32[768,200]{0,1:T(8,128)} %collective-permute-done.9) | data formatting | bytes 1228800 | tf_op jit(solution)/shard_map/ppermute | solution.py:10
  72.5 2.1 %gather_fusion.1 = f32[768,200]{1,0:T(8,128)S(1)} fusion(f32[768,200]{1,0:T(8,128)S(1)} %copy.8, s32[1024]{0:T(1024)S(1)} %pad_clamp_fusion), kind=kCustom, calls=%fused_computation.1 | custom fusion | bytes 1231872 | tf_op jit(solution)/shard_map/jit(_take)/gather | solution.py:76
  74.9 1.1 %pad_maximum_fusion = f32[768,400]{0,1:T(8,128)} fusion(f32[768,200]{0,1:T(8,128)S(1)} %sub.15, f32[768,200]{0,1:T(8,128)S(1)} %sub.14), kind=kLoop, calls=%fused_computation.16 | loop fusion | flops 307200 | bytes 2457600 | tf_op jit(solution)/shard_map/concatenate | solution.py:103
  (26 shorter events, 4.3 us)
Async XLA Ops:
  0.0 5.9 %copy-start.1 = (bf16[800,400]{0,1:T(8,128)(2,1)S(1)}, bf16[800,400]{0,1:T(8,128)(2,1)}, u32[]{:S(2)}) copy-start(bf16[800,400]{0,1:T(8,128)(2,1)} %param.6) | copy-start | bytes 1920004
  0.0 5.8 %copy-start.3 = (s32[400]{0:T(512)S(1)}, s32[400]{0:T(512)}, u32[]{:S(2)}) copy-start(s32[400]{0:T(512)} %param.8) | copy-start | bytes 4804
  0.0 5.8 %copy-start.2 = (s32[6400]{0:T(1024)S(1)}, s32[6400]{0:T(1024)}, u32[]{:S(2)}) copy-start(s32[6400]{0:T(1024)} %param.7) | copy-start | bytes 76804
  1.2 11.4 %collective-permute-start = (bf16[800,200]{0,1:T(8,128)(2,1)S(1)}, bf16[800,200]{0,1:T(8,128)(2,1)S(1)}, u32[]{:S(2)}, u32[]{:S(2)}) collective-permute-start(bf16[800,200]{0,1:T(8,128)(2,1)S(1)} %get-tuple-element.11), channel_id=1, source_target_pairs={{0,16},{8,24},{16,0},{24,8},{1,17},{9,25},{17,1},{25,9},{2,18},{10... | collective-permute-start | bytes 960008 | tf_op jit(solution)/shard_map/ppermute | solution.py:10
  4.3 12.8 %collective-permute-start.1 = (bf16[800,200]{0,1:T(8,128)(2,1)S(1)}, bf16[800,200]{0,1:T(8,128)(2,1)S(1)}, u32[]{:S(2)}, u32[]{:S(2)}) collective-permute-start(bf16[800,200]{0,1:T(8,128)(2,1)S(1)} %get-tuple-element.11), channel_id=1, source_target_pairs={{0,8},{8,0},{16,24},{24,16},{1,9},{9,1},{17,25},{25,17},{2,10},{10... | collective-permute-start | bytes 960008 | tf_op jit(solution)/shard_map/ppermute | solution.py:10
  12.6 9.6 %collective-permute-start.2 = (bf16[800,200]{0,1:T(8,128)(2,1)S(1)}, bf16[800,200]{0,1:T(8,128)(2,1)S(1)}, u32[]{:S(2)}, u32[]{:S(2)}) collective-permute-start(bf16[800,200]{0,1:T(8,128)(2,1)S(1)} %collective-permute-done), channel_id=1, source_target_pairs={{0,8},{8,0},{16,24},{24,16},{1,9},{9,1},{17,25},{25,17},{2,10},{10... | collective-permute-start | bytes 960008 | tf_op jit(solution)/shard_map/ppermute | solution.py:10
  14.3 15.8 %copy-start = (bf16[1536,3200]{1,0:T(8,128)(2,1)S(1)}, bf16[1536,3200]{1,0:T(8,128)(2,1)}, u32[]{:S(2)}) copy-start(bf16[1536,3200]{1,0:T(8,128)(2,1)} %param.5) | copy-start | bytes 29491204
  24.6 7.8 %collective-permute-start.3 = (f32[768,200]{0,1:T(8,128)S(1)}, f32[768,200]{0,1:T(8,128)S(1)}, u32[]{:S(2)}, u32[]{:S(2)}) collective-permute-start(f32[768,200]{0,1:T(8,128)S(1)} %convolution_add_fusion.6), channel_id=1, source_target_pairs={{0,1},{1,0},{2,3},{3,2},{4,5},{5,4},{6,7},{7,6},{8,9},{9,8},{10,11... | collective-permute-start | bytes 1843208 | tf_op jit(solution)/shard_map/ppermute | solution.py:10
  27.2 10.8 %collective-permute-start.5 = (bf16[800,200]{0,1:T(8,128)(2,1)S(1)}, bf16[800,200]{0,1:T(8,128)(2,1)S(1)}, u32[]{:S(2)}, u32[]{:S(2)}) collective-permute-start(bf16[800,200]{0,1:T(8,128)(2,1)S(1)} %get-tuple-element.8), channel_id=1, source_target_pairs={{0,8},{8,0},{16,24},{24,16},{1,9},{9,1},{17,25},{25,17},{2,10},{10... | collective-permute-start | bytes 960008 | tf_op jit(solution)/shard_map/ppermute | solution.py:10
  28.7 11.2 %collective-permute-start.6 = (bf16[800,200]{0,1:T(8,128)(2,1)S(1)}, bf16[800,200]{0,1:T(8,128)(2,1)S(1)}, u32[]{:S(2)}, u32[]{:S(2)}) collective-permute-start(bf16[800,200]{0,1:T(8,128)(2,1)S(1)} %get-tuple-element.8), channel_id=1, source_target_pairs={{0,16},{8,24},{16,0},{24,8},{1,17},{9,25},{17,1},{25,9},{2,18},{10... | collective-permute-start | bytes 960008 | tf_op jit(solution)/shard_map/ppermute | solution.py:10
  33.6 23.4 %collective-permute-start.4 = (f32[768,200]{0,1:T(8,128)S(1)}, f32[768,200]{0,1:T(8,128)S(1)}, u32[]{:S(2)}, u32[]{:S(2)}) collective-permute-start(f32[768,200]{0,1:T(8,128)S(1)} %fusion.1), channel_id=1, source_target_pairs={{0,16},{8,24},{16,0},{24,8},{1,17},{9,25},{17,1},{25,9},{2,18},{10... | collective-permute-start | bytes 1843208 | tf_op jit(solution)/shard_map/ppermute | solution.py:10
  40.0 8.9 %collective-permute-start.7 = (bf16[800,200]{0,1:T(8,128)(2,1)S(1)}, bf16[800,200]{0,1:T(8,128)(2,1)S(1)}, u32[]{:S(2)}, u32[]{:S(2)}) collective-permute-start(bf16[800,200]{0,1:T(8,128)(2,1)S(1)} %collective-permute-done.6), channel_id=1, source_target_pairs={{0,8},{8,0},{16,24},{24,16},{1,9},{9,1},{17,25},{25,17},{2,10},{10... | collective-permute-start | bytes 960008 | tf_op jit(solution)/shard_map/ppermute | solution.py:10
  50.1 3.4 %collective-permute-start.8 = (f32[768,200]{0,1:T(8,128)S(1)}, f32[768,200]{0,1:T(8,128)S(1)}, u32[]{:S(2)}, u32[]{:S(2)}) collective-permute-start(f32[768,200]{0,1:T(8,128)S(1)} %convolution_add_fusion), channel_id=1, source_target_pairs={{0,1},{1,0},{2,3},{3,2},{4,5},{5,4},{6,7},{7,6},{8,9},{9,8},{10,11... | collective-permute-start | bytes 1843208 | tf_op jit(solution)/shard_map/ppermute | solution.py:10
  54.7 16.4 %collective-permute-start.9 = (f32[768,200]{0,1:T(8,128)S(1)}, f32[768,200]{0,1:T(8,128)}, u32[]{:S(2)}, u32[]{:S(2)}) collective-permute-start(f32[768,200]{0,1:T(8,128)S(1)} %fusion), channel_id=1, source_target_pairs={{0,16},{8,24},{16,0},{24,8},{1,17},{9,25},{17,1},{25,9},{2,18},{10... | collective-permute-start | bytes 1843208 | tf_op jit(solution)/shard_map/ppermute | solution.py:10

commit v11 on v10

--- a/solution.py
+++ b/solution.py
@@ -56,10 +56,17 @@
     groups = gather_prow(integrals, prow_idx, prow_count, via_x, hold)
     block_rows = amplitudes.shape[0] // cuts_count
     sent = []
-    for s in range(1, cuts_count):
-        other = jnp.bitwise_xor(cuts_idx, s)
-        sent.append((s, contract(amplitudes, groups, other * block_rows, block_rows, labels, irrep_cols)))
-    kept = contract(amplitudes, groups, cuts_idx * block_rows, block_rows, labels, irrep_cols)
+    if via_x:
+        terms = contract(amplitudes, groups, 0, amplitudes.shape[0], labels, irrep_cols)
+        for s in range(1, cuts_count):
+            other = jnp.bitwise_xor(cuts_idx, s)
+            sent.append((s, lax.dynamic_slice_in_dim(terms, other * block_rows, block_rows)))
+        kept = lax.dynamic_slice_in_dim(terms, cuts_idx * block_rows, block_rows)
+    else:
+        for s in range(1, cuts_count):
+            other = jnp.bitwise_xor(cuts_idx, s)
+            sent.append((s, contract(amplitudes, groups, other * block_rows, block_rows, labels, irrep_cols)))
+        kept = contract(amplitudes, groups, cuts_idx * block_rows, block_rows, labels, irrep_cols)
     pieces = pieces if block_rows % (8 * pieces) == 0 else 1
     step = block_rows // pieces
     half = prow_count // 2

time: 76.4 us -> 87.3 us (1.14)
  waiting for transfers between devices: 28.4 us -> 36.5 us
  starting transfers between devices: 12.1 us -> 13.1 us
    ppermute x10, waiting for transfers between devices: 28.4 us -> 36.5 us  [swap(): lax.ppermute(value, axis, [(i, i ^ mask) for i in range(lax.axis_size(axi...]
    ppermute x10, starting transfers between devices: 12.1 us -> 13.1 us  [swap(): lax.ppermute(value, axis, [(i, i ^ mask) for i in range(lax.axis_size(axi...]
    dot_general x16 -> x8, matrix products: 25.6 us -> 26.2 us  [contract(): product = jnp.dot(window, blocked, preferred_element_type=jnp.float32)]
  transfers between devices with their start and end apart: 10 -> 10, of which waited for: 6 -> 7; matrix products, arithmetic and copies ran while one was open for 35% -> 27% of each run, Pallas kernels for 0% -> 0%
where the time goes in v11:
time: 87.3 us; the launch traced here: 86.8 us
  waiting for transfers between devices  36.5 us (42%)
  matrix products  26.2 us (30%)
  starting transfers between devices  13.1 us (15%)
  local copies, waits for them, and re-layouts  8.53 us (10%)
  other arithmetic  2.25 us (3%)
    ppermute x10, waiting for transfers between devices, swap(): lax.ppermute(value, axis, [(i, i ^ mask) for i in range(lax.axis_size(axi...  36.5 us
    dot_general x8, matrix products, contract(): product = jnp.dot(window, blocked, preferred_element_type=jnp.float32)  26.2 us
    ppermute x10, starting transfers between devices, swap(): lax.ppermute(value, axis, [(i, i ^ mask) for i in range(lax.axis_size(axi...  13.1 us
    gather x4, local copies, waits for them, and re-layouts, antisym(): jnp.take(fetched, local, axis=0, mode='clip')  4.72 us
    slice x1, local copies, waits for them, and re-layouts, shards(): integrals[:, j * step:(j + 1) * step]  1.95 us
  transfers between devices with their start and end apart: 10, of which 7 were waited for; matrix products, arithmetic and copies ran while one was open for 27% of the time, Pallas kernels for 0%

profile of v11, /device:TPU:0, one launch (start us, length us, event | category | flops | bytes accessed | tf_op | source)
XLA Modules:
  0.0 86.8 jit_solution(2321211635445112192)
XLA Ops:
  0.0 2.0 %fusion.51 = (bf16[800,200]{0,1:T(8,128)(2,1)}, bf16[800,200]{0,1:T(8,128)(2,1)S(1)}) fusion(bf16[800,400]{0,1:T(8,128)(2,1)} %param.6), kind=kLoop, calls=%fused_computation.74 | loop fusion | bytes 1280000 | tf_op jit(solution)/shard_map/slice | solution.py:106
  2.0 3.0 %collective-permute-start = (bf16[800,200]{0,1:T(8,128)(2,1)}, bf16[800,200]{0,1:T(8,128)(2,1)S(1)}, u32[]{:S(2)}, u32[]{:S(2)}) collective-permute-start(bf16[800,200]{0,1:T(8,128)(2,1)} %get-tuple-element.11), channel_id=1, source_target_pairs={{0,16},{8,24},{16,0},{24,8},{1,17},{9,25},{17,1},{25,9},{2,18},{10... | collective-permute-start | bytes 960008 | tf_op jit(solution)/shard_map/ppermute | solution.py:10
  4.9 1.5 %collective-permute-start.1 = (bf16[800,200]{0,1:T(8,128)(2,1)}, bf16[800,200]{0,1:T(8,128)(2,1)S(1)}, u32[]{:S(2)}, u32[]{:S(2)}) collective-permute-start(bf16[800,200]{0,1:T(8,128)(2,1)} %get-tuple-element.11), channel_id=1, source_target_pairs={{0,8},{8,0},{16,24},{24,16},{1,9},{9,1},{17,25},{25,17},{2,10},{10... | collective-permute-start | bytes 960008 | tf_op jit(solution)/shard_map/ppermute | solution.py:10
  6.6 3.3 %fusion.8 = f32[1536,200]{0,1:T(8,128)S(1)} fusion(bf16[1536,3200]{1,0:T(8,128)(2,1)} %param.5, s32[]{:T(128)S(6)} %select_n.73, s32[800]{0:T(1024)S(1)} %get-tuple-element.15, s32[200]{0:T(256)S(1)} %get-tuple-element.18, bf16[800,400]{0,1:T(8,128)(2,1)S(1)} %copy-done), kind=kOutput, calls=%fused_computation.16 | convolution fusion | flops 491840000 | bytes 4344836 | tf_op jit(solution)/shard_map/dot_general | solution.py:44
  9.9 3.6 %collective-permute-done = bf16[800,200]{0,1:T(8,128)(2,1)S(1)} collective-permute-done((bf16[800,200]{0,1:T(8,128)(2,1)}, bf16[800,200]{0,1:T(8,128)(2,1)S(1)}, u32[]{:S(2)}, u32[]{:S(2)}) %collective-permute-start) | collective-permute-done | bytes 320032 | tf_op jit(solution)/shard_map/ppermute | solution.py:10
  13.5 1.7 %collective-permute-start.2 = (bf16[800,200]{0,1:T(8,128)(2,1)S(1)}, bf16[800,200]{0,1:T(8,128)(2,1)S(1)}, u32[]{:S(2)}, u32[]{:S(2)}) collective-permute-start(bf16[800,200]{0,1:T(8,128)(2,1)S(1)} %collective-permute-done), channel_id=1, source_target_pairs={{0,8},{8,0},{16,24},{24,16},{1,9},{9,1},{17,25},{25,17},{2,10},{10... | collective-permute-start | bytes 960008 | tf_op jit(solution)/shard_map/ppermute | solution.py:10
  15.2 3.3 %convolution_add_fusion.5 = f32[1536,200]{0,1:T(8,128)S(1)} fusion(f32[1536,200]{0,1:T(8,128)S(1)} %fusion.8, bf16[1536,3200]{1,0:T(8,128)(2,1)} %param.5, s32[]{:T(128)S(6)} %select_n.78, bf16[800,200]{0,1:T(8,128)(2,1)S(1)} %collective-permute-done, s32[800]{0:T(1024)S(1)} %get-tuple-element.14, s32[200]{0:T(256)S(1)} %get-tuple-element.18), kind=kOutput, calls=%fused_computation.7 | convolution fusion | flops 492147200 | bytes 5534116 | tf_op jit(solution)/shard_map/dot_general | solution.py:44
  18.5 3.3 %convolution_add_fusion.4 = f32[1536,200]{0,1:T(8,128)S(1)} fusion(f32[1536,200]{0,1:T(8,128)S(1)} %convolution_add_fusion.5, bf16[1536,3200]{1,0:T(8,128)(2,1)} %param.5, s32[]{:T(128)S(6)} %select_n.81, bf16[800,200]{0,1:T(8,128)(2,1)S(1)} %collective-permute-done.1, s32[800]{0:T(1024)S(1)} %get-tuple-element.16, s32[200]{0:T(256)S(1)} %get-tuple-element.18), kind=kOutput, calls=%fused_computation.6 | convolution fusion | flops 492147200 | bytes 5534116 | tf_op jit(solution)/shard_map/dot_general | solution.py:44
  21.8 1.2 %collective-permute-done.2 = bf16[800,200]{0,1:T(8,128)(2,1)S(1)} collective-permute-done((bf16[800,200]{0,1:T(8,128)(2,1)S(1)}, bf16[800,200]{0,1:T(8,128)(2,1)S(1)}, u32[]{:S(2)}, u32[]{:S(2)}) %collective-permute-start.2) | collective-permute-done | bytes 320032 | tf_op jit(solution)/shard_map/ppermute | solution.py:10
  23.1 3.2 %convolution_add_fusion.3 = f32[1536,200]{0,1:T(8,128)S(1)} fusion(f32[1536,200]{0,1:T(8,128)S(1)} %convolution_add_fusion.4, bf16[1536,3200]{1,0:T(8,128)(2,1)} %param.5, s32[]{:T(128)S(6)} %select_n.84, bf16[800,200]{0,1:T(8,128)(2,1)S(1)} %collective-permute-done.2, s32[800]{0:T(1024)S(1)} %get-tuple-element.13, s32[200]{0:T(256)S(1)} %get-tuple-element.18), kind=kOutput, calls=%fused_computation.5 | convolution fusion | flops 492147200 | bytes 5534116 | tf_op jit(solution)/shard_map/dot_general | solution.py:44
  26.4 1.6 %collective-permute-start.5 = (bf16[800,200]{0,1:T(8,128)(2,1)S(1)}, bf16[800,200]{0,1:T(8,128)(2,1)S(1)}, u32[]{:S(2)}, u32[]{:S(2)}) collective-permute-start(bf16[800,200]{0,1:T(8,128)(2,1)S(1)} %get-tuple-element.8), channel_id=1, source_target_pairs={{0,8},{8,0},{16,24},{24,16},{1,9},{9,1},{17,25},{25,17},{2,10},{10... | collective-permute-start | bytes 960008 | tf_op jit(solution)/shard_map/ppermute | solution.py:10
  28.0 1.5 %collective-permute-start.6 = (bf16[800,200]{0,1:T(8,128)(2,1)S(1)}, bf16[800,200]{0,1:T(8,128)(2,1)}, u32[]{:S(2)}, u32[]{:S(2)}) collective-permute-start(bf16[800,200]{0,1:T(8,128)(2,1)S(1)} %get-tuple-element.8), channel_id=1, source_target_pairs={{0,16},{8,24},{16,0},{24,8},{1,17},{9,25},{17,1},{25,9},{2,18},{10... | collective-permute-start | bytes 960008 | tf_op jit(solution)/shard_map/ppermute | solution.py:10
  29.6 7.6 %collective-permute-done.5 = bf16[800,200]{0,1:T(8,128)(2,1)S(1)} collective-permute-done((bf16[800,200]{0,1:T(8,128)(2,1)S(1)}, bf16[800,200]{0,1:T(8,128)(2,1)S(1)}, u32[]{:S(2)}, u32[]{:S(2)}) %collective-permute-start.5) | collective-permute-done | bytes 320032 | tf_op jit(solution)/shard_map/ppermute | solution.py:10
  37.2 1.3 %collective-permute-done.6 = bf16[800,200]{0,1:T(8,128)(2,1)} collective-permute-done((bf16[800,200]{0,1:T(8,128)(2,1)S(1)}, bf16[800,200]{0,1:T(8,128)(2,1)}, u32[]{:S(2)}, u32[]{:S(2)}) %collective-permute-start.6) | collective-permute-done | bytes 320032 | tf_op jit(solution)/shard_map/ppermute | solution.py:10
  38.5 0.5 collective-permute-start.7
  39.0 3.3 %fusion.4 = f32[1536,200]{0,1:T(8,128)S(1)} fusion(bf16[1536,3200]{1,0:T(8,128)(2,1)} %param.5, s32[]{:T(128)S(6)} %select_n.78, bf16[800,200]{0,1:T(8,128)(2,1)} %collective-permute-done.6, s32[800]{0:T(1024)S(1)} %get-tuple-element.14, s32[200]{0:T(256)S(1)} %get-tuple-element.17), kind=kOutput, calls=%fused_computation.12 | convolution fusion | flops 491840000 | bytes 4343716 | tf_op jit(solution)/shard_map/dot_general | solution.py:44
  42.3 3.3 %convolution_add_fusion.2 = f32[1536,200]{0,1:T(8,128)S(1)} fusion(f32[1536,200]{0,1:T(8,128)S(1)} %fusion.4, bf16[1536,3200]{1,0:T(8,128)(2,1)} %param.5, s32[]{:T(128)S(6)} %select_n.73, bf16[800,200]{0,1:T(8,128)(2,1)S(1)} %get-tuple-element.8, s32[800]{0:T(1024)S(1)} %get-tuple-element.15, s32[200]{0:T(256)S(1)} %get-tuple-element.17), kind=kOutput, calls=%fused_computation.4 | convolution fusion | flops 492147200 | bytes 5534116 | tf_op jit(solution)/shard_map/dot_general | solution.py:44
  45.7 3.3 %convolution_add_fusion.1 = f32[1536,200]{0,1:T(8,128)S(1)} fusion(f32[1536,200]{0,1:T(8,128)S(1)} %convolution_add_fusion.2, bf16[1536,3200]{1,0:T(8,128)(2,1)} %param.5, s32[]{:T(128)S(6)} %select_n.81, bf16[800,200]{0,1:T(8,128)(2,1)S(1)} %collective-permute-done.5, s32[800]{0:T(1024)S(1)} %get-tuple-element.16, s32[200]{0:T(256)S(1)} %get-tuple-element.17), kind=kOutput, calls=%fused_computation.3 | convolution fusion | flops 492147200 | bytes 5534116 | tf_op jit(solution)/shard_map/dot_general | solution.py:44
  49.0 3.2 %convolution_add_fusion = f32[1536,200]{0,1:T(8,128)S(1)} fusion(f32[1536,200]{0,1:T(8,128)S(1)} %convolution_add_fusion.1, bf16[1536,3200]{1,0:T(8,128)(2,1)} %param.5, s32[]{:T(128)S(6)} %select_n.84, bf16[800,200]{0,1:T(8,128)(2,1)S(1)} %collective-permute-done.7, s32[800]{0:T(1024)S(1)} %get-tuple-element.13, s32[200]{0:T(256)S(1)} %get-tuple-element.17), kind=kOutput, calls=%fused_computation.2 | convolution fusion | flops 492147200 | bytes 5534116 | tf_op jit(solution)/shard_map/dot_general | solution.py:44
  52.4 1.6 %collective-permute-start.4 = (f32[768,200]{0,1:T(8,128)S(1)}, f32[768,200]{0,1:T(8,128)S(1)}, u32[]{:S(2)}, u32[]{:S(2)}) collective-permute-start(f32[768,200]{0,1:T(8,128)S(1)} %dynamic-slice_add_fusion.1), channel_id=1, source_target_pairs={{0,16},{8,24},{16,0},{24,8},{1,17},{9,25},{17,1},{25,9},{2,18},{10... | collective-permute-start | bytes 1843208 | tf_op jit(solution)/shard_map/ppermute | solution.py:10
  54.0 0.4 collective-permute-done.8
  54.5 1.6 %collective-permute-start.9 = (f32[768,200]{0,1:T(8,128)S(1)}, f32[768,200]{0,1:T(8,128)}, u32[]{:S(2)}, u32[]{:S(2)}) collective-permute-start(f32[768,200]{0,1:T(8,128)S(1)} %dynamic-slice_add_fusion), channel_id=1, source_target_pairs={{0,16},{8,24},{16,0},{24,8},{1,17},{9,25},{17,1},{25,9},{2,18},{10... | collective-permute-start | bytes 1843208 | tf_op jit(solution)/shard_map/ppermute | solution.py:10
  56.1 0.8 dynamic-slice_subtract_fusion
  56.9 12.2 %collective-permute-done.4 = f32[768,200]{0,1:T(8,128)S(1)} collective-permute-done((f32[768,200]{0,1:T(8,128)S(1)}, f32[768,200]{0,1:T(8,128)S(1)}, u32[]{:S(2)}, u32[]{:S(2)}) %collective-permute-start.4) | collective-permute-done | bytes 614432 | tf_op jit(solution)/shard_map/ppermute | solution.py:10
  69.1 0.3 copy.6
  69.4 2.1 %gather_fusion = f32[768,200]{1,0:T(8,128)S(1)} fusion(f32[768,200]{1,0:T(8,128)S(1)} %copy.6, s32[1024]{0:T(1024)S(1)} %pad_clamp_fusion), kind=kCustom, calls=%fused_computation | custom fusion | bytes 1231872 | tf_op jit(solution)/shard_map/jit(_take)/gather | solution.py:83
  71.5 0.2 copy.7
  71.8 10.1 %collective-permute-done.9 = f32[768,200]{0,1:T(8,128)} collective-permute-done((f32[768,200]{0,1:T(8,128)S(1)}, f32[768,200]{0,1:T(8,128)}, u32[]{:S(2)}, u32[]{:S(2)}) %collective-permute-start.9) | collective-permute-done | bytes 614432 | tf_op jit(solution)/shard_map/ppermute | solution.py:10
  81.9 1.3 %copy.8 = f32[768,200]{1,0:T(8,128)S(1)} copy(f32[768,200]{0,1:T(8,128)} %collective-permute-done.9) | data formatting | bytes 1228800 | tf_op jit(solution)/shard_map/ppermute | solution.py:10
  83.2 2.1 %gather_fusion.1 = f32[768,200]{1,0:T(8,128)S(1)} fusion(f32[768,200]{1,0:T(8,128)S(1)} %copy.8, s32[1024]{0:T(1024)S(1)} %pad_clamp_fusion), kind=kCustom, calls=%fused_computation.1 | custom fusion | bytes 1231872 | tf_op jit(solution)/shard_map/jit(_take)/gather | solution.py:83
  85.4 0.2 copy.9
  85.7 1.1 %pad_maximum_fusion = f32[768,400]{0,1:T(8,128)} fusion(f32[768,200]{0,1:T(8,128)S(1)} %sub.15, f32[768,200]{0,1:T(8,128)S(1)} %sub.14), kind=kLoop, calls=%fused_computation.18 | loop fusion | flops 307200 | bytes 2457600 | tf_op jit(solution)/shard_map/concatenate | solution.py:110
  (20 shorter events, 0.8 us)
Async XLA Ops:
  0.0 6.6 %copy-start = (bf16[800,400]{0,1:T(8,128)(2,1)S(1)}, bf16[800,400]{0,1:T(8,128)(2,1)}, u32[]{:S(2)}) copy-start(bf16[800,400]{0,1:T(8,128)(2,1)} %param.6) | copy-start | bytes 1920004
  0.0 6.4 %copy-start.2 = (s32[400]{0:T(512)S(1)}, s32[400]{0:T(512)}, u32[]{:S(2)}) copy-start(s32[400]{0:T(512)} %param.8) | copy-start | bytes 4804
  0.0 6.5 %copy-start.1 = (s32[6400]{0:T(1024)S(1)}, s32[6400]{0:T(1024)}, u32[]{:S(2)}) copy-start(s32[6400]{0:T(1024)} %param.7) | copy-start | bytes 76804
  2.0 11.5 %collective-permute-start = (bf16[800,200]{0,1:T(8,128)(2,1)}, bf16[800,200]{0,1:T(8,128)(2,1)S(1)}, u32[]{:S(2)}, u32[]{:S(2)}) collective-permute-start(bf16[800,200]{0,1:T(8,128)(2,1)} %get-tuple-element.11), channel_id=1, source_target_pairs={{0,16},{8,24},{16,0},{24,8},{1,17},{9,25},{17,1},{25,9},{2,18},{10... | collective-permute-start | bytes 960008 | tf_op jit(solution)/shard_map/ppermute | solution.py:10
  4.9 13.6 %collective-permute-start.1 = (bf16[800,200]{0,1:T(8,128)(2,1)}, bf16[800,200]{0,1:T(8,128)(2,1)S(1)}, u32[]{:S(2)}, u32[]{:S(2)}) collective-permute-start(bf16[800,200]{0,1:T(8,128)(2,1)} %get-tuple-element.11), channel_id=1, source_target_pairs={{0,8},{8,0},{16,24},{24,16},{1,9},{9,1},{17,25},{25,17},{2,10},{10... | collective-permute-start | bytes 960008 | tf_op jit(solution)/shard_map/ppermute | solution.py:10
  13.5 9.6 %collective-permute-start.2 = (bf16[800,200]{0,1:T(8,128)(2,1)S(1)}, bf16[800,200]{0,1:T(8,128)(2,1)S(1)}, u32[]{:S(2)}, u32[]{:S(2)}) collective-permute-start(bf16[800,200]{0,1:T(8,128)(2,1)S(1)} %collective-permute-done), channel_id=1, source_target_pairs={{0,8},{8,0},{16,24},{24,16},{1,9},{9,1},{17,25},{25,17},{2,10},{10... | collective-permute-start | bytes 960008 | tf_op jit(solution)/shard_map/ppermute | solution.py:10
  26.3 3.2 %collective-permute-start.3 = (f32[768,200]{0,1:T(8,128)S(1)}, f32[768,200]{0,1:T(8,128)S(1)}, u32[]{:S(2)}, u32[]{:S(2)}) collective-permute-start(f32[768,200]{0,1:T(8,128)S(1)} %constant_dynamic-slice_fusion.1), channel_id=1, source_target_pairs={{0,1},{1,0},{2,3},{3,2},{4,5},{5,4},{6,7},{7,6},{8,9},{9,8},{10,11... | collective-permute-start | bytes 1843208 | tf_op jit(solution)/shard_map/ppermute | solution.py:10
  26.4 10.8 %collective-permute-start.5 = (bf16[800,200]{0,1:T(8,128)(2,1)S(1)}, bf16[800,200]{0,1:T(8,128)(2,1)S(1)}, u32[]{:S(2)}, u32[]{:S(2)}) collective-permute-start(bf16[800,200]{0,1:T(8,128)(2,1)S(1)} %get-tuple-element.8), channel_id=1, source_target_pairs={{0,8},{8,0},{16,24},{24,16},{1,9},{9,1},{17,25},{25,17},{2,10},{10... | collective-permute-start | bytes 960008 | tf_op jit(solution)/shard_map/ppermute | solution.py:10
  28.0 10.5 %collective-permute-start.6 = (bf16[800,200]{0,1:T(8,128)(2,1)S(1)}, bf16[800,200]{0,1:T(8,128)(2,1)}, u32[]{:S(2)}, u32[]{:S(2)}) collective-permute-start(bf16[800,200]{0,1:T(8,128)(2,1)S(1)} %get-tuple-element.8), channel_id=1, source_target_pairs={{0,16},{8,24},{16,0},{24,8},{1,17},{9,25},{17,1},{25,9},{2,18},{10... | collective-permute-start | bytes 960008 | tf_op jit(solution)/shard_map/ppermute | solution.py:10
  38.5 10.5 %collective-permute-start.7 = (bf16[800,200]{0,1:T(8,128)(2,1)}, bf16[800,200]{0,1:T(8,128)(2,1)S(1)}, u32[]{:S(2)}, u32[]{:S(2)}) collective-permute-start(bf16[800,200]{0,1:T(8,128)(2,1)} %collective-permute-done.6), channel_id=1, source_target_pairs={{0,8},{8,0},{16,24},{24,16},{1,9},{9,1},{17,25},{25,17},{2,10},{10... | collective-permute-start | bytes 960008 | tf_op jit(solution)/shard_map/ppermute | solution.py:10
  52.3 2.1 %collective-permute-start.8 = (f32[768,200]{0,1:T(8,128)S(1)}, f32[768,200]{0,1:T(8,128)S(1)}, u32[]{:S(2)}, u32[]{:S(2)}) collective-permute-start(f32[768,200]{0,1:T(8,128)S(1)} %constant_dynamic-slice_fusion), channel_id=1, source_target_pairs={{0,1},{1,0},{2,3},{3,2},{4,5},{5,4},{6,7},{7,6},{8,9},{9,8},{10,11... | collective-permute-start | bytes 1843208 | tf_op jit(solution)/shard_map/ppermute | solution.py:10
  52.4 16.7 %collective-permute-start.4 = (f32[768,200]{0,1:T(8,128)S(1)}, f32[768,200]{0,1:T(8,128)S(1)}, u32[]{:S(2)}, u32[]{:S(2)}) collective-permute-start(f32[768,200]{0,1:T(8,128)S(1)} %dynamic-slice_add_fusion.1), channel_id=1, source_target_pairs={{0,16},{8,24},{16,0},{24,8},{1,17},{9,25},{17,1},{25,9},{2,18},{10... | collective-permute-start | bytes 1843208 | tf_op jit(solution)/shard_map/ppermute | solution.py:10
  54.5 27.4 %collective-permute-start.9 = (f32[768,200]{0,1:T(8,128)S(1)}, f32[768,200]{0,1:T(8,128)}, u32[]{:S(2)}, u32[]{:S(2)}) collective-permute-start(f32[768,200]{0,1:T(8,128)S(1)} %dynamic-slice_add_fusion), channel_id=1, source_target_pairs={{0,16},{8,24},{16,0},{24,8},{1,17},{9,25},{17,1},{25,9},{2,18},{10... | collective-permute-start | bytes 1843208 | tf_op jit(solution)/shard_map/ppermute | solution.py:10

commit v12 on v8

--- a/solution.py
+++ b/solution.py
@@ -18,9 +18,9 @@
         from_y = swap(own, "prow", 2)
         diag_a = swap(from_y[:half], "prow", 1)
         diag_b = swap(from_x[half:], "prow", 2)
-        base = jnp.bitwise_xor(prow_idx, 3) * count
+        diag = jnp.concatenate([diag_a, diag_b], axis=0)
         return [[(own, prow_idx * count)], [(from_y, jnp.bitwise_xor(prow_idx, 2) * count)],
-                [(from_x, jnp.bitwise_xor(prow_idx, 1) * count)], [(diag_a, base), (diag_b, base + half)]]
+                [(from_x, jnp.bitwise_xor(prow_idx, 1) * count)], [(diag, jnp.bitwise_xor(prow_idx, 3) * count)]]
     groups = [[(own, prow_idx * count)]]
     for s in range(1, prow_count):
         groups.append([(swap(own, "prow", s), jnp.bitwise_xor(prow_idx, s) * count)])
@@ -71,7 +71,7 @@
     partner_block = jnp.bitwise_xor(prow_idx, half) * cuts_count + cuts_idx
     mine = lax.dynamic_slice(mirror_row, (own_block * block_rows,), (block_rows,))
     local = mine - partner_block * block_rows
-    return cycle - jnp.take(fetched, local, axis=0, mode="clip")
+    return cycle - fetched.at[local].get(mode="promise_in_bounds")
 
 
 def solution(mesh):

time: 73.5 us -> 74.7 us (1.016)
  waiting for transfers between devices: 38.4 us -> 41.8 us
  matrix products: 14.5 us -> 13.4 us
  local copies, waits for them, and re-layouts: 5.1 us -> 4.26 us
    ppermute x8, waiting for transfers between devices: 38.4 us -> 41.8 us  [swap(): lax.ppermute(value, axis, [(i, i ^ mask) for i in range(lax.axis_size(axi...]
    dot_general x10 -> x8, matrix products: 14.5 us -> 13.4 us  [contract(): product = jnp.dot(window, blocked, preferred_element_type=jnp.float32)]
    dynamic_slice x2 -> x1, local copies, waits for them, and re-layouts: 1.73 us -> 0.89 us  [contract(): lax.dynamic_slice_in_dim(labels, o, b.shape[0])[:, None]]
    select_n x0 -> x1, other arithmetic: none -> 0.77 us  [shards(): return cycle - fetched.at[local].get(mode='promise_in_bounds')]
    sub x2 -> x1, other arithmetic: 3.2 us -> 2.43 us  [shards(): return cycle - fetched.at[local].get(mode='promise_in_bounds')]
  transfers between devices with their start and end apart: 8 -> 8, of which waited for: 5 -> 5; matrix products, arithmetic and copies ran while one was open for 21% -> 17% of each run, Pallas kernels for 0% -> 0%
where the time goes in v12:
time: 74.7 us; the launch traced here: 74.4 us
  waiting for transfers between devices  41.8 us (56%)
  matrix products  13.4 us (18%)
  starting transfers between devices  10.4 us (14%)
  other arithmetic  4.49 us (6%)
  local copies, waits for them, and re-layouts  4.26 us (6%)
    ppermute x8, waiting for transfers between devices, swap(): lax.ppermute(value, axis, [(i, i ^ mask) for i in range(lax.axis_size(axi...  41.8 us
    dot_general x8, matrix products, contract(): product = jnp.dot(window, blocked, preferred_element_type=jnp.float32)  13.4 us
    ppermute x8, starting transfers between devices, swap(): lax.ppermute(value, axis, [(i, i ^ mask) for i in range(lax.axis_size(axi...  10.4 us
    gather x2, local copies, waits for them, and re-layouts, shards(): return cycle - fetched.at[local].get(mode='promise_in_bounds')  2.59 us
    sub x1, other arithmetic, shards(): return cycle - fetched.at[local].get(mode='promise_in_bounds')  2.43 us
  transfers between devices with their start and end apart: 8, of which 5 were waited for; matrix products, arithmetic and copies ran while one was open for 17% of the time, Pallas kernels for 0%

profile of v12, /device:TPU:0, one launch (start us, length us, event | category | flops | bytes accessed | tf_op | source)
XLA Modules:
  0.0 74.4 jit_solution(14056956661675093705)
XLA Ops:
  0.0 3.0 %collective-permute-start = (bf16[800,400]{0,1:T(8,128)(2,1)}, bf16[800,400]{0,1:T(8,128)(2,1)S(1)}, u32[]{:S(2)}, u32[]{:S(2)}) collective-permute-start(bf16[800,400]{0,1:T(8,128)(2,1)} %param.6), channel_id=1, source_target_pairs={{0,16},{8,24},{16,0},{24,8},{1,17},{9,25},{17,1},{25,9},{2,18},{10... | collective-permute-start | bytes 1920008 | tf_op jit(solution)/shard_map/ppermute | solution.py:10
  3.0 1.5 %collective-permute-start.1 = (bf16[800,400]{0,1:T(8,128)(2,1)}, bf16[800,400]{0,1:T(8,128)(2,1)S(1)}, u32[]{:S(2)}, u32[]{:S(2)}) collective-permute-start(bf16[800,400]{0,1:T(8,128)(2,1)} %param.6), channel_id=1, source_target_pairs={{0,8},{8,0},{16,24},{24,16},{1,9},{9,1},{17,25},{25,17},{2,10},{10... | collective-permute-start | bytes 1920008 | tf_op jit(solution)/shard_map/ppermute | solution.py:10
  4.5 0.9 %fusion.21 = (s32[800]{0:T(1024)S(1)}, s32[800]{0:T(1024)S(1)}, s32[800]{0:T(1024)S(1)}, s32[800]{0:T(1024)S(1)}) fusion(s32[6400]{0:T(1024)} %param.7, s32[]{:T(128)S(6)} %dynamic_slice.61, s32[]{:T(128)S(6)} %dynamic_slice.58, s32[]{:T(128)S(6)} %dynamic_slice.55, s32[]{:T(128)S(6)} %dynamic_slice.64), kind=kLoop, calls=%fused_computation.36 | loop fusion | bytes 25616 | tf_op jit(solution)/shard_map/dynamic_slice | solution.py:36
  5.4 3.0 %fusion.12 = f32[768,400]{0,1:T(8,128)S(1)} fusion(bf16[1536,3200]{1,0:T(8,128)(2,1)} %param.5, s32[]{:T(128)S(6)} %select_n.71, s32[]{:T(128)S(6)} %select_n.73, bf16[800,400]{0,1:T(8,128)(2,1)} %param.6, s32[800]{0:T(1024)S(1)} %get-tuple-element.11, s32[400]{0:T(512)} %param.8), kind=kOutput, calls=%fused_computation.21 | convolution fusion | flops 492160000 | bytes 3327112 | tf_op jit(solution)/shard_map/dot_general | solution.py:38
  8.3 10.9 %collective-permute-done = bf16[800,400]{0,1:T(8,128)(2,1)S(1)} collective-permute-done((bf16[800,400]{0,1:T(8,128)(2,1)}, bf16[800,400]{0,1:T(8,128)(2,1)S(1)}, u32[]{:S(2)}, u32[]{:S(2)}) %collective-permute-start) | collective-permute-done | bytes 640032 | tf_op jit(solution)/shard_map/ppermute | solution.py:10
  19.3 1.8 %collective-permute-start.2 = (bf16[400,400]{0,1:T(8,128)(2,1)S(1)}, bf16[400,400]{0,1:T(8,128)(2,1)S(1)}, u32[]{:S(2)}, u32[]{:S(2)}) collective-permute-start(bf16[400,400]{0,1:T(8,128)(2,1)S(1)} %slice.26), channel_id=1, source_target_pairs={{0,8},{8,0},{16,24},{24,16},{1,9},{9,1},{17,25},{25,17},{2,10},{10... | collective-permute-start | bytes 960008 | tf_op jit(solution)/shard_map/ppermute | solution.py:10
  21.0 0.0 collective-permute-done.1
  21.0 0.2 slice.27
  21.3 1.6 %collective-permute-start.3 = (bf16[400,400]{0,1:T(8,128)(2,1)S(1)}, bf16[400,400]{0,1:T(8,128)(2,1)S(1)}, u32[]{:S(2)}, u32[]{:S(2)}) collective-permute-start(bf16[400,400]{0,1:T(8,128)(2,1)S(1)} %slice.27), channel_id=1, source_target_pairs={{0,16},{8,24},{16,0},{24,8},{1,17},{9,25},{17,1},{25,9},{2,18},{10... | collective-permute-start | bytes 960008 | tf_op jit(solution)/shard_map/ppermute | solution.py:10
  22.8 2.8 %fusion.6 = f32[768,400]{0,1:T(8,128)S(1)} fusion(bf16[1536,3200]{1,0:T(8,128)(2,1)} %param.5, s32[]{:T(128)S(6)} %select_n.87, s32[]{:T(128)S(6)} %select_n.73, bf16[800,400]{0,1:T(8,128)(2,1)} %param.6, s32[800]{0:T(1024)S(1)} %get-tuple-element.11, s32[400]{0:T(512)S(1)} %copy-done.1), kind=kOutput, calls=%fused_computation.15 | convolution fusion | flops 492160000 | bytes 3326664 | tf_op jit(solution)/shard_map/dot_general | solution.py:38
  25.6 1.3 %convolution_add_fusion.1 = f32[768,400]{0,1:T(8,128)S(1)} fusion(f32[768,400]{0,1:T(8,128)S(1)} %fusion.6, bf16[1536,3200]{1,0:T(8,128)(2,1)S(1)} %copy-done, s32[]{:T(128)S(6)} %select_n.87, s32[]{:T(128)S(6)} %select_n.78, bf16[800,400]{0,1:T(8,128)(2,1)S(1)} %collective-permute-done, s32[800]{0:T(1024)S(1)} %get-tuple-element.10, s32[400]{0:T(512)S(1)} %copy-done.1), kind=kOutput, calls=%fused_computation.7 | convolution fusion | flops 492467200 | bytes 4556808 | tf_op jit(solution)/shard_map/dot_general | solution.py:38
  26.9 3.1 %collective-permute-done.2 = bf16[400,400]{0,1:T(8,128)(2,1)S(1)} collective-permute-done((bf16[400,400]{0,1:T(8,128)(2,1)S(1)}, bf16[400,400]{0,1:T(8,128)(2,1)S(1)}, u32[]{:S(2)}, u32[]{:S(2)}) %collective-permute-start.2) | collective-permute-done | bytes 320032 | tf_op jit(solution)/shard_map/ppermute | solution.py:10
  30.0 1.4 %collective-permute-done.3 = bf16[400,400]{0,1:T(8,128)(2,1)S(1)} collective-permute-done((bf16[400,400]{0,1:T(8,128)(2,1)S(1)}, bf16[400,400]{0,1:T(8,128)(2,1)S(1)}, u32[]{:S(2)}, u32[]{:S(2)}) %collective-permute-start.3) | collective-permute-done | bytes 320032 | tf_op jit(solution)/shard_map/ppermute | solution.py:10
  31.4 1.2 %fusion.2 = f32[768,400]{0,1:T(8,128)S(1)} fusion(bf16[1536,3200]{1,0:T(8,128)(2,1)S(1)} %copy-done, s32[]{:T(128)S(6)} %select_n.87, s32[]{:T(128)S(6)} %select_n.84, bf16[400,400]{0,1:T(8,128)(2,1)S(1)} %collective-permute-done.3, bf16[400,400]{0,1:T(8,128)(2,1)S(1)} %collective-permute-done.2, s32[800]{0:T(1024)S(1)} %get-tuple-element.12, ...), kind=kOutput, calls=%fused_computation.11 | convolution fusion | flops 493440000 | bytes 3430408 | tf_op jit(solution)/shard_map/dot_general | solution.py:38
  32.6 1.3 %fusion = f32[768,400]{0,1:T(8,128)S(1)} fusion(f32[768,400]{0,1:T(8,128)S(1)} %fusion.2, f32[768,400]{0,1:T(8,128)S(1)} %convolution_add_fusion.1, bf16[1536,3200]{1,0:T(8,128)(2,1)S(1)} %copy-done, s32[]{:T(128)S(6)} %select_n.87, s32[]{:T(128)S(6)} %select_n.81, bf16[800,400]{0,1:T(8,128)(2,1)S(1)} %collective-permute-done.1, ...), kind=kOutput, calls=%fused_computation.6 | convolution fusion | flops 492774400 | bytes 5785608 | tf_op jit(solution)/shard_map/dot_general | solution.py:38
  33.9 0.1 fusion.20
  34.0 0.1 collective-permute-start.4
  34.1 0.5 collective-permute-start.5
  34.6 1.3 %convolution_add_fusion.3 = f32[768,400]{0,1:T(8,128)S(1)} fusion(f32[768,400]{0,1:T(8,128)S(1)} %fusion.12, bf16[1536,3200]{1,0:T(8,128)(2,1)S(1)} %copy-done, s32[]{:T(128)S(6)} %select_n.71, s32[]{:T(128)S(6)} %select_n.78, bf16[800,400]{0,1:T(8,128)(2,1)S(1)} %collective-permute-done, s32[800]{0:T(1024)S(1)} %get-tuple-element.10, s32[400]{0:T(512)S(1)} %copy-done.1), kind=kOutput, calls=%fused_computation.10 | convolution fusion | flops 492467200 | bytes 4556808 | tf_op jit(solution)/shard_map/dot_general | solution.py:38
  35.9 1.3 %fusion.8 = f32[768,400]{0,1:T(8,128)S(1)} fusion(bf16[1536,3200]{1,0:T(8,128)(2,1)S(1)} %copy-done, s32[]{:T(128)S(6)} %select_n.71, s32[]{:T(128)S(6)} %select_n.84, bf16[400,400]{0,1:T(8,128)(2,1)S(1)} %collective-permute-done.3, bf16[400,400]{0,1:T(8,128)(2,1)S(1)} %collective-permute-done.2, s32[800]{0:T(1024)S(1)} %get-tuple-element.12, ...), kind=kOutput, calls=%fused_computation.17 | convolution fusion | flops 493440000 | bytes 3430408 | tf_op jit(solution)/shard_map/dot_general | solution.py:38
  37.1 1.3 %fusion.1 = f32[768,400]{0,1:T(8,128)S(1)} fusion(f32[768,400]{0,1:T(8,128)S(1)} %fusion.8, f32[768,400]{0,1:T(8,128)S(1)} %convolution_add_fusion.3, bf16[1536,3200]{1,0:T(8,128)(2,1)S(1)} %copy-done, s32[]{:T(128)S(6)} %select_n.71, s32[]{:T(128)S(6)} %select_n.81, bf16[800,400]{0,1:T(8,128)(2,1)S(1)} %collective-permute-done.1, ...), kind=kOutput, calls=%fused_computation.9 | convolution fusion | flops 492774400 | bytes 5785608 | tf_op jit(solution)/shard_map/dot_general | solution.py:38
  38.4 1.2 %slice_add_fusion.1 = (f32[384,400]{0,1:T(8,128)}, f32[384,400]{0,1:T(8,128)}) fusion(f32[384,400]{0,1:T(8,128)S(1)} %collective-permute-done.4, f32[768,400]{0,1:T(8,128)S(1)} %fusion.1, f32[384,400]{0,1:T(8,128)S(1)} %collective-permute-done.5), kind=kLoop, calls=%fused_computation.26 | loop fusion | flops 307200 | bytes 3686400 | tf_op jit(solution)/shard_map/add | solution.py:65
  39.6 1.6 %collective-permute-start.6 = (f32[384,400]{0,1:T(8,128)}, f32[384,400]{0,1:T(8,128)S(1)}, u32[]{:S(2)}, u32[]{:S(2)}) collective-permute-start(f32[384,400]{0,1:T(8,128)} %get-tuple-element.5), channel_id=1, source_target_pairs={{0,16},{8,24},{16,0},{24,8},{1,17},{9,25},{17,1},{25,9},{2,18},{10... | collective-permute-start | bytes 1843208 | tf_op jit(solution)/shard_map/ppermute | solution.py:10
  41.2 0.5 collective-permute-start.7
  41.6 0.8 %compare_select_fusion.10 = s32[768]{0:T(1024)S(1)} fusion(s32[6144]{0:T(1024)} %param.9, s32[]{:T(128)S(6)} %select_n.88, s32[]{:T(128)S(6)} %mul.43), kind=kLoop, calls=%fused_computation.27 | loop fusion | flops 3072 | bytes 6152 | tf_op jit(solution)/shard_map/select_n | solution.py:74
  42.4 14.1 %collective-permute-done.6 = f32[384,400]{0,1:T(8,128)S(1)} collective-permute-done((f32[384,400]{0,1:T(8,128)}, f32[384,400]{0,1:T(8,128)S(1)}, u32[]{:S(2)}, u32[]{:S(2)}) %collective-permute-start.6) | collective-permute-done | bytes 614432 | tf_op jit(solution)/shard_map/ppermute | solution.py:10
  56.5 12.3 %collective-permute-done.7 = f32[384,400]{0,1:T(8,128)S(1)} collective-permute-done((f32[384,400]{0,1:T(8,128)}, f32[384,400]{0,1:T(8,128)S(1)}, u32[]{:S(2)}, u32[]{:S(2)}) %collective-permute-start.7) | collective-permute-done | bytes 614432 | tf_op jit(solution)/shard_map/ppermute | solution.py:10
  68.8 0.1 pad_maximum_fusion
  68.9 0.5 copy.6
  69.4 2.2 %gather_fusion = f32[768,400]{1,0:T(8,128)S(1)} fusion(f32[768,400]{1,0:T(8,128)S(1)} %copy.6, s32[1024]{0:T(1024)S(1)} %pad_clamp_fusion), kind=kCustom, calls=%fused_computation | custom fusion | bytes 2460672 | tf_op jit(solution)/shard_map/gather | solution.py:74
  71.6 0.4 copy.7
  72.0 2.4 %maximum_subtract_fusion = f32[768,400]{0,1:T(8,128)} fusion(f32[768,400]{0,1:T(8,128)S(1)} %copy.7, f32[384,400]{0,1:T(8,128)} %get-tuple-element.6, f32[384,400]{0,1:T(8,128)} %get-tuple-element.5), kind=kLoop, calls=%fused_computation.23 | loop fusion | flops 614400 | bytes 3686400 | tf_op jit(solution)/shard_map/sub | solution.py:74
  (8 shorter events, 0.0 us)
Async XLA Ops:
  0.0 19.2 %collective-permute-start = (bf16[800,400]{0,1:T(8,128)(2,1)}, bf16[800,400]{0,1:T(8,128)(2,1)S(1)}, u32[]{:S(2)}, u32[]{:S(2)}) collective-permute-start(bf16[800,400]{0,1:T(8,128)(2,1)} %param.6), channel_id=1, source_target_pairs={{0,16},{8,24},{16,0},{24,8},{1,17},{9,25},{17,1},{25,9},{2,18},{10... | collective-permute-start | bytes 1920008 | tf_op jit(solution)/shard_map/ppermute | solution.py:10
  3.0 18.1 %collective-permute-start.1 = (bf16[800,400]{0,1:T(8,128)(2,1)}, bf16[800,400]{0,1:T(8,128)(2,1)S(1)}, u32[]{:S(2)}, u32[]{:S(2)}) collective-permute-start(bf16[800,400]{0,1:T(8,128)(2,1)} %param.6), channel_id=1, source_target_pairs={{0,8},{8,0},{16,24},{24,16},{1,9},{9,1},{17,25},{25,17},{2,10},{10... | collective-permute-start | bytes 1920008 | tf_op jit(solution)/shard_map/ppermute | solution.py:10
  4.5 18.4 %copy-start.1 = (s32[400]{0:T(512)S(1)}, s32[400]{0:T(512)}, u32[]{:S(2)}) copy-start(s32[400]{0:T(512)} %param.8) | copy-start | bytes 4804
  5.3 20.3 %copy-start = (bf16[1536,3200]{1,0:T(8,128)(2,1)S(1)}, bf16[1536,3200]{1,0:T(8,128)(2,1)}, u32[]{:S(2)}) copy-start(bf16[1536,3200]{1,0:T(8,128)(2,1)} %param.5) | copy-start | bytes 29491204
  19.3 10.7 %collective-permute-start.2 = (bf16[400,400]{0,1:T(8,128)(2,1)S(1)}, bf16[400,400]{0,1:T(8,128)(2,1)S(1)}, u32[]{:S(2)}, u32[]{:S(2)}) collective-permute-start(bf16[400,400]{0,1:T(8,128)(2,1)S(1)} %slice.26), channel_id=1, source_target_pairs={{0,8},{8,0},{16,24},{24,16},{1,9},{9,1},{17,25},{25,17},{2,10},{10... | collective-permute-start | bytes 960008 | tf_op jit(solution)/shard_map/ppermute | solution.py:10
  21.3 10.1 %collective-permute-start.3 = (bf16[400,400]{0,1:T(8,128)(2,1)S(1)}, bf16[400,400]{0,1:T(8,128)(2,1)S(1)}, u32[]{:S(2)}, u32[]{:S(2)}) collective-permute-start(bf16[400,400]{0,1:T(8,128)(2,1)S(1)} %slice.27), channel_id=1, source_target_pairs={{0,16},{8,24},{16,0},{24,8},{1,17},{9,25},{17,1},{25,9},{2,18},{10... | collective-permute-start | bytes 960008 | tf_op jit(solution)/shard_map/ppermute | solution.py:10
  34.0 4.4 %collective-permute-start.4 = (f32[384,400]{0,1:T(8,128)S(1)}, f32[384,400]{0,1:T(8,128)S(1)}, u32[]{:S(2)}, u32[]{:S(2)}) collective-permute-start(f32[384,400]{0,1:T(8,128)S(1)} %get-tuple-element.7), channel_id=1, source_target_pairs={{0,1},{1,0},{2,3},{3,2},{4,5},{5,4},{6,7},{7,6},{8,9},{9,8},{10,11... | collective-permute-start | bytes 1843208 | tf_op jit(solution)/shard_map/ppermute | solution.py:10
  34.1 4.3 %collective-permute-start.5 = (f32[384,400]{0,1:T(8,128)S(1)}, f32[384,400]{0,1:T(8,128)S(1)}, u32[]{:S(2)}, u32[]{:S(2)}) collective-permute-start(f32[384,400]{0,1:T(8,128)S(1)} %get-tuple-element.8), channel_id=1, source_target_pairs={{0,1},{1,0},{2,3},{3,2},{4,5},{5,4},{6,7},{7,6},{8,9},{9,8},{10,11... | collective-permute-start | bytes 1843208 | tf_op jit(solution)/shard_map/ppermute | solution.py:10
  39.6 16.9 %collective-permute-start.6 = (f32[384,400]{0,1:T(8,128)}, f32[384,400]{0,1:T(8,128)S(1)}, u32[]{:S(2)}, u32[]{:S(2)}) collective-permute-start(f32[384,400]{0,1:T(8,128)} %get-tuple-element.5), channel_id=1, source_target_pairs={{0,16},{8,24},{16,0},{24,8},{1,17},{9,25},{17,1},{25,9},{2,18},{10... | collective-permute-start | bytes 1843208 | tf_op jit(solution)/shard_map/ppermute | solution.py:10
  41.2 27.7 %collective-permute-start.7 = (f32[384,400]{0,1:T(8,128)}, f32[384,400]{0,1:T(8,128)S(1)}, u32[]{:S(2)}, u32[]{:S(2)}) collective-permute-start(f32[384,400]{0,1:T(8,128)} %get-tuple-element.6), channel_id=1, source_target_pairs={{0,16},{8,24},{16,0},{24,8},{1,17},{9,25},{17,1},{25,9},{2,18},{10... | collective-permute-start | bytes 1843208 | tf_op jit(solution)/shard_map/ppermute | solution.py:10

commit v13 on v8

--- a/solution.py
+++ b/solution.py
@@ -27,16 +27,21 @@
     return groups
 
 
-def contract(amplitudes, groups, first, rows, labels, irrep_cols):
-    band = lax.dynamic_slice_in_dim(amplitudes, first, rows, axis=0)
-    terms = None
-    for group in groups:
-        for b, o in group:
-            window = lax.dynamic_slice_in_dim(band, o, b.shape[0], axis=1)
-            same = lax.dynamic_slice_in_dim(labels, o, b.shape[0])[:, None] == irrep_cols[None, :]
-            blocked = jnp.where(same, b, jnp.zeros_like(b))
-            product = jnp.dot(window, blocked, preferred_element_type=jnp.float32)
-            terms = product if terms is None else terms + product
+def contract(amplitudes, groups, firsts, rows, labels, irrep_cols):
+    bands = [lax.dynamic_slice_in_dim(amplitudes, first, rows, axis=0) for first in firsts]
+    terms = [None] * len(bands)
+    for g, group in enumerate(groups):
+        if g == len(groups) - 1 and g > 0:
+            blocks, held = lax.optimization_barrier((tuple(b for b, _ in group), tuple(terms)))
+            group = [(b, o) for b, (_, o) in zip(blocks, group)]
+            terms = list(held)
+        for i, band in enumerate(bands):
+            for b, o in group:
+                window = lax.dynamic_slice_in_dim(band, o, b.shape[0], axis=1)
+                same = lax.dynamic_slice_in_dim(labels, o, b.shape[0])[:, None] == irrep_cols[None, :]
+                blocked = jnp.where(same, b, jnp.zeros_like(b))
+                product = jnp.dot(window, blocked, preferred_element_type=jnp.float32)
+                terms[i] = product if terms[i] is None else terms[i] + product
     return terms
 
 
@@ -49,11 +54,11 @@
     labels = lax.dynamic_slice_in_dim(irrep_rows, cuts_idx * width, width)
     groups = gather_prow(integrals, prow_idx, prow_count)
     block_rows = amplitudes.shape[0] // cuts_count
-    sent = []
-    for s in range(1, cuts_count):
-        other = jnp.bitwise_xor(cuts_idx, s)
-        sent.append((s, contract(amplitudes, groups, other * block_rows, block_rows, labels, irrep_cols)))
-    kept = contract(amplitudes, groups, cuts_idx * block_rows, block_rows, labels, irrep_cols)
+    others = list(range(1, cuts_count))
+    firsts = [jnp.bitwise_xor(cuts_idx, s) * block_rows for s in others] + [cuts_idx * block_rows]
+    terms = contract(amplitudes, groups, firsts, block_rows, labels, irrep_cols)
+    sent = list(zip(others, terms[:-1]))
+    kept = terms[-1]
     pieces = 2 if block_rows % 16 == 0 else 1
     step = block_rows // pieces
     half = prow_count // 2

time: 73.5 us -> 72.5 us (0.986)
  waiting for transfers between devices: 38.4 us -> 37.4 us
    ppermute x8, waiting for transfers between devices: 38.4 us -> 37.4 us  [swap(): lax.ppermute(value, axis, [(i, i ^ mask) for i in range(lax.axis_size(axi...]
  transfers between devices with their start and end apart: 8 -> 8, of which waited for: 5 -> 6; matrix products, arithmetic and copies ran while one was open for 21% -> 22% of each run, Pallas kernels for 0% -> 0%
where the time goes in v13:
time: 72.5 us; the launch traced here: 72.1 us
  waiting for transfers between devices  37.4 us (52%)
  matrix products  14.5 us (20%)
  starting transfers between devices  10.4 us (14%)
  local copies, waits for them, and re-layouts  5.1 us (7%)
  other arithmetic  4.49 us (6%)
    ppermute x8, waiting for transfers between devices, swap(): lax.ppermute(value, axis, [(i, i ^ mask) for i in range(lax.axis_size(axi...  37.4 us
    dot_general x10, matrix products, contract(): product = jnp.dot(window, blocked, preferred_element_type=jnp.float32)  14.5 us
    ppermute x8, starting transfers between devices, swap(): lax.ppermute(value, axis, [(i, i ^ mask) for i in range(lax.axis_size(axi...  10.4 us
    gather x2, local copies, waits for them, and re-layouts, shards(): return cycle - jnp.take(fetched, local, axis=0, mode='clip')  2.59 us
    sub x1, other arithmetic, shards(): return cycle - jnp.take(fetched, local, axis=0, mode='clip')  2.43 us
    dynamic_slice x2, local copies, waits for them, and re-layouts, contract(): lax.dynamic_slice_in_dim(labels, o, b.shape[0])[:, None]  1.73 us
  transfers between devices with their start and end apart: 8, of which 6 were waited for; matrix products, arithmetic and copies ran while one was open for 22% of the time, Pallas kernels for 0%

profile of v13, /device:TPU:0, one launch (start us, length us, event | category | flops | bytes accessed | tf_op | source)
XLA Modules:
  0.0 72.1 jit_solution(2620089630827154935)
XLA Ops:
  0.0 3.0 %collective-permute-start = (bf16[800,400]{0,1:T(8,128)(2,1)}, bf16[800,400]{0,1:T(8,128)(2,1)S(1)}, u32[]{:S(2)}, u32[]{:S(2)}) collective-permute-start(bf16[800,400]{0,1:T(8,128)(2,1)} %param.6), channel_id=1, source_target_pairs={{0,16},{8,24},{16,0},{24,8},{1,17},{9,25},{17,1},{25,9},{2,18},{10... | collective-permute-start | bytes 1920008 | tf_op jit(solution)/shard_map/ppermute | solution.py:10
  3.0 1.5 %collective-permute-start.2 = (bf16[800,400]{0,1:T(8,128)(2,1)}, bf16[800,400]{0,1:T(8,128)(2,1)S(1)}, u32[]{:S(2)}, u32[]{:S(2)}) collective-permute-start(bf16[800,400]{0,1:T(8,128)(2,1)} %param.6), channel_id=1, source_target_pairs={{0,8},{8,0},{16,24},{24,16},{1,9},{9,1},{17,25},{25,17},{2,10},{10... | collective-permute-start | bytes 1920008 | tf_op jit(solution)/shard_map/ppermute | solution.py:10
  4.5 0.9 %fusion.32 = (s32[800]{0:T(1024)S(1)}, s32[800]{0:T(1024)S(1)}, s32[800]{0:T(1024)S(1)}) fusion(s32[6400]{0:T(1024)} %param.7, s32[]{:T(128)S(6)} %dynamic_slice.73, s32[]{:T(128)S(6)} %dynamic_slice.70, s32[]{:T(128)S(6)} %dynamic_slice.67), kind=kLoop, calls=%fused_computation.46 | loop fusion | bytes 19212 | tf_op jit(solution)/shard_map/dynamic_slice | solution.py:41
  5.3 0.8 %fusion.31 = (s32[400]{0:T(512)S(1)}, s32[400]{0:T(512)S(1)}) fusion(s32[6400]{0:T(1024)} %param.7, s32[]{:T(128)S(6)} %dynamic_slice.82, s32[]{:T(128)S(6)} %dynamic_slice.79), kind=kLoop, calls=%fused_computation.45 | loop fusion | bytes 6408 | tf_op jit(solution)/shard_map/dynamic_slice | solution.py:41
  6.2 3.0 %fusion.6 = f32[768,400]{0,1:T(8,128)S(1)} fusion(bf16[1536,3200]{1,0:T(8,128)(2,1)} %param.5, s32[]{:T(128)S(6)} %select_n.81, s32[]{:T(128)S(6)} %select_n.83, bf16[800,400]{0,1:T(8,128)(2,1)} %param.6, s32[800]{0:T(1024)S(1)} %get-tuple-element.21, s32[400]{0:T(512)} %param.8), kind=kOutput, calls=%fused_computation.14 | convolution fusion | flops 492160000 | bytes 3327112 | tf_op jit(solution)/shard_map/dot_general | solution.py:43
  9.2 3.3 %fusion.2 = f32[768,400]{0,1:T(8,128)S(1)} fusion(bf16[1536,3200]{1,0:T(8,128)(2,1)} %param.5, s32[]{:T(128)S(6)} %select_n.94, s32[]{:T(128)S(6)} %select_n.83, bf16[800,400]{0,1:T(8,128)(2,1)} %param.6, s32[800]{0:T(1024)S(1)} %get-tuple-element.21, s32[400]{0:T(512)S(1)} %copy-done.1), kind=kOutput, calls=%fused_computation.10 | convolution fusion | flops 492160000 | bytes 3326664 | tf_op jit(solution)/shard_map/dot_general | solution.py:43
  12.5 6.7 %collective-permute-done = bf16[800,400]{0,1:T(8,128)(2,1)S(1)} collective-permute-done((bf16[800,400]{0,1:T(8,128)(2,1)}, bf16[800,400]{0,1:T(8,128)(2,1)S(1)}, u32[]{:S(2)}, u32[]{:S(2)}) %collective-permute-start) | collective-permute-done | bytes 640032 | tf_op jit(solution)/shard_map/ppermute | solution.py:10
  19.3 1.8 %collective-permute-start.1 = (bf16[400,400]{0,1:T(8,128)(2,1)S(1)}, bf16[400,400]{0,1:T(8,128)(2,1)S(1)}, u32[]{:S(2)}, u32[]{:S(2)}) collective-permute-start(bf16[400,400]{0,1:T(8,128)(2,1)S(1)} %slice.26), channel_id=1, source_target_pairs={{0,8},{8,0},{16,24},{24,16},{1,9},{9,1},{17,25},{25,17},{2,10},{10... | collective-permute-start | bytes 960008 | tf_op jit(solution)/shard_map/ppermute | solution.py:10
  21.0 0.2 slice.27
  21.2 1.6 %collective-permute-start.3 = (bf16[400,400]{0,1:T(8,128)(2,1)S(1)}, bf16[400,400]{0,1:T(8,128)(2,1)S(1)}, u32[]{:S(2)}, u32[]{:S(2)}) collective-permute-start(bf16[400,400]{0,1:T(8,128)(2,1)S(1)} %slice.27), channel_id=1, source_target_pairs={{0,16},{8,24},{16,0},{24,8},{1,17},{9,25},{17,1},{25,9},{2,18},{10... | collective-permute-start | bytes 960008 | tf_op jit(solution)/shard_map/ppermute | solution.py:10
  22.8 1.3 %convolution_add_fusion.3 = f32[768,400]{0,1:T(8,128)S(1)} fusion(f32[768,400]{0,1:T(8,128)S(1)} %fusion.6, bf16[1536,3200]{1,0:T(8,128)(2,1)S(1)} %copy-done, s32[]{:T(128)S(6)} %select_n.81, s32[]{:T(128)S(6)} %select_n.88, bf16[800,400]{0,1:T(8,128)(2,1)S(1)} %collective-permute-done, s32[800]{0:T(1024)S(1)} %get-tuple-element.20, s32[400]{0:T(512)S(1)} %copy-done.1), kind=kOutput, calls=%fused_computation.7 | convolution fusion | flops 492467200 | bytes 4556808 | tf_op jit(solution)/shard_map/dot_general | solution.py:43
  24.1 1.3 %convolution_add_fusion.1 = f32[768,400]{0,1:T(8,128)S(1)} fusion(f32[768,400]{0,1:T(8,128)S(1)} %fusion.2, bf16[1536,3200]{1,0:T(8,128)(2,1)S(1)} %copy-done, s32[]{:T(128)S(6)} %select_n.94, s32[]{:T(128)S(6)} %select_n.88, bf16[800,400]{0,1:T(8,128)(2,1)S(1)} %collective-permute-done, s32[800]{0:T(1024)S(1)} %get-tuple-element.20, s32[400]{0:T(512)S(1)} %copy-done.1), kind=kOutput, calls=%fused_computation.5 | convolution fusion | flops 492467200 | bytes 4556808 | tf_op jit(solution)/shard_map/dot_general | solution.py:43
  25.4 1.3 %convolution_add_fusion.2 = f32[768,400]{0,1:T(8,128)S(1)} fusion(f32[768,400]{0,1:T(8,128)S(1)} %convolution_add_fusion.3, bf16[1536,3200]{1,0:T(8,128)(2,1)S(1)} %copy-done, s32[]{:T(128)S(6)} %select_n.81, s32[]{:T(128)S(6)} %select_n.91, bf16[800,400]{0,1:T(8,128)(2,1)S(1)} %collective-permute-done.2, s32[800]{0:T(1024)S(1)} %get-tuple-element.19, ...), kind=kOutput, calls=%fused_computation.6 | convolution fusion | flops 492467200 | bytes 4556808 | tf_op jit(solution)/shard_map/dot_general | solution.py:43
  26.7 1.3 %convolution_add_fusion = f32[768,400]{0,1:T(8,128)S(1)} fusion(f32[768,400]{0,1:T(8,128)S(1)} %convolution_add_fusion.1, bf16[1536,3200]{1,0:T(8,128)(2,1)S(1)} %copy-done, s32[]{:T(128)S(6)} %select_n.94, s32[]{:T(128)S(6)} %select_n.91, bf16[800,400]{0,1:T(8,128)(2,1)S(1)} %collective-permute-done.2, s32[800]{0:T(1024)S(1)} %get-tuple-element.19, ...), kind=kOutput, calls=%fused_computation.4 | convolution fusion | flops 492467200 | bytes 4556808 | tf_op jit(solution)/shard_map/dot_general | solution.py:43
  27.9 2.0 %collective-permute-done.1 = bf16[400,400]{0,1:T(8,128)(2,1)S(1)} collective-permute-done((bf16[400,400]{0,1:T(8,128)(2,1)S(1)}, bf16[400,400]{0,1:T(8,128)(2,1)S(1)}, u32[]{:S(2)}, u32[]{:S(2)}) %collective-permute-start.1) | collective-permute-done | bytes 320032 | tf_op jit(solution)/shard_map/ppermute | solution.py:10
  30.0 1.4 %collective-permute-done.3 = bf16[400,400]{0,1:T(8,128)(2,1)S(1)} collective-permute-done((bf16[400,400]{0,1:T(8,128)(2,1)S(1)}, bf16[400,400]{0,1:T(8,128)(2,1)S(1)}, u32[]{:S(2)}, u32[]{:S(2)}) %collective-permute-start.3) | collective-permute-done | bytes 320032 | tf_op jit(solution)/shard_map/ppermute | solution.py:10
  31.4 0.8 %fusion.12 = f32[768,400]{0,1:T(8,128)S(1)} fusion(bf16[1536,3200]{1,0:T(8,128)(2,1)S(1)} %copy-done, s32[]{:T(128)S(6)} %select_n.81, s32[]{:T(128)S(6)} %select_n.96, bf16[400,400]{0,1:T(8,128)(2,1)S(1)} %collective-permute-done.1, s32[400]{0:T(512)S(1)} %get-tuple-element.18, s32[400]{0:T(512)S(1)} %copy-done.1), kind=kOutput, calls=%fused_computation.24 | convolution fusion | flops 246080000 | bytes 2428936 | tf_op jit(solution)/shard_map/dot_general | solution.py:43
  32.2 0.8 %add_add_fusion = f32[768,400]{0,1:T(8,128)S(1)} fusion(f32[768,400]{0,1:T(8,128)S(1)} %convolution_add_fusion.2, f32[768,400]{0,1:T(8,128)S(1)} %fusion.12, bf16[1536,3200]{1,0:T(8,128)(2,1)S(1)} %copy-done, s32[]{:T(128)S(6)} %select_n.81, s32[]{:T(128)S(6)} %select_n.99, bf16[400,400]{0,1:T(8,128)(2,1)S(1)} %collective-permute-done.3, ...), kind=kOutput, calls=%fused_computation.18 | convolution fusion | flops 246694400 | bytes 4886536 | tf_op jit(solution)/shard_map/dot_general | solution.py:43
  33.2 0.5 collective-permute-start.5
  33.7 0.8 %fusion.18 = f32[768,400]{0,1:T(8,128)S(1)} fusion(bf16[1536,3200]{1,0:T(8,128)(2,1)S(1)} %copy-done, s32[]{:T(128)S(6)} %select_n.94, s32[]{:T(128)S(6)} %select_n.96, bf16[400,400]{0,1:T(8,128)(2,1)S(1)} %collective-permute-done.1, s32[400]{0:T(512)S(1)} %get-tuple-element.18, s32[400]{0:T(512)S(1)} %copy-done.1), kind=kOutput, calls=%fused_computation.28 | convolution fusion | flops 246080000 | bytes 2428936 | tf_op jit(solution)/shard_map/dot_general | solution.py:43
  34.4 0.8 %add_add_fusion.1 = f32[768,400]{0,1:T(8,128)S(1)} fusion(f32[768,400]{0,1:T(8,128)S(1)} %convolution_add_fusion, f32[768,400]{0,1:T(8,128)S(1)} %fusion.18, bf16[1536,3200]{1,0:T(8,128)(2,1)S(1)} %copy-done, s32[]{:T(128)S(6)} %select_n.94, s32[]{:T(128)S(6)} %select_n.99, bf16[400,400]{0,1:T(8,128)(2,1)S(1)} %collective-permute-done.3, ...), kind=kOutput, calls=%fused_computation.19 | convolution fusion | flops 246694400 | bytes 4886536 | tf_op jit(solution)/shard_map/dot_general | solution.py:43
  35.3 0.8 %collective-permute-done.5 = f32[384,400]{0,1:T(8,128)S(1)} collective-permute-done((f32[384,400]{0,1:T(8,128)S(1)}, f32[384,400]{0,1:T(8,128)S(1)}, u32[]{:S(2)}, u32[]{:S(2)}) %collective-permute-start.5) | collective-permute-done | bytes 614432 | tf_op jit(solution)/shard_map/ppermute | solution.py:10
  36.1 1.2 %slice_add_fusion.1 = (f32[384,400]{0,1:T(8,128)}, f32[384,400]{0,1:T(8,128)}) fusion(f32[384,400]{0,1:T(8,128)S(1)} %collective-permute-done.4, f32[768,400]{0,1:T(8,128)S(1)} %add_add_fusion.1, f32[384,400]{0,1:T(8,128)S(1)} %collective-permute-done.5), kind=kLoop, calls=%fused_computation.31 | loop fusion | flops 307200 | bytes 3686400 | tf_op jit(solution)/shard_map/add | solution.py:70
  37.3 1.5 %collective-permute-start.6 = (f32[384,400]{0,1:T(8,128)}, f32[384,400]{0,1:T(8,128)S(1)}, u32[]{:S(2)}, u32[]{:S(2)}) collective-permute-start(f32[384,400]{0,1:T(8,128)} %get-tuple-element.13), channel_id=1, source_target_pairs={{0,16},{8,24},{16,0},{24,8},{1,17},{9,25},{17,1},{25,9},{2,18},{10... | collective-permute-start | bytes 1843208 | tf_op jit(solution)/shard_map/ppermute | solution.py:10
  38.8 0.5 collective-permute-start.7
  39.3 0.8 %dynamic-slice_subtract_fusion = s32[768]{0:T(1024)S(1)} fusion(s32[6144]{0:T(1024)} %param.9, s32[]{:T(128)S(6)} %select_n.101, s32[]{:T(128)S(6)} %mul.43), kind=kLoop, calls=%fused_computation.33 | loop fusion | flops 768 | bytes 6152 | tf_op jit(solution)/shard_map/sub | solution.py:78
  40.1 14.1 %collective-permute-done.6 = f32[384,400]{0,1:T(8,128)S(1)} collective-permute-done((f32[384,400]{0,1:T(8,128)}, f32[384,400]{0,1:T(8,128)S(1)}, u32[]{:S(2)}, u32[]{:S(2)}) %collective-permute-start.6) | collective-permute-done | bytes 614432 | tf_op jit(solution)/shard_map/ppermute | solution.py:10
  54.2 12.4 %collective-permute-done.7 = f32[384,400]{0,1:T(8,128)S(1)} collective-permute-done((f32[384,400]{0,1:T(8,128)}, f32[384,400]{0,1:T(8,128)S(1)}, u32[]{:S(2)}, u32[]{:S(2)}) %collective-permute-start.7) | collective-permute-done | bytes 614432 | tf_op jit(solution)/shard_map/ppermute | solution.py:10
  66.6 0.5 copy.6
  67.1 2.2 %gather_fusion = f32[768,400]{1,0:T(8,128)S(1)} fusion(f32[768,400]{1,0:T(8,128)S(1)} %copy.6, s32[1024]{0:T(1024)S(1)} %pad_clamp_fusion), kind=kCustom, calls=%fused_computation | custom fusion | bytes 2460672 | tf_op jit(solution)/shard_map/jit(_take)/gather | solution.py:79
  69.3 0.4 copy.7
  69.7 2.4 %maximum_subtract_fusion = f32[768,400]{0,1:T(8,128)} fusion(f32[768,400]{0,1:T(8,128)S(1)} %copy.7, f32[384,400]{0,1:T(8,128)} %get-tuple-element.14, f32[384,400]{0,1:T(8,128)} %get-tuple-element.13), kind=kLoop, calls=%fused_computation.16 | loop fusion | flops 614400 | bytes 3686400 | tf_op jit(solution)/shard_map/sub | solution.py:79
  (11 shorter events, 0.3 us)
Async XLA Ops:
  0.0 19.2 %collective-permute-start = (bf16[800,400]{0,1:T(8,128)(2,1)}, bf16[800,400]{0,1:T(8,128)(2,1)S(1)}, u32[]{:S(2)}, u32[]{:S(2)}) collective-permute-start(bf16[800,400]{0,1:T(8,128)(2,1)} %param.6), channel_id=1, source_target_pairs={{0,16},{8,24},{16,0},{24,8},{1,17},{9,25},{17,1},{25,9},{2,18},{10... | collective-permute-start | bytes 1920008 | tf_op jit(solution)/shard_map/ppermute | solution.py:10
  3.0 18.1 %collective-permute-start.2 = (bf16[800,400]{0,1:T(8,128)(2,1)}, bf16[800,400]{0,1:T(8,128)(2,1)S(1)}, u32[]{:S(2)}, u32[]{:S(2)}) collective-permute-start(bf16[800,400]{0,1:T(8,128)(2,1)} %param.6), channel_id=1, source_target_pairs={{0,8},{8,0},{16,24},{24,16},{1,9},{9,1},{17,25},{25,17},{2,10},{10... | collective-permute-start | bytes 1920008 | tf_op jit(solution)/shard_map/ppermute | solution.py:10
  4.5 4.7 %copy-start.1 = (s32[400]{0:T(512)S(1)}, s32[400]{0:T(512)}, u32[]{:S(2)}) copy-start(s32[400]{0:T(512)} %param.8) | copy-start | bytes 4804
  6.2 16.6 %copy-start = (bf16[1536,3200]{1,0:T(8,128)(2,1)S(1)}, bf16[1536,3200]{1,0:T(8,128)(2,1)}, u32[]{:S(2)}) copy-start(bf16[1536,3200]{1,0:T(8,128)(2,1)} %param.5) | copy-start | bytes 29491204
  19.3 10.7 %collective-permute-start.1 = (bf16[400,400]{0,1:T(8,128)(2,1)S(1)}, bf16[400,400]{0,1:T(8,128)(2,1)S(1)}, u32[]{:S(2)}, u32[]{:S(2)}) collective-permute-start(bf16[400,400]{0,1:T(8,128)(2,1)S(1)} %slice.26), channel_id=1, source_target_pairs={{0,8},{8,0},{16,24},{24,16},{1,9},{9,1},{17,25},{25,17},{2,10},{10... | collective-permute-start | bytes 960008 | tf_op jit(solution)/shard_map/ppermute | solution.py:10
  21.2 10.1 %collective-permute-start.3 = (bf16[400,400]{0,1:T(8,128)(2,1)S(1)}, bf16[400,400]{0,1:T(8,128)(2,1)S(1)}, u32[]{:S(2)}, u32[]{:S(2)}) collective-permute-start(bf16[400,400]{0,1:T(8,128)(2,1)S(1)} %slice.27), channel_id=1, source_target_pairs={{0,16},{8,24},{16,0},{24,8},{1,17},{9,25},{17,1},{25,9},{2,18},{10... | collective-permute-start | bytes 960008 | tf_op jit(solution)/shard_map/ppermute | solution.py:10
  33.1 2.2 %collective-permute-start.4 = (f32[384,400]{0,1:T(8,128)S(1)}, f32[384,400]{0,1:T(8,128)S(1)}, u32[]{:S(2)}, u32[]{:S(2)}) collective-permute-start(f32[384,400]{0,1:T(8,128)S(1)} %get-tuple-element.15), channel_id=1, source_target_pairs={{0,1},{1,0},{2,3},{3,2},{4,5},{5,4},{6,7},{7,6},{8,9},{9,8},{10,11... | collective-permute-start | bytes 1843208 | tf_op jit(solution)/shard_map/ppermute | solution.py:10
  33.2 2.9 %collective-permute-start.5 = (f32[384,400]{0,1:T(8,128)S(1)}, f32[384,400]{0,1:T(8,128)S(1)}, u32[]{:S(2)}, u32[]{:S(2)}) collective-permute-start(f32[384,400]{0,1:T(8,128)S(1)} %get-tuple-element.16), channel_id=1, source_target_pairs={{0,1},{1,0},{2,3},{3,2},{4,5},{5,4},{6,7},{7,6},{8,9},{9,8},{10,11... | collective-permute-start | bytes 1843208 | tf_op jit(solution)/shard_map/ppermute | solution.py:10
  37.3 16.9 %collective-permute-start.6 = (f32[384,400]{0,1:T(8,128)}, f32[384,400]{0,1:T(8,128)S(1)}, u32[]{:S(2)}, u32[]{:S(2)}) collective-permute-start(f32[384,400]{0,1:T(8,128)} %get-tuple-element.13), channel_id=1, source_target_pairs={{0,16},{8,24},{16,0},{24,8},{1,17},{9,25},{17,1},{25,9},{2,18},{10... | collective-permute-start | bytes 1843208 | tf_op jit(solution)/shard_map/ppermute | solution.py:10
  38.8 27.7 %collective-permute-start.7 = (f32[384,400]{0,1:T(8,128)}, f32[384,400]{0,1:T(8,128)S(1)}, u32[]{:S(2)}, u32[]{:S(2)}) collective-permute-start(f32[384,400]{0,1:T(8,128)} %get-tuple-element.14), channel_id=1, source_target_pairs={{0,16},{8,24},{16,0},{24,8},{1,17},{9,25},{17,1},{25,9},{2,18},{10... | collective-permute-start | bytes 1843208 | tf_op jit(solution)/shard_map/ppermute | solution.py:10

commit v14 on v13

--- a/solution.py
+++ b/solution.py
@@ -59,7 +59,7 @@
     terms = contract(amplitudes, groups, firsts, block_rows, labels, irrep_cols)
     sent = list(zip(others, terms[:-1]))
     kept = terms[-1]
-    pieces = 2 if block_rows % 16 == 0 else 1
+    pieces = 1
     step = block_rows // pieces
     half = prow_count // 2
     fetched = []

time: 72.5 us -> 72.4 us (level)
  local copies, waits for them, and re-layouts: 5.1 us -> 6.1 us
  other arithmetic: 4.49 us -> 3.53 us
  starting transfers between devices: 10.4 us -> 9.47 us
  waiting for transfers between devices: 37.4 us -> 38.2 us
    gather x2, local copies, waits for them, and re-layouts: 2.59 us -> 3.65 us  [shards(): return cycle - jnp.take(fetched, local, axis=0, mode='clip')]
    ppermute x8 -> x6, starting transfers between devices: 10.4 us -> 9.47 us  [swap(): lax.ppermute(value, axis, [(i, i ^ mask) for i in range(lax.axis_size(axi...]
    add x1, other arithmetic: 1.19 us -> 0.3 us  [shards(): total = total + swap(part[h * step:(h + 1) * step], 'cuts', s)]
    ppermute x8 -> x6, waiting for transfers between devices: 37.4 us -> 38.2 us  [swap(): lax.ppermute(value, axis, [(i, i ^ mask) for i in range(lax.axis_size(axi...]
  transfers between devices with their start and end apart: 8 -> 6, of which waited for: 6 -> 5; matrix products, arithmetic and copies ran while one was open for 22% -> 22% of each run, Pallas kernels for 0% -> 0%
where the time goes in v14:
time: 72.4 us; the launch traced here: 72 us
  waiting for transfers between devices  38.2 us (53%)
  matrix products  14.5 us (20%)
  starting transfers between devices  9.47 us (13%)
  local copies, waits for them, and re-layouts  6.1 us (8%)
  other arithmetic  3.53 us (5%)
    ppermute x6, waiting for transfers between devices, swap(): lax.ppermute(value, axis, [(i, i ^ mask) for i in range(lax.axis_size(axi...  38.2 us
    dot_general x10, matrix products, contract(): product = jnp.dot(window, blocked, preferred_element_type=jnp.float32)  14.5 us
    ppermute x6, starting transfers between devices, swap(): lax.ppermute(value, axis, [(i, i ^ mask) for i in range(lax.axis_size(axi...  9.47 us
    gather x2, local copies, waits for them, and re-layouts, shards(): return cycle - jnp.take(fetched, local, axis=0, mode='clip')  3.65 us
    sub x1, other arithmetic, shards(): return cycle - jnp.take(fetched, local, axis=0, mode='clip')  2.46 us
    dynamic_slice x2, local copies, waits for them, and re-layouts, contract(): lax.dynamic_slice_in_dim(labels, o, b.shape[0])[:, None]  1.73 us
  transfers between devices with their start and end apart: 6, of which 5 were waited for; matrix products, arithmetic and copies ran while one was open for 22% of the time, Pallas kernels for 0%

profile of v14, /device:TPU:0, one launch (start us, length us, event | category | flops | bytes accessed | tf_op | source)
XLA Modules:
  0.0 72.0 jit_solution(16256278406039273335)
XLA Ops:
  0.0 3.0 %collective-permute-start = (bf16[800,400]{0,1:T(8,128)(2,1)}, bf16[800,400]{0,1:T(8,128)(2,1)S(1)}, u32[]{:S(2)}, u32[]{:S(2)}) collective-permute-start(bf16[800,400]{0,1:T(8,128)(2,1)} %param.6), channel_id=1, source_target_pairs={{0,16},{8,24},{16,0},{24,8},{1,17},{9,25},{17,1},{25,9},{2,18},{10... | collective-permute-start | bytes 1920008 | tf_op jit(solution)/shard_map/ppermute | solution.py:10
  3.0 1.5 %collective-permute-start.2 = (bf16[800,400]{0,1:T(8,128)(2,1)}, bf16[800,400]{0,1:T(8,128)(2,1)S(1)}, u32[]{:S(2)}, u32[]{:S(2)}) collective-permute-start(bf16[800,400]{0,1:T(8,128)(2,1)} %param.6), channel_id=1, source_target_pairs={{0,8},{8,0},{16,24},{24,16},{1,9},{9,1},{17,25},{25,17},{2,10},{10... | collective-permute-start | bytes 1920008 | tf_op jit(solution)/shard_map/ppermute | solution.py:10
  4.5 0.9 %fusion.29 = (s32[800]{0:T(1024)S(1)}, s32[800]{0:T(1024)S(1)}, s32[800]{0:T(1024)S(1)}) fusion(s32[6400]{0:T(1024)} %param.7, s32[]{:T(128)S(6)} %dynamic_slice.73, s32[]{:T(128)S(6)} %dynamic_slice.70, s32[]{:T(128)S(6)} %dynamic_slice.67), kind=kLoop, calls=%fused_computation.41 | loop fusion | bytes 19212 | tf_op jit(solution)/shard_map/dynamic_slice | solution.py:41
  5.3 0.8 %fusion.28 = (s32[400]{0:T(512)S(1)}, s32[400]{0:T(512)S(1)}) fusion(s32[6400]{0:T(1024)} %param.7, s32[]{:T(128)S(6)} %dynamic_slice.82, s32[]{:T(128)S(6)} %dynamic_slice.79), kind=kLoop, calls=%fused_computation.40 | loop fusion | bytes 6408 | tf_op jit(solution)/shard_map/dynamic_slice | solution.py:41
  6.2 3.0 %fusion.6 = f32[768,400]{0,1:T(8,128)S(1)} fusion(bf16[1536,3200]{1,0:T(8,128)(2,1)} %param.5, s32[]{:T(128)S(6)} %select_n.81, s32[]{:T(128)S(6)} %select_n.83, bf16[800,400]{0,1:T(8,128)(2,1)} %param.6, s32[800]{0:T(1024)S(1)} %get-tuple-element.17, s32[400]{0:T(512)} %param.8), kind=kOutput, calls=%fused_computation.14 | convolution fusion | flops 492160000 | bytes 3327112 | tf_op jit(solution)/shard_map/dot_general | solution.py:43
  9.2 3.3 %fusion.2 = f32[768,400]{0,1:T(8,128)S(1)} fusion(bf16[1536,3200]{1,0:T(8,128)(2,1)} %param.5, s32[]{:T(128)S(6)} %select_n.94, s32[]{:T(128)S(6)} %select_n.83, bf16[800,400]{0,1:T(8,128)(2,1)} %param.6, s32[800]{0:T(1024)S(1)} %get-tuple-element.17, s32[400]{0:T(512)S(1)} %copy-done.3), kind=kOutput, calls=%fused_computation.10 | convolution fusion | flops 492160000 | bytes 3326664 | tf_op jit(solution)/shard_map/dot_general | solution.py:43
  12.5 6.7 %collective-permute-done = bf16[800,400]{0,1:T(8,128)(2,1)S(1)} collective-permute-done((bf16[800,400]{0,1:T(8,128)(2,1)}, bf16[800,400]{0,1:T(8,128)(2,1)S(1)}, u32[]{:S(2)}, u32[]{:S(2)}) %collective-permute-start) | collective-permute-done | bytes 640032 | tf_op jit(solution)/shard_map/ppermute | solution.py:10
  19.3 1.8 %collective-permute-start.1 = (bf16[400,400]{0,1:T(8,128)(2,1)S(1)}, bf16[400,400]{0,1:T(8,128)(2,1)S(1)}, u32[]{:S(2)}, u32[]{:S(2)}) collective-permute-start(bf16[400,400]{0,1:T(8,128)(2,1)S(1)} %slice.10), channel_id=1, source_target_pairs={{0,8},{8,0},{16,24},{24,16},{1,9},{9,1},{17,25},{25,17},{2,10},{10... | collective-permute-start | bytes 960008 | tf_op jit(solution)/shard_map/ppermute | solution.py:10
  21.0 0.2 slice.11
  21.2 1.6 %collective-permute-start.3 = (bf16[400,400]{0,1:T(8,128)(2,1)S(1)}, bf16[400,400]{0,1:T(8,128)(2,1)S(1)}, u32[]{:S(2)}, u32[]{:S(2)}) collective-permute-start(bf16[400,400]{0,1:T(8,128)(2,1)S(1)} %slice.11), channel_id=1, source_target_pairs={{0,16},{8,24},{16,0},{24,8},{1,17},{9,25},{17,1},{25,9},{2,18},{10... | collective-permute-start | bytes 960008 | tf_op jit(solution)/shard_map/ppermute | solution.py:10
  22.8 1.3 %convolution_add_fusion.3 = f32[768,400]{0,1:T(8,128)S(1)} fusion(f32[768,400]{0,1:T(8,128)S(1)} %fusion.6, bf16[1536,3200]{1,0:T(8,128)(2,1)S(1)} %copy-done, s32[]{:T(128)S(6)} %select_n.81, s32[]{:T(128)S(6)} %select_n.88, bf16[800,400]{0,1:T(8,128)(2,1)S(1)} %collective-permute-done, s32[800]{0:T(1024)S(1)} %get-tuple-element.16, s32[400]{0:T(512)S(1)} %copy-done.3), kind=kOutput, calls=%fused_computation.7 | convolution fusion | flops 492467200 | bytes 4556808 | tf_op jit(solution)/shard_map/dot_general | solution.py:43
  24.1 1.3 %convolution_add_fusion.1 = f32[768,400]{0,1:T(8,128)S(1)} fusion(f32[768,400]{0,1:T(8,128)S(1)} %fusion.2, bf16[1536,3200]{1,0:T(8,128)(2,1)S(1)} %copy-done, s32[]{:T(128)S(6)} %select_n.94, s32[]{:T(128)S(6)} %select_n.88, bf16[800,400]{0,1:T(8,128)(2,1)S(1)} %collective-permute-done, s32[800]{0:T(1024)S(1)} %get-tuple-element.16, s32[400]{0:T(512)S(1)} %copy-done.3), kind=kOutput, calls=%fused_computation.5 | convolution fusion | flops 492467200 | bytes 4556808 | tf_op jit(solution)/shard_map/dot_general | solution.py:43
  25.4 1.3 %convolution_add_fusion.2 = f32[768,400]{0,1:T(8,128)S(1)} fusion(f32[768,400]{0,1:T(8,128)S(1)} %convolution_add_fusion.3, bf16[1536,3200]{1,0:T(8,128)(2,1)S(1)} %copy-done, s32[]{:T(128)S(6)} %select_n.81, s32[]{:T(128)S(6)} %select_n.91, bf16[800,400]{0,1:T(8,128)(2,1)S(1)} %collective-permute-done.2, s32[800]{0:T(1024)S(1)} %get-tuple-element.15, ...), kind=kOutput, calls=%fused_computation.6 | convolution fusion | flops 492467200 | bytes 4556808 | tf_op jit(solution)/shard_map/dot_general | solution.py:43
  26.7 1.3 %convolution_add_fusion = f32[768,400]{0,1:T(8,128)S(1)} fusion(f32[768,400]{0,1:T(8,128)S(1)} %convolution_add_fusion.1, bf16[1536,3200]{1,0:T(8,128)(2,1)S(1)} %copy-done, s32[]{:T(128)S(6)} %select_n.94, s32[]{:T(128)S(6)} %select_n.91, bf16[800,400]{0,1:T(8,128)(2,1)S(1)} %collective-permute-done.2, s32[800]{0:T(1024)S(1)} %get-tuple-element.15, ...), kind=kOutput, calls=%fused_computation.4 | convolution fusion | flops 492467200 | bytes 4556808 | tf_op jit(solution)/shard_map/dot_general | solution.py:43
  27.9 2.0 %collective-permute-done.1 = bf16[400,400]{0,1:T(8,128)(2,1)S(1)} collective-permute-done((bf16[400,400]{0,1:T(8,128)(2,1)S(1)}, bf16[400,400]{0,1:T(8,128)(2,1)S(1)}, u32[]{:S(2)}, u32[]{:S(2)}) %collective-permute-start.1) | collective-permute-done | bytes 320032 | tf_op jit(solution)/shard_map/ppermute | solution.py:10
  30.0 1.4 %collective-permute-done.3 = bf16[400,400]{0,1:T(8,128)(2,1)S(1)} collective-permute-done((bf16[400,400]{0,1:T(8,128)(2,1)S(1)}, bf16[400,400]{0,1:T(8,128)(2,1)S(1)}, u32[]{:S(2)}, u32[]{:S(2)}) %collective-permute-start.3) | collective-permute-done | bytes 320032 | tf_op jit(solution)/shard_map/ppermute | solution.py:10
  31.4 0.8 %fusion.12 = f32[768,400]{0,1:T(8,128)S(1)} fusion(bf16[1536,3200]{1,0:T(8,128)(2,1)S(1)} %copy-done, s32[]{:T(128)S(6)} %select_n.81, s32[]{:T(128)S(6)} %select_n.96, bf16[400,400]{0,1:T(8,128)(2,1)S(1)} %collective-permute-done.1, s32[400]{0:T(512)S(1)} %get-tuple-element.14, s32[400]{0:T(512)S(1)} %copy-done.3), kind=kOutput, calls=%fused_computation.22 | convolution fusion | flops 246080000 | bytes 2428936 | tf_op jit(solution)/shard_map/dot_general | solution.py:43
  32.2 0.8 %add_add_fusion = f32[768,400]{0,1:T(8,128)S(1)} fusion(f32[768,400]{0,1:T(8,128)S(1)} %convolution_add_fusion.2, f32[768,400]{0,1:T(8,128)S(1)} %fusion.12, bf16[1536,3200]{1,0:T(8,128)(2,1)S(1)} %copy-done, s32[]{:T(128)S(6)} %select_n.81, s32[]{:T(128)S(6)} %select_n.99, bf16[400,400]{0,1:T(8,128)(2,1)S(1)} %collective-permute-done.3, ...), kind=kOutput, calls=%fused_computation.16 | convolution fusion | flops 246694400 | bytes 4886536 | tf_op jit(solution)/shard_map/dot_general | solution.py:43
  33.0 0.1 collective-permute-start.4
  33.1 0.8 %fusion.14 = f32[768,400]{0,1:T(8,128)S(1)} fusion(bf16[1536,3200]{1,0:T(8,128)(2,1)S(1)} %copy-done, s32[]{:T(128)S(6)} %select_n.94, s32[]{:T(128)S(6)} %select_n.99, bf16[400,400]{0,1:T(8,128)(2,1)S(1)} %collective-permute-done.3, s32[400]{0:T(512)S(1)} %get-tuple-element.13, s32[400]{0:T(512)S(1)} %copy-done.3), kind=kOutput, calls=%fused_computation.24 | convolution fusion | flops 246080000 | bytes 2428936 | tf_op jit(solution)/shard_map/dot_general | solution.py:43
  33.9 0.8 %fusion.16 = f32[768,400]{0,1:T(8,128)S(1)} fusion(bf16[1536,3200]{1,0:T(8,128)(2,1)S(1)} %copy-done, s32[]{:T(128)S(6)} %select_n.94, s32[]{:T(128)S(6)} %select_n.96, bf16[400,400]{0,1:T(8,128)(2,1)S(1)} %collective-permute-done.1, s32[400]{0:T(512)S(1)} %get-tuple-element.14, s32[400]{0:T(512)S(1)} %copy-done.3), kind=kOutput, calls=%fused_computation.26 | convolution fusion | flops 246080000 | bytes 2428936 | tf_op jit(solution)/shard_map/dot_general | solution.py:43
  34.7 1.3 %collective-permute-done.4 = f32[768,400]{0,1:T(8,128)S(1)} collective-permute-done((f32[768,400]{0,1:T(8,128)S(1)}, f32[768,400]{0,1:T(8,128)S(1)}, u32[]{:S(2)}, u32[]{:S(2)}) %collective-permute-start.4) | collective-permute-done | bytes 1228832 | tf_op jit(solution)/shard_map/ppermute | solution.py:10
  36.0 0.3 add_add_fusion.1
  36.3 0.0 copy-start.1
  36.3 1.6 %collective-permute-start.5 = (f32[768,400]{0,1:T(8,128)S(1)}, f32[768,400]{0,1:T(8,128)S(1)}, u32[]{:S(2)}, u32[]{:S(2)}) collective-permute-start(f32[768,400]{0,1:T(8,128)S(1)} %add_add_fusion.1), channel_id=1, source_target_pairs={{0,16},{8,24},{16,0},{24,8},{1,17},{9,25},{17,1},{25,9},{2,18},{10... | collective-permute-start | bytes 3686408 | tf_op jit(solution)/shard_map/ppermute | solution.py:10
  37.9 0.8 %dynamic-slice_subtract_fusion = s32[768]{0:T(1024)S(1)} fusion(s32[6144]{0:T(1024)} %param.9, s32[]{:T(128)S(6)} %select_n.101, s32[]{:T(128)S(6)} %mul.43), kind=kLoop, calls=%fused_computation.29 | loop fusion | flops 768 | bytes 6152 | tf_op jit(solution)/shard_map/sub | solution.py:78
  38.6 26.8 %collective-permute-done.5 = f32[768,400]{0,1:T(8,128)S(1)} collective-permute-done((f32[768,400]{0,1:T(8,128)S(1)}, f32[768,400]{0,1:T(8,128)S(1)}, u32[]{:S(2)}, u32[]{:S(2)}) %collective-permute-start.5) | collective-permute-done | bytes 1228832 | tf_op jit(solution)/shard_map/ppermute | solution.py:10
  65.4 0.5 copy.6
  65.9 2.2 %gather_fusion = f32[768,400]{1,0:T(8,128)S(1)} fusion(f32[768,400]{1,0:T(8,128)S(1)} %copy.6, s32[1024]{0:T(1024)S(1)} %pad_clamp_fusion), kind=kCustom, calls=%fused_computation | custom fusion | bytes 2460672 | tf_op jit(solution)/shard_map/jit(_take)/gather | solution.py:79
  68.1 0.0 copy-start.2
  68.1 1.5 %copy.7 = f32[768,400]{0,1:T(8,128)} copy(f32[768,400]{1,0:T(8,128)S(1)} %gather_fusion) | data formatting | bytes 2457600 | tf_op jit(solution)/shard_map/jit(_take)/gather | solution.py:79
  69.6 2.5 %sub.11 = f32[768,400]{0,1:T(8,128)} subtract(f32[768,400]{0,1:T(8,128)S(1)} %copy-done.2, f32[768,400]{0,1:T(8,128)} %copy.7) | non-fusion elementwise | flops 307200 | bytes 3686400 | tf_op jit(solution)/shard_map/sub | solution.py:79
  (9 shorter events, 0.0 us)
Async XLA Ops:
  0.0 19.2 %collective-permute-start = (bf16[800,400]{0,1:T(8,128)(2,1)}, bf16[800,400]{0,1:T(8,128)(2,1)S(1)}, u32[]{:S(2)}, u32[]{:S(2)}) collective-permute-start(bf16[800,400]{0,1:T(8,128)(2,1)} %param.6), channel_id=1, source_target_pairs={{0,16},{8,24},{16,0},{24,8},{1,17},{9,25},{17,1},{25,9},{2,18},{10... | collective-permute-start | bytes 1920008 | tf_op jit(solution)/shard_map/ppermute | solution.py:10
  3.0 18.1 %collective-permute-start.2 = (bf16[800,400]{0,1:T(8,128)(2,1)}, bf16[800,400]{0,1:T(8,128)(2,1)S(1)}, u32[]{:S(2)}, u32[]{:S(2)}) collective-permute-start(bf16[800,400]{0,1:T(8,128)(2,1)} %param.6), channel_id=1, source_target_pairs={{0,8},{8,0},{16,24},{24,16},{1,9},{9,1},{17,25},{25,17},{2,10},{10... | collective-permute-start | bytes 1920008 | tf_op jit(solution)/shard_map/ppermute | solution.py:10
  4.5 4.7 %copy-start.3 = (s32[400]{0:T(512)S(1)}, s32[400]{0:T(512)}, u32[]{:S(2)}) copy-start(s32[400]{0:T(512)} %param.8) | copy-start | bytes 4804
  6.2 16.6 %copy-start = (bf16[1536,3200]{1,0:T(8,128)(2,1)S(1)}, bf16[1536,3200]{1,0:T(8,128)(2,1)}, u32[]{:S(2)}) copy-start(bf16[1536,3200]{1,0:T(8,128)(2,1)} %param.5) | copy-start | bytes 29491204
  19.3 10.7 %collective-permute-start.1 = (bf16[400,400]{0,1:T(8,128)(2,1)S(1)}, bf16[400,400]{0,1:T(8,128)(2,1)S(1)}, u32[]{:S(2)}, u32[]{:S(2)}) collective-permute-start(bf16[400,400]{0,1:T(8,128)(2,1)S(1)} %slice.10), channel_id=1, source_target_pairs={{0,8},{8,0},{16,24},{24,16},{1,9},{9,1},{17,25},{25,17},{2,10},{10... | collective-permute-start | bytes 960008 | tf_op jit(solution)/shard_map/ppermute | solution.py:10
  21.2 10.1 %collective-permute-start.3 = (bf16[400,400]{0,1:T(8,128)(2,1)S(1)}, bf16[400,400]{0,1:T(8,128)(2,1)S(1)}, u32[]{:S(2)}, u32[]{:S(2)}) collective-permute-start(bf16[400,400]{0,1:T(8,128)(2,1)S(1)} %slice.11), channel_id=1, source_target_pairs={{0,16},{8,24},{16,0},{24,8},{1,17},{9,25},{17,1},{25,9},{2,18},{10... | collective-permute-start | bytes 960008 | tf_op jit(solution)/shard_map/ppermute | solution.py:10
  33.0 3.0 %collective-permute-start.4 = (f32[768,400]{0,1:T(8,128)S(1)}, f32[768,400]{0,1:T(8,128)S(1)}, u32[]{:S(2)}, u32[]{:S(2)}) collective-permute-start(f32[768,400]{0,1:T(8,128)S(1)} %add_add_fusion), channel_id=1, source_target_pairs={{0,1},{1,0},{2,3},{3,2},{4,5},{5,4},{6,7},{7,6},{8,9},{9,8},{10,11... | collective-permute-start | bytes 3686408 | tf_op jit(solution)/shard_map/ppermute | solution.py:10
  36.3 2.4 %copy-start.1 = (f32[768,400]{0,1:T(8,128)}, f32[768,400]{0,1:T(8,128)S(1)}, u32[]{:S(2)}) copy-start(f32[768,400]{0,1:T(8,128)S(1)} %add_add_fusion.1) | copy-start | bytes 3686404
  36.3 29.1 %collective-permute-start.5 = (f32[768,400]{0,1:T(8,128)S(1)}, f32[768,400]{0,1:T(8,128)S(1)}, u32[]{:S(2)}, u32[]{:S(2)}) collective-permute-start(f32[768,400]{0,1:T(8,128)S(1)} %add_add_fusion.1), channel_id=1, source_target_pairs={{0,16},{8,24},{16,0},{24,8},{1,17},{9,25},{17,1},{25,9},{2,18},{10... | collective-permute-start | bytes 3686408 | tf_op jit(solution)/shard_map/ppermute | solution.py:10
  68.1 1.5 %copy-start.2 = (f32[768,400]{0,1:T(8,128)S(1)}, f32[768,400]{0,1:T(8,128)}, u32[]{:S(2)}) copy-start(f32[768,400]{0,1:T(8,128)} %copy-done.1) | copy-start | bytes 3686404

commit v15 on v14

--- a/solution.py
+++ b/solution.py
@@ -12,6 +12,18 @@
 
 def gather_prow(own, prow_idx, prow_count):
     count = own.shape[0]
+    if prow_count == 4 and count % 32 == 0:
+        h = count // 2
+        q = count // 4
+        sends = [(swap(own[:h], "prow", 1), swap(own[:h], "prow", 2)),
+                 (swap(own[h:], "prow", 1), swap(own[h:], "prow", 2))]
+        diags = [jnp.concatenate([swap(y[:q], "prow", 1), swap(x[q:], "prow", 2)], axis=0) for x, y in sends]
+        base = [jnp.bitwise_xor(prow_idx, m) * count for m in range(4)]
+        return [[(own, base[0])],
+                [(sends[0][0], base[1]), (sends[0][1], base[2])],
+                [(sends[1][0], base[1] + h), (sends[1][1], base[2] + h)],
+                [(diags[0], base[3])],
+                [(diags[1], base[3] + h)]]
     if prow_count == 4 and count % 32 == 0:
         half = count // 2
         from_x = swap(own, "prow", 1)

time: 72.4 us -> 79.4 us (1.097)
  starting transfers between devices: 9.47 us -> 13 us
  matrix products: 14.5 us -> 17.9 us
  waiting for transfers between devices: 38.2 us -> 37.4 us
    ppermute x6 -> x10, starting transfers between devices: 9.47 us -> 13 us  [swap(): lax.ppermute(value, axis, [(i, i ^ mask) for i in range(lax.axis_size(axi...]
    dot_general x10 -> x14, matrix products: 14.5 us -> 17.9 us  [contract(): product = jnp.dot(window, blocked, preferred_element_type=jnp.float32)]
    slice x2 -> x5, local copies, waits for them, and re-layouts: 0.23 us -> 2.32 us  [the longest x1 2.05 us: gather_prow(): own[:h]]
    dynamic_slice x2, local copies, waits for them, and re-layouts: 1.73 us -> 0.19 us  [contract(): lax.dynamic_slice_in_dim(labels, o, b.shape[0])[:, None]]
    ppermute x6 -> x10, waiting for transfers between devices: 38.2 us -> 37.4 us  [swap(): lax.ppermute(value, axis, [(i, i ^ mask) for i in range(lax.axis_size(axi...]
  transfers between devices with their start and end apart: 6 -> 10, of which waited for: 5 -> 4; matrix products, arithmetic and copies ran while one was open for 22% -> 21% of each run, Pallas kernels for 0% -> 0%
where the time goes in v15:
time: 79.4 us; the launch traced here: 79.1 us
  waiting for transfers between devices  37.4 us (47%)
  matrix products  17.9 us (23%)
  starting transfers between devices  13 us (16%)
  local copies, waits for them, and re-layouts  6.66 us (8%)
  other arithmetic  3.93 us (5%)
    ppermute x10, waiting for transfers between devices, swap(): lax.ppermute(value, axis, [(i, i ^ mask) for i in range(lax.axis_size(axi...  37.4 us
    dot_general x14, matrix products, contract(): product = jnp.dot(window, blocked, preferred_element_type=jnp.float32)  17.9 us
    ppermute x10, starting transfers between devices, swap(): lax.ppermute(value, axis, [(i, i ^ mask) for i in range(lax.axis_size(axi...  13 us
    gather x2, local copies, waits for them, and re-layouts, shards(): return cycle - jnp.take(fetched, local, axis=0, mode='clip')  3.67 us
    sub x1, other arithmetic, shards(): return cycle - jnp.take(fetched, local, axis=0, mode='clip')  2.46 us
    slice x1, local copies, waits for them, and re-layouts, gather_prow(): own[:h]  2.05 us
  transfers between devices with their start and end apart: 10, of which 4 were waited for; matrix products, arithmetic and copies ran while one was open for 21% of the time, Pallas kernels for 0%

profile of v15, /device:TPU:0, one launch (start us, length us, event | category | flops | bytes accessed | tf_op | source)
XLA Modules:
  0.0 79.1 jit_solution(5656636240599760405)
XLA Ops:
  0.0 2.0 %fusion.42 = (bf16[400,400]{0,1:T(8,128)(2,1)}, bf16[400,400]{0,1:T(8,128)(2,1)S(1)}) fusion(bf16[800,400]{0,1:T(8,128)(2,1)} %param.6), kind=kLoop, calls=%fused_computation.58 | loop fusion | bytes 1280000 | tf_op jit(solution)/shard_map/slice | solution.py:18
  2.1 3.0 %collective-permute-start.5 = (bf16[400,400]{0,1:T(8,128)(2,1)}, bf16[400,400]{0,1:T(8,128)(2,1)S(1)}, u32[]{:S(2)}, u32[]{:S(2)}) collective-permute-start(bf16[400,400]{0,1:T(8,128)(2,1)} %get-tuple-element.11), channel_id=1, source_target_pairs={{0,16},{8,24},{16,0},{24,8},{1,17},{9,25},{17,1},{25,9},{2,18},{10... | collective-permute-start | bytes 960008 | tf_op jit(solution)/shard_map/ppermute | solution.py:10
  5.0 1.5 %collective-permute-start.4 = (bf16[400,400]{0,1:T(8,128)(2,1)}, bf16[400,400]{0,1:T(8,128)(2,1)S(1)}, u32[]{:S(2)}, u32[]{:S(2)}) collective-permute-start(bf16[400,400]{0,1:T(8,128)(2,1)} %get-tuple-element.11), channel_id=1, source_target_pairs={{0,8},{8,0},{16,24},{24,16},{1,9},{9,1},{17,25},{25,17},{2,10},{10... | collective-permute-start | bytes 960008 | tf_op jit(solution)/shard_map/ppermute | solution.py:10
  6.5 0.5 collective-permute-start
  7.1 2.8 %fusion.6 = f32[768,400]{0,1:T(8,128)S(1)} fusion(bf16[1536,3200]{1,0:T(8,128)(2,1)} %param.5, s32[]{:T(128)S(6)} %select_n.127, s32[]{:T(128)S(6)} %select_n.107, bf16[800,400]{0,1:T(8,128)(2,1)} %param.6, s32[800]{0:T(1024)S(1)} %dynamic_slice.92, s32[400]{0:T(512)S(1)} %copy-done.3), kind=kOutput, calls=%fused_computation.12 | convolution fusion | flops 492160000 | bytes 3326664 | tf_op jit(solution)/shard_map/dot_general | solution.py:55
  10.0 2.9 %fusion.8 = f32[768,400]{0,1:T(8,128)S(1)} fusion(bf16[1536,3200]{1,0:T(8,128)(2,1)} %param.5, s32[]{:T(128)S(6)} %select_n.105, s32[]{:T(128)S(6)} %select_n.107, bf16[800,400]{0,1:T(8,128)(2,1)} %param.6, s32[800]{0:T(1024)S(1)} %dynamic_slice.92, s32[400]{0:T(512)S(1)} %copy-done.3), kind=kOutput, calls=%fused_computation.14 | convolution fusion | flops 492160000 | bytes 3326664 | tf_op jit(solution)/shard_map/dot_general | solution.py:55
  13.0 2.5 %collective-permute-done.5 = bf16[400,400]{0,1:T(8,128)(2,1)S(1)} collective-permute-done((bf16[400,400]{0,1:T(8,128)(2,1)}, bf16[400,400]{0,1:T(8,128)(2,1)S(1)}, u32[]{:S(2)}, u32[]{:S(2)}) %collective-permute-start.5) | collective-permute-done | bytes 320032 | tf_op jit(solution)/shard_map/ppermute | solution.py:10
  15.5 2.1 %collective-permute-start.6 = (bf16[200,400]{0,1:T(8,128)(2,1)S(1)}, bf16[200,400]{0,1:T(8,128)(2,1)S(1)}, u32[]{:S(2)}, u32[]{:S(2)}) collective-permute-start(bf16[200,400]{0,1:T(8,128)(2,1)S(1)} %slice.30), channel_id=1, source_target_pairs={{0,8},{8,0},{16,24},{24,16},{1,9},{9,1},{17,25},{25,17},{2,10},{10... | collective-permute-start | bytes 480008 | tf_op jit(solution)/shard_map/ppermute | solution.py:10
  17.8 1.6 %collective-permute-start.7 = (bf16[200,400]{0,1:T(8,128)(2,1)S(1)}, bf16[200,400]{0,1:T(8,128)(2,1)S(1)}, u32[]{:S(2)}, u32[]{:S(2)}) collective-permute-start(bf16[200,400]{0,1:T(8,128)(2,1)S(1)} %slice.31), channel_id=1, source_target_pairs={{0,16},{8,24},{16,0},{24,8},{1,17},{9,25},{17,1},{25,9},{2,18},{10... | collective-permute-start | bytes 480008 | tf_op jit(solution)/shard_map/ppermute | solution.py:10
  19.4 4.9 %collective-permute-done = bf16[400,400]{0,1:T(8,128)(2,1)S(1)} collective-permute-done((bf16[400,400]{0,1:T(8,128)(2,1)S(1)}, bf16[400,400]{0,1:T(8,128)(2,1)S(1)}, u32[]{:S(2)}, u32[]{:S(2)}) %collective-permute-start) | collective-permute-done | bytes 320032 | tf_op jit(solution)/shard_map/ppermute | solution.py:10
  24.3 2.1 %collective-permute-start.1 = (bf16[200,400]{0,1:T(8,128)(2,1)S(1)}, bf16[200,400]{0,1:T(8,128)(2,1)S(1)}, u32[]{:S(2)}, u32[]{:S(2)}) collective-permute-start(bf16[200,400]{0,1:T(8,128)(2,1)S(1)} %slice.28), channel_id=1, source_target_pairs={{0,8},{8,0},{16,24},{24,16},{1,9},{9,1},{17,25},{25,17},{2,10},{10... | collective-permute-start | bytes 480008 | tf_op jit(solution)/shard_map/ppermute | solution.py:10
  26.6 1.6 %collective-permute-start.3 = (bf16[200,400]{0,1:T(8,128)(2,1)S(1)}, bf16[200,400]{0,1:T(8,128)(2,1)S(1)}, u32[]{:S(2)}, u32[]{:S(2)}) collective-permute-start(bf16[200,400]{0,1:T(8,128)(2,1)S(1)} %slice.29), channel_id=1, source_target_pairs={{0,16},{8,24},{16,0},{24,8},{1,17},{9,25},{17,1},{25,9},{2,18},{10... | collective-permute-start | bytes 480008 | tf_op jit(solution)/shard_map/ppermute | solution.py:10
  28.1 2.0 %fusion.16 = f32[768,400]{0,1:T(8,128)S(1)} fusion(bf16[1536,3200]{1,0:T(8,128)(2,1)} %param.5, s32[]{:T(128)S(6)} %select_n.127, s32[]{:T(128)S(6)} %select_n.121, bf16[400,400]{0,1:T(8,128)(2,1)S(1)} %collective-permute-done, s32[400]{0:T(512)S(1)} %get-tuple-element.14, s32[400]{0:T(512)S(1)} %copy-done.3), kind=kOutput, calls=%fused_computation.29 | convolution fusion | flops 246080000 | bytes 2338440 | tf_op jit(solution)/shard_map/dot_general | solution.py:55
  30.1 2.0 %fusion.24 = f32[768,400]{0,1:T(8,128)S(1)} fusion(bf16[1536,3200]{1,0:T(8,128)(2,1)} %param.5, s32[]{:T(128)S(6)} %select_n.105, s32[]{:T(128)S(6)} %select_n.121, bf16[400,400]{0,1:T(8,128)(2,1)S(1)} %collective-permute-done, s32[400]{0:T(512)S(1)} %get-tuple-element.14, s32[400]{0:T(512)S(1)} %copy-done.3), kind=kOutput, calls=%fused_computation.37 | convolution fusion | flops 246080000 | bytes 2338440 | tf_op jit(solution)/shard_map/dot_general | solution.py:55
  32.1 0.8 fusion.18
  32.9 0.8 %convolution_add_fusion.1 = f32[768,400]{0,1:T(8,128)S(1)} fusion(f32[768,400]{0,1:T(8,128)S(1)} %fusion.6, bf16[1536,3200]{1,0:T(8,128)(2,1)S(1)} %copy-done, s32[]{:T(128)S(6)} %select_n.127, s32[]{:T(128)S(6)} %select_n.112, bf16[400,400]{0,1:T(8,128)(2,1)S(1)} %collective-permute-done.4, s32[400]{0:T(512)S(1)} %get-tuple-element.17, s32[400]{0:T(512)S(1)} %copy-done.3), kind=kOutput, calls=%fused_computation.6 | convolution fusion | flops 246387200 | bytes 3657736 | tf_op jit(solution)/shard_map/dot_general | solution.py:55
  33.7 0.8 %convolution_add_fusion.3 = f32[768,400]{0,1:T(8,128)S(1)} fusion(f32[768,400]{0,1:T(8,128)S(1)} %fusion.8, bf16[1536,3200]{1,0:T(8,128)(2,1)S(1)} %copy-done, s32[]{:T(128)S(6)} %select_n.105, s32[]{:T(128)S(6)} %select_n.112, bf16[400,400]{0,1:T(8,128)(2,1)S(1)} %collective-permute-done.4, s32[400]{0:T(512)S(1)} %get-tuple-element.17, s32[400]{0:T(512)S(1)} %copy-done.3), kind=kOutput, calls=%fused_computation.11 | convolution fusion | flops 246387200 | bytes 3657736 | tf_op jit(solution)/shard_map/dot_general | solution.py:55
  34.5 0.8 fusion.26
  35.4 0.8 %fusion.14 = f32[768,400]{0,1:T(8,128)S(1)} fusion(bf16[1536,3200]{1,0:T(8,128)(2,1)S(1)} %copy-done, s32[]{:T(128)S(6)} %select_n.127, s32[]{:T(128)S(6)} %select_n.124, bf16[200,400]{0,1:T(8,128)(2,1)S(1)} %collective-permute-done.7, bf16[200,400]{0,1:T(8,128)(2,1)S(1)} %collective-permute-done.6, s32[400]{0:T(512)S(1)} %get-tuple-element.18, ...), kind=kOutput, calls=%fused_computation.27 | convolution fusion | flops 246720000 | bytes 2428936 | tf_op jit(solution)/shard_map/dot_general | solution.py:55
  36.2 0.8 %fusion.22 = f32[768,400]{0,1:T(8,128)S(1)} fusion(bf16[1536,3200]{1,0:T(8,128)(2,1)S(1)} %copy-done, s32[]{:T(128)S(6)} %select_n.105, s32[]{:T(128)S(6)} %select_n.124, bf16[200,400]{0,1:T(8,128)(2,1)S(1)} %collective-permute-done.7, bf16[200,400]{0,1:T(8,128)(2,1)S(1)} %collective-permute-done.6, s32[400]{0:T(512)S(1)} %get-tuple-element.18, ...), kind=kOutput, calls=%fused_computation.35 | convolution fusion | flops 246720000 | bytes 2428936 | tf_op jit(solution)/shard_map/dot_general | solution.py:55
  37.2 0.9 %fusion.2 = f32[768,400]{0,1:T(8,128)S(1)} fusion(f32[768,400]{0,1:T(8,128)S(1)} %fusion.14, f32[768,400]{0,1:T(8,128)S(1)} %fusion.16, f32[768,400]{0,1:T(8,128)S(1)} %fusion.18, f32[768,400]{0,1:T(8,128)S(1)} %convolution_add_fusion.1, bf16[1536,3200]{1,0:T(8,128)(2,1)S(1)} %copy-done, s32[]{:T(128)S(6)} %select_n.127, s32[]{:T(128)S(6)} %select_n.115, ...), kind=kOutput, calls=%fused_computation.5 | convolution fusion | flops 247308800 | bytes 7344136 | tf_op jit(solution)/shard_map/dot_general | solution.py:55
  38.1 0.9 %fusion.5 = f32[768,400]{0,1:T(8,128)S(1)} fusion(f32[768,400]{0,1:T(8,128)S(1)} %fusion.22, f32[768,400]{0,1:T(8,128)S(1)} %fusion.24, f32[768,400]{0,1:T(8,128)S(1)} %fusion.26, f32[768,400]{0,1:T(8,128)S(1)} %convolution_add_fusion.3, bf16[1536,3200]{1,0:T(8,128)(2,1)S(1)} %copy-done, s32[]{:T(128)S(6)} %select_n.105, s32[]{:T(128)S(6)} %select_n.115, ...), kind=kOutput, calls=%fused_computation.10 | convolution fusion | flops 247308800 | bytes 7344136 | tf_op jit(solution)/shard_map/dot_general | solution.py:55
  39.0 0.8 fusion.10
  40.2 0.8 fusion.12
  41.0 2.1 %collective-permute-done.8 = f32[768,400]{0,1:T(8,128)S(1)} collective-permute-done((f32[768,400]{0,1:T(8,128)S(1)}, f32[768,400]{0,1:T(8,128)S(1)}, u32[]{:S(2)}, u32[]{:S(2)}) %collective-permute-start.8) | collective-permute-done | bytes 1228832 | tf_op jit(solution)/shard_map/ppermute | solution.py:10
  43.4 0.6 collective-permute-start.9
  43.9 0.8 dynamic-slice_subtract_fusion
  44.7 27.8 %collective-permute-done.9 = f32[768,400]{0,1:T(8,128)S(1)} collective-permute-done((f32[768,400]{0,1:T(8,128)S(1)}, f32[768,400]{0,1:T(8,128)S(1)}, u32[]{:S(2)}, u32[]{:S(2)}) %collective-permute-start.9) | collective-permute-done | bytes 1228832 | tf_op jit(solution)/shard_map/ppermute | solution.py:10
  72.5 0.5 copy.6
  73.0 2.2 %gather_fusion = f32[768,400]{1,0:T(8,128)S(1)} fusion(f32[768,400]{1,0:T(8,128)S(1)} %copy.6, s32[1024]{0:T(1024)S(1)} %pad_clamp_fusion), kind=kCustom, calls=%fused_computation | custom fusion | bytes 2460672 | tf_op jit(solution)/shard_map/jit(_take)/gather | solution.py:91
  75.1 1.5 %copy.7 = f32[768,400]{0,1:T(8,128)} copy(f32[768,400]{1,0:T(8,128)S(1)} %gather_fusion) | data formatting | bytes 2457600 | tf_op jit(solution)/shard_map/jit(_take)/gather | solution.py:91
  76.6 2.5 %sub.11 = f32[768,400]{0,1:T(8,128)} subtract(f32[768,400]{0,1:T(8,128)S(1)} %copy-done.2, f32[768,400]{0,1:T(8,128)} %copy.7) | non-fusion elementwise | flops 307200 | bytes 3686400 | tf_op jit(solution)/shard_map/sub | solution.py:91
  (28 shorter events, 1.3 us)
Async XLA Ops:
  0.0 7.1 %copy-start.4 = (s32[6400]{0:T(1024)S(1)}, s32[6400]{0:T(1024)}, u32[]{:S(2)}) copy-start(s32[6400]{0:T(1024)} %param.7) | copy-start | bytes 76804
  0.0 7.1 %copy-start.3 = (s32[400]{0:T(512)S(1)}, s32[400]{0:T(512)}, u32[]{:S(2)}) copy-start(s32[400]{0:T(512)} %param.8) | copy-start | bytes 4804
  2.1 13.5 %collective-permute-start.5 = (bf16[400,400]{0,1:T(8,128)(2,1)}, bf16[400,400]{0,1:T(8,128)(2,1)S(1)}, u32[]{:S(2)}, u32[]{:S(2)}) collective-permute-start(bf16[400,400]{0,1:T(8,128)(2,1)} %get-tuple-element.11), channel_id=1, source_target_pairs={{0,16},{8,24},{16,0},{24,8},{1,17},{9,25},{17,1},{25,9},{2,18},{10... | collective-permute-start | bytes 960008 | tf_op jit(solution)/shard_map/ppermute | solution.py:10
  5.0 12.6 %collective-permute-start.4 = (bf16[400,400]{0,1:T(8,128)(2,1)}, bf16[400,400]{0,1:T(8,128)(2,1)S(1)}, u32[]{:S(2)}, u32[]{:S(2)}) collective-permute-start(bf16[400,400]{0,1:T(8,128)(2,1)} %get-tuple-element.11), channel_id=1, source_target_pairs={{0,8},{8,0},{16,24},{24,16},{1,9},{9,1},{17,25},{25,17},{2,10},{10... | collective-permute-start | bytes 960008 | tf_op jit(solution)/shard_map/ppermute | solution.py:10
  6.5 17.8 %collective-permute-start = (bf16[400,400]{0,1:T(8,128)(2,1)S(1)}, bf16[400,400]{0,1:T(8,128)(2,1)S(1)}, u32[]{:S(2)}, u32[]{:S(2)}) collective-permute-start(bf16[400,400]{0,1:T(8,128)(2,1)S(1)} %get-tuple-element.12), channel_id=1, source_target_pairs={{0,16},{8,24},{16,0},{24,8},{1,17},{9,25},{17,1},{25,9},{2,18},{10... | collective-permute-start | bytes 960008 | tf_op jit(solution)/shard_map/ppermute | solution.py:10
  7.0 19.4 %collective-permute-start.2 = (bf16[400,400]{0,1:T(8,128)(2,1)S(1)}, bf16[400,400]{0,1:T(8,128)(2,1)S(1)}, u32[]{:S(2)}, u32[]{:S(2)}) collective-permute-start(bf16[400,400]{0,1:T(8,128)(2,1)S(1)} %get-tuple-element.12), channel_id=1, source_target_pairs={{0,8},{8,0},{16,24},{24,16},{1,9},{9,1},{17,25},{25,17},{2,10},{10... | collective-permute-start | bytes 960008 | tf_op jit(solution)/shard_map/ppermute | solution.py:10
  10.0 22.1 %copy-start = (bf16[1536,3200]{1,0:T(8,128)(2,1)S(1)}, bf16[1536,3200]{1,0:T(8,128)(2,1)}, u32[]{:S(2)}) copy-start(bf16[1536,3200]{1,0:T(8,128)(2,1)} %param.5) | copy-start | bytes 29491204
  15.5 19.8 %collective-permute-start.6 = (bf16[200,400]{0,1:T(8,128)(2,1)S(1)}, bf16[200,400]{0,1:T(8,128)(2,1)S(1)}, u32[]{:S(2)}, u32[]{:S(2)}) collective-permute-start(bf16[200,400]{0,1:T(8,128)(2,1)S(1)} %slice.30), channel_id=1, source_target_pairs={{0,8},{8,0},{16,24},{24,16},{1,9},{9,1},{17,25},{25,17},{2,10},{10... | collective-permute-start | bytes 480008 | tf_op jit(solution)/shard_map/ppermute | solution.py:10
  17.8 17.6 %collective-permute-start.7 = (bf16[200,400]{0,1:T(8,128)(2,1)S(1)}, bf16[200,400]{0,1:T(8,128)(2,1)S(1)}, u32[]{:S(2)}, u32[]{:S(2)}) collective-permute-start(bf16[200,400]{0,1:T(8,128)(2,1)S(1)} %slice.31), channel_id=1, source_target_pairs={{0,16},{8,24},{16,0},{24,8},{1,17},{9,25},{17,1},{25,9},{2,18},{10... | collective-permute-start | bytes 480008 | tf_op jit(solution)/shard_map/ppermute | solution.py:10
  24.3 12.7 %collective-permute-start.1 = (bf16[200,400]{0,1:T(8,128)(2,1)S(1)}, bf16[200,400]{0,1:T(8,128)(2,1)S(1)}, u32[]{:S(2)}, u32[]{:S(2)}) collective-permute-start(bf16[200,400]{0,1:T(8,128)(2,1)S(1)} %slice.28), channel_id=1, source_target_pairs={{0,8},{8,0},{16,24},{24,16},{1,9},{9,1},{17,25},{25,17},{2,10},{10... | collective-permute-start | bytes 480008 | tf_op jit(solution)/shard_map/ppermute | solution.py:10
  26.6 10.5 %collective-permute-start.3 = (bf16[200,400]{0,1:T(8,128)(2,1)S(1)}, bf16[200,400]{0,1:T(8,128)(2,1)S(1)}, u32[]{:S(2)}, u32[]{:S(2)}) collective-permute-start(bf16[200,400]{0,1:T(8,128)(2,1)S(1)} %slice.29), channel_id=1, source_target_pairs={{0,16},{8,24},{16,0},{24,8},{1,17},{9,25},{17,1},{25,9},{2,18},{10... | collective-permute-start | bytes 480008 | tf_op jit(solution)/shard_map/ppermute | solution.py:10
  40.1 3.0 %collective-permute-start.8 = (f32[768,400]{0,1:T(8,128)S(1)}, f32[768,400]{0,1:T(8,128)S(1)}, u32[]{:S(2)}, u32[]{:S(2)}) collective-permute-start(f32[768,400]{0,1:T(8,128)S(1)} %add.173), channel_id=1, source_target_pairs={{0,1},{1,0},{2,3},{3,2},{4,5},{5,4},{6,7},{7,6},{8,9},{9,8},{10,11... | collective-permute-start | bytes 3686408 | tf_op jit(solution)/shard_map/ppermute | solution.py:10
  43.3 1.4 %copy-start.1 = (f32[768,400]{0,1:T(8,128)}, f32[768,400]{0,1:T(8,128)S(1)}, u32[]{:S(2)}) copy-start(f32[768,400]{0,1:T(8,128)S(1)} %add_add_fusion) | copy-start | bytes 3686404
  43.4 29.1 %collective-permute-start.9 = (f32[768,400]{0,1:T(8,128)S(1)}, f32[768,400]{0,1:T(8,128)S(1)}, u32[]{:S(2)}, u32[]{:S(2)}) collective-permute-start(f32[768,400]{0,1:T(8,128)S(1)} %add_add_fusion), channel_id=1, source_target_pairs={{0,16},{8,24},{16,0},{24,8},{1,17},{9,25},{17,1},{25,9},{2,18},{10... | collective-permute-start | bytes 3686408 | tf_op jit(solution)/shard_map/ppermute | solution.py:10
  75.1 1.5 %copy-start.2 = (f32[768,400]{0,1:T(8,128)S(1)}, f32[768,400]{0,1:T(8,128)}, u32[]{:S(2)}) copy-start(f32[768,400]{0,1:T(8,128)} %copy-done.1) | copy-start | bytes 3686404

commit v16 on v14

--- a/solution.py
+++ b/solution.py
@@ -59,24 +59,23 @@
     terms = contract(amplitudes, groups, firsts, block_rows, labels, irrep_cols)
     sent = list(zip(others, terms[:-1]))
     kept = terms[-1]
-    pieces = 1
-    step = block_rows // pieces
+    cycle = kept
+    for s, part in sent:
+        cycle = cycle + swap(part, "cuts", s)
     half = prow_count // 2
-    fetched = []
-    cycle = []
-    for h in range(pieces):
-        total = kept[h * step:(h + 1) * step]
-        for s, part in sent:
-            total = total + swap(part[h * step:(h + 1) * step], "cuts", s)
-        cycle.append(total)
-        fetched.append(swap(total, "prow", half))
-    cycle = jnp.concatenate(cycle, axis=0) if pieces > 1 else cycle[0]
-    fetched = jnp.concatenate(fetched, axis=0) if pieces > 1 else fetched[0]
     own_block = prow_idx * cuts_count + cuts_idx
     partner_block = jnp.bitwise_xor(prow_idx, half) * cuts_count + cuts_idx
     mine = lax.dynamic_slice(mirror_row, (own_block * block_rows,), (block_rows,))
     local = mine - partner_block * block_rows
-    return cycle - jnp.take(fetched, local, axis=0, mode="clip")
+    cols = cycle.shape[1]
+    pieces = 2 if cols % 16 == 0 else 1
+    step = cols // pieces
+    results = []
+    for j in range(pieces):
+        piece = cycle[:, j * step:(j + 1) * step]
+        fetched = swap(piece, "prow", half)
+        results.append(piece - jnp.take(fetched, local, axis=0, mode="clip"))
+    return jnp.concatenate(results, axis=1) if pieces > 1 else results[0]
 
 
 def solution(mesh):

time: 72.4 us -> 71.6 us (0.989)
  local copies, waits for them, and re-layouts: 6.1 us -> 9.2 us
  waiting for transfers between devices: 38.2 us -> 35.2 us
  other arithmetic: 3.53 us -> 2.25 us
    ppermute x6 -> x7, waiting for transfers between devices: 38.2 us -> 35.2 us  [swap(): lax.ppermute(value, axis, [(i, i ^ mask) for i in range(lax.axis_size(axi...]
    sub x1 -> x2, other arithmetic: 2.46 us -> 1.17 us  [shards(): results.append(piece - jnp.take(fetched, local, axis=0, mode='clip'))]
    ppermute x1 -> x2, local copies, waits for them, and re-layouts: 0.46 us -> 1.6 us  [swap(): lax.ppermute(value, axis, [(i, i ^ mask) for i in range(lax.axis_size(axi...]
    gather x2 -> x4, local copies, waits for them, and re-layouts: 3.65 us -> 4.72 us  [shards(): results.append(piece - jnp.take(fetched, local, axis=0, mode='clip'))]
    slice x0 -> x1, local copies, waits for them, and re-layouts: none -> 0.92 us  [shards(): piece = cycle[:, j * step:(j + 1) * step]]
    ppermute x6 -> x7, starting transfers between devices: 9.47 us -> 9.92 us  [swap(): lax.ppermute(value, axis, [(i, i ^ mask) for i in range(lax.axis_size(axi...]
  transfers between devices with their start and end apart: 6 -> 7, of which waited for: 5 -> 6; matrix products, arithmetic and copies ran while one was open for 22% -> 26% of each run, Pallas kernels for 0% -> 0%
where the time goes in v16:
time: 71.6 us; the launch traced here: 71.2 us
  waiting for transfers between devices  35.2 us (49%)
  matrix products  14.5 us (20%)
  starting transfers between devices  9.92 us (14%)
  local copies, waits for them, and re-layouts  9.2 us (13%)
  other arithmetic  2.25 us (3%)
    ppermute x7, waiting for transfers between devices, swap(): lax.ppermute(value, axis, [(i, i ^ mask) for i in range(lax.axis_size(axi...  35.2 us
    dot_general x10, matrix products, contract(): product = jnp.dot(window, blocked, preferred_element_type=jnp.float32)  14.5 us
    ppermute x7, starting transfers between devices, swap(): lax.ppermute(value, axis, [(i, i ^ mask) for i in range(lax.axis_size(axi...  9.92 us
    gather x4, local copies, waits for them, and re-layouts, shards(): results.append(piece - jnp.take(fetched, local, axis=0, mode='clip'))  4.72 us
    dynamic_slice x2, local copies, waits for them, and re-layouts, contract(): lax.dynamic_slice_in_dim(labels, o, b.shape[0])[:, None]  1.73 us
    ppermute x2, local copies, waits for them, and re-layouts, swap(): lax.ppermute(value, axis, [(i, i ^ mask) for i in range(lax.axis_size(axi...  1.6 us
  transfers between devices with their start and end apart: 7, of which 6 were waited for; matrix products, arithmetic and copies ran while one was open for 26% of the time, Pallas kernels for 0%

profile of v16, /device:TPU:0, one launch (start us, length us, event | category | flops | bytes accessed | tf_op | source)
XLA Modules:
  0.0 71.2 jit_solution(5391772352912765303)
XLA Ops:
  0.0 3.0 %collective-permute-start = (bf16[800,400]{0,1:T(8,128)(2,1)}, bf16[800,400]{0,1:T(8,128)(2,1)S(1)}, u32[]{:S(2)}, u32[]{:S(2)}) collective-permute-start(bf16[800,400]{0,1:T(8,128)(2,1)} %param.6), channel_id=1, source_target_pairs={{0,16},{8,24},{16,0},{24,8},{1,17},{9,25},{17,1},{25,9},{2,18},{10... | collective-permute-start | bytes 1920008 | tf_op jit(solution)/shard_map/ppermute | solution.py:10
  3.0 1.5 %collective-permute-start.2 = (bf16[800,400]{0,1:T(8,128)(2,1)}, bf16[800,400]{0,1:T(8,128)(2,1)S(1)}, u32[]{:S(2)}, u32[]{:S(2)}) collective-permute-start(bf16[800,400]{0,1:T(8,128)(2,1)} %param.6), channel_id=1, source_target_pairs={{0,8},{8,0},{16,24},{24,16},{1,9},{9,1},{17,25},{25,17},{2,10},{10... | collective-permute-start | bytes 1920008 | tf_op jit(solution)/shard_map/ppermute | solution.py:10
  4.5 0.9 %fusion.30 = (s32[800]{0:T(1024)S(1)}, s32[800]{0:T(1024)S(1)}, s32[800]{0:T(1024)S(1)}) fusion(s32[6400]{0:T(1024)} %param.7, s32[]{:T(128)S(6)} %dynamic_slice.73, s32[]{:T(128)S(6)} %dynamic_slice.70, s32[]{:T(128)S(6)} %dynamic_slice.67), kind=kLoop, calls=%fused_computation.46 | loop fusion | bytes 19212 | tf_op jit(solution)/shard_map/dynamic_slice | solution.py:41
  5.3 0.8 %fusion.29 = (s32[400]{0:T(512)S(1)}, s32[400]{0:T(512)S(1)}) fusion(s32[6400]{0:T(1024)} %param.7, s32[]{:T(128)S(6)} %dynamic_slice.82, s32[]{:T(128)S(6)} %dynamic_slice.79), kind=kLoop, calls=%fused_computation.45 | loop fusion | bytes 6408 | tf_op jit(solution)/shard_map/dynamic_slice | solution.py:41
  6.2 3.0 %fusion.6 = f32[768,400]{0,1:T(8,128)S(1)} fusion(bf16[1536,3200]{1,0:T(8,128)(2,1)} %param.5, s32[]{:T(128)S(6)} %select_n.81, s32[]{:T(128)S(6)} %select_n.83, bf16[800,400]{0,1:T(8,128)(2,1)} %param.6, s32[800]{0:T(1024)S(1)} %get-tuple-element.21, s32[400]{0:T(512)} %param.8), kind=kOutput, calls=%fused_computation.15 | convolution fusion | flops 492160000 | bytes 3327112 | tf_op jit(solution)/shard_map/dot_general | solution.py:43
  9.2 3.3 %fusion.2 = f32[768,400]{0,1:T(8,128)S(1)} fusion(bf16[1536,3200]{1,0:T(8,128)(2,1)} %param.5, s32[]{:T(128)S(6)} %select_n.94, s32[]{:T(128)S(6)} %select_n.83, bf16[800,400]{0,1:T(8,128)(2,1)} %param.6, s32[800]{0:T(1024)S(1)} %get-tuple-element.21, s32[400]{0:T(512)S(1)} %copy-done.1), kind=kOutput, calls=%fused_computation.11 | convolution fusion | flops 492160000 | bytes 3326664 | tf_op jit(solution)/shard_map/dot_general | solution.py:43
  12.5 6.7 %collective-permute-done = bf16[800,400]{0,1:T(8,128)(2,1)S(1)} collective-permute-done((bf16[800,400]{0,1:T(8,128)(2,1)}, bf16[800,400]{0,1:T(8,128)(2,1)S(1)}, u32[]{:S(2)}, u32[]{:S(2)}) %collective-permute-start) | collective-permute-done | bytes 640032 | tf_op jit(solution)/shard_map/ppermute | solution.py:10
  19.3 1.8 %collective-permute-start.1 = (bf16[400,400]{0,1:T(8,128)(2,1)S(1)}, bf16[400,400]{0,1:T(8,128)(2,1)S(1)}, u32[]{:S(2)}, u32[]{:S(2)}) collective-permute-start(bf16[400,400]{0,1:T(8,128)(2,1)S(1)} %slice.20), channel_id=1, source_target_pairs={{0,8},{8,0},{16,24},{24,16},{1,9},{9,1},{17,25},{25,17},{2,10},{10... | collective-permute-start | bytes 960008 | tf_op jit(solution)/shard_map/ppermute | solution.py:10
  21.2 1.6 %collective-permute-start.3 = (bf16[400,400]{0,1:T(8,128)(2,1)S(1)}, bf16[400,400]{0,1:T(8,128)(2,1)S(1)}, u32[]{:S(2)}, u32[]{:S(2)}) collective-permute-start(bf16[400,400]{0,1:T(8,128)(2,1)S(1)} %slice.21), channel_id=1, source_target_pairs={{0,16},{8,24},{16,0},{24,8},{1,17},{9,25},{17,1},{25,9},{2,18},{10... | collective-permute-start | bytes 960008 | tf_op jit(solution)/shard_map/ppermute | solution.py:10
  22.8 1.3 %convolution_add_fusion.3 = f32[768,400]{0,1:T(8,128)S(1)} fusion(f32[768,400]{0,1:T(8,128)S(1)} %fusion.6, bf16[1536,3200]{1,0:T(8,128)(2,1)S(1)} %copy-done, s32[]{:T(128)S(6)} %select_n.81, s32[]{:T(128)S(6)} %select_n.88, bf16[800,400]{0,1:T(8,128)(2,1)S(1)} %collective-permute-done, s32[800]{0:T(1024)S(1)} %get-tuple-element.20, s32[400]{0:T(512)S(1)} %copy-done.1), kind=kOutput, calls=%fused_computation.8 | convolution fusion | flops 492467200 | bytes 4556808 | tf_op jit(solution)/shard_map/dot_general | solution.py:43
  24.1 1.3 %convolution_add_fusion.1 = f32[768,400]{0,1:T(8,128)S(1)} fusion(f32[768,400]{0,1:T(8,128)S(1)} %fusion.2, bf16[1536,3200]{1,0:T(8,128)(2,1)S(1)} %copy-done, s32[]{:T(128)S(6)} %select_n.94, s32[]{:T(128)S(6)} %select_n.88, bf16[800,400]{0,1:T(8,128)(2,1)S(1)} %collective-permute-done, s32[800]{0:T(1024)S(1)} %get-tuple-element.20, s32[400]{0:T(512)S(1)} %copy-done.1), kind=kOutput, calls=%fused_computation.6 | convolution fusion | flops 492467200 | bytes 4556808 | tf_op jit(solution)/shard_map/dot_general | solution.py:43
  25.4 1.3 %convolution_add_fusion.2 = f32[768,400]{0,1:T(8,128)S(1)} fusion(f32[768,400]{0,1:T(8,128)S(1)} %convolution_add_fusion.3, bf16[1536,3200]{1,0:T(8,128)(2,1)S(1)} %copy-done, s32[]{:T(128)S(6)} %select_n.81, s32[]{:T(128)S(6)} %select_n.91, bf16[800,400]{0,1:T(8,128)(2,1)S(1)} %collective-permute-done.2, s32[800]{0:T(1024)S(1)} %get-tuple-element.19, ...), kind=kOutput, calls=%fused_computation.7 | convolution fusion | flops 492467200 | bytes 4556808 | tf_op jit(solution)/shard_map/dot_general | solution.py:43
  26.7 1.3 %convolution_add_fusion = f32[768,400]{0,1:T(8,128)S(1)} fusion(f32[768,400]{0,1:T(8,128)S(1)} %convolution_add_fusion.1, bf16[1536,3200]{1,0:T(8,128)(2,1)S(1)} %copy-done, s32[]{:T(128)S(6)} %select_n.94, s32[]{:T(128)S(6)} %select_n.91, bf16[800,400]{0,1:T(8,128)(2,1)S(1)} %collective-permute-done.2, s32[800]{0:T(1024)S(1)} %get-tuple-element.19, ...), kind=kOutput, calls=%fused_computation.5 | convolution fusion | flops 492467200 | bytes 4556808 | tf_op jit(solution)/shard_map/dot_general | solution.py:43
  27.9 2.0 %collective-permute-done.1 = bf16[400,400]{0,1:T(8,128)(2,1)S(1)} collective-permute-done((bf16[400,400]{0,1:T(8,128)(2,1)S(1)}, bf16[400,400]{0,1:T(8,128)(2,1)S(1)}, u32[]{:S(2)}, u32[]{:S(2)}) %collective-permute-start.1) | collective-permute-done | bytes 320032 | tf_op jit(solution)/shard_map/ppermute | solution.py:10
  30.0 1.4 %collective-permute-done.3 = bf16[400,400]{0,1:T(8,128)(2,1)S(1)} collective-permute-done((bf16[400,400]{0,1:T(8,128)(2,1)S(1)}, bf16[400,400]{0,1:T(8,128)(2,1)S(1)}, u32[]{:S(2)}, u32[]{:S(2)}) %collective-permute-start.3) | collective-permute-done | bytes 320032 | tf_op jit(solution)/shard_map/ppermute | solution.py:10
  31.4 0.8 %fusion.12 = f32[768,400]{0,1:T(8,128)S(1)} fusion(bf16[1536,3200]{1,0:T(8,128)(2,1)S(1)} %copy-done, s32[]{:T(128)S(6)} %select_n.81, s32[]{:T(128)S(6)} %select_n.96, bf16[400,400]{0,1:T(8,128)(2,1)S(1)} %collective-permute-done.1, s32[400]{0:T(512)S(1)} %get-tuple-element.18, s32[400]{0:T(512)S(1)} %copy-done.1), kind=kOutput, calls=%fused_computation.24 | convolution fusion | flops 246080000 | bytes 2428936 | tf_op jit(solution)/shard_map/dot_general | solution.py:43
  32.2 0.8 %add_add_fusion = f32[768,400]{0,1:T(8,128)S(1)} fusion(f32[768,400]{0,1:T(8,128)S(1)} %convolution_add_fusion.2, f32[768,400]{0,1:T(8,128)S(1)} %fusion.12, bf16[1536,3200]{1,0:T(8,128)(2,1)S(1)} %copy-done, s32[]{:T(128)S(6)} %select_n.81, s32[]{:T(128)S(6)} %select_n.99, bf16[400,400]{0,1:T(8,128)(2,1)S(1)} %collective-permute-done.3, ...), kind=kOutput, calls=%fused_computation.18 | convolution fusion | flops 246694400 | bytes 4886536 | tf_op jit(solution)/shard_map/dot_general | solution.py:43
  33.1 0.8 %fusion.14 = f32[768,400]{0,1:T(8,128)S(1)} fusion(bf16[1536,3200]{1,0:T(8,128)(2,1)S(1)} %copy-done, s32[]{:T(128)S(6)} %select_n.94, s32[]{:T(128)S(6)} %select_n.99, bf16[400,400]{0,1:T(8,128)(2,1)S(1)} %collective-permute-done.3, s32[400]{0:T(512)S(1)} %get-tuple-element.17, s32[400]{0:T(512)S(1)} %copy-done.1), kind=kOutput, calls=%fused_computation.26 | convolution fusion | flops 246080000 | bytes 2428936 | tf_op jit(solution)/shard_map/dot_general | solution.py:43
  33.9 0.8 %fusion.16 = f32[768,400]{0,1:T(8,128)S(1)} fusion(bf16[1536,3200]{1,0:T(8,128)(2,1)S(1)} %copy-done, s32[]{:T(128)S(6)} %select_n.94, s32[]{:T(128)S(6)} %select_n.96, bf16[400,400]{0,1:T(8,128)(2,1)S(1)} %collective-permute-done.1, s32[400]{0:T(512)S(1)} %get-tuple-element.18, s32[400]{0:T(512)S(1)} %copy-done.1), kind=kOutput, calls=%fused_computation.28 | convolution fusion | flops 246080000 | bytes 2428936 | tf_op jit(solution)/shard_map/dot_general | solution.py:43
  34.7 1.3 %collective-permute-done.4 = f32[768,400]{0,1:T(8,128)S(1)} collective-permute-done((f32[768,400]{0,1:T(8,128)S(1)}, f32[768,400]{0,1:T(8,128)S(1)}, u32[]{:S(2)}, u32[]{:S(2)}) %collective-permute-start.4) | collective-permute-done | bytes 1228832 | tf_op jit(solution)/shard_map/ppermute | solution.py:10
  36.0 0.3 add_add_fusion.1
  36.3 0.9 %fusion.28 = (f32[768,200]{0,1:T(8,128)}, f32[768,200]{0,1:T(8,128)S(1)}) fusion(f32[768,400]{0,1:T(8,128)S(1)} %add_add_fusion.1), kind=kLoop, calls=%fused_computation.44 | loop fusion | bytes 2457600 | tf_op jit(solution)/shard_map/slice | solution.py:75
  37.2 1.5 %collective-permute-start.6 = (f32[768,200]{0,1:T(8,128)S(1)}, f32[768,200]{0,1:T(8,128)S(1)}, u32[]{:S(2)}, u32[]{:S(2)}) collective-permute-start(f32[768,200]{0,1:T(8,128)S(1)} %get-tuple-element.16), channel_id=1, source_target_pairs={{0,16},{8,24},{16,0},{24,8},{1,17},{9,25},{17,1},{25,9},{2,18},{10... | collective-permute-start | bytes 1843208 | tf_op jit(solution)/shard_map/ppermute | solution.py:10
  38.7 0.5 collective-permute-start.5
  39.2 0.8 %dynamic-slice_subtract_fusion = s32[768]{0:T(1024)S(1)} fusion(s32[6144]{0:T(1024)} %param.9, s32[]{:T(128)S(6)} %select_n.101, s32[]{:T(128)S(6)} %mul.43), kind=kLoop, calls=%fused_computation.31 | loop fusion | flops 768 | bytes 6152 | tf_op jit(solution)/shard_map/sub | solution.py:69
  40.0 13.9 %collective-permute-done.6 = f32[768,200]{0,1:T(8,128)S(1)} collective-permute-done((f32[768,200]{0,1:T(8,128)S(1)}, f32[768,200]{0,1:T(8,128)S(1)}, u32[]{:S(2)}, u32[]{:S(2)}) %collective-permute-start.6) | collective-permute-done | bytes 614432 | tf_op jit(solution)/shard_map/ppermute | solution.py:10
  53.9 0.3 copy.8
  54.2 2.1 %gather_fusion.1 = f32[768,200]{1,0:T(8,128)S(1)} fusion(f32[768,200]{1,0:T(8,128)S(1)} %copy.8, s32[1024]{0:T(1024)S(1)} %pad_clamp_fusion), kind=kCustom, calls=%fused_computation.1 | custom fusion | bytes 1231872 | tf_op jit(solution)/shard_map/jit(_take)/gather | solution.py:77
  56.5 9.8 %collective-permute-done.5 = f32[768,200]{0,1:T(8,128)} collective-permute-done((f32[768,200]{0,1:T(8,128)}, f32[768,200]{0,1:T(8,128)}, u32[]{:S(2)}, u32[]{:S(2)}) %collective-permute-start.5) | collective-permute-done | bytes 614432 | tf_op jit(solution)/shard_map/ppermute | solution.py:10
  66.4 1.3 %copy.6 = f32[768,200]{1,0:T(8,128)S(1)} copy(f32[768,200]{0,1:T(8,128)} %collective-permute-done.5) | data formatting | bytes 1228800 | tf_op jit(solution)/shard_map/ppermute | solution.py:10
  67.7 2.1 %gather_fusion = f32[768,200]{1,0:T(8,128)S(1)} fusion(f32[768,200]{1,0:T(8,128)S(1)} %copy.6, s32[1024]{0:T(1024)S(1)} %pad_clamp_fusion), kind=kCustom, calls=%fused_computation | custom fusion | bytes 1231872 | tf_op jit(solution)/shard_map/jit(_take)/gather | solution.py:77
  70.1 1.2 %slice_subtract_fusion.1 = (f32[768,400]{0,1:T(8,128)}, f32[768,400]{0,1:T(8,128)}) fusion(f32[768,200]{0,1:T(8,128)S(1)} %copy.7, f32[768,400]{0,1:T(8,128)S(1)} %add_add_fusion.1, f32[768,200]{0,1:T(8,128)S(1)} %copy.9, f32[768,400]{0,1:T(8,128)} %custom-call.4), kind=kLoop, output_to_operand_aliasing={{0}: (3, {}), {1}: (3, {})}, calls=%fused_computation.43 | loop fusion | flops 307200 | bytes 3686400 | tf_op jit(solution)/shard_map/sub | solution.py:77
  (12 shorter events, 0.8 us)
Async XLA Ops:
  0.0 19.2 %collective-permute-start = (bf16[800,400]{0,1:T(8,128)(2,1)}, bf16[800,400]{0,1:T(8,128)(2,1)S(1)}, u32[]{:S(2)}, u32[]{:S(2)}) collective-permute-start(bf16[800,400]{0,1:T(8,128)(2,1)} %param.6), channel_id=1, source_target_pairs={{0,16},{8,24},{16,0},{24,8},{1,17},{9,25},{17,1},{25,9},{2,18},{10... | collective-permute-start | bytes 1920008 | tf_op jit(solution)/shard_map/ppermute | solution.py:10
  3.0 18.1 %collective-permute-start.2 = (bf16[800,400]{0,1:T(8,128)(2,1)}, bf16[800,400]{0,1:T(8,128)(2,1)S(1)}, u32[]{:S(2)}, u32[]{:S(2)}) collective-permute-start(bf16[800,400]{0,1:T(8,128)(2,1)} %param.6), channel_id=1, source_target_pairs={{0,8},{8,0},{16,24},{24,16},{1,9},{9,1},{17,25},{25,17},{2,10},{10... | collective-permute-start | bytes 1920008 | tf_op jit(solution)/shard_map/ppermute | solution.py:10
  4.5 4.7 %copy-start.1 = (s32[400]{0:T(512)S(1)}, s32[400]{0:T(512)}, u32[]{:S(2)}) copy-start(s32[400]{0:T(512)} %param.8) | copy-start | bytes 4804
  6.2 16.6 %copy-start = (bf16[1536,3200]{1,0:T(8,128)(2,1)S(1)}, bf16[1536,3200]{1,0:T(8,128)(2,1)}, u32[]{:S(2)}) copy-start(bf16[1536,3200]{1,0:T(8,128)(2,1)} %param.5) | copy-start | bytes 29491204
  19.3 10.7 %collective-permute-start.1 = (bf16[400,400]{0,1:T(8,128)(2,1)S(1)}, bf16[400,400]{0,1:T(8,128)(2,1)S(1)}, u32[]{:S(2)}, u32[]{:S(2)}) collective-permute-start(bf16[400,400]{0,1:T(8,128)(2,1)S(1)} %slice.20), channel_id=1, source_target_pairs={{0,8},{8,0},{16,24},{24,16},{1,9},{9,1},{17,25},{25,17},{2,10},{10... | collective-permute-start | bytes 960008 | tf_op jit(solution)/shard_map/ppermute | solution.py:10
  21.2 10.1 %collective-permute-start.3 = (bf16[400,400]{0,1:T(8,128)(2,1)S(1)}, bf16[400,400]{0,1:T(8,128)(2,1)S(1)}, u32[]{:S(2)}, u32[]{:S(2)}) collective-permute-start(bf16[400,400]{0,1:T(8,128)(2,1)S(1)} %slice.21), channel_id=1, source_target_pairs={{0,16},{8,24},{16,0},{24,8},{1,17},{9,25},{17,1},{25,9},{2,18},{10... | collective-permute-start | bytes 960008 | tf_op jit(solution)/shard_map/ppermute | solution.py:10
  33.0 3.0 %collective-permute-start.4 = (f32[768,400]{0,1:T(8,128)S(1)}, f32[768,400]{0,1:T(8,128)S(1)}, u32[]{:S(2)}, u32[]{:S(2)}) collective-permute-start(f32[768,400]{0,1:T(8,128)S(1)} %add_add_fusion), channel_id=1, source_target_pairs={{0,1},{1,0},{2,3},{3,2},{4,5},{5,4},{6,7},{7,6},{8,9},{9,8},{10,11... | collective-permute-start | bytes 3686408 | tf_op jit(solution)/shard_map/ppermute | solution.py:10
  37.2 16.7 %collective-permute-start.6 = (f32[768,200]{0,1:T(8,128)S(1)}, f32[768,200]{0,1:T(8,128)S(1)}, u32[]{:S(2)}, u32[]{:S(2)}) collective-permute-start(f32[768,200]{0,1:T(8,128)S(1)} %get-tuple-element.16), channel_id=1, source_target_pairs={{0,16},{8,24},{16,0},{24,8},{1,17},{9,25},{17,1},{25,9},{2,18},{10... | collective-permute-start | bytes 1843208 | tf_op jit(solution)/shard_map/ppermute | solution.py:10
  38.7 27.6 %collective-permute-start.5 = (f32[768,200]{0,1:T(8,128)}, f32[768,200]{0,1:T(8,128)}, u32[]{:S(2)}, u32[]{:S(2)}) collective-permute-start(f32[768,200]{0,1:T(8,128)} %get-tuple-element.15), channel_id=1, source_target_pairs={{0,16},{8,24},{16,0},{24,8},{1,17},{9,25},{17,1},{25,9},{2,18},{10... | collective-permute-start | bytes 1843208 | tf_op jit(solution)/shard_map/ppermute | solution.py:10

commit v17 on v16

--- a/solution.py
+++ b/solution.py
@@ -59,20 +59,19 @@
     terms = contract(amplitudes, groups, firsts, block_rows, labels, irrep_cols)
     sent = list(zip(others, terms[:-1]))
     kept = terms[-1]
-    cycle = kept
-    for s, part in sent:
-        cycle = cycle + swap(part, "cuts", s)
     half = prow_count // 2
     own_block = prow_idx * cuts_count + cuts_idx
     partner_block = jnp.bitwise_xor(prow_idx, half) * cuts_count + cuts_idx
     mine = lax.dynamic_slice(mirror_row, (own_block * block_rows,), (block_rows,))
     local = mine - partner_block * block_rows
-    cols = cycle.shape[1]
+    cols = kept.shape[1]
     pieces = 2 if cols % 16 == 0 else 1
     step = cols // pieces
     results = []
     for j in range(pieces):
-        piece = cycle[:, j * step:(j + 1) * step]
+        piece = kept[:, j * step:(j + 1) * step]
+        for s, part in sent:
+            piece = piece + swap(part[:, j * step:(j + 1) * step], "cuts", s)
         fetched = swap(piece, "prow", half)
         results.append(piece - jnp.take(fetched, local, axis=0, mode="clip"))
     return jnp.concatenate(results, axis=1) if pieces > 1 else results[0]

time: 71.6 us -> 70.8 us (0.989)
  local copies, waits for them, and re-layouts: 9.2 us -> 8.36 us
    concatenate x0 -> x1, other arithmetic: none -> 1.11 us  [shards(): return jnp.concatenate(results, axis=1) if pieces > 1 else results[0]]
    sub x2, other arithmetic: 1.17 us -> 0.17 us  [shards(): results.append(piece - jnp.take(fetched, local, axis=0, mode='clip'))]
    slice x1, local copies, waits for them, and re-layouts: 0.92 us -> 0.08 us  [shards(): piece = piece + swap(part[:, j * step:(j + 1) * step], 'cuts', s)]
    ppermute x7 -> x8, waiting for transfers between devices: 35.2 us -> 34.6 us  [swap(): lax.ppermute(value, axis, [(i, i ^ mask) for i in range(lax.axis_size(axi...]
    ppermute x7 -> x8, starting transfers between devices: 9.92 us -> 10.5 us  [swap(): lax.ppermute(value, axis, [(i, i ^ mask) for i in range(lax.axis_size(axi...]
  transfers between devices with their start and end apart: 7 -> 8, of which waited for: 6 -> 6; matrix products, arithmetic and copies ran while one was open for 26% -> 26% of each run, Pallas kernels for 0% -> 0%
where the time goes in v17:
time: 70.8 us; the launch traced here: 70.4 us
  waiting for transfers between devices  34.6 us (49%)
  matrix products  14.5 us (20%)
  starting transfers between devices  10.5 us (15%)
  local copies, waits for them, and re-layouts  8.36 us (12%)
  other arithmetic  2.27 us (3%)
    ppermute x8, waiting for transfers between devices, swap(): lax.ppermute(value, axis, [(i, i ^ mask) for i in range(lax.axis_size(axi...  34.6 us
    dot_general x10, matrix products, contract(): product = jnp.dot(window, blocked, preferred_element_type=jnp.float32)  14.5 us
    ppermute x8, starting transfers between devices, swap(): lax.ppermute(value, axis, [(i, i ^ mask) for i in range(lax.axis_size(axi...  10.5 us
    gather x4, local copies, waits for them, and re-layouts, shards(): results.append(piece - jnp.take(fetched, local, axis=0, mode='clip'))  4.72 us
    dynamic_slice x2, local copies, waits for them, and re-layouts, contract(): lax.dynamic_slice_in_dim(labels, o, b.shape[0])[:, None]  1.73 us
    ppermute x2, local copies, waits for them, and re-layouts, swap(): lax.ppermute(value, axis, [(i, i ^ mask) for i in range(lax.axis_size(axi...  1.6 us
  transfers between devices with their start and end apart: 8, of which 6 were waited for; matrix products, arithmetic and copies ran while one was open for 26% of the time, Pallas kernels for 0%

profile of v17, /device:TPU:0, one launch (start us, length us, event | category | flops | bytes accessed | tf_op | source)
XLA Modules:
  0.0 70.4 jit_solution(3063659634923158166)
XLA Ops:
  0.0 3.0 %collective-permute-start = (bf16[800,400]{0,1:T(8,128)(2,1)}, bf16[800,400]{0,1:T(8,128)(2,1)S(1)}, u32[]{:S(2)}, u32[]{:S(2)}) collective-permute-start(bf16[800,400]{0,1:T(8,128)(2,1)} %param.6), channel_id=1, source_target_pairs={{0,16},{8,24},{16,0},{24,8},{1,17},{9,25},{17,1},{25,9},{2,18},{10... | collective-permute-start | bytes 1920008 | tf_op jit(solution)/shard_map/ppermute | solution.py:10
  3.0 1.5 %collective-permute-start.2 = (bf16[800,400]{0,1:T(8,128)(2,1)}, bf16[800,400]{0,1:T(8,128)(2,1)S(1)}, u32[]{:S(2)}, u32[]{:S(2)}) collective-permute-start(bf16[800,400]{0,1:T(8,128)(2,1)} %param.6), channel_id=1, source_target_pairs={{0,8},{8,0},{16,24},{24,16},{1,9},{9,1},{17,25},{25,17},{2,10},{10... | collective-permute-start | bytes 1920008 | tf_op jit(solution)/shard_map/ppermute | solution.py:10
  4.5 0.9 %fusion.32 = (s32[800]{0:T(1024)S(1)}, s32[800]{0:T(1024)S(1)}, s32[800]{0:T(1024)S(1)}) fusion(s32[6400]{0:T(1024)} %param.7, s32[]{:T(128)S(6)} %dynamic_slice.73, s32[]{:T(128)S(6)} %dynamic_slice.70, s32[]{:T(128)S(6)} %dynamic_slice.67), kind=kLoop, calls=%fused_computation.46 | loop fusion | bytes 19212 | tf_op jit(solution)/shard_map/dynamic_slice | solution.py:41
  5.3 0.8 %fusion.31 = (s32[400]{0:T(512)S(1)}, s32[400]{0:T(512)S(1)}) fusion(s32[6400]{0:T(1024)} %param.7, s32[]{:T(128)S(6)} %dynamic_slice.82, s32[]{:T(128)S(6)} %dynamic_slice.79), kind=kLoop, calls=%fused_computation.45 | loop fusion | bytes 6408 | tf_op jit(solution)/shard_map/dynamic_slice | solution.py:41
  6.2 3.0 %fusion.6 = f32[768,400]{0,1:T(8,128)S(1)} fusion(bf16[1536,3200]{1,0:T(8,128)(2,1)} %param.5, s32[]{:T(128)S(6)} %select_n.81, s32[]{:T(128)S(6)} %select_n.83, bf16[800,400]{0,1:T(8,128)(2,1)} %param.6, s32[800]{0:T(1024)S(1)} %get-tuple-element.21, s32[400]{0:T(512)} %param.8), kind=kOutput, calls=%fused_computation.15 | convolution fusion | flops 492160000 | bytes 3327112 | tf_op jit(solution)/shard_map/dot_general | solution.py:43
  9.2 3.3 %fusion.2 = f32[768,400]{0,1:T(8,128)S(1)} fusion(bf16[1536,3200]{1,0:T(8,128)(2,1)} %param.5, s32[]{:T(128)S(6)} %select_n.94, s32[]{:T(128)S(6)} %select_n.83, bf16[800,400]{0,1:T(8,128)(2,1)} %param.6, s32[800]{0:T(1024)S(1)} %get-tuple-element.21, s32[400]{0:T(512)S(1)} %copy-done.1), kind=kOutput, calls=%fused_computation.11 | convolution fusion | flops 492160000 | bytes 3326664 | tf_op jit(solution)/shard_map/dot_general | solution.py:43
  12.5 6.7 %collective-permute-done = bf16[800,400]{0,1:T(8,128)(2,1)S(1)} collective-permute-done((bf16[800,400]{0,1:T(8,128)(2,1)}, bf16[800,400]{0,1:T(8,128)(2,1)S(1)}, u32[]{:S(2)}, u32[]{:S(2)}) %collective-permute-start) | collective-permute-done | bytes 640032 | tf_op jit(solution)/shard_map/ppermute | solution.py:10
  19.3 1.8 %collective-permute-start.1 = (bf16[400,400]{0,1:T(8,128)(2,1)S(1)}, bf16[400,400]{0,1:T(8,128)(2,1)S(1)}, u32[]{:S(2)}, u32[]{:S(2)}) collective-permute-start(bf16[400,400]{0,1:T(8,128)(2,1)S(1)} %slice.28), channel_id=1, source_target_pairs={{0,8},{8,0},{16,24},{24,16},{1,9},{9,1},{17,25},{25,17},{2,10},{10... | collective-permute-start | bytes 960008 | tf_op jit(solution)/shard_map/ppermute | solution.py:10
  21.2 1.6 %collective-permute-start.3 = (bf16[400,400]{0,1:T(8,128)(2,1)S(1)}, bf16[400,400]{0,1:T(8,128)(2,1)S(1)}, u32[]{:S(2)}, u32[]{:S(2)}) collective-permute-start(bf16[400,400]{0,1:T(8,128)(2,1)S(1)} %slice.29), channel_id=1, source_target_pairs={{0,16},{8,24},{16,0},{24,8},{1,17},{9,25},{17,1},{25,9},{2,18},{10... | collective-permute-start | bytes 960008 | tf_op jit(solution)/shard_map/ppermute | solution.py:10
  22.8 1.3 %convolution_add_fusion.3 = f32[768,400]{0,1:T(8,128)S(1)} fusion(f32[768,400]{0,1:T(8,128)S(1)} %fusion.6, bf16[1536,3200]{1,0:T(8,128)(2,1)S(1)} %copy-done, s32[]{:T(128)S(6)} %select_n.81, s32[]{:T(128)S(6)} %select_n.88, bf16[800,400]{0,1:T(8,128)(2,1)S(1)} %collective-permute-done, s32[800]{0:T(1024)S(1)} %get-tuple-element.20, s32[400]{0:T(512)S(1)} %copy-done.1), kind=kOutput, calls=%fused_computation.8 | convolution fusion | flops 492467200 | bytes 4556808 | tf_op jit(solution)/shard_map/dot_general | solution.py:43
  24.1 1.3 %convolution_add_fusion.1 = f32[768,400]{0,1:T(8,128)S(1)} fusion(f32[768,400]{0,1:T(8,128)S(1)} %fusion.2, bf16[1536,3200]{1,0:T(8,128)(2,1)S(1)} %copy-done, s32[]{:T(128)S(6)} %select_n.94, s32[]{:T(128)S(6)} %select_n.88, bf16[800,400]{0,1:T(8,128)(2,1)S(1)} %collective-permute-done, s32[800]{0:T(1024)S(1)} %get-tuple-element.20, s32[400]{0:T(512)S(1)} %copy-done.1), kind=kOutput, calls=%fused_computation.6 | convolution fusion | flops 492467200 | bytes 4556808 | tf_op jit(solution)/shard_map/dot_general | solution.py:43
  25.4 1.3 %convolution_add_fusion.2 = f32[768,400]{0,1:T(8,128)S(1)} fusion(f32[768,400]{0,1:T(8,128)S(1)} %convolution_add_fusion.3, bf16[1536,3200]{1,0:T(8,128)(2,1)S(1)} %copy-done, s32[]{:T(128)S(6)} %select_n.81, s32[]{:T(128)S(6)} %select_n.91, bf16[800,400]{0,1:T(8,128)(2,1)S(1)} %collective-permute-done.2, s32[800]{0:T(1024)S(1)} %get-tuple-element.19, ...), kind=kOutput, calls=%fused_computation.7 | convolution fusion | flops 492467200 | bytes 4556808 | tf_op jit(solution)/shard_map/dot_general | solution.py:43
  26.7 1.3 %convolution_add_fusion = f32[768,400]{0,1:T(8,128)S(1)} fusion(f32[768,400]{0,1:T(8,128)S(1)} %convolution_add_fusion.1, bf16[1536,3200]{1,0:T(8,128)(2,1)S(1)} %copy-done, s32[]{:T(128)S(6)} %select_n.94, s32[]{:T(128)S(6)} %select_n.91, bf16[800,400]{0,1:T(8,128)(2,1)S(1)} %collective-permute-done.2, s32[800]{0:T(1024)S(1)} %get-tuple-element.19, ...), kind=kOutput, calls=%fused_computation.5 | convolution fusion | flops 492467200 | bytes 4556808 | tf_op jit(solution)/shard_map/dot_general | solution.py:43
  27.9 2.0 %collective-permute-done.1 = bf16[400,400]{0,1:T(8,128)(2,1)S(1)} collective-permute-done((bf16[400,400]{0,1:T(8,128)(2,1)S(1)}, bf16[400,400]{0,1:T(8,128)(2,1)S(1)}, u32[]{:S(2)}, u32[]{:S(2)}) %collective-permute-start.1) | collective-permute-done | bytes 320032 | tf_op jit(solution)/shard_map/ppermute | solution.py:10
  30.0 1.4 %collective-permute-done.3 = bf16[400,400]{0,1:T(8,128)(2,1)S(1)} collective-permute-done((bf16[400,400]{0,1:T(8,128)(2,1)S(1)}, bf16[400,400]{0,1:T(8,128)(2,1)S(1)}, u32[]{:S(2)}, u32[]{:S(2)}) %collective-permute-start.3) | collective-permute-done | bytes 320032 | tf_op jit(solution)/shard_map/ppermute | solution.py:10
  31.4 0.8 %fusion.12 = f32[768,400]{0,1:T(8,128)S(1)} fusion(bf16[1536,3200]{1,0:T(8,128)(2,1)S(1)} %copy-done, s32[]{:T(128)S(6)} %select_n.81, s32[]{:T(128)S(6)} %select_n.96, bf16[400,400]{0,1:T(8,128)(2,1)S(1)} %collective-permute-done.1, s32[400]{0:T(512)S(1)} %get-tuple-element.18, s32[400]{0:T(512)S(1)} %copy-done.1), kind=kOutput, calls=%fused_computation.24 | convolution fusion | flops 246080000 | bytes 2428936 | tf_op jit(solution)/shard_map/dot_general | solution.py:43
  32.2 0.8 %add_add_fusion = f32[768,400]{0,1:T(8,128)S(1)} fusion(f32[768,400]{0,1:T(8,128)S(1)} %convolution_add_fusion.2, f32[768,400]{0,1:T(8,128)S(1)} %fusion.12, bf16[1536,3200]{1,0:T(8,128)(2,1)S(1)} %copy-done, s32[]{:T(128)S(6)} %select_n.81, s32[]{:T(128)S(6)} %select_n.99, bf16[400,400]{0,1:T(8,128)(2,1)S(1)} %collective-permute-done.3, ...), kind=kOutput, calls=%fused_computation.18 | convolution fusion | flops 246694400 | bytes 4886536 | tf_op jit(solution)/shard_map/dot_general | solution.py:43
  33.2 0.5 collective-permute-start.6
  33.7 0.8 %fusion.18 = f32[768,400]{0,1:T(8,128)S(1)} fusion(bf16[1536,3200]{1,0:T(8,128)(2,1)S(1)} %copy-done, s32[]{:T(128)S(6)} %select_n.94, s32[]{:T(128)S(6)} %select_n.96, bf16[400,400]{0,1:T(8,128)(2,1)S(1)} %collective-permute-done.1, s32[400]{0:T(512)S(1)} %get-tuple-element.18, s32[400]{0:T(512)S(1)} %copy-done.1), kind=kOutput, calls=%fused_computation.28 | convolution fusion | flops 246080000 | bytes 2428936 | tf_op jit(solution)/shard_map/dot_general | solution.py:43
  34.4 0.8 %add_add_fusion.1 = f32[768,400]{0,1:T(8,128)S(1)} fusion(f32[768,400]{0,1:T(8,128)S(1)} %convolution_add_fusion, f32[768,400]{0,1:T(8,128)S(1)} %fusion.18, bf16[1536,3200]{1,0:T(8,128)(2,1)S(1)} %copy-done, s32[]{:T(128)S(6)} %select_n.94, s32[]{:T(128)S(6)} %select_n.99, bf16[400,400]{0,1:T(8,128)(2,1)S(1)} %collective-permute-done.3, ...), kind=kOutput, calls=%fused_computation.19 | convolution fusion | flops 246694400 | bytes 4886536 | tf_op jit(solution)/shard_map/dot_general | solution.py:43
  35.3 0.8 %collective-permute-done.6 = f32[768,200]{0,1:T(8,128)S(1)} collective-permute-done((f32[768,200]{0,1:T(8,128)S(1)}, f32[768,200]{0,1:T(8,128)S(1)}, u32[]{:S(2)}, u32[]{:S(2)}) %collective-permute-start.6) | collective-permute-done | bytes 614432 | tf_op jit(solution)/shard_map/ppermute | solution.py:10
  36.3 1.6 %collective-permute-start.5 = (f32[768,200]{0,1:T(8,128)S(1)}, f32[768,200]{0,1:T(8,128)S(1)}, u32[]{:S(2)}, u32[]{:S(2)}) collective-permute-start(f32[768,200]{0,1:T(8,128)S(1)} %get-tuple-element.13), channel_id=1, source_target_pairs={{0,16},{8,24},{16,0},{24,8},{1,17},{9,25},{17,1},{25,9},{2,18},{10... | collective-permute-start | bytes 1843208 | tf_op jit(solution)/shard_map/ppermute | solution.py:10
  37.9 0.5 collective-permute-start.7
  38.4 0.8 %dynamic-slice_subtract_fusion = s32[768]{0:T(1024)S(1)} fusion(s32[6144]{0:T(1024)} %param.9, s32[]{:T(128)S(6)} %select_n.101, s32[]{:T(128)S(6)} %mul.43), kind=kLoop, calls=%fused_computation.33 | loop fusion | flops 768 | bytes 6152 | tf_op jit(solution)/shard_map/sub | solution.py:66
  39.1 13.9 %collective-permute-done.5 = f32[768,200]{0,1:T(8,128)S(1)} collective-permute-done((f32[768,200]{0,1:T(8,128)S(1)}, f32[768,200]{0,1:T(8,128)S(1)}, u32[]{:S(2)}, u32[]{:S(2)}) %collective-permute-start.5) | collective-permute-done | bytes 614432 | tf_op jit(solution)/shard_map/ppermute | solution.py:10
  53.0 0.3 copy.6
  53.3 2.1 %gather_fusion = f32[768,200]{1,0:T(8,128)S(1)} fusion(f32[768,200]{1,0:T(8,128)S(1)} %copy.6, s32[1024]{0:T(1024)S(1)} %pad_clamp_fusion), kind=kCustom, calls=%fused_computation | custom fusion | bytes 1231872 | tf_op jit(solution)/shard_map/jit(_take)/gather | solution.py:76
  55.4 0.2 copy.7
  55.8 9.7 %collective-permute-done.7 = f32[768,200]{0,1:T(8,128)} collective-permute-done((f32[768,200]{0,1:T(8,128)S(1)}, f32[768,200]{0,1:T(8,128)}, u32[]{:S(2)}, u32[]{:S(2)}) %collective-permute-start.7) | collective-permute-done | bytes 614432 | tf_op jit(solution)/shard_map/ppermute | solution.py:10
  65.5 1.3 %copy.8 = f32[768,200]{1,0:T(8,128)S(1)} copy(f32[768,200]{0,1:T(8,128)} %collective-permute-done.7) | data formatting | bytes 1228800 | tf_op jit(solution)/shard_map/ppermute | solution.py:10
  66.8 2.1 %gather_fusion.1 = f32[768,200]{1,0:T(8,128)S(1)} fusion(f32[768,200]{1,0:T(8,128)S(1)} %copy.8, s32[1024]{0:T(1024)S(1)} %pad_clamp_fusion), kind=kCustom, calls=%fused_computation.1 | custom fusion | bytes 1231872 | tf_op jit(solution)/shard_map/jit(_take)/gather | solution.py:76
  69.3 1.1 %pad_maximum_fusion = f32[768,400]{0,1:T(8,128)} fusion(f32[768,200]{0,1:T(8,128)S(1)} %sub.15, f32[768,200]{0,1:T(8,128)S(1)} %sub.14), kind=kLoop, calls=%fused_computation.17 | loop fusion | flops 307200 | bytes 2457600 | tf_op jit(solution)/shard_map/concatenate | solution.py:77
  (15 shorter events, 1.0 us)
Async XLA Ops:
  0.0 19.2 %collective-permute-start = (bf16[800,400]{0,1:T(8,128)(2,1)}, bf16[800,400]{0,1:T(8,128)(2,1)S(1)}, u32[]{:S(2)}, u32[]{:S(2)}) collective-permute-start(bf16[800,400]{0,1:T(8,128)(2,1)} %param.6), channel_id=1, source_target_pairs={{0,16},{8,24},{16,0},{24,8},{1,17},{9,25},{17,1},{25,9},{2,18},{10... | collective-permute-start | bytes 1920008 | tf_op jit(solution)/shard_map/ppermute | solution.py:10
  3.0 18.1 %collective-permute-start.2 = (bf16[800,400]{0,1:T(8,128)(2,1)}, bf16[800,400]{0,1:T(8,128)(2,1)S(1)}, u32[]{:S(2)}, u32[]{:S(2)}) collective-permute-start(bf16[800,400]{0,1:T(8,128)(2,1)} %param.6), channel_id=1, source_target_pairs={{0,8},{8,0},{16,24},{24,16},{1,9},{9,1},{17,25},{25,17},{2,10},{10... | collective-permute-start | bytes 1920008 | tf_op jit(solution)/shard_map/ppermute | solution.py:10
  4.5 4.7 %copy-start.1 = (s32[400]{0:T(512)S(1)}, s32[400]{0:T(512)}, u32[]{:S(2)}) copy-start(s32[400]{0:T(512)} %param.8) | copy-start | bytes 4804
  6.2 16.6 %copy-start = (bf16[1536,3200]{1,0:T(8,128)(2,1)S(1)}, bf16[1536,3200]{1,0:T(8,128)(2,1)}, u32[]{:S(2)}) copy-start(bf16[1536,3200]{1,0:T(8,128)(2,1)} %param.5) | copy-start | bytes 29491204
  19.3 10.7 %collective-permute-start.1 = (bf16[400,400]{0,1:T(8,128)(2,1)S(1)}, bf16[400,400]{0,1:T(8,128)(2,1)S(1)}, u32[]{:S(2)}, u32[]{:S(2)}) collective-permute-start(bf16[400,400]{0,1:T(8,128)(2,1)S(1)} %slice.28), channel_id=1, source_target_pairs={{0,8},{8,0},{16,24},{24,16},{1,9},{9,1},{17,25},{25,17},{2,10},{10... | collective-permute-start | bytes 960008 | tf_op jit(solution)/shard_map/ppermute | solution.py:10
  21.2 10.1 %collective-permute-start.3 = (bf16[400,400]{0,1:T(8,128)(2,1)S(1)}, bf16[400,400]{0,1:T(8,128)(2,1)S(1)}, u32[]{:S(2)}, u32[]{:S(2)}) collective-permute-start(bf16[400,400]{0,1:T(8,128)(2,1)S(1)} %slice.29), channel_id=1, source_target_pairs={{0,16},{8,24},{16,0},{24,8},{1,17},{9,25},{17,1},{25,9},{2,18},{10... | collective-permute-start | bytes 960008 | tf_op jit(solution)/shard_map/ppermute | solution.py:10
  33.1 2.2 %collective-permute-start.4 = (f32[768,200]{0,1:T(8,128)S(1)}, f32[768,200]{0,1:T(8,128)S(1)}, u32[]{:S(2)}, u32[]{:S(2)}) collective-permute-start(f32[768,200]{0,1:T(8,128)S(1)} %get-tuple-element.15), channel_id=1, source_target_pairs={{0,1},{1,0},{2,3},{3,2},{4,5},{5,4},{6,7},{7,6},{8,9},{9,8},{10,11... | collective-permute-start | bytes 1843208 | tf_op jit(solution)/shard_map/ppermute | solution.py:10
  33.2 2.9 %collective-permute-start.6 = (f32[768,200]{0,1:T(8,128)S(1)}, f32[768,200]{0,1:T(8,128)S(1)}, u32[]{:S(2)}, u32[]{:S(2)}) collective-permute-start(f32[768,200]{0,1:T(8,128)S(1)} %get-tuple-element.16), channel_id=1, source_target_pairs={{0,1},{1,0},{2,3},{3,2},{4,5},{5,4},{6,7},{7,6},{8,9},{9,8},{10,11... | collective-permute-start | bytes 1843208 | tf_op jit(solution)/shard_map/ppermute | solution.py:10
  36.3 16.8 %collective-permute-start.5 = (f32[768,200]{0,1:T(8,128)S(1)}, f32[768,200]{0,1:T(8,128)S(1)}, u32[]{:S(2)}, u32[]{:S(2)}) collective-permute-start(f32[768,200]{0,1:T(8,128)S(1)} %get-tuple-element.13), channel_id=1, source_target_pairs={{0,16},{8,24},{16,0},{24,8},{1,17},{9,25},{17,1},{25,9},{2,18},{10... | collective-permute-start | bytes 1843208 | tf_op jit(solution)/shard_map/ppermute | solution.py:10
  37.9 27.6 %collective-permute-start.7 = (f32[768,200]{0,1:T(8,128)S(1)}, f32[768,200]{0,1:T(8,128)}, u32[]{:S(2)}, u32[]{:S(2)}) collective-permute-start(f32[768,200]{0,1:T(8,128)S(1)} %get-tuple-element.14), channel_id=1, source_target_pairs={{0,16},{8,24},{16,0},{24,8},{1,17},{9,25},{17,1},{25,9},{2,18},{10... | collective-permute-start | bytes 1843208 | tf_op jit(solution)/shard_map/ppermute | solution.py:10

commit v18 on v17

--- a/solution.py
+++ b/solution.py
@@ -64,6 +64,8 @@
     partner_block = jnp.bitwise_xor(prow_idx, half) * cuts_count + cuts_idx
     mine = lax.dynamic_slice(mirror_row, (own_block * block_rows,), (block_rows,))
     local = mine - partner_block * block_rows
+    theirs = lax.dynamic_slice(mirror_row, (partner_block * block_rows,), (block_rows,))
+    wanted = theirs - own_block * block_rows
     cols = kept.shape[1]
     pieces = 2 if cols % 16 == 0 else 1
     step = cols // pieces
@@ -72,8 +74,12 @@
         piece = kept[:, j * step:(j + 1) * step]
         for s, part in sent:
             piece = piece + swap(part[:, j * step:(j + 1) * step], "cuts", s)
-        fetched = swap(piece, "prow", half)
-        results.append(piece - jnp.take(fetched, local, axis=0, mode="clip"))
+        if j == pieces - 1 and pieces > 1:
+            fetched = swap(jnp.take(piece, wanted, axis=0, mode="clip"), "prow", half)
+            results.append(piece - fetched)
+        else:
+            fetched = swap(piece, "prow", half)
+            results.append(piece - jnp.take(fetched, local, axis=0, mode="clip"))
     return jnp.concatenate(results, axis=1) if pieces > 1 else results[0]
 
 

time: 70.8 us -> 67 us (0.946)
  waiting for transfers between devices: 34.6 us -> 29.9 us
  local copies, waits for them, and re-layouts: 8.36 us -> 9.19 us
    ppermute x8, waiting for transfers between devices: 34.6 us -> 29.9 us  [swap(): lax.ppermute(value, axis, [(i, i ^ mask) for i in range(lax.axis_size(axi...]
    gather x0 -> x2, local copies, waits for them, and re-layouts: none -> 3.19 us  [shards(): fetched = swap(jnp.take(piece, wanted, axis=0, mode='clip'), 'prow', half)]
    gather x4 -> x2, local copies, waits for them, and re-layouts: 4.72 us -> 2.36 us  [shards(): results.append(piece - jnp.take(fetched, local, axis=0, mode='clip'))]
    ppermute x2 -> x1, local copies, waits for them, and re-layouts: 1.6 us -> 1.34 us  [swap(): lax.ppermute(value, axis, [(i, i ^ mask) for i in range(lax.axis_size(axi...]
  transfers between devices with their start and end apart: 8 -> 8, of which waited for: 6 -> 6; matrix products, arithmetic and copies ran while one was open for 26% -> 35% of each run, Pallas kernels for 0% -> 0%
where the time goes in v18:
time: 67 us; the launch traced here: 66.5 us
  waiting for transfers between devices  29.9 us (45%)
  matrix products  14.6 us (22%)
  starting transfers between devices  10.5 us (16%)
  local copies, waits for them, and re-layouts  9.19 us (14%)
  other arithmetic  2.25 us (3%)
    ppermute x8, waiting for transfers between devices, swap(): lax.ppermute(value, axis, [(i, i ^ mask) for i in range(lax.axis_size(axi...  29.9 us
    dot_general x10, matrix products, contract(): product = jnp.dot(window, blocked, preferred_element_type=jnp.float32)  14.6 us
    ppermute x8, starting transfers between devices, swap(): lax.ppermute(value, axis, [(i, i ^ mask) for i in range(lax.axis_size(axi...  10.5 us
    gather x2, local copies, waits for them, and re-layouts, shards(): fetched = swap(jnp.take(piece, wanted, axis=0, mode='clip'), 'prow', half)  3.19 us
    gather x2, local copies, waits for them, and re-layouts, shards(): results.append(piece - jnp.take(fetched, local, axis=0, mode='clip'))  2.36 us
    dynamic_slice x2, local copies, waits for them, and re-layouts, contract(): lax.dynamic_slice_in_dim(labels, o, b.shape[0])[:, None]  1.73 us
  transfers between devices with their start and end apart: 8, of which 6 were waited for; matrix products, arithmetic and copies ran while one was open for 35% of the time, Pallas kernels for 0%

profile of v18, /device:TPU:0, one launch (start us, length us, event | category | flops | bytes accessed | tf_op | source)
XLA Modules:
  0.0 66.5 jit_solution(4651484820070842906)
XLA Ops:
  0.0 3.0 %collective-permute-start = (bf16[800,400]{0,1:T(8,128)(2,1)}, bf16[800,400]{0,1:T(8,128)(2,1)S(1)}, u32[]{:S(2)}, u32[]{:S(2)}) collective-permute-start(bf16[800,400]{0,1:T(8,128)(2,1)} %param.6), channel_id=1, source_target_pairs={{0,16},{8,24},{16,0},{24,8},{1,17},{9,25},{17,1},{25,9},{2,18},{10... | collective-permute-start | bytes 1920008 | tf_op jit(solution)/shard_map/ppermute | solution.py:10
  3.0 1.5 %collective-permute-start.2 = (bf16[800,400]{0,1:T(8,128)(2,1)}, bf16[800,400]{0,1:T(8,128)(2,1)S(1)}, u32[]{:S(2)}, u32[]{:S(2)}) collective-permute-start(bf16[800,400]{0,1:T(8,128)(2,1)} %param.6), channel_id=1, source_target_pairs={{0,8},{8,0},{16,24},{24,16},{1,9},{9,1},{17,25},{25,17},{2,10},{10... | collective-permute-start | bytes 1920008 | tf_op jit(solution)/shard_map/ppermute | solution.py:10
  4.5 0.8 %dynamic-slice_subtract_fusion.1 = (s32[768]{0:T(1024)S(1)}, s32[768]{0:T(1024)S(1)}) fusion(s32[6144]{0:T(1024)} %param.9, s32[]{:T(128)S(6)} %select_n.104, s32[]{:T(128)S(6)} %mul.45, s32[]{:T(128)S(6)} %mul.43, s32[]{:T(128)S(6)} %select_n.105), kind=kLoop, calls=%fused_computation.35 | loop fusion | flops 1536 | bytes 12304 | tf_op jit(solution)/shard_map/sub | solution.py:66
  5.3 0.9 %fusion.32 = (s32[800]{0:T(1024)S(1)}, s32[800]{0:T(1024)S(1)}, s32[800]{0:T(1024)S(1)}) fusion(s32[6400]{0:T(1024)} %param.7, s32[]{:T(128)S(6)} %dynamic_slice.76, s32[]{:T(128)S(6)} %dynamic_slice.73, s32[]{:T(128)S(6)} %dynamic_slice.70), kind=kLoop, calls=%fused_computation.48 | loop fusion | bytes 19212 | tf_op jit(solution)/shard_map/dynamic_slice | solution.py:41
  6.1 0.8 %fusion.31 = (s32[400]{0:T(512)S(1)}, s32[400]{0:T(512)S(1)}) fusion(s32[6400]{0:T(1024)} %param.7, s32[]{:T(128)S(6)} %dynamic_slice.85, s32[]{:T(128)S(6)} %dynamic_slice.82), kind=kLoop, calls=%fused_computation.47 | loop fusion | bytes 6408 | tf_op jit(solution)/shard_map/dynamic_slice | solution.py:41
  7.0 3.0 %fusion.6 = f32[768,400]{0,1:T(8,128)S(1)} fusion(bf16[1536,3200]{1,0:T(8,128)(2,1)} %param.5, s32[]{:T(128)S(6)} %select_n.84, s32[]{:T(128)S(6)} %select_n.86, bf16[800,400]{0,1:T(8,128)(2,1)} %param.6, s32[800]{0:T(1024)S(1)} %get-tuple-element.21, s32[400]{0:T(512)} %param.8), kind=kOutput, calls=%fused_computation.15 | convolution fusion | flops 492160000 | bytes 3327112 | tf_op jit(solution)/shard_map/dot_general | solution.py:43
  10.0 3.3 %fusion.2 = f32[768,400]{0,1:T(8,128)S(1)} fusion(bf16[1536,3200]{1,0:T(8,128)(2,1)} %param.5, s32[]{:T(128)S(6)} %select_n.97, s32[]{:T(128)S(6)} %select_n.86, bf16[800,400]{0,1:T(8,128)(2,1)} %param.6, s32[800]{0:T(1024)S(1)} %get-tuple-element.21, s32[400]{0:T(512)S(1)} %copy-done.1), kind=kOutput, calls=%fused_computation.11 | convolution fusion | flops 492160000 | bytes 3326664 | tf_op jit(solution)/shard_map/dot_general | solution.py:43
  13.3 5.9 %collective-permute-done = bf16[800,400]{0,1:T(8,128)(2,1)S(1)} collective-permute-done((bf16[800,400]{0,1:T(8,128)(2,1)}, bf16[800,400]{0,1:T(8,128)(2,1)S(1)}, u32[]{:S(2)}, u32[]{:S(2)}) %collective-permute-start) | collective-permute-done | bytes 640032 | tf_op jit(solution)/shard_map/ppermute | solution.py:10
  19.3 1.8 %collective-permute-start.1 = (bf16[400,400]{0,1:T(8,128)(2,1)S(1)}, bf16[400,400]{0,1:T(8,128)(2,1)S(1)}, u32[]{:S(2)}, u32[]{:S(2)}) collective-permute-start(bf16[400,400]{0,1:T(8,128)(2,1)S(1)} %slice.28), channel_id=1, source_target_pairs={{0,8},{8,0},{16,24},{24,16},{1,9},{9,1},{17,25},{25,17},{2,10},{10... | collective-permute-start | bytes 960008 | tf_op jit(solution)/shard_map/ppermute | solution.py:10
  21.2 1.6 %collective-permute-start.3 = (bf16[400,400]{0,1:T(8,128)(2,1)S(1)}, bf16[400,400]{0,1:T(8,128)(2,1)S(1)}, u32[]{:S(2)}, u32[]{:S(2)}) collective-permute-start(bf16[400,400]{0,1:T(8,128)(2,1)S(1)} %slice.29), channel_id=1, source_target_pairs={{0,16},{8,24},{16,0},{24,8},{1,17},{9,25},{17,1},{25,9},{2,18},{10... | collective-permute-start | bytes 960008 | tf_op jit(solution)/shard_map/ppermute | solution.py:10
  22.8 1.3 %convolution_add_fusion.3 = f32[768,400]{0,1:T(8,128)S(1)} fusion(f32[768,400]{0,1:T(8,128)S(1)} %fusion.6, bf16[1536,3200]{1,0:T(8,128)(2,1)S(1)} %copy-done, s32[]{:T(128)S(6)} %select_n.84, s32[]{:T(128)S(6)} %select_n.91, bf16[800,400]{0,1:T(8,128)(2,1)S(1)} %collective-permute-done, s32[800]{0:T(1024)S(1)} %get-tuple-element.20, s32[400]{0:T(512)S(1)} %copy-done.1), kind=kOutput, calls=%fused_computation.8 | convolution fusion | flops 492467200 | bytes 4556808 | tf_op jit(solution)/shard_map/dot_general | solution.py:43
  24.1 1.3 %convolution_add_fusion.1 = f32[768,400]{0,1:T(8,128)S(1)} fusion(f32[768,400]{0,1:T(8,128)S(1)} %fusion.2, bf16[1536,3200]{1,0:T(8,128)(2,1)S(1)} %copy-done, s32[]{:T(128)S(6)} %select_n.97, s32[]{:T(128)S(6)} %select_n.91, bf16[800,400]{0,1:T(8,128)(2,1)S(1)} %collective-permute-done, s32[800]{0:T(1024)S(1)} %get-tuple-element.20, s32[400]{0:T(512)S(1)} %copy-done.1), kind=kOutput, calls=%fused_computation.6 | convolution fusion | flops 492467200 | bytes 4556808 | tf_op jit(solution)/shard_map/dot_general | solution.py:43
  25.4 1.3 %convolution_add_fusion.2 = f32[768,400]{0,1:T(8,128)S(1)} fusion(f32[768,400]{0,1:T(8,128)S(1)} %convolution_add_fusion.3, bf16[1536,3200]{1,0:T(8,128)(2,1)S(1)} %copy-done, s32[]{:T(128)S(6)} %select_n.84, s32[]{:T(128)S(6)} %select_n.94, bf16[800,400]{0,1:T(8,128)(2,1)S(1)} %collective-permute-done.2, s32[800]{0:T(1024)S(1)} %get-tuple-element.19, ...), kind=kOutput, calls=%fused_computation.7 | convolution fusion | flops 492467200 | bytes 4556808 | tf_op jit(solution)/shard_map/dot_general | solution.py:43
  26.7 1.3 %convolution_add_fusion = f32[768,400]{0,1:T(8,128)S(1)} fusion(f32[768,400]{0,1:T(8,128)S(1)} %convolution_add_fusion.1, bf16[1536,3200]{1,0:T(8,128)(2,1)S(1)} %copy-done, s32[]{:T(128)S(6)} %select_n.97, s32[]{:T(128)S(6)} %select_n.94, bf16[800,400]{0,1:T(8,128)(2,1)S(1)} %collective-permute-done.2, s32[800]{0:T(1024)S(1)} %get-tuple-element.19, ...), kind=kOutput, calls=%fused_computation.5 | convolution fusion | flops 492467200 | bytes 4556808 | tf_op jit(solution)/shard_map/dot_general | solution.py:43
  27.9 2.0 %collective-permute-done.1 = bf16[400,400]{0,1:T(8,128)(2,1)S(1)} collective-permute-done((bf16[400,400]{0,1:T(8,128)(2,1)S(1)}, bf16[400,400]{0,1:T(8,128)(2,1)S(1)}, u32[]{:S(2)}, u32[]{:S(2)}) %collective-permute-start.1) | collective-permute-done | bytes 320032 | tf_op jit(solution)/shard_map/ppermute | solution.py:10
  30.0 1.4 %collective-permute-done.3 = bf16[400,400]{0,1:T(8,128)(2,1)S(1)} collective-permute-done((bf16[400,400]{0,1:T(8,128)(2,1)S(1)}, bf16[400,400]{0,1:T(8,128)(2,1)S(1)}, u32[]{:S(2)}, u32[]{:S(2)}) %collective-permute-start.3) | collective-permute-done | bytes 320032 | tf_op jit(solution)/shard_map/ppermute | solution.py:10
  31.4 0.8 %fusion.12 = f32[768,400]{0,1:T(8,128)S(1)} fusion(bf16[1536,3200]{1,0:T(8,128)(2,1)S(1)} %copy-done, s32[]{:T(128)S(6)} %select_n.84, s32[]{:T(128)S(6)} %select_n.99, bf16[400,400]{0,1:T(8,128)(2,1)S(1)} %collective-permute-done.1, s32[400]{0:T(512)S(1)} %get-tuple-element.18, s32[400]{0:T(512)S(1)} %copy-done.1), kind=kOutput, calls=%fused_computation.24 | convolution fusion | flops 246080000 | bytes 2428936 | tf_op jit(solution)/shard_map/dot_general | solution.py:43
  32.2 0.8 %add_add_fusion = f32[768,400]{0,1:T(8,128)S(1)} fusion(f32[768,400]{0,1:T(8,128)S(1)} %convolution_add_fusion.2, f32[768,400]{0,1:T(8,128)S(1)} %fusion.12, bf16[1536,3200]{1,0:T(8,128)(2,1)S(1)} %copy-done, s32[]{:T(128)S(6)} %select_n.84, s32[]{:T(128)S(6)} %select_n.102, bf16[400,400]{0,1:T(8,128)(2,1)S(1)} %collective-permute-done.3, ...), kind=kOutput, calls=%fused_computation.18 | convolution fusion | flops 246694400 | bytes 4886536 | tf_op jit(solution)/shard_map/dot_general | solution.py:43
  33.2 0.5 collective-permute-start.6
  33.7 0.8 %fusion.18 = f32[768,400]{0,1:T(8,128)S(1)} fusion(bf16[1536,3200]{1,0:T(8,128)(2,1)S(1)} %copy-done, s32[]{:T(128)S(6)} %select_n.97, s32[]{:T(128)S(6)} %select_n.99, bf16[400,400]{0,1:T(8,128)(2,1)S(1)} %collective-permute-done.1, s32[400]{0:T(512)S(1)} %get-tuple-element.18, s32[400]{0:T(512)S(1)} %copy-done.1), kind=kOutput, calls=%fused_computation.28 | convolution fusion | flops 246080000 | bytes 2428936 | tf_op jit(solution)/shard_map/dot_general | solution.py:43
  34.4 0.8 %add_add_fusion.1 = f32[768,400]{0,1:T(8,128)S(1)} fusion(f32[768,400]{0,1:T(8,128)S(1)} %convolution_add_fusion, f32[768,400]{0,1:T(8,128)S(1)} %fusion.18, bf16[1536,3200]{1,0:T(8,128)(2,1)S(1)} %copy-done, s32[]{:T(128)S(6)} %select_n.97, s32[]{:T(128)S(6)} %select_n.102, bf16[400,400]{0,1:T(8,128)(2,1)S(1)} %collective-permute-done.3, ...), kind=kOutput, calls=%fused_computation.19 | convolution fusion | flops 246694400 | bytes 4886536 | tf_op jit(solution)/shard_map/dot_general | solution.py:43
  35.3 0.8 %collective-permute-done.6 = f32[768,200]{0,1:T(8,128)S(1)} collective-permute-done((f32[768,200]{0,1:T(8,128)S(1)}, f32[768,200]{0,1:T(8,128)S(1)}, u32[]{:S(2)}, u32[]{:S(2)}) %collective-permute-start.6) | collective-permute-done | bytes 614432 | tf_op jit(solution)/shard_map/ppermute | solution.py:10
  36.2 1.6 %collective-permute-start.5 = (f32[768,200]{0,1:T(8,128)S(1)}, f32[768,200]{0,1:T(8,128)}, u32[]{:S(2)}, u32[]{:S(2)}) collective-permute-start(f32[768,200]{0,1:T(8,128)S(1)} %get-tuple-element.13), channel_id=1, source_target_pairs={{0,16},{8,24},{16,0},{24,8},{1,17},{9,25},{17,1},{25,9},{2,18},{10... | collective-permute-start | bytes 1843208 | tf_op jit(solution)/shard_map/ppermute | solution.py:10
  37.8 0.3 copy.8
  38.1 2.1 %gather_fusion.1 = f32[768,200]{1,0:T(8,128)S(1)} fusion(f32[768,200]{1,0:T(8,128)S(1)} %copy.8, s32[1024]{0:T(1024)S(1)} %pad_clamp_fusion), kind=kCustom, calls=%fused_computation.1 | custom fusion | bytes 1231872 | tf_op jit(solution)/shard_map/jit(_take)/gather | solution.py:78
  40.2 1.1 %copy.9 = f32[768,200]{0,1:T(8,128)} copy(f32[768,200]{1,0:T(8,128)S(1)} %gather_fusion.1) | data formatting | bytes 1228800 | tf_op jit(solution)/shard_map/jit(_take)/gather | solution.py:78
  41.3 0.5 collective-permute-start.7
  41.8 11.3 %collective-permute-done.5 = f32[768,200]{0,1:T(8,128)} collective-permute-done((f32[768,200]{0,1:T(8,128)S(1)}, f32[768,200]{0,1:T(8,128)}, u32[]{:S(2)}, u32[]{:S(2)}) %collective-permute-start.5) | collective-permute-done | bytes 614432 | tf_op jit(solution)/shard_map/ppermute | solution.py:10
  53.1 1.3 %copy.6 = f32[768,200]{1,0:T(8,128)S(1)} copy(f32[768,200]{0,1:T(8,128)} %collective-permute-done.5) | data formatting | bytes 1228800 | tf_op jit(solution)/shard_map/ppermute | solution.py:10
  54.4 2.1 %gather_fusion = f32[768,200]{1,0:T(8,128)S(1)} fusion(f32[768,200]{1,0:T(8,128)S(1)} %copy.6, s32[1024]{0:T(1024)S(1)} %pad_clamp_fusion.1), kind=kCustom, calls=%fused_computation | custom fusion | bytes 1231872 | tf_op jit(solution)/shard_map/jit(_take)/gather | solution.py:82
  56.9 8.4 %collective-permute-done.7 = f32[768,200]{0,1:T(8,128)S(1)} collective-permute-done((f32[768,200]{0,1:T(8,128)}, f32[768,200]{0,1:T(8,128)S(1)}, u32[]{:S(2)}, u32[]{:S(2)}) %collective-permute-start.7) | collective-permute-done | bytes 614432 | tf_op jit(solution)/shard_map/ppermute | solution.py:10
  65.4 1.1 %pad_maximum_fusion = f32[768,400]{0,1:T(8,128)} fusion(f32[768,200]{0,1:T(8,128)S(1)} %sub.23, f32[768,200]{0,1:T(8,128)S(1)} %sub.20), kind=kLoop, calls=%fused_computation.17 | loop fusion | flops 307200 | bytes 2457600 | tf_op jit(solution)/shard_map/concatenate | solution.py:83
  (16 shorter events, 1.0 us)
Async XLA Ops:
  0.0 19.2 %collective-permute-start = (bf16[800,400]{0,1:T(8,128)(2,1)}, bf16[800,400]{0,1:T(8,128)(2,1)S(1)}, u32[]{:S(2)}, u32[]{:S(2)}) collective-permute-start(bf16[800,400]{0,1:T(8,128)(2,1)} %param.6), channel_id=1, source_target_pairs={{0,16},{8,24},{16,0},{24,8},{1,17},{9,25},{17,1},{25,9},{2,18},{10... | collective-permute-start | bytes 1920008 | tf_op jit(solution)/shard_map/ppermute | solution.py:10
  3.0 18.1 %collective-permute-start.2 = (bf16[800,400]{0,1:T(8,128)(2,1)}, bf16[800,400]{0,1:T(8,128)(2,1)S(1)}, u32[]{:S(2)}, u32[]{:S(2)}) collective-permute-start(bf16[800,400]{0,1:T(8,128)(2,1)} %param.6), channel_id=1, source_target_pairs={{0,8},{8,0},{16,24},{24,16},{1,9},{9,1},{17,25},{25,17},{2,10},{10... | collective-permute-start | bytes 1920008 | tf_op jit(solution)/shard_map/ppermute | solution.py:10
  4.5 5.5 %copy-start.1 = (s32[400]{0:T(512)S(1)}, s32[400]{0:T(512)}, u32[]{:S(2)}) copy-start(s32[400]{0:T(512)} %param.8) | copy-start | bytes 4804
  7.0 15.8 %copy-start = (bf16[1536,3200]{1,0:T(8,128)(2,1)S(1)}, bf16[1536,3200]{1,0:T(8,128)(2,1)}, u32[]{:S(2)}) copy-start(bf16[1536,3200]{1,0:T(8,128)(2,1)} %param.5) | copy-start | bytes 29491204
  19.3 10.7 %collective-permute-start.1 = (bf16[400,400]{0,1:T(8,128)(2,1)S(1)}, bf16[400,400]{0,1:T(8,128)(2,1)S(1)}, u32[]{:S(2)}, u32[]{:S(2)}) collective-permute-start(bf16[400,400]{0,1:T(8,128)(2,1)S(1)} %slice.28), channel_id=1, source_target_pairs={{0,8},{8,0},{16,24},{24,16},{1,9},{9,1},{17,25},{25,17},{2,10},{10... | collective-permute-start | bytes 960008 | tf_op jit(solution)/shard_map/ppermute | solution.py:10
  21.2 10.1 %collective-permute-start.3 = (bf16[400,400]{0,1:T(8,128)(2,1)S(1)}, bf16[400,400]{0,1:T(8,128)(2,1)S(1)}, u32[]{:S(2)}, u32[]{:S(2)}) collective-permute-start(bf16[400,400]{0,1:T(8,128)(2,1)S(1)} %slice.29), channel_id=1, source_target_pairs={{0,16},{8,24},{16,0},{24,8},{1,17},{9,25},{17,1},{25,9},{2,18},{10... | collective-permute-start | bytes 960008 | tf_op jit(solution)/shard_map/ppermute | solution.py:10
  33.1 2.2 %collective-permute-start.4 = (f32[768,200]{0,1:T(8,128)S(1)}, f32[768,200]{0,1:T(8,128)S(1)}, u32[]{:S(2)}, u32[]{:S(2)}) collective-permute-start(f32[768,200]{0,1:T(8,128)S(1)} %get-tuple-element.15), channel_id=1, source_target_pairs={{0,1},{1,0},{2,3},{3,2},{4,5},{5,4},{6,7},{7,6},{8,9},{9,8},{10,11... | collective-permute-start | bytes 1843208 | tf_op jit(solution)/shard_map/ppermute | solution.py:10
  33.2 2.9 %collective-permute-start.6 = (f32[768,200]{0,1:T(8,128)S(1)}, f32[768,200]{0,1:T(8,128)S(1)}, u32[]{:S(2)}, u32[]{:S(2)}) collective-permute-start(f32[768,200]{0,1:T(8,128)S(1)} %get-tuple-element.16), channel_id=1, source_target_pairs={{0,1},{1,0},{2,3},{3,2},{4,5},{5,4},{6,7},{7,6},{8,9},{9,8},{10,11... | collective-permute-start | bytes 1843208 | tf_op jit(solution)/shard_map/ppermute | solution.py:10
  36.2 16.9 %collective-permute-start.5 = (f32[768,200]{0,1:T(8,128)S(1)}, f32[768,200]{0,1:T(8,128)}, u32[]{:S(2)}, u32[]{:S(2)}) collective-permute-start(f32[768,200]{0,1:T(8,128)S(1)} %get-tuple-element.13), channel_id=1, source_target_pairs={{0,16},{8,24},{16,0},{24,8},{1,17},{9,25},{17,1},{25,9},{2,18},{10... | collective-permute-start | bytes 1843208 | tf_op jit(solution)/shard_map/ppermute | solution.py:10
  41.3 24.1 %collective-permute-start.7 = (f32[768,200]{0,1:T(8,128)}, f32[768,200]{0,1:T(8,128)S(1)}, u32[]{:S(2)}, u32[]{:S(2)}) collective-permute-start(f32[768,200]{0,1:T(8,128)} %copy.9), channel_id=1, source_target_pairs={{0,16},{8,24},{16,0},{24,8},{1,17},{9,25},{17,1},{25,9},{2,18},{10... | collective-permute-start | bytes 1843208 | tf_op jit(solution)/shard_map/ppermute | solution.py:10

commit v19 on v18

--- a/solution.py
+++ b/solution.py
@@ -20,7 +20,7 @@
         diag_b = swap(from_x[half:], "prow", 2)
         base = jnp.bitwise_xor(prow_idx, 3) * count
         return [[(own, prow_idx * count)], [(from_y, jnp.bitwise_xor(prow_idx, 2) * count)],
-                [(from_x, jnp.bitwise_xor(prow_idx, 1) * count)], [(diag_a, base), (diag_b, base + half)]]
+                [(from_x, jnp.bitwise_xor(prow_idx, 1) * count)], [(diag_b, base + half)], [(diag_a, base)]]
     groups = [[(own, prow_idx * count)]]
     for s in range(1, prow_count):
         groups.append([(swap(own, "prow", s), jnp.bitwise_xor(prow_idx, s) * count)])

time: 67 us -> 72.4 us (1.081)
  waiting for transfers between devices: 29.9 us -> 33.2 us
  other arithmetic: 2.25 us -> 3.62 us
  starting transfers between devices: 10.5 us -> 9.19 us
  matrix products: 14.6 us -> 15.7 us
  local copies, waits for them, and re-layouts: 9.19 us -> 10 us
    ppermute x8, waiting for transfers between devices: 29.9 us -> 33.2 us  [swap(): lax.ppermute(value, axis, [(i, i ^ mask) for i in range(lax.axis_size(axi...]
    ppermute x8, starting transfers between devices: 10.5 us -> 9.19 us  [swap(): lax.ppermute(value, axis, [(i, i ^ mask) for i in range(lax.axis_size(axi...]
    dot_general x10, matrix products: 14.6 us -> 15.7 us  [contract(): product = jnp.dot(window, blocked, preferred_element_type=jnp.float32)]
    add x1, other arithmetic: 0.16 us -> 1.23 us  [shards(): piece = piece + swap(part[:, j * step:(j + 1) * step], 'cuts', s)]
    slice x1, local copies, waits for them, and re-layouts: 0.08 us -> 0.9 us  [shards(): piece = piece + swap(part[:, j * step:(j + 1) * step], 'cuts', s)]
  transfers between devices with their start and end apart: 8 -> 8, of which waited for: 6 -> 4; matrix products, arithmetic and copies ran while one was open for 35% -> 35% of each run, Pallas kernels for 0% -> 0%
where the time goes in v19:
time: 72.4 us; the launch traced here: 71.9 us
  waiting for transfers between devices  33.2 us (46%)
  matrix products  15.7 us (22%)
  local copies, waits for them, and re-layouts  10 us (14%)
  starting transfers between devices  9.19 us (13%)
  other arithmetic  3.62 us (5%)
    ppermute x8, waiting for transfers between devices, swap(): lax.ppermute(value, axis, [(i, i ^ mask) for i in range(lax.axis_size(axi...  33.2 us
    dot_general x10, matrix products, contract(): product = jnp.dot(window, blocked, preferred_element_type=jnp.float32)  15.7 us
    ppermute x8, starting transfers between devices, swap(): lax.ppermute(value, axis, [(i, i ^ mask) for i in range(lax.axis_size(axi...  9.19 us
    gather x2, local copies, waits for them, and re-layouts, shards(): fetched = swap(jnp.take(piece, wanted, axis=0, mode='clip'), 'prow', half)  3.19 us
    gather x2, local copies, waits for them, and re-layouts, shards(): results.append(piece - jnp.take(fetched, local, axis=0, mode='clip'))  2.36 us
    dynamic_slice x2, local copies, waits for them, and re-layouts, contract(): lax.dynamic_slice_in_dim(labels, o, b.shape[0])[:, None]  1.73 us
  transfers between devices with their start and end apart: 8, of which 4 were waited for; matrix products, arithmetic and copies ran while one was open for 35% of the time, Pallas kernels for 0%

profile of v19, /device:TPU:0, one launch (start us, length us, event | category | flops | bytes accessed | tf_op | source)
XLA Modules:
  0.0 71.9 jit_solution(10243473330492402405)
XLA Ops:
  0.0 3.0 %collective-permute-start = (bf16[800,400]{0,1:T(8,128)(2,1)}, bf16[800,400]{0,1:T(8,128)(2,1)S(1)}, u32[]{:S(2)}, u32[]{:S(2)}) collective-permute-start(bf16[800,400]{0,1:T(8,128)(2,1)} %param.6), channel_id=1, source_target_pairs={{0,16},{8,24},{16,0},{24,8},{1,17},{9,25},{17,1},{25,9},{2,18},{10... | collective-permute-start | bytes 1920008 | tf_op jit(solution)/shard_map/ppermute | solution.py:10
  3.0 1.5 %collective-permute-start.2 = (bf16[800,400]{0,1:T(8,128)(2,1)}, bf16[800,400]{0,1:T(8,128)(2,1)S(1)}, u32[]{:S(2)}, u32[]{:S(2)}) collective-permute-start(bf16[800,400]{0,1:T(8,128)(2,1)} %param.6), channel_id=1, source_target_pairs={{0,8},{8,0},{16,24},{24,16},{1,9},{9,1},{17,25},{25,17},{2,10},{10... | collective-permute-start | bytes 1920008 | tf_op jit(solution)/shard_map/ppermute | solution.py:10
  4.5 0.9 %fusion.30 = (s32[800]{0:T(1024)S(1)}, s32[800]{0:T(1024)S(1)}, s32[800]{0:T(1024)S(1)}) fusion(s32[6400]{0:T(1024)} %param.7, s32[]{:T(128)S(6)} %dynamic_slice.76, s32[]{:T(128)S(6)} %dynamic_slice.73, s32[]{:T(128)S(6)} %dynamic_slice.70), kind=kLoop, calls=%fused_computation.48 | loop fusion | bytes 19212 | tf_op jit(solution)/shard_map/dynamic_slice | solution.py:41
  5.3 0.8 %fusion.29 = (s32[400]{0:T(512)S(1)}, s32[400]{0:T(512)S(1)}) fusion(s32[6400]{0:T(1024)} %param.7, s32[]{:T(128)S(6)} %dynamic_slice.86, s32[]{:T(128)S(6)} %dynamic_slice.79), kind=kLoop, calls=%fused_computation.47 | loop fusion | bytes 6408 | tf_op jit(solution)/shard_map/dynamic_slice | solution.py:41
  6.2 3.0 %fusion.4 = f32[768,400]{0,1:T(8,128)S(1)} fusion(bf16[1536,3200]{1,0:T(8,128)(2,1)} %param.5, s32[]{:T(128)S(6)} %select_n.100, s32[]{:T(128)S(6)} %select_n.86, bf16[800,400]{0,1:T(8,128)(2,1)} %param.6, s32[800]{0:T(1024)S(1)} %get-tuple-element.19, s32[400]{0:T(512)} %param.8), kind=kOutput, calls=%fused_computation.13 | convolution fusion | flops 492160000 | bytes 3327112 | tf_op jit(solution)/shard_map/dot_general | solution.py:43
  9.2 3.3 %fusion.8 = f32[768,400]{0,1:T(8,128)S(1)} fusion(bf16[1536,3200]{1,0:T(8,128)(2,1)} %param.5, s32[]{:T(128)S(6)} %select_n.84, s32[]{:T(128)S(6)} %select_n.86, bf16[800,400]{0,1:T(8,128)(2,1)} %param.6, s32[800]{0:T(1024)S(1)} %get-tuple-element.19, s32[400]{0:T(512)S(1)} %copy-done.1), kind=kOutput, calls=%fused_computation.17 | convolution fusion | flops 492160000 | bytes 3326664 | tf_op jit(solution)/shard_map/dot_general | solution.py:43
  12.5 8.2 %collective-permute-done.2 = bf16[800,400]{0,1:T(8,128)(2,1)S(1)} collective-permute-done((bf16[800,400]{0,1:T(8,128)(2,1)}, bf16[800,400]{0,1:T(8,128)(2,1)S(1)}, u32[]{:S(2)}, u32[]{:S(2)}) %collective-permute-start.2) | collective-permute-done | bytes 640032 | tf_op jit(solution)/shard_map/ppermute | solution.py:10
  20.9 0.4 collective-permute-start.3
  21.3 1.8 %collective-permute-start.1 = (bf16[400,400]{0,1:T(8,128)(2,1)S(1)}, bf16[400,400]{0,1:T(8,128)(2,1)S(1)}, u32[]{:S(2)}, u32[]{:S(2)}) collective-permute-start(bf16[400,400]{0,1:T(8,128)(2,1)S(1)} %slice.28), channel_id=1, source_target_pairs={{0,8},{8,0},{16,24},{24,16},{1,9},{9,1},{17,25},{25,17},{2,10},{10... | collective-permute-start | bytes 960008 | tf_op jit(solution)/shard_map/ppermute | solution.py:10
  23.1 1.3 %convolution_add_fusion.1 = f32[768,400]{0,1:T(8,128)S(1)} fusion(f32[768,400]{0,1:T(8,128)S(1)} %fusion.4, bf16[1536,3200]{1,0:T(8,128)(2,1)S(1)} %copy-done, s32[]{:T(128)S(6)} %select_n.100, s32[]{:T(128)S(6)} %select_n.91, bf16[800,400]{0,1:T(8,128)(2,1)S(1)} %collective-permute-done, s32[800]{0:T(1024)S(1)} %get-tuple-element.18, s32[400]{0:T(512)S(1)} %copy-done.1), kind=kOutput, calls=%fused_computation.7 | convolution fusion | flops 492467200 | bytes 4556808 | tf_op jit(solution)/shard_map/dot_general | solution.py:43
  24.3 1.3 %convolution_add_fusion.3 = f32[768,400]{0,1:T(8,128)S(1)} fusion(f32[768,400]{0,1:T(8,128)S(1)} %fusion.8, bf16[1536,3200]{1,0:T(8,128)(2,1)S(1)} %copy-done, s32[]{:T(128)S(6)} %select_n.84, s32[]{:T(128)S(6)} %select_n.91, bf16[800,400]{0,1:T(8,128)(2,1)S(1)} %collective-permute-done, s32[800]{0:T(1024)S(1)} %get-tuple-element.18, s32[400]{0:T(512)S(1)} %copy-done.1), kind=kOutput, calls=%fused_computation.10 | convolution fusion | flops 492467200 | bytes 4556808 | tf_op jit(solution)/shard_map/dot_general | solution.py:43
  25.6 5.4 %collective-permute-done.3 = bf16[400,400]{0,1:T(8,128)(2,1)S(1)} collective-permute-done((bf16[400,400]{0,1:T(8,128)(2,1)S(1)}, bf16[400,400]{0,1:T(8,128)(2,1)S(1)}, u32[]{:S(2)}, u32[]{:S(2)}) %collective-permute-start.3) | collective-permute-done | bytes 320032 | tf_op jit(solution)/shard_map/ppermute | solution.py:10
  31.0 0.8 %fusion.14 = f32[768,400]{0,1:T(8,128)S(1)} fusion(bf16[1536,3200]{1,0:T(8,128)(2,1)S(1)} %copy-done, s32[]{:T(128)S(6)} %select_n.100, s32[]{:T(128)S(6)} %select_n.97, bf16[400,400]{0,1:T(8,128)(2,1)S(1)} %collective-permute-done.3, s32[400]{0:T(512)S(1)} %get-tuple-element.16, s32[400]{0:T(512)S(1)} %copy-done.1), kind=kOutput, calls=%fused_computation.26 | convolution fusion | flops 246080000 | bytes 2428936 | tf_op jit(solution)/shard_map/dot_general | solution.py:43
  31.8 0.8 %fusion.16 = f32[768,400]{0,1:T(8,128)S(1)} fusion(bf16[1536,3200]{1,0:T(8,128)(2,1)S(1)} %copy-done, s32[]{:T(128)S(6)} %select_n.84, s32[]{:T(128)S(6)} %select_n.97, bf16[400,400]{0,1:T(8,128)(2,1)S(1)} %collective-permute-done.3, s32[400]{0:T(512)S(1)} %get-tuple-element.16, s32[400]{0:T(512)S(1)} %copy-done.1), kind=kOutput, calls=%fused_computation.28 | convolution fusion | flops 246080000 | bytes 2428936 | tf_op jit(solution)/shard_map/dot_general | solution.py:43
  32.6 1.3 %fusion = f32[768,400]{0,1:T(8,128)S(1)} fusion(f32[768,400]{0,1:T(8,128)S(1)} %fusion.14, f32[768,400]{0,1:T(8,128)S(1)} %convolution_add_fusion.1, bf16[1536,3200]{1,0:T(8,128)(2,1)S(1)} %copy-done, s32[]{:T(128)S(6)} %select_n.100, s32[]{:T(128)S(6)} %select_n.94, bf16[800,400]{0,1:T(8,128)(2,1)S(1)} %collective-permute-done.2, ...), kind=kOutput, calls=%fused_computation.6 | convolution fusion | flops 492774400 | bytes 5785608 | tf_op jit(solution)/shard_map/dot_general | solution.py:43
  33.9 1.3 %fusion.1 = f32[768,400]{0,1:T(8,128)S(1)} fusion(f32[768,400]{0,1:T(8,128)S(1)} %fusion.16, f32[768,400]{0,1:T(8,128)S(1)} %convolution_add_fusion.3, bf16[1536,3200]{1,0:T(8,128)(2,1)S(1)} %copy-done, s32[]{:T(128)S(6)} %select_n.84, s32[]{:T(128)S(6)} %select_n.94, bf16[800,400]{0,1:T(8,128)(2,1)S(1)} %collective-permute-done.2, ...), kind=kOutput, calls=%fused_computation.9 | convolution fusion | flops 492774400 | bytes 5785608 | tf_op jit(solution)/shard_map/dot_general | solution.py:43
  35.2 0.8 %fusion.10 = f32[768,400]{0,1:T(8,128)S(1)} fusion(bf16[1536,3200]{1,0:T(8,128)(2,1)S(1)} %copy-done, s32[]{:T(128)S(6)} %select_n.84, s32[]{:T(128)S(6)} %select_n.102, bf16[400,400]{0,1:T(8,128)(2,1)S(1)} %collective-permute-done.1, s32[400]{0:T(512)S(1)} %get-tuple-element.15, s32[400]{0:T(512)S(1)} %copy-done.1), kind=kOutput, calls=%fused_computation.22 | convolution fusion | flops 246080000 | bytes 2428936 | tf_op jit(solution)/shard_map/dot_general | solution.py:43
  36.1 0.9 %fusion.28 = (f32[768,200]{0,1:T(8,128)}, f32[768,200]{0,1:T(8,128)S(1)}) fusion(f32[768,400]{0,1:T(8,128)S(1)} %add.127), kind=kLoop, calls=%fused_computation.46 | loop fusion | bytes 2457600 | tf_op jit(solution)/shard_map/slice | solution.py:76
  37.0 0.5 collective-permute-start.6
  37.5 0.8 %dynamic-slice_subtract_fusion.1 = (s32[768]{0:T(1024)S(1)}, s32[768]{0:T(1024)S(1)}) fusion(s32[6144]{0:T(1024)} %param.9, s32[]{:T(128)S(6)} %select_n.104, s32[]{:T(128)S(6)} %mul.45, s32[]{:T(128)S(6)} %mul.43, s32[]{:T(128)S(6)} %select_n.105), kind=kLoop, calls=%fused_computation.35 | loop fusion | flops 1536 | bytes 12304 | tf_op jit(solution)/shard_map/sub | solution.py:66
  38.3 2.0 %fusion.12 = f32[768,400]{0,1:T(8,128)S(1)} fusion(bf16[1536,3200]{1,0:T(8,128)(2,1)} %param.5, s32[]{:T(128)S(6)} %select_n.100, s32[]{:T(128)S(6)} %select_n.102, bf16[400,400]{0,1:T(8,128)(2,1)S(1)} %collective-permute-done.1, s32[400]{0:T(512)S(1)} %get-tuple-element.15, s32[400]{0:T(512)S(1)} %copy-done.1), kind=kOutput, calls=%fused_computation.24 | convolution fusion | flops 246080000 | bytes 2338440 | tf_op jit(solution)/shard_map/dot_general | solution.py:43
  40.5 1.2 %slice_add_fusion.1 = (f32[768,200]{0,1:T(8,128)S(1)}, f32[768,200]{0,1:T(8,128)S(1)}) fusion(f32[768,200]{0,1:T(8,128)S(1)} %collective-permute-done.4, f32[768,400]{0,1:T(8,128)S(1)} %add.126, f32[768,200]{0,1:T(8,128)} %collective-permute-done.6), kind=kLoop, calls=%fused_computation.31 | loop fusion | flops 307200 | bytes 3686400 | tf_op jit(solution)/shard_map/add | solution.py:76
  41.8 0.6 collective-permute-start.5
  42.4 0.3 copy.8
  42.7 2.1 %gather_fusion.1 = f32[768,200]{1,0:T(8,128)S(1)} fusion(f32[768,200]{1,0:T(8,128)S(1)} %copy.8, s32[1024]{0:T(1024)S(1)} %pad_clamp_fusion), kind=kCustom, calls=%fused_computation.1 | custom fusion | bytes 1231872 | tf_op jit(solution)/shard_map/jit(_take)/gather | solution.py:78
  44.8 1.1 %copy.9 = f32[768,200]{0,1:T(8,128)} copy(f32[768,200]{1,0:T(8,128)S(1)} %gather_fusion.1) | data formatting | bytes 1228800 | tf_op jit(solution)/shard_map/jit(_take)/gather | solution.py:78
  45.9 1.5 %collective-permute-start.7 = (f32[768,200]{0,1:T(8,128)}, f32[768,200]{0,1:T(8,128)S(1)}, u32[]{:S(2)}, u32[]{:S(2)}) collective-permute-start(f32[768,200]{0,1:T(8,128)} %copy.9), channel_id=1, source_target_pairs={{0,16},{8,24},{16,0},{24,8},{1,17},{9,25},{17,1},{25,9},{2,18},{10... | collective-permute-start | bytes 1843208 | tf_op jit(solution)/shard_map/ppermute | solution.py:10
  47.3 11.3 %collective-permute-done.5 = f32[768,200]{0,1:T(8,128)} collective-permute-done((f32[768,200]{0,1:T(8,128)S(1)}, f32[768,200]{0,1:T(8,128)}, u32[]{:S(2)}, u32[]{:S(2)}) %collective-permute-start.5) | collective-permute-done | bytes 614432 | tf_op jit(solution)/shard_map/ppermute | solution.py:10
  58.6 1.3 %copy.6 = f32[768,200]{1,0:T(8,128)S(1)} copy(f32[768,200]{0,1:T(8,128)} %collective-permute-done.5) | data formatting | bytes 1228800 | tf_op jit(solution)/shard_map/ppermute | solution.py:10
  60.0 2.1 %gather_fusion = f32[768,200]{1,0:T(8,128)S(1)} fusion(f32[768,200]{1,0:T(8,128)S(1)} %copy.6, s32[1024]{0:T(1024)S(1)} %pad_clamp_fusion.1), kind=kCustom, calls=%fused_computation | custom fusion | bytes 1231872 | tf_op jit(solution)/shard_map/jit(_take)/gather | solution.py:82
  62.5 8.3 %collective-permute-done.7 = f32[768,200]{0,1:T(8,128)S(1)} collective-permute-done((f32[768,200]{0,1:T(8,128)}, f32[768,200]{0,1:T(8,128)S(1)}, u32[]{:S(2)}, u32[]{:S(2)}) %collective-permute-start.7) | collective-permute-done | bytes 614432 | tf_op jit(solution)/shard_map/ppermute | solution.py:10
  70.8 1.1 %pad_maximum_fusion = f32[768,400]{0,1:T(8,128)} fusion(f32[768,200]{0,1:T(8,128)S(1)} %sub.23, f32[768,200]{0,1:T(8,128)S(1)} %sub.20), kind=kLoop, calls=%fused_computation.19 | loop fusion | flops 307200 | bytes 2457600 | tf_op jit(solution)/shard_map/concatenate | solution.py:83
  (18 shorter events, 1.0 us)
Async XLA Ops:
  0.0 21.3 %collective-permute-start = (bf16[800,400]{0,1:T(8,128)(2,1)}, bf16[800,400]{0,1:T(8,128)(2,1)S(1)}, u32[]{:S(2)}, u32[]{:S(2)}) collective-permute-start(bf16[800,400]{0,1:T(8,128)(2,1)} %param.6), channel_id=1, source_target_pairs={{0,16},{8,24},{16,0},{24,8},{1,17},{9,25},{17,1},{25,9},{2,18},{10... | collective-permute-start | bytes 1920008 | tf_op jit(solution)/shard_map/ppermute | solution.py:10
  3.0 17.7 %collective-permute-start.2 = (bf16[800,400]{0,1:T(8,128)(2,1)}, bf16[800,400]{0,1:T(8,128)(2,1)S(1)}, u32[]{:S(2)}, u32[]{:S(2)}) collective-permute-start(bf16[800,400]{0,1:T(8,128)(2,1)} %param.6), channel_id=1, source_target_pairs={{0,8},{8,0},{16,24},{24,16},{1,9},{9,1},{17,25},{25,17},{2,10},{10... | collective-permute-start | bytes 1920008 | tf_op jit(solution)/shard_map/ppermute | solution.py:10
  4.5 4.7 %copy-start.1 = (s32[400]{0:T(512)S(1)}, s32[400]{0:T(512)}, u32[]{:S(2)}) copy-start(s32[400]{0:T(512)} %param.8) | copy-start | bytes 4804
  6.2 16.9 %copy-start = (bf16[1536,3200]{1,0:T(8,128)(2,1)S(1)}, bf16[1536,3200]{1,0:T(8,128)(2,1)}, u32[]{:S(2)}) copy-start(bf16[1536,3200]{1,0:T(8,128)(2,1)} %param.5) | copy-start | bytes 29491204
  20.9 10.1 %collective-permute-start.3 = (bf16[400,400]{0,1:T(8,128)(2,1)S(1)}, bf16[400,400]{0,1:T(8,128)(2,1)S(1)}, u32[]{:S(2)}, u32[]{:S(2)}) collective-permute-start(bf16[400,400]{0,1:T(8,128)(2,1)S(1)} %slice.29), channel_id=1, source_target_pairs={{0,16},{8,24},{16,0},{24,8},{1,17},{9,25},{17,1},{25,9},{2,18},{10... | collective-permute-start | bytes 960008 | tf_op jit(solution)/shard_map/ppermute | solution.py:10
  21.3 13.9 %collective-permute-start.1 = (bf16[400,400]{0,1:T(8,128)(2,1)S(1)}, bf16[400,400]{0,1:T(8,128)(2,1)S(1)}, u32[]{:S(2)}, u32[]{:S(2)}) collective-permute-start(bf16[400,400]{0,1:T(8,128)(2,1)S(1)} %slice.28), channel_id=1, source_target_pairs={{0,8},{8,0},{16,24},{24,16},{1,9},{9,1},{17,25},{25,17},{2,10},{10... | collective-permute-start | bytes 960008 | tf_op jit(solution)/shard_map/ppermute | solution.py:10
  37.0 3.5 %collective-permute-start.4 = (f32[768,200]{0,1:T(8,128)}, f32[768,200]{0,1:T(8,128)S(1)}, u32[]{:S(2)}, u32[]{:S(2)}) collective-permute-start(f32[768,200]{0,1:T(8,128)} %get-tuple-element.13), channel_id=1, source_target_pairs={{0,1},{1,0},{2,3},{3,2},{4,5},{5,4},{6,7},{7,6},{8,9},{9,8},{10,11... | collective-permute-start | bytes 1843208 | tf_op jit(solution)/shard_map/ppermute | solution.py:10
  37.0 3.5 %collective-permute-start.6 = (f32[768,200]{0,1:T(8,128)S(1)}, f32[768,200]{0,1:T(8,128)}, u32[]{:S(2)}, u32[]{:S(2)}) collective-permute-start(f32[768,200]{0,1:T(8,128)S(1)} %get-tuple-element.14), channel_id=1, source_target_pairs={{0,1},{1,0},{2,3},{3,2},{4,5},{5,4},{6,7},{7,6},{8,9},{9,8},{10,11... | collective-permute-start | bytes 1843208 | tf_op jit(solution)/shard_map/ppermute | solution.py:10
  41.8 16.9 %collective-permute-start.5 = (f32[768,200]{0,1:T(8,128)S(1)}, f32[768,200]{0,1:T(8,128)}, u32[]{:S(2)}, u32[]{:S(2)}) collective-permute-start(f32[768,200]{0,1:T(8,128)S(1)} %get-tuple-element.11), channel_id=1, source_target_pairs={{0,16},{8,24},{16,0},{24,8},{1,17},{9,25},{17,1},{25,9},{2,18},{10... | collective-permute-start | bytes 1843208 | tf_op jit(solution)/shard_map/ppermute | solution.py:10
  45.9 24.9 %collective-permute-start.7 = (f32[768,200]{0,1:T(8,128)}, f32[768,200]{0,1:T(8,128)S(1)}, u32[]{:S(2)}, u32[]{:S(2)}) collective-permute-start(f32[768,200]{0,1:T(8,128)} %copy.9), channel_id=1, source_target_pairs={{0,16},{8,24},{16,0},{24,8},{1,17},{9,25},{17,1},{25,9},{2,18},{10... | collective-permute-start | bytes 1843208 | tf_op jit(solution)/shard_map/ppermute | solution.py:10

commit v20 on v19

--- a/solution.py
+++ b/solution.py
@@ -1,8 +1,6 @@
 import jax
 import jax.numpy as jnp
 from jax import lax
-from jax.experimental import pallas as pl
-from jax.experimental.pallas import tpu as pltpu
 from jax.sharding import PartitionSpec as P
 
 
@@ -18,9 +16,9 @@
         from_y = swap(own, "prow", 2)
         diag_a = swap(from_y[:half], "prow", 1)
         diag_b = swap(from_x[half:], "prow", 2)
-        base = jnp.bitwise_xor(prow_idx, 3) * count
+        diag = jnp.concatenate([diag_a, diag_b], axis=0)
         return [[(own, prow_idx * count)], [(from_y, jnp.bitwise_xor(prow_idx, 2) * count)],
-                [(from_x, jnp.bitwise_xor(prow_idx, 1) * count)], [(diag_b, base + half)], [(diag_a, base)]]
+                [(from_x, jnp.bitwise_xor(prow_idx, 1) * count)], [(diag, jnp.bitwise_xor(prow_idx, 3) * count)]]
     groups = [[(own, prow_idx * count)]]
     for s in range(1, prow_count):
         groups.append([(swap(own, "prow", s), jnp.bitwise_xor(prow_idx, s) * count)])

time: 72.4 us -> 70.9 us (0.979)
  local copies, waits for them, and re-layouts: 10 us -> 8.1 us
  waiting for transfers between devices: 33.2 us -> 31.8 us
  other arithmetic: 3.62 us -> 4.92 us
  starting transfers between devices: 9.19 us -> 10.4 us
    ppermute x8, waiting for transfers between devices: 33.2 us -> 31.8 us  [swap(): lax.ppermute(value, axis, [(i, i ^ mask) for i in range(lax.axis_size(axi...]
    ppermute x8, starting transfers between devices: 9.19 us -> 10.4 us  [swap(): lax.ppermute(value, axis, [(i, i ^ mask) for i in range(lax.axis_size(axi...]
    ppermute x1, local copies, waits for them, and re-layouts: 1.34 us -> 0.26 us  [swap(): lax.ppermute(value, axis, [(i, i ^ mask) for i in range(lax.axis_size(axi...]
    sub x1, other arithmetic: 0.06 us -> 1.14 us  [shards(): results.append(piece - fetched)]
    dynamic_slice x2 -> x1, local copies, waits for them, and re-layouts: 1.73 us -> 0.89 us  [contract(): lax.dynamic_slice_in_dim(labels, o, b.shape[0])[:, None]]
    dot_general x10 -> x8, matrix products: 15.7 us -> 15.1 us  [contract(): product = jnp.dot(window, blocked, preferred_element_type=jnp.float32)]
  transfers between devices with their start and end apart: 8 -> 8, of which waited for: 4 -> 5; matrix products, arithmetic and copies ran while one was open for 35% -> 31% of each run, Pallas kernels for 0% -> 0%
where the time goes in v20:
time: 70.9 us; the launch traced here: 70.5 us
  waiting for transfers between devices  31.8 us (45%)
  matrix products  15.1 us (21%)
  starting transfers between devices  10.4 us (15%)
  local copies, waits for them, and re-layouts  8.1 us (11%)
  other arithmetic  4.92 us (7%)
    ppermute x8, waiting for transfers between devices, swap(): lax.ppermute(value, axis, [(i, i ^ mask) for i in range(lax.axis_size(axi...  31.8 us
    dot_general x8, matrix products, contract(): product = jnp.dot(window, blocked, preferred_element_type=jnp.float32)  15.1 us
    ppermute x8, starting transfers between devices, swap(): lax.ppermute(value, axis, [(i, i ^ mask) for i in range(lax.axis_size(axi...  10.4 us
    gather x2, local copies, waits for them, and re-layouts, shards(): fetched = swap(jnp.take(piece, wanted, axis=0, mode='clip'), 'prow', half)  3.19 us
    gather x2, local copies, waits for them, and re-layouts, shards(): results.append(piece - jnp.take(fetched, local, axis=0, mode='clip'))  2.36 us
  transfers between devices with their start and end apart: 8, of which 5 were waited for; matrix products, arithmetic and copies ran while one was open for 31% of the time, Pallas kernels for 0%

profile of v20, /device:TPU:0, one launch (start us, length us, event | category | flops | bytes accessed | tf_op | source)
XLA Modules:
  0.0 70.5 jit_solution(11928722925623848135)
XLA Ops:
  0.0 3.0 %collective-permute-start = (bf16[800,400]{0,1:T(8,128)(2,1)}, bf16[800,400]{0,1:T(8,128)(2,1)S(1)}, u32[]{:S(2)}, u32[]{:S(2)}) collective-permute-start(bf16[800,400]{0,1:T(8,128)(2,1)} %param.6), channel_id=1, source_target_pairs={{0,16},{8,24},{16,0},{24,8},{1,17},{9,25},{17,1},{25,9},{2,18},{10... | collective-permute-start | bytes 1920008 | tf_op jit(solution)/shard_map/ppermute | solution.py:8
  3.0 1.5 %collective-permute-start.2 = (bf16[800,400]{0,1:T(8,128)(2,1)}, bf16[800,400]{0,1:T(8,128)(2,1)S(1)}, u32[]{:S(2)}, u32[]{:S(2)}) collective-permute-start(bf16[800,400]{0,1:T(8,128)(2,1)} %param.6), channel_id=1, source_target_pairs={{0,8},{8,0},{16,24},{24,16},{1,9},{9,1},{17,25},{25,17},{2,10},{10... | collective-permute-start | bytes 1920008 | tf_op jit(solution)/shard_map/ppermute | solution.py:8
  4.5 0.9 %fusion.21 = (s32[800]{0:T(1024)S(1)}, s32[800]{0:T(1024)S(1)}, s32[800]{0:T(1024)S(1)}, s32[800]{0:T(1024)S(1)}) fusion(s32[6400]{0:T(1024)} %param.7, s32[]{:T(128)S(6)} %dynamic_slice.70, s32[]{:T(128)S(6)} %dynamic_slice.61, s32[]{:T(128)S(6)} %dynamic_slice.58, s32[]{:T(128)S(6)} %dynamic_slice.64), kind=kLoop, calls=%fused_computation.39 | loop fusion | bytes 25616 | tf_op jit(solution)/shard_map/dynamic_slice | solution.py:39
  5.4 3.0 %fusion.10 = f32[768,400]{0,1:T(8,128)S(1)} fusion(bf16[1536,3200]{1,0:T(8,128)(2,1)} %param.5, s32[]{:T(128)S(6)} %select_n.71, s32[]{:T(128)S(6)} %select_n.73, bf16[800,400]{0,1:T(8,128)(2,1)} %param.6, s32[800]{0:T(1024)S(1)} %get-tuple-element.17, s32[400]{0:T(512)} %param.8), kind=kOutput, calls=%fused_computation.20 | convolution fusion | flops 492160000 | bytes 3327112 | tf_op jit(solution)/shard_map/dot_general | solution.py:41
  8.3 3.3 %fusion.6 = f32[768,400]{0,1:T(8,128)S(1)} fusion(bf16[1536,3200]{1,0:T(8,128)(2,1)} %param.5, s32[]{:T(128)S(6)} %select_n.84, s32[]{:T(128)S(6)} %select_n.73, bf16[800,400]{0,1:T(8,128)(2,1)} %param.6, s32[800]{0:T(1024)S(1)} %get-tuple-element.17, s32[400]{0:T(512)S(1)} %copy-done.1), kind=kOutput, calls=%fused_computation.16 | convolution fusion | flops 492160000 | bytes 3326664 | tf_op jit(solution)/shard_map/dot_general | solution.py:41
  11.6 7.6 %collective-permute-done = bf16[800,400]{0,1:T(8,128)(2,1)S(1)} collective-permute-done((bf16[800,400]{0,1:T(8,128)(2,1)}, bf16[800,400]{0,1:T(8,128)(2,1)S(1)}, u32[]{:S(2)}, u32[]{:S(2)}) %collective-permute-start) | collective-permute-done | bytes 640032 | tf_op jit(solution)/shard_map/ppermute | solution.py:8
  19.3 1.8 %collective-permute-start.1 = (bf16[400,400]{0,1:T(8,128)(2,1)S(1)}, bf16[400,400]{0,1:T(8,128)(2,1)S(1)}, u32[]{:S(2)}, u32[]{:S(2)}) collective-permute-start(bf16[400,400]{0,1:T(8,128)(2,1)S(1)} %slice.28), channel_id=1, source_target_pairs={{0,8},{8,0},{16,24},{24,16},{1,9},{9,1},{17,25},{25,17},{2,10},{10... | collective-permute-start | bytes 960008 | tf_op jit(solution)/shard_map/ppermute | solution.py:8
  21.3 1.6 %collective-permute-start.3 = (bf16[400,400]{0,1:T(8,128)(2,1)S(1)}, bf16[400,400]{0,1:T(8,128)(2,1)S(1)}, u32[]{:S(2)}, u32[]{:S(2)}) collective-permute-start(bf16[400,400]{0,1:T(8,128)(2,1)S(1)} %slice.29), channel_id=1, source_target_pairs={{0,16},{8,24},{16,0},{24,8},{1,17},{9,25},{17,1},{25,9},{2,18},{10... | collective-permute-start | bytes 960008 | tf_op jit(solution)/shard_map/ppermute | solution.py:8
  22.8 1.3 %convolution_add_fusion.3 = f32[768,400]{0,1:T(8,128)S(1)} fusion(f32[768,400]{0,1:T(8,128)S(1)} %fusion.10, bf16[1536,3200]{1,0:T(8,128)(2,1)S(1)} %copy-done, s32[]{:T(128)S(6)} %select_n.71, s32[]{:T(128)S(6)} %select_n.78, bf16[800,400]{0,1:T(8,128)(2,1)S(1)} %collective-permute-done, s32[800]{0:T(1024)S(1)} %get-tuple-element.16, s32[400]{0:T(512)S(1)} %copy-done.1), kind=kOutput, calls=%fused_computation.9 | convolution fusion | flops 492467200 | bytes 4556808 | tf_op jit(solution)/shard_map/dot_general | solution.py:41
  24.1 1.3 %convolution_add_fusion.1 = f32[768,400]{0,1:T(8,128)S(1)} fusion(f32[768,400]{0,1:T(8,128)S(1)} %fusion.6, bf16[1536,3200]{1,0:T(8,128)(2,1)S(1)} %copy-done, s32[]{:T(128)S(6)} %select_n.84, s32[]{:T(128)S(6)} %select_n.78, bf16[800,400]{0,1:T(8,128)(2,1)S(1)} %collective-permute-done, s32[800]{0:T(1024)S(1)} %get-tuple-element.16, s32[400]{0:T(512)S(1)} %copy-done.1), kind=kOutput, calls=%fused_computation.7 | convolution fusion | flops 492467200 | bytes 4556808 | tf_op jit(solution)/shard_map/dot_general | solution.py:41
  25.4 1.3 %convolution_add_fusion.2 = f32[768,400]{0,1:T(8,128)S(1)} fusion(f32[768,400]{0,1:T(8,128)S(1)} %convolution_add_fusion.3, bf16[1536,3200]{1,0:T(8,128)(2,1)S(1)} %copy-done, s32[]{:T(128)S(6)} %select_n.71, s32[]{:T(128)S(6)} %select_n.81, bf16[800,400]{0,1:T(8,128)(2,1)S(1)} %collective-permute-done.2, s32[800]{0:T(1024)S(1)} %get-tuple-element.18, ...), kind=kOutput, calls=%fused_computation.8 | convolution fusion | flops 492467200 | bytes 4556808 | tf_op jit(solution)/shard_map/dot_general | solution.py:41
  26.7 1.3 %convolution_add_fusion = f32[768,400]{0,1:T(8,128)S(1)} fusion(f32[768,400]{0,1:T(8,128)S(1)} %convolution_add_fusion.1, bf16[1536,3200]{1,0:T(8,128)(2,1)S(1)} %copy-done, s32[]{:T(128)S(6)} %select_n.84, s32[]{:T(128)S(6)} %select_n.81, bf16[800,400]{0,1:T(8,128)(2,1)S(1)} %collective-permute-done.2, s32[800]{0:T(1024)S(1)} %get-tuple-element.18, ...), kind=kOutput, calls=%fused_computation.6 | convolution fusion | flops 492467200 | bytes 4556808 | tf_op jit(solution)/shard_map/dot_general | solution.py:41
  28.0 2.0 %collective-permute-done.1 = bf16[400,400]{0,1:T(8,128)(2,1)S(1)} collective-permute-done((bf16[400,400]{0,1:T(8,128)(2,1)S(1)}, bf16[400,400]{0,1:T(8,128)(2,1)S(1)}, u32[]{:S(2)}, u32[]{:S(2)}) %collective-permute-start.1) | collective-permute-done | bytes 320032 | tf_op jit(solution)/shard_map/ppermute | solution.py:8
  30.0 1.4 %collective-permute-done.3 = bf16[400,400]{0,1:T(8,128)(2,1)S(1)} collective-permute-done((bf16[400,400]{0,1:T(8,128)(2,1)S(1)}, bf16[400,400]{0,1:T(8,128)(2,1)S(1)}, u32[]{:S(2)}, u32[]{:S(2)}) %collective-permute-start.3) | collective-permute-done | bytes 320032 | tf_op jit(solution)/shard_map/ppermute | solution.py:8
  31.6 1.2 %fusion = f32[768,400]{0,1:T(8,128)S(1)} fusion(bf16[1536,3200]{1,0:T(8,128)(2,1)S(1)} %copy-done, s32[]{:T(128)S(6)} %select_n.71, s32[]{:T(128)S(6)} %select_n.86, bf16[800,400]{0,1:T(8,128)(2,1)S(1)} %pad_maximum_fusion.1, s32[800]{0:T(1024)S(1)} %get-tuple-element.15, s32[400]{0:T(512)S(1)} %copy-done.1), kind=kOutput, calls=%fused_computation.10 | convolution fusion | flops 492160000 | bytes 3328008 | tf_op jit(solution)/shard_map/dot_general | solution.py:41
  33.0 0.9 %fusion.20 = (f32[768,200]{0,1:T(8,128)}, f32[768,200]{0,1:T(8,128)S(1)}) fusion(f32[768,400]{0,1:T(8,128)S(1)} %add.101), kind=kLoop, calls=%fused_computation.38 | loop fusion | bytes 2457600 | tf_op jit(solution)/shard_map/slice | solution.py:74
  33.9 0.5 collective-permute-start.6
  34.4 0.8 %dynamic-slice_subtract_fusion.1 = (s32[768]{0:T(1024)S(1)}, s32[768]{0:T(1024)S(1)}) fusion(s32[6144]{0:T(1024)} %param.9, s32[]{:T(128)S(6)} %select_n.88, s32[]{:T(128)S(6)} %mul.45, s32[]{:T(128)S(6)} %mul.43, s32[]{:T(128)S(6)} %select_n.89), kind=kLoop, calls=%fused_computation.29 | loop fusion | flops 1536 | bytes 12304 | tf_op jit(solution)/shard_map/sub | solution.py:64
  35.2 2.6 %fusion.2 = f32[768,400]{0,1:T(8,128)S(1)} fusion(bf16[1536,3200]{1,0:T(8,128)(2,1)} %param.5, s32[]{:T(128)S(6)} %select_n.84, s32[]{:T(128)S(6)} %select_n.86, bf16[800,400]{0,1:T(8,128)(2,1)S(1)} %pad_maximum_fusion.1, s32[800]{0:T(1024)S(1)} %get-tuple-element.15, s32[400]{0:T(512)S(1)} %copy-done.1), kind=kOutput, calls=%fused_computation.12 | convolution fusion | flops 492160000 | bytes 3249864 | tf_op jit(solution)/shard_map/dot_general | solution.py:41
  37.9 1.2 %slice_add_fusion.1 = (f32[768,200]{0,1:T(8,128)S(1)}, f32[768,200]{0,1:T(8,128)S(1)}) fusion(f32[768,200]{0,1:T(8,128)S(1)} %collective-permute-done.4, f32[768,400]{0,1:T(8,128)S(1)} %add.100, f32[768,200]{0,1:T(8,128)} %collective-permute-done.6), kind=kLoop, calls=%fused_computation.25 | loop fusion | flops 307200 | bytes 3686400 | tf_op jit(solution)/shard_map/add | solution.py:74
  39.2 1.7 %collective-permute-start.5 = (f32[768,200]{0,1:T(8,128)S(1)}, f32[768,200]{0,1:T(8,128)S(1)}, u32[]{:S(2)}, u32[]{:S(2)}) collective-permute-start(f32[768,200]{0,1:T(8,128)S(1)} %get-tuple-element.11), channel_id=1, source_target_pairs={{0,16},{8,24},{16,0},{24,8},{1,17},{9,25},{17,1},{25,9},{2,18},{10... | collective-permute-start | bytes 1843208 | tf_op jit(solution)/shard_map/ppermute | solution.py:8
  40.8 0.3 copy.8
  41.1 2.1 %gather_fusion.1 = f32[768,200]{1,0:T(8,128)S(1)} fusion(f32[768,200]{1,0:T(8,128)S(1)} %copy.8, s32[1024]{0:T(1024)S(1)} %pad_clamp_fusion), kind=kCustom, calls=%fused_computation.1 | custom fusion | bytes 1231872 | tf_op jit(solution)/shard_map/jit(_take)/gather | solution.py:76
  43.2 1.1 %copy.9 = f32[768,200]{0,1:T(8,128)} copy(f32[768,200]{1,0:T(8,128)S(1)} %gather_fusion.1) | data formatting | bytes 1228800 | tf_op jit(solution)/shard_map/jit(_take)/gather | solution.py:76
  44.3 0.4 collective-permute-start.7
  44.7 11.2 %collective-permute-done.5 = f32[768,200]{0,1:T(8,128)S(1)} collective-permute-done((f32[768,200]{0,1:T(8,128)S(1)}, f32[768,200]{0,1:T(8,128)S(1)}, u32[]{:S(2)}, u32[]{:S(2)}) %collective-permute-start.5) | collective-permute-done | bytes 614432 | tf_op jit(solution)/shard_map/ppermute | solution.py:8
  56.0 0.3 copy.6
  56.2 2.1 %gather_fusion = f32[768,200]{1,0:T(8,128)S(1)} fusion(f32[768,200]{1,0:T(8,128)S(1)} %copy.6, s32[1024]{0:T(1024)S(1)} %pad_clamp_fusion.1), kind=kCustom, calls=%fused_computation | custom fusion | bytes 1231872 | tf_op jit(solution)/shard_map/jit(_take)/gather | solution.py:80
  58.3 0.2 copy.7
  58.7 9.6 %collective-permute-done.7 = f32[768,200]{0,1:T(8,128)} collective-permute-done((f32[768,200]{0,1:T(8,128)}, f32[768,200]{0,1:T(8,128)}, u32[]{:S(2)}, u32[]{:S(2)}) %collective-permute-start.7) | collective-permute-done | bytes 614432 | tf_op jit(solution)/shard_map/ppermute | solution.py:8
  68.3 1.1 %sub.23 = f32[768,200]{0,1:T(8,128)S(1)} subtract(f32[768,200]{0,1:T(8,128)S(1)} %get-tuple-element.12, f32[768,200]{0,1:T(8,128)} %collective-permute-done.7) | non-fusion elementwise | flops 153600 | bytes 1843200 | tf_op jit(solution)/shard_map/sub | solution.py:77
  69.4 1.1 %pad_maximum_fusion = f32[768,400]{0,1:T(8,128)} fusion(f32[768,200]{0,1:T(8,128)S(1)} %sub.23, f32[768,200]{0,1:T(8,128)S(1)} %sub.20), kind=kLoop, calls=%fused_computation.22 | loop fusion | flops 307200 | bytes 2457600 | tf_op jit(solution)/shard_map/concatenate | solution.py:81
  (16 shorter events, 0.9 us)
Async XLA Ops:
  0.0 19.2 %collective-permute-start = (bf16[800,400]{0,1:T(8,128)(2,1)}, bf16[800,400]{0,1:T(8,128)(2,1)S(1)}, u32[]{:S(2)}, u32[]{:S(2)}) collective-permute-start(bf16[800,400]{0,1:T(8,128)(2,1)} %param.6), channel_id=1, source_target_pairs={{0,16},{8,24},{16,0},{24,8},{1,17},{9,25},{17,1},{25,9},{2,18},{10... | collective-permute-start | bytes 1920008 | tf_op jit(solution)/shard_map/ppermute | solution.py:8
  3.0 18.1 %collective-permute-start.2 = (bf16[800,400]{0,1:T(8,128)(2,1)}, bf16[800,400]{0,1:T(8,128)(2,1)S(1)}, u32[]{:S(2)}, u32[]{:S(2)}) collective-permute-start(bf16[800,400]{0,1:T(8,128)(2,1)} %param.6), channel_id=1, source_target_pairs={{0,8},{8,0},{16,24},{24,16},{1,9},{9,1},{17,25},{25,17},{2,10},{10... | collective-permute-start | bytes 1920008 | tf_op jit(solution)/shard_map/ppermute | solution.py:8
  4.5 3.9 %copy-start.1 = (s32[400]{0:T(512)S(1)}, s32[400]{0:T(512)}, u32[]{:S(2)}) copy-start(s32[400]{0:T(512)} %param.8) | copy-start | bytes 4804
  5.3 17.5 %copy-start = (bf16[1536,3200]{1,0:T(8,128)(2,1)S(1)}, bf16[1536,3200]{1,0:T(8,128)(2,1)}, u32[]{:S(2)}) copy-start(bf16[1536,3200]{1,0:T(8,128)(2,1)} %param.5) | copy-start | bytes 29491204
  19.3 10.7 %collective-permute-start.1 = (bf16[400,400]{0,1:T(8,128)(2,1)S(1)}, bf16[400,400]{0,1:T(8,128)(2,1)S(1)}, u32[]{:S(2)}, u32[]{:S(2)}) collective-permute-start(bf16[400,400]{0,1:T(8,128)(2,1)S(1)} %slice.28), channel_id=1, source_target_pairs={{0,8},{8,0},{16,24},{24,16},{1,9},{9,1},{17,25},{25,17},{2,10},{10... | collective-permute-start | bytes 960008 | tf_op jit(solution)/shard_map/ppermute | solution.py:8
  21.3 10.1 %collective-permute-start.3 = (bf16[400,400]{0,1:T(8,128)(2,1)S(1)}, bf16[400,400]{0,1:T(8,128)(2,1)S(1)}, u32[]{:S(2)}, u32[]{:S(2)}) collective-permute-start(bf16[400,400]{0,1:T(8,128)(2,1)S(1)} %slice.29), channel_id=1, source_target_pairs={{0,16},{8,24},{16,0},{24,8},{1,17},{9,25},{17,1},{25,9},{2,18},{10... | collective-permute-start | bytes 960008 | tf_op jit(solution)/shard_map/ppermute | solution.py:8
  33.9 4.0 %collective-permute-start.4 = (f32[768,200]{0,1:T(8,128)}, f32[768,200]{0,1:T(8,128)S(1)}, u32[]{:S(2)}, u32[]{:S(2)}) collective-permute-start(f32[768,200]{0,1:T(8,128)} %get-tuple-element.13), channel_id=1, source_target_pairs={{0,1},{1,0},{2,3},{3,2},{4,5},{5,4},{6,7},{7,6},{8,9},{9,8},{10,11... | collective-permute-start | bytes 1843208 | tf_op jit(solution)/shard_map/ppermute | solution.py:8
  33.9 4.0 %collective-permute-start.6 = (f32[768,200]{0,1:T(8,128)S(1)}, f32[768,200]{0,1:T(8,128)}, u32[]{:S(2)}, u32[]{:S(2)}) collective-permute-start(f32[768,200]{0,1:T(8,128)S(1)} %get-tuple-element.14), channel_id=1, source_target_pairs={{0,1},{1,0},{2,3},{3,2},{4,5},{5,4},{6,7},{7,6},{8,9},{9,8},{10,11... | collective-permute-start | bytes 1843208 | tf_op jit(solution)/shard_map/ppermute | solution.py:8
  39.2 16.8 %collective-permute-start.5 = (f32[768,200]{0,1:T(8,128)S(1)}, f32[768,200]{0,1:T(8,128)S(1)}, u32[]{:S(2)}, u32[]{:S(2)}) collective-permute-start(f32[768,200]{0,1:T(8,128)S(1)} %get-tuple-element.11), channel_id=1, source_target_pairs={{0,16},{8,24},{16,0},{24,8},{1,17},{9,25},{17,1},{25,9},{2,18},{10... | collective-permute-start | bytes 1843208 | tf_op jit(solution)/shard_map/ppermute | solution.py:8
  44.3 24.0 %collective-permute-start.7 = (f32[768,200]{0,1:T(8,128)}, f32[768,200]{0,1:T(8,128)}, u32[]{:S(2)}, u32[]{:S(2)}) collective-permute-start(f32[768,200]{0,1:T(8,128)} %copy.9), channel_id=1, source_target_pairs={{0,16},{8,24},{16,0},{24,8},{1,17},{9,25},{17,1},{25,9},{2,18},{10... | collective-permute-start | bytes 1843208 | tf_op jit(solution)/shard_map/ppermute | solution.py:8

commit v21 on v19

v21 whole, which is shorter than its diff:
```python
import jax
import jax.numpy as jnp
from jax import lax
from jax.experimental import pallas as pl
from jax.experimental.pallas import tpu as pltpu
from jax.sharding import PartitionSpec as P


def swap(value, axis, mask):
    return lax.ppermute(value, axis, [(i, i ^ mask) for i in range(lax.axis_size(axis))])


def gather_prow(own, prow_idx, prow_count, pieces):
    count, cols = own.shape
    step = cols // pieces
    if prow_count == 4 and count % 32 == 0 and pieces == 2:
        half = count // 2
        from_x = swap(own, "prow", 1)
        from_y = swap(own, "prow", 2)
        diag_a = swap(from_y[:half, :step], "prow", 1)
        diag_b = swap(from_x[half:, :step], "prow", 2)
        rest, _ = lax.optimization_barrier((from_y[:, step:], diag_a))
        diag_c = swap(rest, "prow", 1)
        base = jnp.bitwise_xor(prow_idx, 3) * count
        return [[(own, prow_idx * count, 0)], [(from_y, jnp.bitwise_xor(prow_idx, 2) * count, 0)],
                [(from_x, jnp.bitwise_xor(prow_idx, 1) * count, 0)],
                [(diag_a, base, 0), (diag_b, base + half, 0)], [(diag_c, base, step)]]
    groups = [[(own, prow_idx * count, 0)]]
    for s in range(1, prow_count):
        groups.append([(swap(own, "prow", s), jnp.bitwise_xor(prow_idx, s) * count, 0)])
    return groups


def contract(amplitudes, groups, firsts, rows, labels, irrep_cols, pieces):
    bands = [lax.dynamic_slice_in_dim(amplitudes, first, rows, axis=0) for first in firsts]
    cols = irrep_cols.shape[0]
    step = cols // pieces
    full = [None] * len(bands)
    parts = [None] * len(bands)
    split = [g for g, group in enumerate(groups) if any(b.shape[1] != cols for b, _, _ in group)]
    held_at = split[0] if split else len(groups) - 1
    for g, group in enumerate(groups):
        if g == held_at and g > 0:
            blocks, held = lax.optimization_barrier((tuple(b for b, _, _ in group), (tuple(full), tuple(parts))))
            group = [(b, o, c) for b, (_, o, c) in zip(blocks, group)]
            full, parts = list(held[0]), list(held[1])
        for i, band in enumerate(bands):
            for b, o, c in group:
                w = b.shape[1]
                window = lax.dynamic_slice_in_dim(band, o, b.shape[0], axis=1)
                same = lax.dynamic_slice_in_dim(labels, o, b.shape[0])[:, None] == irrep_cols[None, c:c + w]
                blocked = jnp.where(same, b, jnp.zeros_like(b))
                product = jnp.dot(window, blocked, preferred_element_type=jnp.float32)
                if w != cols and parts[i] is None:
                    parts[i] = tuple(full[i][:, j * step:(j + 1) * step] for j in range(pieces))
                    full[i] = None
                if parts[i] is None:
                    full[i] = product if full[i] is None else full[i] + product
                elif w == cols:
                    parts[i] = tuple(p + product[:, j * step:(j + 1) * step] for j, p in enumerate(parts[i]))
                else:
                    j = c // step
                    parts[i] = parts[i][:j] + (parts[i][j] + product,) + parts[i][j + 1:]
    return [p if p is not None else tuple(t[:, j * step:(j + 1) * step] for j in range(pieces))
            for p, t in zip(parts, full)]


def shards(amplitudes, integrals, irrep_rows, irrep_cols, mirror_row):
    prow_count = lax.axis_size("prow")
    cuts_count = lax.axis_size("cuts")
    prow_idx = lax.axis_index("prow")
    cuts_idx = lax.axis_index("cuts")
    width = amplitudes.shape[1]
    cols = integrals.shape[1]
    pieces = 2 if cols % 16 == 0 else 1
    labels = lax.dynamic_slice_in_dim(irrep_rows, cuts_idx * width, width)
    groups = gather_prow(integrals, prow_idx, prow_count, pieces)
    block_rows = amplitudes.shape[0] // cuts_count
    others = list(range(1, cuts_count))
    firsts = [jnp.bitwise_xor(cuts_idx, s) * block_rows for s in others] + [cuts_idx * block_rows]
    late = groups[-1] if pieces > 1 and all(c == cols - cols // pieces for _, _, c in groups[-1]) else None
    if late is not None:
        groups = groups[:-1]
    terms = contract(amplitudes, groups, firsts, block_rows, labels, irrep_cols, pieces)
    terms = [list(t) for t in terms]
    half = prow_count // 2
    own_block = prow_idx * cuts_count + cuts_idx
    partner_block = jnp.bitwise_xor(prow_idx, half) * cuts_count + cuts_idx
    mine = lax.dynamic_slice(mirror_row, (own_block * block_rows,), (block_rows,))
    local = mine - partner_block * block_rows
    theirs = lax.dynamic_slice(mirror_row, (partner_block * block_rows,), (block_rows,))
    wanted = theirs - own_block * block_rows
    results = []
    previous = None
    for j in range(pieces):
        if late is not None and j == pieces - 1:
            blocks, _ = lax.optimization_barrier((tuple(b for b, _, _ in late), previous))
            for i, first in enumerate(firsts):
                band = lax.dynamic_slice_in_dim(amplitudes, first, block_rows, axis=0)
                for b, (_, o, c) in zip(blocks, late):
                    window = lax.dynamic_slice_in_dim(band, o, b.shape[0], axis=1)
                    same = lax.dynamic_slice_in_dim(labels, o, b.shape[0])[:, None] == irrep_cols[None, c:]
                    blocked = jnp.where(same, b, jnp.zeros_like(b))
                    terms[i][j] = terms[i][j] + jnp.dot(window, blocked, preferred_element_type=jnp.float32)
        piece = terms[-1][j]
        for s, part in zip(others, terms[:-1]):
            piece = piece + swap(part[j], "cuts", s)
        previous = piece
        if j == pieces - 1 and pieces > 1:
            fetched = swap(jnp.take(piece, wanted, axis=0, mode="clip"), "prow", half)
            results.append(piece - fetched)
        else:
            fetched = swap(piece, "prow", half)
            results.append(piece - jnp.take(fetched, local, axis=0, mode="clip"))
    return jnp.concatenate(results, axis=1) if pieces > 1 else results[0]


def solution(mesh):
    placed = (P("prow", "cuts"), P(("cuts", "prow"), "pcol"), P(), P("pcol"), P())
    return jax.shard_map(
        shards, mesh=mesh, in_specs=placed, out_specs=P(("prow", "cuts"), "pcol"), check_vma=False
    )
```

time: 72.4 us -> 76 us (1.050)
  matrix products: 15.7 us -> 19 us
  waiting for transfers between devices: 33.2 us -> 31.1 us
  starting transfers between devices: 9.19 us -> 10.7 us
  other arithmetic: 3.62 us -> 4.61 us
    dot_general x0 -> x2, matrix products: none -> 3.68 us  [shards(): jnp.dot(window, blocked, preferred_element_type=jnp.float32)]
    ppermute x8 -> x9, waiting for transfers between devices: 33.2 us -> 31.1 us  [swap(): lax.ppermute(value, axis, [(i, i ^ mask) for i in range(lax.axis_size(axi...]
    ppermute x8 -> x9, starting transfers between devices: 9.19 us -> 10.7 us  [swap(): lax.ppermute(value, axis, [(i, i ^ mask) for i in range(lax.axis_size(axi...]
    sub x1, other arithmetic: 0.06 us -> 1.19 us  [shards(): results.append(piece - fetched)]
    dynamic_slice x0 -> x1, local copies, waits for them, and re-layouts: none -> 0.89 us  [shards(): lax.dynamic_slice_in_dim(labels, o, b.shape[0])[:, None]]
    dynamic_slice x2 -> x1, local copies, waits for them, and re-layouts: 1.73 us -> 0.85 us  [contract(): lax.dynamic_slice_in_dim(labels, o, b.shape[0])[:, None]]
    add x3 -> x2, other arithmetic: 1.54 us -> 1.4 us  [shards(): piece = piece + swap(part[j], 'cuts', s)]
  transfers between devices with their start and end apart: 8 -> 9, of which waited for: 4 -> 4; matrix products, arithmetic and copies ran while one was open for 35% -> 38% of each run, Pallas kernels for 0% -> 0%
where the time goes in v21:
time: 76 us; the launch traced here: 75.5 us
  waiting for transfers between devices  31.1 us (41%)
  matrix products  19 us (25%)
  starting transfers between devices  10.7 us (14%)
  local copies, waits for them, and re-layouts  9.89 us (13%)
  other arithmetic  4.61 us (6%)
    ppermute x9, waiting for transfers between devices, swap(): lax.ppermute(value, axis, [(i, i ^ mask) for i in range(lax.axis_size(axi...  31.1 us
    dot_general x10, matrix products, contract(): product = jnp.dot(window, blocked, preferred_element_type=jnp.float32)  15.4 us
    ppermute x9, starting transfers between devices, swap(): lax.ppermute(value, axis, [(i, i ^ mask) for i in range(lax.axis_size(axi...  10.7 us
    dot_general x2, matrix products, shards(): jnp.dot(window, blocked, preferred_element_type=jnp.float32)  3.68 us
    gather x2, local copies, waits for them, and re-layouts, shards(): fetched = swap(jnp.take(piece, wanted, axis=0, mode='clip'), 'prow', half)  3.19 us
    gather x2, local copies, waits for them, and re-layouts, shards(): results.append(piece - jnp.take(fetched, local, axis=0, mode='clip'))  2.36 us
  transfers between devices with their start and end apart: 9, of which 4 were waited for; matrix products, arithmetic and copies ran while one was open for 38% of the time, Pallas kernels for 0%

profile of v21, /device:TPU:0, one launch (start us, length us, event | category | flops | bytes accessed | tf_op | source)
XLA Modules:
  0.0 75.5 jit_solution(1123576742651463948)
XLA Ops:
  0.0 3.0 %collective-permute-start = (bf16[800,400]{0,1:T(8,128)(2,1)}, bf16[800,400]{0,1:T(8,128)(2,1)S(1)}, u32[]{:S(2)}, u32[]{:S(2)}) collective-permute-start(bf16[800,400]{0,1:T(8,128)(2,1)} %param.6), channel_id=1, source_target_pairs={{0,16},{8,24},{16,0},{24,8},{1,17},{9,25},{17,1},{25,9},{2,18},{10... | collective-permute-start | bytes 1920008 | tf_op jit(solution)/shard_map/ppermute | solution.py:10
  3.0 1.5 %collective-permute-start.2 = (bf16[800,400]{0,1:T(8,128)(2,1)}, bf16[800,400]{0,1:T(8,128)(2,1)S(1)}, u32[]{:S(2)}, u32[]{:S(2)}) collective-permute-start(bf16[800,400]{0,1:T(8,128)(2,1)} %param.6), channel_id=1, source_target_pairs={{0,8},{8,0},{16,24},{24,16},{1,9},{9,1},{17,25},{25,17},{2,10},{10... | collective-permute-start | bytes 1920008 | tf_op jit(solution)/shard_map/ppermute | solution.py:10
  4.5 0.8 %fusion.38 = (s32[200]{0:T(256)S(1)}, s32[200]{0:T(256)S(1)}) fusion(s32[400]{0:T(512)} %param.8), kind=kLoop, calls=%fused_computation.55 | loop fusion | bytes 3200 | tf_op jit(solution)/shard_map/slice | solution.py:102
  5.3 0.9 %fusion.36 = (s32[800]{0:T(1024)S(1)}, s32[800]{0:T(1024)S(1)}, s32[800]{0:T(1024)S(1)}, s32[800]{0:T(1024)S(1)}) fusion(s32[6400]{0:T(1024)} %param.7, s32[]{:T(128)S(6)} %dynamic_slice.105, s32[]{:T(128)S(6)} %dynamic_slice.90, s32[]{:T(128)S(6)} %dynamic_slice.87, s32[]{:T(128)S(6)} %dynamic_slice.84), kind=kLoop, calls=%fused_computation.53 | loop fusion | bytes 25616 | tf_op jit(solution)/shard_map/dynamic_slice | solution.py:102
  6.2 0.8 %fusion.37 = (s32[400]{0:T(512)S(1)}, s32[400]{0:T(512)S(1)}) fusion(s32[6400]{0:T(1024)} %param.7, s32[]{:T(128)S(6)} %dynamic_slice.99, s32[]{:T(128)S(6)} %dynamic_slice.96), kind=kLoop, calls=%fused_computation.54 | loop fusion | bytes 6408 | tf_op jit(solution)/shard_map/dynamic_slice | solution.py:51
  7.0 3.0 %fusion.10 = f32[768,400]{0,1:T(8,128)S(1)} fusion(bf16[1536,3200]{1,0:T(8,128)(2,1)} %param.5, s32[]{:T(128)S(6)} %select_n.97, s32[]{:T(128)S(6)} %select_n.99, bf16[800,400]{0,1:T(8,128)(2,1)} %param.6, s32[800]{0:T(1024)S(1)} %get-tuple-element.20, s32[400]{0:T(512)} %param.8), kind=kOutput, calls=%fused_computation.19 | convolution fusion | flops 492160000 | bytes 3327112 | tf_op jit(solution)/shard_map/dot_general | solution.py:53
  10.0 3.1 %fusion.6 = f32[768,400]{0,1:T(8,128)S(1)} fusion(bf16[1536,3200]{1,0:T(8,128)(2,1)} %param.5, s32[]{:T(128)S(6)} %select_n.110, s32[]{:T(128)S(6)} %select_n.99, bf16[800,400]{0,1:T(8,128)(2,1)S(1)} %copy-done.2, s32[800]{0:T(1024)S(1)} %get-tuple-element.20, s32[400]{0:T(512)S(1)} %copy-done.1), kind=kOutput, calls=%fused_computation.15 | convolution fusion | flops 492160000 | bytes 3249864 | tf_op jit(solution)/shard_map/dot_general | solution.py:53
  13.2 6.1 %collective-permute-done = bf16[800,400]{0,1:T(8,128)(2,1)S(1)} collective-permute-done((bf16[800,400]{0,1:T(8,128)(2,1)}, bf16[800,400]{0,1:T(8,128)(2,1)S(1)}, u32[]{:S(2)}, u32[]{:S(2)}) %collective-permute-start) | collective-permute-done | bytes 640032 | tf_op jit(solution)/shard_map/ppermute | solution.py:10
  19.2 1.8 %collective-permute-start.1 = (bf16[400,200]{0,1:T(8,128)(2,1)S(1)}, bf16[400,200]{0,1:T(8,128)(2,1)S(1)}, u32[]{:S(2)}, u32[]{:S(2)}) collective-permute-start(bf16[400,200]{0,1:T(8,128)(2,1)S(1)} %slice.44), channel_id=1, source_target_pairs={{0,8},{8,0},{16,24},{24,16},{1,9},{9,1},{17,25},{25,17},{2,10},{10... | collective-permute-start | bytes 480008 | tf_op jit(solution)/shard_map/ppermute | solution.py:10
  21.2 1.6 %collective-permute-start.3 = (bf16[400,200]{0,1:T(8,128)(2,1)S(1)}, bf16[400,200]{0,1:T(8,128)(2,1)S(1)}, u32[]{:S(2)}, u32[]{:S(2)}) collective-permute-start(bf16[400,200]{0,1:T(8,128)(2,1)S(1)} %slice.45), channel_id=1, source_target_pairs={{0,16},{8,24},{16,0},{24,8},{1,17},{9,25},{17,1},{25,9},{2,18},{10... | collective-permute-start | bytes 480008 | tf_op jit(solution)/shard_map/ppermute | solution.py:10
  22.7 2.7 %convolution_add_fusion.3 = f32[768,400]{0,1:T(8,128)S(1)} fusion(f32[768,400]{0,1:T(8,128)S(1)} %fusion.10, bf16[1536,3200]{1,0:T(8,128)(2,1)} %param.5, s32[]{:T(128)S(6)} %select_n.97, s32[]{:T(128)S(6)} %select_n.104, bf16[800,400]{0,1:T(8,128)(2,1)S(1)} %collective-permute-done, s32[800]{0:T(1024)S(1)} %get-tuple-element.19, s32[400]{0:T(512)S(1)} %copy-done.1), kind=kOutput, calls=%fused_computation.8 | convolution fusion | flops 492467200 | bytes 4478664 | tf_op jit(solution)/shard_map/dot_general | solution.py:53
  25.4 1.3 %convolution_add_fusion.1 = f32[768,400]{0,1:T(8,128)S(1)} fusion(f32[768,400]{0,1:T(8,128)S(1)} %fusion.6, bf16[1536,3200]{1,0:T(8,128)(2,1)S(1)} %copy-done, s32[]{:T(128)S(6)} %select_n.110, s32[]{:T(128)S(6)} %select_n.104, bf16[800,400]{0,1:T(8,128)(2,1)S(1)} %collective-permute-done, s32[800]{0:T(1024)S(1)} %get-tuple-element.19, s32[400]{0:T(512)S(1)} %copy-done.1), kind=kOutput, calls=%fused_computation.6 | convolution fusion | flops 492467200 | bytes 4556808 | tf_op jit(solution)/shard_map/dot_general | solution.py:53
  26.7 1.3 %convolution_add_fusion.2 = f32[768,400]{0,1:T(8,128)S(1)} fusion(f32[768,400]{0,1:T(8,128)S(1)} %convolution_add_fusion.3, bf16[1536,3200]{1,0:T(8,128)(2,1)S(1)} %copy-done, s32[]{:T(128)S(6)} %select_n.97, s32[]{:T(128)S(6)} %select_n.107, bf16[800,400]{0,1:T(8,128)(2,1)S(1)} %collective-permute-done.2, s32[800]{0:T(1024)S(1)} %get-tuple-element.18, ...), kind=kOutput, calls=%fused_computation.7 | convolution fusion | flops 492467200 | bytes 4556808 | tf_op jit(solution)/shard_map/dot_general | solution.py:53
  28.0 1.3 %convolution_add_fusion = f32[768,400]{0,1:T(8,128)S(1)} fusion(f32[768,400]{0,1:T(8,128)S(1)} %convolution_add_fusion.1, bf16[1536,3200]{1,0:T(8,128)(2,1)S(1)} %copy-done, s32[]{:T(128)S(6)} %select_n.110, s32[]{:T(128)S(6)} %select_n.107, bf16[800,400]{0,1:T(8,128)(2,1)S(1)} %collective-permute-done.2, s32[800]{0:T(1024)S(1)} %get-tuple-element.18, ...), kind=kOutput, calls=%fused_computation.5 | convolution fusion | flops 492467200 | bytes 4556808 | tf_op jit(solution)/shard_map/dot_general | solution.py:53
  29.3 0.7 fusion.14
  30.0 0.7 add_add_fusion.1
  31.3 0.7 fusion.16
  32.0 0.7 fusion.18
  33.0 8.7 %collective-permute-done.6 = bf16[800,200]{0,1:T(8,128)(2,1)S(1)} collective-permute-done((bf16[800,200]{0,1:T(8,128)(2,1)S(1)}, bf16[800,200]{0,1:T(8,128)(2,1)S(1)}, u32[]{:S(2)}, u32[]{:S(2)}) %collective-permute-start.6) | collective-permute-done | bytes 320032 | tf_op jit(solution)/shard_map/ppermute | solution.py:10
  41.6 1.1 %slice_add_fusion = f32[768,200]{0,1:T(8,128)S(1)} fusion(f32[768,400]{0,1:T(8,128)S(1)} %convolution_add_fusion.2, bf16[800,200]{0,1:T(8,128)(2,1)S(1)} %collective-permute-done.6, s32[800]{0:T(1024)S(1)} %get-tuple-element.17, s32[200]{0:T(256)S(1)} %get-tuple-element.25, bf16[1536,3200]{1,0:T(8,128)(2,1)S(1)} %copy-done, s32[]{:T(128)S(6)} %select_n.97, ...), kind=kOutput, calls=%fused_computation.31 | convolution fusion | flops 246233600 | bytes 2968584 | tf_op jit(solution)/shard_map/dot_general | solution.py:104
  42.8 0.8 %dynamic-slice_subtract_fusion.1 = (s32[768]{0:T(1024)S(1)}, s32[768]{0:T(1024)S(1)}) fusion(s32[6144]{0:T(1024)} %param.9, s32[]{:T(128)S(6)} %select_n.117, s32[]{:T(128)S(6)} %mul.45, s32[]{:T(128)S(6)} %mul.43, s32[]{:T(128)S(6)} %select_n.120), kind=kLoop, calls=%fused_computation.40 | loop fusion | flops 1536 | bytes 12304 | tf_op jit(solution)/shard_map/sub | solution.py:90
  44.2 2.6 %fusion.2 = f32[768,200]{0,1:T(8,128)S(1)} fusion(bf16[1536,3200]{1,0:T(8,128)(2,1)} %param.5, s32[]{:T(128)S(6)} %select_n.110, s32[]{:T(128)S(6)} %select_n.118, bf16[800,200]{0,1:T(8,128)(2,1)S(1)} %collective-permute-done.6, s32[800]{0:T(1024)S(1)} %get-tuple-element.17, s32[200]{0:T(256)S(1)} %get-tuple-element.25), kind=kOutput, calls=%fused_computation.11 | convolution fusion | flops 246080000 | bytes 2314664 | tf_op jit(solution)/shard_map/dot_general | solution.py:104
  46.8 1.2 %add_add_fusion = f32[768,200]{0,1:T(8,128)S(1)} fusion(f32[768,200]{0,1:T(8,128)} %collective-permute-done.7, f32[768,200]{0,1:T(8,128)S(1)} %fusion.2, f32[768,400]{0,1:T(8,128)S(1)} %convolution_add_fusion), kind=kLoop, calls=%fused_computation.32 | loop fusion | flops 307200 | bytes 2457600 | tf_op jit(solution)/shard_map/add | solution.py:107
  48.3 2.1 %gather_fusion.1 = f32[768,200]{1,0:T(8,128)S(1)} fusion(f32[768,200]{1,0:T(8,128)S(1)} %copy.8, s32[1024]{0:T(1024)S(1)} %pad_clamp_fusion), kind=kCustom, calls=%fused_computation.1 | custom fusion | bytes 1231872 | tf_op jit(solution)/shard_map/jit(_take)/gather | solution.py:110
  50.4 1.1 %copy.9 = f32[768,200]{0,1:T(8,128)} copy(f32[768,200]{1,0:T(8,128)S(1)} %gather_fusion.1) | data formatting | bytes 1228800 | tf_op jit(solution)/shard_map/jit(_take)/gather | solution.py:110
  51.5 1.6 %collective-permute-start.8 = (f32[768,200]{0,1:T(8,128)}, f32[768,200]{0,1:T(8,128)}, u32[]{:S(2)}, u32[]{:S(2)}) collective-permute-start(f32[768,200]{0,1:T(8,128)} %copy.9), channel_id=1, source_target_pairs={{0,16},{8,24},{16,0},{24,8},{1,17},{9,25},{17,1},{25,9},{2,18},{10... | collective-permute-start | bytes 1843208 | tf_op jit(solution)/shard_map/ppermute | solution.py:10
  53.1 7.4 %collective-permute-done.5 = f32[768,200]{0,1:T(8,128)} collective-permute-done((f32[768,200]{0,1:T(8,128)S(1)}, f32[768,200]{0,1:T(8,128)}, u32[]{:S(2)}, u32[]{:S(2)}) %collective-permute-start.5) | collective-permute-done | bytes 614432 | tf_op jit(solution)/shard_map/ppermute | solution.py:10
  60.5 1.3 %copy.6 = f32[768,200]{1,0:T(8,128)S(1)} copy(f32[768,200]{0,1:T(8,128)} %collective-permute-done.5) | data formatting | bytes 1228800 | tf_op jit(solution)/shard_map/ppermute | solution.py:10
  61.8 2.1 %gather_fusion = f32[768,200]{1,0:T(8,128)S(1)} fusion(f32[768,200]{1,0:T(8,128)S(1)} %copy.6, s32[1024]{0:T(1024)S(1)} %pad_clamp_fusion.1), kind=kCustom, calls=%fused_computation | custom fusion | bytes 1231872 | tf_op jit(solution)/shard_map/jit(_take)/gather | solution.py:114
  64.3 8.9 %collective-permute-done.8 = f32[768,200]{0,1:T(8,128)} collective-permute-done((f32[768,200]{0,1:T(8,128)}, f32[768,200]{0,1:T(8,128)}, u32[]{:S(2)}, u32[]{:S(2)}) %collective-permute-start.8) | collective-permute-done | bytes 614432 | tf_op jit(solution)/shard_map/ppermute | solution.py:10
  73.2 1.2 %sub.23 = f32[768,200]{0,1:T(8,128)S(1)} subtract(f32[768,200]{0,1:T(8,128)S(1)} %add_add_fusion, f32[768,200]{0,1:T(8,128)} %collective-permute-done.8) | non-fusion elementwise | flops 153600 | bytes 1843200 | tf_op jit(solution)/shard_map/sub | solution.py:111
  74.4 1.1 %pad_maximum_fusion = f32[768,400]{0,1:T(8,128)} fusion(f32[768,200]{0,1:T(8,128)S(1)} %sub.23, f32[768,200]{0,1:T(8,128)S(1)} %sub.20), kind=kLoop, calls=%fused_computation.21 | loop fusion | flops 307200 | bytes 2457600 | tf_op jit(solution)/shard_map/concatenate | solution.py:115
  (24 shorter events, 2.3 us)
Async XLA Ops:
  0.0 19.2 %collective-permute-start = (bf16[800,400]{0,1:T(8,128)(2,1)}, bf16[800,400]{0,1:T(8,128)(2,1)S(1)}, u32[]{:S(2)}, u32[]{:S(2)}) collective-permute-start(bf16[800,400]{0,1:T(8,128)(2,1)} %param.6), channel_id=1, source_target_pairs={{0,16},{8,24},{16,0},{24,8},{1,17},{9,25},{17,1},{25,9},{2,18},{10... | collective-permute-start | bytes 1920008 | tf_op jit(solution)/shard_map/ppermute | solution.py:10
  3.0 18.1 %collective-permute-start.2 = (bf16[800,400]{0,1:T(8,128)(2,1)}, bf16[800,400]{0,1:T(8,128)(2,1)S(1)}, u32[]{:S(2)}, u32[]{:S(2)}) collective-permute-start(bf16[800,400]{0,1:T(8,128)(2,1)} %param.6), channel_id=1, source_target_pairs={{0,8},{8,0},{16,24},{24,16},{1,9},{9,1},{17,25},{25,17},{2,10},{10... | collective-permute-start | bytes 1920008 | tf_op jit(solution)/shard_map/ppermute | solution.py:10
  5.3 4.7 %copy-start.1 = (s32[400]{0:T(512)S(1)}, s32[400]{0:T(512)}, u32[]{:S(2)}) copy-start(s32[400]{0:T(512)} %param.8) | copy-start | bytes 4804
  5.3 4.7 %copy-start.2 = (bf16[800,400]{0,1:T(8,128)(2,1)S(1)}, bf16[800,400]{0,1:T(8,128)(2,1)}, u32[]{:S(2)}) copy-start(bf16[800,400]{0,1:T(8,128)(2,1)} %param.6) | copy-start | bytes 1920004
  7.0 18.4 %copy-start = (bf16[1536,3200]{1,0:T(8,128)(2,1)S(1)}, bf16[1536,3200]{1,0:T(8,128)(2,1)}, u32[]{:S(2)}) copy-start(bf16[1536,3200]{1,0:T(8,128)(2,1)} %param.5) | copy-start | bytes 29491204
  19.2 10.0 %collective-permute-start.1 = (bf16[400,200]{0,1:T(8,128)(2,1)S(1)}, bf16[400,200]{0,1:T(8,128)(2,1)S(1)}, u32[]{:S(2)}, u32[]{:S(2)}) collective-permute-start(bf16[400,200]{0,1:T(8,128)(2,1)S(1)} %slice.44), channel_id=1, source_target_pairs={{0,8},{8,0},{16,24},{24,16},{1,9},{9,1},{17,25},{25,17},{2,10},{10... | collective-permute-start | bytes 480008 | tf_op jit(solution)/shard_map/ppermute | solution.py:10
  21.2 8.1 %collective-permute-start.3 = (bf16[400,200]{0,1:T(8,128)(2,1)S(1)}, bf16[400,200]{0,1:T(8,128)(2,1)S(1)}, u32[]{:S(2)}, u32[]{:S(2)}) collective-permute-start(bf16[400,200]{0,1:T(8,128)(2,1)S(1)} %slice.45), channel_id=1, source_target_pairs={{0,16},{8,24},{16,0},{24,8},{1,17},{9,25},{17,1},{25,9},{2,18},{10... | collective-permute-start | bytes 480008 | tf_op jit(solution)/shard_map/ppermute | solution.py:10
  30.7 2.1 %collective-permute-start.4 = (f32[768,200]{0,1:T(8,128)S(1)}, f32[768,200]{0,1:T(8,128)S(1)}, u32[]{:S(2)}, u32[]{:S(2)}) collective-permute-start(f32[768,200]{0,1:T(8,128)S(1)} %add_add_fusion.1), channel_id=1, source_target_pairs={{0,1},{1,0},{2,3},{3,2},{4,5},{5,4},{6,7},{7,6},{8,9},{9,8},{10,11... | collective-permute-start | bytes 1843208 | tf_op jit(solution)/shard_map/ppermute | solution.py:10
  30.8 10.8 %collective-permute-start.6 = (bf16[800,200]{0,1:T(8,128)(2,1)S(1)}, bf16[800,200]{0,1:T(8,128)(2,1)S(1)}, u32[]{:S(2)}, u32[]{:S(2)}) collective-permute-start(bf16[800,200]{0,1:T(8,128)(2,1)S(1)} %slice.46), channel_id=1, source_target_pairs={{0,8},{8,0},{16,24},{24,16},{1,9},{9,1},{17,25},{25,17},{2,10},{10... | collective-permute-start | bytes 960008 | tf_op jit(solution)/shard_map/ppermute | solution.py:10
  42.8 4.1 %collective-permute-start.7 = (f32[768,200]{0,1:T(8,128)S(1)}, f32[768,200]{0,1:T(8,128)}, u32[]{:S(2)}, u32[]{:S(2)}) collective-permute-start(f32[768,200]{0,1:T(8,128)S(1)} %slice_add_fusion), channel_id=1, source_target_pairs={{0,1},{1,0},{2,3},{3,2},{4,5},{5,4},{6,7},{7,6},{8,9},{9,8},{10,11... | collective-permute-start | bytes 1843208 | tf_op jit(solution)/shard_map/ppermute | solution.py:10
  43.7 16.8 %collective-permute-start.5 = (f32[768,200]{0,1:T(8,128)S(1)}, f32[768,200]{0,1:T(8,128)}, u32[]{:S(2)}, u32[]{:S(2)}) collective-permute-start(f32[768,200]{0,1:T(8,128)S(1)} %add_add_fusion.2), channel_id=1, source_target_pairs={{0,16},{8,24},{16,0},{24,8},{1,17},{9,25},{17,1},{25,9},{2,18},{10... | collective-permute-start | bytes 1843208 | tf_op jit(solution)/shard_map/ppermute | solution.py:10
  51.5 21.7 %collective-permute-start.8 = (f32[768,200]{0,1:T(8,128)}, f32[768,200]{0,1:T(8,128)}, u32[]{:S(2)}, u32[]{:S(2)}) collective-permute-start(f32[768,200]{0,1:T(8,128)} %copy.9), channel_id=1, source_target_pairs={{0,16},{8,24},{16,0},{24,8},{1,17},{9,25},{17,1},{25,9},{2,18},{10... | collective-permute-start | bytes 1843208 | tf_op jit(solution)/shard_map/ppermute | solution.py:10

commit v22 on v18

--- a/solution.py
+++ b/solution.py
@@ -67,7 +67,7 @@
     theirs = lax.dynamic_slice(mirror_row, (partner_block * block_rows,), (block_rows,))
     wanted = theirs - own_block * block_rows
     cols = kept.shape[1]
-    pieces = 2 if cols % 16 == 0 else 1
+    pieces = 4 if cols % 4 == 0 else 1
     step = cols // pieces
     results = []
     for j in range(pieces):

time: 67 us -> 70.1 us (1.046)
  starting transfers between devices: 10.5 us -> 13.1 us
  waiting for transfers between devices: 29.9 us -> 28.7 us
  other arithmetic: 2.25 us -> 3.28 us
    gather x2 -> x6, local copies, waits for them, and re-layouts: 2.36 us -> 5.27 us  [shards(): results.append(piece - jnp.take(fetched, local, axis=0, mode='clip'))]
    ppermute x8 -> x12, starting transfers between devices: 10.5 us -> 13.1 us  [swap(): lax.ppermute(value, axis, [(i, i ^ mask) for i in range(lax.axis_size(axi...]
    gather x2, local copies, waits for them, and re-layouts: 3.19 us -> 1.76 us  [shards(): fetched = swap(jnp.take(piece, wanted, axis=0, mode='clip'), 'prow', half)]
    ppermute x8 -> x12, waiting for transfers between devices: 29.9 us -> 28.7 us  [swap(): lax.ppermute(value, axis, [(i, i ^ mask) for i in range(lax.axis_size(axi...]
    sub x1, other arithmetic: 0.06 us -> 1 us  [shards(): results.append(piece - fetched)]
    ppermute x1 -> x3, local copies, waits for them, and re-layouts: 1.34 us -> 0.52 us  [swap(): lax.ppermute(value, axis, [(i, i ^ mask) for i in range(lax.axis_size(axi...]
  transfers between devices with their start and end apart: 8 -> 12, of which waited for: 6 -> 10; matrix products, arithmetic and copies ran while one was open for 35% -> 33% of each run, Pallas kernels for 0% -> 0%
where the time goes in v22:
time: 70.1 us; the launch traced here: 69.6 us
  waiting for transfers between devices  28.7 us (41%)
  matrix products  14.6 us (21%)
  starting transfers between devices  13.1 us (19%)
  local copies, waits for them, and re-layouts  9.77 us (14%)
  other arithmetic  3.28 us (5%)
    ppermute x12, waiting for transfers between devices, swap(): lax.ppermute(value, axis, [(i, i ^ mask) for i in range(lax.axis_size(axi...  28.7 us
    dot_general x10, matrix products, contract(): product = jnp.dot(window, blocked, preferred_element_type=jnp.float32)  14.6 us
    ppermute x12, starting transfers between devices, swap(): lax.ppermute(value, axis, [(i, i ^ mask) for i in range(lax.axis_size(axi...  13.1 us
    gather x6, local copies, waits for them, and re-layouts, shards(): results.append(piece - jnp.take(fetched, local, axis=0, mode='clip'))  5.27 us
    gather x2, local copies, waits for them, and re-layouts, shards(): fetched = swap(jnp.take(piece, wanted, axis=0, mode='clip'), 'prow', half)  1.76 us
    dynamic_slice x2, local copies, waits for them, and re-layouts, contract(): lax.dynamic_slice_in_dim(labels, o, b.shape[0])[:, None]  1.73 us
  transfers between devices with their start and end apart: 12, of which 10 were waited for; matrix products, arithmetic and copies ran while one was open for 33% of the time, Pallas kernels for 0%

profile of v22, /device:TPU:0, one launch (start us, length us, event | category | flops | bytes accessed | tf_op | source)
XLA Modules:
  0.0 69.6 jit_solution(4532631902094929027)
XLA Ops:
  0.0 3.0 %collective-permute-start = (bf16[800,400]{0,1:T(8,128)(2,1)}, bf16[800,400]{0,1:T(8,128)(2,1)S(1)}, u32[]{:S(2)}, u32[]{:S(2)}) collective-permute-start(bf16[800,400]{0,1:T(8,128)(2,1)} %param.6), channel_id=1, source_target_pairs={{0,16},{8,24},{16,0},{24,8},{1,17},{9,25},{17,1},{25,9},{2,18},{10... | collective-permute-start | bytes 1920008 | tf_op jit(solution)/shard_map/ppermute | solution.py:10
  3.0 1.5 %collective-permute-start.2 = (bf16[800,400]{0,1:T(8,128)(2,1)}, bf16[800,400]{0,1:T(8,128)(2,1)S(1)}, u32[]{:S(2)}, u32[]{:S(2)}) collective-permute-start(bf16[800,400]{0,1:T(8,128)(2,1)} %param.6), channel_id=1, source_target_pairs={{0,8},{8,0},{16,24},{24,16},{1,9},{9,1},{17,25},{25,17},{2,10},{10... | collective-permute-start | bytes 1920008 | tf_op jit(solution)/shard_map/ppermute | solution.py:10
  4.5 0.8 %dynamic-slice_subtract_fusion.1 = (s32[768]{0:T(1024)S(1)}, s32[768]{0:T(1024)S(1)}) fusion(s32[6144]{0:T(1024)} %param.9, s32[]{:T(128)S(6)} %select_n.104, s32[]{:T(128)S(6)} %mul.45, s32[]{:T(128)S(6)} %mul.43, s32[]{:T(128)S(6)} %select_n.105), kind=kLoop, calls=%fused_computation.39 | loop fusion | flops 1536 | bytes 12304 | tf_op jit(solution)/shard_map/sub | solution.py:66
  5.3 0.9 %fusion.32 = (s32[800]{0:T(1024)S(1)}, s32[800]{0:T(1024)S(1)}, s32[800]{0:T(1024)S(1)}) fusion(s32[6400]{0:T(1024)} %param.7, s32[]{:T(128)S(6)} %dynamic_slice.76, s32[]{:T(128)S(6)} %dynamic_slice.73, s32[]{:T(128)S(6)} %dynamic_slice.70), kind=kLoop, calls=%fused_computation.52 | loop fusion | bytes 19212 | tf_op jit(solution)/shard_map/dynamic_slice | solution.py:41
  6.1 0.8 %fusion.31 = (s32[400]{0:T(512)S(1)}, s32[400]{0:T(512)S(1)}) fusion(s32[6400]{0:T(1024)} %param.7, s32[]{:T(128)S(6)} %dynamic_slice.85, s32[]{:T(128)S(6)} %dynamic_slice.82), kind=kLoop, calls=%fused_computation.51 | loop fusion | bytes 6408 | tf_op jit(solution)/shard_map/dynamic_slice | solution.py:41
  7.0 3.0 %fusion.6 = f32[768,400]{0,1:T(8,128)S(1)} fusion(bf16[1536,3200]{1,0:T(8,128)(2,1)} %param.5, s32[]{:T(128)S(6)} %select_n.84, s32[]{:T(128)S(6)} %select_n.86, bf16[800,400]{0,1:T(8,128)(2,1)} %param.6, s32[800]{0:T(1024)S(1)} %get-tuple-element.25, s32[400]{0:T(512)} %param.8), kind=kOutput, calls=%fused_computation.17 | convolution fusion | flops 492160000 | bytes 3327112 | tf_op jit(solution)/shard_map/dot_general | solution.py:43
  10.0 3.3 %fusion.2 = f32[768,400]{0,1:T(8,128)S(1)} fusion(bf16[1536,3200]{1,0:T(8,128)(2,1)} %param.5, s32[]{:T(128)S(6)} %select_n.97, s32[]{:T(128)S(6)} %select_n.86, bf16[800,400]{0,1:T(8,128)(2,1)} %param.6, s32[800]{0:T(1024)S(1)} %get-tuple-element.25, s32[400]{0:T(512)S(1)} %copy-done.1), kind=kOutput, calls=%fused_computation.13 | convolution fusion | flops 492160000 | bytes 3326664 | tf_op jit(solution)/shard_map/dot_general | solution.py:43
  13.3 5.9 %collective-permute-done = bf16[800,400]{0,1:T(8,128)(2,1)S(1)} collective-permute-done((bf16[800,400]{0,1:T(8,128)(2,1)}, bf16[800,400]{0,1:T(8,128)(2,1)S(1)}, u32[]{:S(2)}, u32[]{:S(2)}) %collective-permute-start) | collective-permute-done | bytes 640032 | tf_op jit(solution)/shard_map/ppermute | solution.py:10
  19.3 1.8 %collective-permute-start.1 = (bf16[400,400]{0,1:T(8,128)(2,1)S(1)}, bf16[400,400]{0,1:T(8,128)(2,1)S(1)}, u32[]{:S(2)}, u32[]{:S(2)}) collective-permute-start(bf16[400,400]{0,1:T(8,128)(2,1)S(1)} %slice.48), channel_id=1, source_target_pairs={{0,8},{8,0},{16,24},{24,16},{1,9},{9,1},{17,25},{25,17},{2,10},{10... | collective-permute-start | bytes 960008 | tf_op jit(solution)/shard_map/ppermute | solution.py:10
  21.3 1.6 %collective-permute-start.3 = (bf16[400,400]{0,1:T(8,128)(2,1)S(1)}, bf16[400,400]{0,1:T(8,128)(2,1)S(1)}, u32[]{:S(2)}, u32[]{:S(2)}) collective-permute-start(bf16[400,400]{0,1:T(8,128)(2,1)S(1)} %slice.49), channel_id=1, source_target_pairs={{0,16},{8,24},{16,0},{24,8},{1,17},{9,25},{17,1},{25,9},{2,18},{10... | collective-permute-start | bytes 960008 | tf_op jit(solution)/shard_map/ppermute | solution.py:10
  22.8 1.3 %convolution_add_fusion.3 = f32[768,400]{0,1:T(8,128)S(1)} fusion(f32[768,400]{0,1:T(8,128)S(1)} %fusion.6, bf16[1536,3200]{1,0:T(8,128)(2,1)S(1)} %copy-done, s32[]{:T(128)S(6)} %select_n.84, s32[]{:T(128)S(6)} %select_n.91, bf16[800,400]{0,1:T(8,128)(2,1)S(1)} %collective-permute-done, s32[800]{0:T(1024)S(1)} %get-tuple-element.24, s32[400]{0:T(512)S(1)} %copy-done.1), kind=kOutput, calls=%fused_computation.10 | convolution fusion | flops 492467200 | bytes 4556808 | tf_op jit(solution)/shard_map/dot_general | solution.py:43
  24.1 1.3 %convolution_add_fusion.1 = f32[768,400]{0,1:T(8,128)S(1)} fusion(f32[768,400]{0,1:T(8,128)S(1)} %fusion.2, bf16[1536,3200]{1,0:T(8,128)(2,1)S(1)} %copy-done, s32[]{:T(128)S(6)} %select_n.97, s32[]{:T(128)S(6)} %select_n.91, bf16[800,400]{0,1:T(8,128)(2,1)S(1)} %collective-permute-done, s32[800]{0:T(1024)S(1)} %get-tuple-element.24, s32[400]{0:T(512)S(1)} %copy-done.1), kind=kOutput, calls=%fused_computation.8 | convolution fusion | flops 492467200 | bytes 4556808 | tf_op jit(solution)/shard_map/dot_general | solution.py:43
  25.4 1.3 %convolution_add_fusion.2 = f32[768,400]{0,1:T(8,128)S(1)} fusion(f32[768,400]{0,1:T(8,128)S(1)} %convolution_add_fusion.3, bf16[1536,3200]{1,0:T(8,128)(2,1)S(1)} %copy-done, s32[]{:T(128)S(6)} %select_n.84, s32[]{:T(128)S(6)} %select_n.94, bf16[800,400]{0,1:T(8,128)(2,1)S(1)} %collective-permute-done.2, s32[800]{0:T(1024)S(1)} %get-tuple-element.23, ...), kind=kOutput, calls=%fused_computation.9 | convolution fusion | flops 492467200 | bytes 4556808 | tf_op jit(solution)/shard_map/dot_general | solution.py:43
  26.7 1.3 %convolution_add_fusion = f32[768,400]{0,1:T(8,128)S(1)} fusion(f32[768,400]{0,1:T(8,128)S(1)} %convolution_add_fusion.1, bf16[1536,3200]{1,0:T(8,128)(2,1)S(1)} %copy-done, s32[]{:T(128)S(6)} %select_n.97, s32[]{:T(128)S(6)} %select_n.94, bf16[800,400]{0,1:T(8,128)(2,1)S(1)} %collective-permute-done.2, s32[800]{0:T(1024)S(1)} %get-tuple-element.23, ...), kind=kOutput, calls=%fused_computation.7 | convolution fusion | flops 492467200 | bytes 4556808 | tf_op jit(solution)/shard_map/dot_general | solution.py:43
  28.0 2.0 %collective-permute-done.1 = bf16[400,400]{0,1:T(8,128)(2,1)S(1)} collective-permute-done((bf16[400,400]{0,1:T(8,128)(2,1)S(1)}, bf16[400,400]{0,1:T(8,128)(2,1)S(1)}, u32[]{:S(2)}, u32[]{:S(2)}) %collective-permute-start.1) | collective-permute-done | bytes 320032 | tf_op jit(solution)/shard_map/ppermute | solution.py:10
  30.0 1.4 %collective-permute-done.3 = bf16[400,400]{0,1:T(8,128)(2,1)S(1)} collective-permute-done((bf16[400,400]{0,1:T(8,128)(2,1)S(1)}, bf16[400,400]{0,1:T(8,128)(2,1)S(1)}, u32[]{:S(2)}, u32[]{:S(2)}) %collective-permute-start.3) | collective-permute-done | bytes 320032 | tf_op jit(solution)/shard_map/ppermute | solution.py:10
  31.4 0.8 %fusion.18 = f32[768,400]{0,1:T(8,128)S(1)} fusion(bf16[1536,3200]{1,0:T(8,128)(2,1)S(1)} %copy-done, s32[]{:T(128)S(6)} %select_n.97, s32[]{:T(128)S(6)} %select_n.99, bf16[400,400]{0,1:T(8,128)(2,1)S(1)} %collective-permute-done.1, s32[400]{0:T(512)S(1)} %get-tuple-element.22, s32[400]{0:T(512)S(1)} %copy-done.1), kind=kOutput, calls=%fused_computation.30 | convolution fusion | flops 246080000 | bytes 2428936 | tf_op jit(solution)/shard_map/dot_general | solution.py:43
  32.2 0.8 %fusion.12 = f32[768,400]{0,1:T(8,128)S(1)} fusion(bf16[1536,3200]{1,0:T(8,128)(2,1)S(1)} %copy-done, s32[]{:T(128)S(6)} %select_n.84, s32[]{:T(128)S(6)} %select_n.99, bf16[400,400]{0,1:T(8,128)(2,1)S(1)} %collective-permute-done.1, s32[400]{0:T(512)S(1)} %get-tuple-element.22, s32[400]{0:T(512)S(1)} %copy-done.1), kind=kOutput, calls=%fused_computation.26 | convolution fusion | flops 246080000 | bytes 2428936 | tf_op jit(solution)/shard_map/dot_general | solution.py:43
  33.0 0.8 %add_add_fusion = f32[768,400]{0,1:T(8,128)S(1)} fusion(f32[768,400]{0,1:T(8,128)S(1)} %convolution_add_fusion.2, f32[768,400]{0,1:T(8,128)S(1)} %fusion.12, bf16[1536,3200]{1,0:T(8,128)(2,1)S(1)} %copy-done, s32[]{:T(128)S(6)} %select_n.84, s32[]{:T(128)S(6)} %select_n.102, bf16[400,400]{0,1:T(8,128)(2,1)S(1)} %collective-permute-done.3, ...), kind=kOutput, calls=%fused_computation.20 | convolution fusion | flops 246694400 | bytes 4886536 | tf_op jit(solution)/shard_map/dot_general | solution.py:43
  35.0 0.8 %add_add_fusion.1 = f32[768,400]{0,1:T(8,128)S(1)} fusion(f32[768,400]{0,1:T(8,128)S(1)} %convolution_add_fusion, f32[768,400]{0,1:T(8,128)S(1)} %fusion.18, bf16[1536,3200]{1,0:T(8,128)(2,1)S(1)} %copy-done, s32[]{:T(128)S(6)} %select_n.97, s32[]{:T(128)S(6)} %select_n.102, bf16[400,400]{0,1:T(8,128)(2,1)S(1)} %collective-permute-done.3, ...), kind=kOutput, calls=%fused_computation.21 | convolution fusion | flops 246694400 | bytes 4886536 | tf_op jit(solution)/shard_map/dot_general | solution.py:43
  37.2 1.6 %collective-permute-start.5 = (f32[768,100]{0,1:T(8,128)S(1)}, f32[768,100]{0,1:T(8,128)S(1)}, u32[]{:S(2)}, u32[]{:S(2)}) collective-permute-start(f32[768,100]{0,1:T(8,128)S(1)} %get-tuple-element.13), channel_id=1, source_target_pairs={{0,16},{8,24},{16,0},{24,8},{1,17},{9,25},{17,1},{25,9},{2,18},{10... | collective-permute-start | bytes 921608 | tf_op jit(solution)/shard_map/ppermute | solution.py:10
  39.3 1.5 %collective-permute-start.9 = (f32[768,100]{0,1:T(8,128)S(1)}, f32[768,100]{0,1:T(8,128)S(1)}, u32[]{:S(2)}, u32[]{:S(2)}) collective-permute-start(f32[768,100]{0,1:T(8,128)S(1)} %get-tuple-element.15), channel_id=1, source_target_pairs={{0,16},{8,24},{16,0},{24,8},{1,17},{9,25},{17,1},{25,9},{2,18},{10... | collective-permute-start | bytes 921608 | tf_op jit(solution)/shard_map/ppermute | solution.py:10
  41.0 1.6 %gather_fusion.3 = f32[768,100]{1,0:T(8,128)S(1)} fusion(f32[768,100]{1,0:T(8,128)S(1)} %copy.12, s32[1024]{0:T(1024)S(1)} %pad_clamp_fusion), kind=kCustom, calls=%fused_computation.3 | custom fusion | bytes 617472 | tf_op jit(solution)/shard_map/jit(_take)/gather | solution.py:78
  43.3 4.3 %collective-permute-done.5 = f32[768,100]{0,1:T(8,128)S(1)} collective-permute-done((f32[768,100]{0,1:T(8,128)S(1)}, f32[768,100]{0,1:T(8,128)S(1)}, u32[]{:S(2)}, u32[]{:S(2)}) %collective-permute-start.5) | collective-permute-done | bytes 307232 | tf_op jit(solution)/shard_map/ppermute | solution.py:10
  47.8 1.6 %gather_fusion = f32[768,100]{1,0:T(8,128)S(1)} fusion(f32[768,100]{1,0:T(8,128)S(1)} %copy.6, s32[1024]{0:T(1024)S(1)} %pad_clamp_fusion.1), kind=kCustom, calls=%fused_computation | custom fusion | bytes 617472 | tf_op jit(solution)/shard_map/jit(_take)/gather | solution.py:82
  49.6 4.9 %collective-permute-done.7 = f32[768,100]{0,1:T(8,128)S(1)} collective-permute-done((f32[768,100]{0,1:T(8,128)S(1)}, f32[768,100]{0,1:T(8,128)S(1)}, u32[]{:S(2)}, u32[]{:S(2)}) %collective-permute-start.7) | collective-permute-done | bytes 307232 | tf_op jit(solution)/shard_map/ppermute | solution.py:10
  54.6 1.6 %gather_fusion.1 = f32[768,100]{1,0:T(8,128)S(1)} fusion(f32[768,100]{1,0:T(8,128)S(1)} %copy.8, s32[1024]{0:T(1024)S(1)} %pad_clamp_fusion.1), kind=kCustom, calls=%fused_computation.1 | custom fusion | bytes 617472 | tf_op jit(solution)/shard_map/jit(_take)/gather | solution.py:82
  56.4 4.9 %collective-permute-done.9 = f32[768,100]{0,1:T(8,128)S(1)} collective-permute-done((f32[768,100]{0,1:T(8,128)S(1)}, f32[768,100]{0,1:T(8,128)S(1)}, u32[]{:S(2)}, u32[]{:S(2)}) %collective-permute-start.9) | collective-permute-done | bytes 307232 | tf_op jit(solution)/shard_map/ppermute | solution.py:10
  61.5 1.6 %gather_fusion.2 = f32[768,100]{1,0:T(8,128)S(1)} fusion(f32[768,100]{1,0:T(8,128)S(1)} %copy.10, s32[1024]{0:T(1024)S(1)} %pad_clamp_fusion.1), kind=kCustom, calls=%fused_computation.2 | custom fusion | bytes 617472 | tf_op jit(solution)/shard_map/jit(_take)/gather | solution.py:82
  63.3 4.2 %collective-permute-done.11 = f32[768,100]{0,1:T(8,128)} collective-permute-done((f32[768,100]{0,1:T(8,128)S(1)}, f32[768,100]{0,1:T(8,128)}, u32[]{:S(2)}, u32[]{:S(2)}) %collective-permute-start.11) | collective-permute-done | bytes 307232 | tf_op jit(solution)/shard_map/ppermute | solution.py:10
  67.4 1.0 %sub.31 = f32[768,100]{0,1:T(8,128)S(1)} subtract(f32[768,100]{0,1:T(8,128)S(1)} %get-tuple-element.14, f32[768,100]{0,1:T(8,128)} %collective-permute-done.11) | non-fusion elementwise | flops 76800 | bytes 921600 | tf_op jit(solution)/shard_map/sub | solution.py:79
  68.5 1.1 %pad_maximum_fusion = f32[768,400]{0,1:T(8,128)} fusion(f32[768,100]{0,1:T(8,128)S(1)} %sub.31, f32[768,100]{0,1:T(8,128)S(1)} %sub.28, f32[768,100]{0,1:T(8,128)S(1)} %sub.27, f32[768,100]{0,1:T(8,128)S(1)} %sub.26), kind=kLoop, calls=%fused_computation.19 | loop fusion | flops 921600 | bytes 2457600 | tf_op jit(solution)/shard_map/concatenate | solution.py:83
  (32 shorter events, 5.4 us)
Async XLA Ops:
  0.0 19.2 %collective-permute-start = (bf16[800,400]{0,1:T(8,128)(2,1)}, bf16[800,400]{0,1:T(8,128)(2,1)S(1)}, u32[]{:S(2)}, u32[]{:S(2)}) collective-permute-start(bf16[800,400]{0,1:T(8,128)(2,1)} %param.6), channel_id=1, source_target_pairs={{0,16},{8,24},{16,0},{24,8},{1,17},{9,25},{17,1},{25,9},{2,18},{10... | collective-permute-start | bytes 1920008 | tf_op jit(solution)/shard_map/ppermute | solution.py:10
  3.0 18.1 %collective-permute-start.2 = (bf16[800,400]{0,1:T(8,128)(2,1)}, bf16[800,400]{0,1:T(8,128)(2,1)S(1)}, u32[]{:S(2)}, u32[]{:S(2)}) collective-permute-start(bf16[800,400]{0,1:T(8,128)(2,1)} %param.6), channel_id=1, source_target_pairs={{0,8},{8,0},{16,24},{24,16},{1,9},{9,1},{17,25},{25,17},{2,10},{10... | collective-permute-start | bytes 1920008 | tf_op jit(solution)/shard_map/ppermute | solution.py:10
  4.5 5.5 %copy-start.1 = (s32[400]{0:T(512)S(1)}, s32[400]{0:T(512)}, u32[]{:S(2)}) copy-start(s32[400]{0:T(512)} %param.8) | copy-start | bytes 4804
  7.0 15.8 %copy-start = (bf16[1536,3200]{1,0:T(8,128)(2,1)S(1)}, bf16[1536,3200]{1,0:T(8,128)(2,1)}, u32[]{:S(2)}) copy-start(bf16[1536,3200]{1,0:T(8,128)(2,1)} %param.5) | copy-start | bytes 29491204
  19.3 10.7 %collective-permute-start.1 = (bf16[400,400]{0,1:T(8,128)(2,1)S(1)}, bf16[400,400]{0,1:T(8,128)(2,1)S(1)}, u32[]{:S(2)}, u32[]{:S(2)}) collective-permute-start(bf16[400,400]{0,1:T(8,128)(2,1)S(1)} %slice.48), channel_id=1, source_target_pairs={{0,8},{8,0},{16,24},{24,16},{1,9},{9,1},{17,25},{25,17},{2,10},{10... | collective-permute-start | bytes 960008 | tf_op jit(solution)/shard_map/ppermute | solution.py:10
  21.3 10.1 %collective-permute-start.3 = (bf16[400,400]{0,1:T(8,128)(2,1)S(1)}, bf16[400,400]{0,1:T(8,128)(2,1)S(1)}, u32[]{:S(2)}, u32[]{:S(2)}) collective-permute-start(bf16[400,400]{0,1:T(8,128)(2,1)S(1)} %slice.49), channel_id=1, source_target_pairs={{0,16},{8,24},{16,0},{24,8},{1,17},{9,25},{17,1},{25,9},{2,18},{10... | collective-permute-start | bytes 960008 | tf_op jit(solution)/shard_map/ppermute | solution.py:10
  33.9 1.9 %collective-permute-start.10 = (f32[768,100]{0,1:T(8,128)S(1)}, f32[768,100]{0,1:T(8,128)S(1)}, u32[]{:S(2)}, u32[]{:S(2)}) collective-permute-start(f32[768,100]{0,1:T(8,128)S(1)} %get-tuple-element.18), channel_id=1, source_target_pairs={{0,1},{1,0},{2,3},{3,2},{4,5},{5,4},{6,7},{7,6},{8,9},{9,8},{10,11... | collective-permute-start | bytes 921608 | tf_op jit(solution)/shard_map/ppermute | solution.py:10
  34.0 2.1 %collective-permute-start.4 = (f32[768,100]{0,1:T(8,128)S(1)}, f32[768,100]{0,1:T(8,128)S(1)}, u32[]{:S(2)}, u32[]{:S(2)}) collective-permute-start(f32[768,100]{0,1:T(8,128)S(1)} %get-tuple-element.17), channel_id=1, source_target_pairs={{0,1},{1,0},{2,3},{3,2},{4,5},{5,4},{6,7},{7,6},{8,9},{9,8},{10,11... | collective-permute-start | bytes 921608 | tf_op jit(solution)/shard_map/ppermute | solution.py:10
  34.5 2.0 %collective-permute-start.6 = (f32[768,100]{0,1:T(8,128)S(1)}, f32[768,100]{0,1:T(8,128)S(1)}, u32[]{:S(2)}, u32[]{:S(2)}) collective-permute-start(f32[768,100]{0,1:T(8,128)S(1)} %get-tuple-element.20), channel_id=1, source_target_pairs={{0,1},{1,0},{2,3},{3,2},{4,5},{5,4},{6,7},{7,6},{8,9},{9,8},{10,11... | collective-permute-start | bytes 921608 | tf_op jit(solution)/shard_map/ppermute | solution.py:10
  34.5 2.4 %collective-permute-start.8 = (f32[768,100]{0,1:T(8,128)S(1)}, f32[768,100]{0,1:T(8,128)S(1)}, u32[]{:S(2)}, u32[]{:S(2)}) collective-permute-start(f32[768,100]{0,1:T(8,128)S(1)} %get-tuple-element.19), channel_id=1, source_target_pairs={{0,1},{1,0},{2,3},{3,2},{4,5},{5,4},{6,7},{7,6},{8,9},{9,8},{10,11... | collective-permute-start | bytes 921608 | tf_op jit(solution)/shard_map/ppermute | solution.py:10
  37.2 10.4 %collective-permute-start.5 = (f32[768,100]{0,1:T(8,128)S(1)}, f32[768,100]{0,1:T(8,128)S(1)}, u32[]{:S(2)}, u32[]{:S(2)}) collective-permute-start(f32[768,100]{0,1:T(8,128)S(1)} %get-tuple-element.13), channel_id=1, source_target_pairs={{0,16},{8,24},{16,0},{24,8},{1,17},{9,25},{17,1},{25,9},{2,18},{10... | collective-permute-start | bytes 921608 | tf_op jit(solution)/shard_map/ppermute | solution.py:10
  38.8 15.7 %collective-permute-start.7 = (f32[768,100]{0,1:T(8,128)S(1)}, f32[768,100]{0,1:T(8,128)S(1)}, u32[]{:S(2)}, u32[]{:S(2)}) collective-permute-start(f32[768,100]{0,1:T(8,128)S(1)} %get-tuple-element.16), channel_id=1, source_target_pairs={{0,16},{8,24},{16,0},{24,8},{1,17},{9,25},{17,1},{25,9},{2,18},{10... | collective-permute-start | bytes 921608 | tf_op jit(solution)/shard_map/ppermute | solution.py:10
  39.3 22.0 %collective-permute-start.9 = (f32[768,100]{0,1:T(8,128)S(1)}, f32[768,100]{0,1:T(8,128)S(1)}, u32[]{:S(2)}, u32[]{:S(2)}) collective-permute-start(f32[768,100]{0,1:T(8,128)S(1)} %get-tuple-element.15), channel_id=1, source_target_pairs={{0,16},{8,24},{16,0},{24,8},{1,17},{9,25},{17,1},{25,9},{2,18},{10... | collective-permute-start | bytes 921608 | tf_op jit(solution)/shard_map/ppermute | solution.py:10
  42.7 24.7 %collective-permute-start.11 = (f32[768,100]{0,1:T(8,128)S(1)}, f32[768,100]{0,1:T(8,128)}, u32[]{:S(2)}, u32[]{:S(2)}) collective-permute-start(f32[768,100]{0,1:T(8,128)S(1)} %copy.13), channel_id=1, source_target_pairs={{0,16},{8,24},{16,0},{24,8},{1,17},{9,25},{17,1},{25,9},{2,18},{10... | collective-permute-start | bytes 921608 | tf_op jit(solution)/shard_map/ppermute | solution.py:10

commit v23 on v22

--- a/solution.py
+++ b/solution.py
@@ -67,13 +67,15 @@
     theirs = lax.dynamic_slice(mirror_row, (partner_block * block_rows,), (block_rows,))
     wanted = theirs - own_block * block_rows
     cols = kept.shape[1]
-    pieces = 4 if cols % 4 == 0 else 1
-    step = cols // pieces
+    first = cols // 3 // 16 * 16
+    bounds = [0, first, cols] if first > 0 else [0, cols]
+    pieces = len(bounds) - 1
     results = []
     for j in range(pieces):
-        piece = kept[:, j * step:(j + 1) * step]
+        lo, hi = bounds[j], bounds[j + 1]
+        piece = kept[:, lo:hi]
         for s, part in sent:
-            piece = piece + swap(part[:, j * step:(j + 1) * step], "cuts", s)
+            piece = piece + swap(part[:, lo:hi], "cuts", s)
         if j == pieces - 1 and pieces > 1:
             fetched = swap(jnp.take(piece, wanted, axis=0, mode="clip"), "prow", half)
             results.append(piece - fetched)

time: 70.1 us -> 81.3 us (1.16)
  waiting for transfers between devices: 28.7 us -> 35.2 us
  matrix products: 14.6 us -> 18 us
  starting transfers between devices: 13.1 us -> 10.4 us
  other arithmetic: 3.28 us -> 5.48 us
  local copies, waits for them, and re-layouts: 9.77 us -> 11.5 us
    ppermute x12 -> x8, waiting for transfers between devices: 28.7 us -> 35.2 us  [swap(): lax.ppermute(value, axis, [(i, i ^ mask) for i in range(lax.axis_size(axi...]
    gather x2, local copies, waits for them, and re-layouts: 1.76 us -> 5.53 us  [shards(): fetched = swap(jnp.take(piece, wanted, axis=0, mode='clip'), 'prow', half)]
    gather x6 -> x2, local copies, waits for them, and re-layouts: 5.27 us -> 1.74 us  [shards(): results.append(piece - jnp.take(fetched, local, axis=0, mode='clip'))]
    dot_general x10, matrix products: 14.6 us -> 18 us  [contract(): product = jnp.dot(window, blocked, preferred_element_type=jnp.float32)]
    ppermute x12 -> x8, starting transfers between devices: 13.1 us -> 10.4 us  [swap(): lax.ppermute(value, axis, [(i, i ^ mask) for i in range(lax.axis_size(axi...]
    add x1 -> x2, other arithmetic: 0.21 us -> 2.28 us  [shards(): piece = piece + swap(part[:, lo:hi], 'cuts', s)]
    slice x1 -> x2, local copies, waits for them, and re-layouts: 0.1 us -> 1.75 us  [shards(): piece = piece + swap(part[:, lo:hi], 'cuts', s)]
  transfers between devices with their start and end apart: 12 -> 8, of which waited for: 10 -> 4; matrix products, arithmetic and copies ran while one was open for 33% -> 37% of each run, Pallas kernels for 0% -> 0%
where the time goes in v23:
time: 81.3 us; the launch traced here: 80.8 us
  waiting for transfers between devices  35.2 us (43%)
  matrix products  18 us (22%)
  local copies, waits for them, and re-layouts  11.5 us (14%)
  starting transfers between devices  10.4 us (13%)
  other arithmetic  5.48 us (7%)
    ppermute x8, waiting for transfers between devices, swap(): lax.ppermute(value, axis, [(i, i ^ mask) for i in range(lax.axis_size(axi...  35.2 us
    dot_general x10, matrix products, contract(): product = jnp.dot(window, blocked, preferred_element_type=jnp.float32)  18 us
    ppermute x8, starting transfers between devices, swap(): lax.ppermute(value, axis, [(i, i ^ mask) for i in range(lax.axis_size(axi...  10.4 us
    gather x2, local copies, waits for them, and re-layouts, shards(): fetched = swap(jnp.take(piece, wanted, axis=0, mode='clip'), 'prow', half)  5.53 us
    add x2, other arithmetic, shards(): piece = piece + swap(part[:, lo:hi], 'cuts', s)  2.28 us
    slice x2, local copies, waits for them, and re-layouts, shards(): piece = piece + swap(part[:, lo:hi], 'cuts', s)  1.75 us
    gather x2, local copies, waits for them, and re-layouts, shards(): results.append(piece - jnp.take(fetched, local, axis=0, mode='clip'))  1.74 us
    dynamic_slice x2, local copies, waits for them, and re-layouts, contract(): lax.dynamic_slice_in_dim(labels, o, b.shape[0])[:, None]  1.73 us
  transfers between devices with their start and end apart: 8, of which 4 were waited for; matrix products, arithmetic and copies ran while one was open for 37% of the time, Pallas kernels for 0%

profile of v23, /device:TPU:0, one launch (start us, length us, event | category | flops | bytes accessed | tf_op | source)
XLA Modules:
  0.0 80.8 jit_solution(2222960821602454970)
XLA Ops:
  0.0 3.0 %collective-permute-start = (bf16[800,400]{0,1:T(8,128)(2,1)}, bf16[800,400]{0,1:T(8,128)(2,1)S(1)}, u32[]{:S(2)}, u32[]{:S(2)}) collective-permute-start(bf16[800,400]{0,1:T(8,128)(2,1)} %param.6), channel_id=1, source_target_pairs={{0,16},{8,24},{16,0},{24,8},{1,17},{9,25},{17,1},{25,9},{2,18},{10... | collective-permute-start | bytes 1920008 | tf_op jit(solution)/shard_map/ppermute | solution.py:10
  3.0 1.5 %collective-permute-start.2 = (bf16[800,400]{0,1:T(8,128)(2,1)}, bf16[800,400]{0,1:T(8,128)(2,1)S(1)}, u32[]{:S(2)}, u32[]{:S(2)}) collective-permute-start(bf16[800,400]{0,1:T(8,128)(2,1)} %param.6), channel_id=1, source_target_pairs={{0,8},{8,0},{16,24},{24,16},{1,9},{9,1},{17,25},{25,17},{2,10},{10... | collective-permute-start | bytes 1920008 | tf_op jit(solution)/shard_map/ppermute | solution.py:10
  4.5 0.9 %fusion.31 = (s32[800]{0:T(1024)S(1)}, s32[800]{0:T(1024)S(1)}, s32[800]{0:T(1024)S(1)}) fusion(s32[6400]{0:T(1024)} %param.7, s32[]{:T(128)S(6)} %dynamic_slice.76, s32[]{:T(128)S(6)} %dynamic_slice.73, s32[]{:T(128)S(6)} %dynamic_slice.70), kind=kLoop, calls=%fused_computation.47 | loop fusion | bytes 19212 | tf_op jit(solution)/shard_map/dynamic_slice | solution.py:41
  5.3 0.8 %fusion.30 = (s32[400]{0:T(512)S(1)}, s32[400]{0:T(512)S(1)}) fusion(s32[6400]{0:T(1024)} %param.7, s32[]{:T(128)S(6)} %dynamic_slice.85, s32[]{:T(128)S(6)} %dynamic_slice.82), kind=kLoop, calls=%fused_computation.46 | loop fusion | bytes 6408 | tf_op jit(solution)/shard_map/dynamic_slice | solution.py:41
  6.2 3.0 %fusion.6 = f32[768,400]{0,1:T(8,128)S(1)} fusion(bf16[1536,3200]{1,0:T(8,128)(2,1)} %param.5, s32[]{:T(128)S(6)} %select_n.84, s32[]{:T(128)S(6)} %select_n.86, bf16[800,400]{0,1:T(8,128)(2,1)} %param.6, s32[800]{0:T(1024)S(1)} %get-tuple-element.17, s32[400]{0:T(512)} %param.8), kind=kOutput, calls=%fused_computation.15 | convolution fusion | flops 492160000 | bytes 3327112 | tf_op jit(solution)/shard_map/dot_general | solution.py:43
  9.2 3.3 %fusion.2 = f32[768,400]{0,1:T(8,128)S(1)} fusion(bf16[1536,3200]{1,0:T(8,128)(2,1)} %param.5, s32[]{:T(128)S(6)} %select_n.97, s32[]{:T(128)S(6)} %select_n.86, bf16[800,400]{0,1:T(8,128)(2,1)} %param.6, s32[800]{0:T(1024)S(1)} %get-tuple-element.17, s32[400]{0:T(512)S(1)} %copy-done.2), kind=kOutput, calls=%fused_computation.11 | convolution fusion | flops 492160000 | bytes 3326664 | tf_op jit(solution)/shard_map/dot_general | solution.py:43
  12.5 6.7 %collective-permute-done = bf16[800,400]{0,1:T(8,128)(2,1)S(1)} collective-permute-done((bf16[800,400]{0,1:T(8,128)(2,1)}, bf16[800,400]{0,1:T(8,128)(2,1)S(1)}, u32[]{:S(2)}, u32[]{:S(2)}) %collective-permute-start) | collective-permute-done | bytes 640032 | tf_op jit(solution)/shard_map/ppermute | solution.py:10
  19.3 1.8 %collective-permute-start.1 = (bf16[400,400]{0,1:T(8,128)(2,1)S(1)}, bf16[400,400]{0,1:T(8,128)(2,1)S(1)}, u32[]{:S(2)}, u32[]{:S(2)}) collective-permute-start(bf16[400,400]{0,1:T(8,128)(2,1)S(1)} %slice.28), channel_id=1, source_target_pairs={{0,8},{8,0},{16,24},{24,16},{1,9},{9,1},{17,25},{25,17},{2,10},{10... | collective-permute-start | bytes 960008 | tf_op jit(solution)/shard_map/ppermute | solution.py:10
  21.2 1.6 %collective-permute-start.3 = (bf16[400,400]{0,1:T(8,128)(2,1)S(1)}, bf16[400,400]{0,1:T(8,128)(2,1)S(1)}, u32[]{:S(2)}, u32[]{:S(2)}) collective-permute-start(bf16[400,400]{0,1:T(8,128)(2,1)S(1)} %slice.29), channel_id=1, source_target_pairs={{0,16},{8,24},{16,0},{24,8},{1,17},{9,25},{17,1},{25,9},{2,18},{10... | collective-permute-start | bytes 960008 | tf_op jit(solution)/shard_map/ppermute | solution.py:10
  22.8 1.3 %convolution_add_fusion.3 = f32[768,400]{0,1:T(8,128)S(1)} fusion(f32[768,400]{0,1:T(8,128)S(1)} %fusion.6, bf16[1536,3200]{1,0:T(8,128)(2,1)S(1)} %copy-done, s32[]{:T(128)S(6)} %select_n.84, s32[]{:T(128)S(6)} %select_n.91, bf16[800,400]{0,1:T(8,128)(2,1)S(1)} %collective-permute-done, s32[800]{0:T(1024)S(1)} %get-tuple-element.16, s32[400]{0:T(512)S(1)} %copy-done.2), kind=kOutput, calls=%fused_computation.8 | convolution fusion | flops 492467200 | bytes 4556808 | tf_op jit(solution)/shard_map/dot_general | solution.py:43
  24.1 1.3 %convolution_add_fusion.1 = f32[768,400]{0,1:T(8,128)S(1)} fusion(f32[768,400]{0,1:T(8,128)S(1)} %fusion.2, bf16[1536,3200]{1,0:T(8,128)(2,1)S(1)} %copy-done, s32[]{:T(128)S(6)} %select_n.97, s32[]{:T(128)S(6)} %select_n.91, bf16[800,400]{0,1:T(8,128)(2,1)S(1)} %collective-permute-done, s32[800]{0:T(1024)S(1)} %get-tuple-element.16, s32[400]{0:T(512)S(1)} %copy-done.2), kind=kOutput, calls=%fused_computation.6 | convolution fusion | flops 492467200 | bytes 4556808 | tf_op jit(solution)/shard_map/dot_general | solution.py:43
  25.4 1.3 %convolution_add_fusion.2 = f32[768,400]{0,1:T(8,128)S(1)} fusion(f32[768,400]{0,1:T(8,128)S(1)} %convolution_add_fusion.3, bf16[1536,3200]{1,0:T(8,128)(2,1)S(1)} %copy-done, s32[]{:T(128)S(6)} %select_n.84, s32[]{:T(128)S(6)} %select_n.94, bf16[800,400]{0,1:T(8,128)(2,1)S(1)} %collective-permute-done.2, s32[800]{0:T(1024)S(1)} %get-tuple-element.15, ...), kind=kOutput, calls=%fused_computation.7 | convolution fusion | flops 492467200 | bytes 4556808 | tf_op jit(solution)/shard_map/dot_general | solution.py:43
  26.7 2.3 %convolution_add_fusion = f32[768,400]{0,1:T(8,128)} fusion(f32[768,400]{0,1:T(8,128)S(1)} %convolution_add_fusion.1, bf16[1536,3200]{1,0:T(8,128)(2,1)S(1)} %copy-done, s32[]{:T(128)S(6)} %select_n.97, s32[]{:T(128)S(6)} %select_n.94, bf16[800,400]{0,1:T(8,128)(2,1)S(1)} %collective-permute-done.2, s32[800]{0:T(1024)S(1)} %get-tuple-element.15, ...), kind=kOutput, calls=%fused_computation.5 | convolution fusion | flops 492467200 | bytes 4556808 | tf_op jit(solution)/shard_map/dot_general | solution.py:43
  29.0 1.0 %collective-permute-done.1 = bf16[400,400]{0,1:T(8,128)(2,1)S(1)} collective-permute-done((bf16[400,400]{0,1:T(8,128)(2,1)S(1)}, bf16[400,400]{0,1:T(8,128)(2,1)S(1)}, u32[]{:S(2)}, u32[]{:S(2)}) %collective-permute-start.1) | collective-permute-done | bytes 320032 | tf_op jit(solution)/shard_map/ppermute | solution.py:10
  30.0 1.4 %collective-permute-done.3 = bf16[400,400]{0,1:T(8,128)(2,1)S(1)} collective-permute-done((bf16[400,400]{0,1:T(8,128)(2,1)S(1)}, bf16[400,400]{0,1:T(8,128)(2,1)S(1)}, u32[]{:S(2)}, u32[]{:S(2)}) %collective-permute-start.3) | collective-permute-done | bytes 320032 | tf_op jit(solution)/shard_map/ppermute | solution.py:10
  31.4 0.8 fusion.12
  32.2 0.8 %add_add_fusion = f32[768,400]{0,1:T(8,128)S(1)} fusion(f32[768,400]{0,1:T(8,128)S(1)} %convolution_add_fusion.2, f32[768,400]{0,1:T(8,128)S(1)} %fusion.12, bf16[1536,3200]{1,0:T(8,128)(2,1)S(1)} %copy-done, s32[]{:T(128)S(6)} %select_n.84, s32[]{:T(128)S(6)} %select_n.102, bf16[400,400]{0,1:T(8,128)(2,1)S(1)} %collective-permute-done.3, ...), kind=kOutput, calls=%fused_computation.18 | convolution fusion | flops 246694400 | bytes 4886536 | tf_op jit(solution)/shard_map/dot_general | solution.py:43
  33.0 1.0 %slice.33 = f32[768,272]{0,1:T(8,128)} slice(f32[768,400]{0,1:T(8,128)S(1)} %add_add_fusion), slice={[0:768], [128:400]} | slice | bytes 1671168 | tf_op jit(solution)/shard_map/slice | solution.py:78
  34.0 0.8 dynamic-slice_subtract_fusion.1
  34.8 0.8 slice.31
  35.5 0.5 collective-permute-start.4
  36.1 2.0 %fusion.18 = f32[768,400]{0,1:T(8,128)S(1)} fusion(bf16[1536,3200]{1,0:T(8,128)(2,1)} %param.5, s32[]{:T(128)S(6)} %select_n.97, s32[]{:T(128)S(6)} %select_n.99, bf16[400,400]{0,1:T(8,128)(2,1)S(1)} %collective-permute-done.1, s32[400]{0:T(512)S(1)} %get-tuple-element.14, s32[400]{0:T(512)S(1)} %copy-done.2), kind=kOutput, calls=%fused_computation.29 | convolution fusion | flops 246080000 | bytes 2338440 | tf_op jit(solution)/shard_map/dot_general | solution.py:43
  38.1 2.0 %add_add_fusion.1 = f32[768,400]{0,1:T(8,128)S(1)} fusion(f32[768,400]{0,1:T(8,128)S(1)} %copy-done.1, f32[768,400]{0,1:T(8,128)S(1)} %fusion.18, bf16[1536,3200]{1,0:T(8,128)(2,1)} %param.5, s32[]{:T(128)S(6)} %select_n.97, s32[]{:T(128)S(6)} %select_n.102, bf16[400,400]{0,1:T(8,128)(2,1)S(1)} %collective-permute-done.3, s32[400]{0:T(512)S(1)} %get-tuple-element.13, ...), kind=kOutput, calls=%fused_computation.19 | convolution fusion | flops 246694400 | bytes 4796040 | tf_op jit(solution)/shard_map/dot_general | solution.py:43
  40.1 1.2 %slice_add_fusion = f32[768,272]{0,1:T(8,128)S(1)} fusion(f32[768,272]{0,1:T(8,128)} %collective-permute-done.6, f32[768,400]{0,1:T(8,128)S(1)} %add_add_fusion.1), kind=kLoop, calls=%fused_computation.20 | loop fusion | flops 208896 | bytes 2506752 | tf_op jit(solution)/shard_map/add | solution.py:78
  41.7 3.0 %gather_fusion.1 = f32[768,272]{1,0:T(8,128)} fusion(f32[768,272]{1,0:T(8,128)S(1)} %copy.8, s32[1024]{0:T(1024)S(1)} %pad_clamp_fusion), kind=kCustom, calls=%fused_computation.1 | custom fusion | bytes 1674240 | tf_op jit(solution)/shard_map/jit(_take)/gather | solution.py:80
  44.7 2.5 %copy.9 = f32[768,272]{0,1:T(8,128)} copy(f32[768,272]{1,0:T(8,128)} %gather_fusion.1) | data formatting | bytes 1671168 | tf_op jit(solution)/shard_map/jit(_take)/gather | solution.py:80
  47.2 1.6 %collective-permute-start.7 = (f32[768,272]{0,1:T(8,128)}, f32[768,272]{0,1:T(8,128)}, u32[]{:S(2)}, u32[]{:S(2)}) collective-permute-start(f32[768,272]{0,1:T(8,128)} %copy.9), channel_id=1, source_target_pairs={{0,16},{8,24},{16,0},{24,8},{1,17},{9,25},{17,1},{25,9},{2,18},{10... | collective-permute-start | bytes 2506760 | tf_op jit(solution)/shard_map/ppermute | solution.py:10
  48.8 1.0 %slice_add_fusion.1 = f32[768,128]{0,1:T(8,128)S(1)} fusion(f32[768,128]{0,1:T(8,128)} %collective-permute-done.4, f32[768,400]{0,1:T(8,128)S(1)} %add_add_fusion.1), kind=kLoop, calls=%fused_computation.31 | loop fusion | flops 98304 | bytes 1179648 | tf_op jit(solution)/shard_map/add | solution.py:78
  50.3 26.1 %collective-permute-done.5 = f32[768,128]{0,1:T(8,128)S(1)} collective-permute-done((f32[768,128]{0,1:T(8,128)S(1)}, f32[768,128]{0,1:T(8,128)S(1)}, u32[]{:S(2)}, u32[]{:S(2)}) %collective-permute-start.5) | collective-permute-done | bytes 393248 | tf_op jit(solution)/shard_map/ppermute | solution.py:10
  76.6 1.6 %gather_fusion = f32[768,128]{1,0:T(8,128)S(1)} fusion(f32[768,128]{1,0:T(8,128)S(1)} %copy.6, s32[1024]{0:T(1024)S(1)} %pad_clamp_fusion.1), kind=kCustom, calls=%fused_computation | custom fusion | bytes 789504 | tf_op jit(solution)/shard_map/jit(_take)/gather | solution.py:84
  78.4 1.2 %sub.23 = f32[768,272]{0,1:T(8,128)S(1)} subtract(f32[768,272]{0,1:T(8,128)S(1)} %slice_add_fusion, f32[768,272]{0,1:T(8,128)} %collective-permute-done.7) | non-fusion elementwise | flops 208896 | bytes 2506752 | tf_op jit(solution)/shard_map/sub | solution.py:81
  79.7 1.1 %pad_maximum_fusion = f32[768,400]{0,1:T(8,128)} fusion(f32[768,272]{0,1:T(8,128)S(1)} %sub.23, f32[768,128]{0,1:T(8,128)S(1)} %sub.20), kind=kLoop, calls=%fused_computation.17 | loop fusion | flops 307200 | bytes 2457600 | tf_op jit(solution)/shard_map/concatenate | solution.py:85
  (20 shorter events, 1.5 us)
Async XLA Ops:
  0.0 19.2 %collective-permute-start = (bf16[800,400]{0,1:T(8,128)(2,1)}, bf16[800,400]{0,1:T(8,128)(2,1)S(1)}, u32[]{:S(2)}, u32[]{:S(2)}) collective-permute-start(bf16[800,400]{0,1:T(8,128)(2,1)} %param.6), channel_id=1, source_target_pairs={{0,16},{8,24},{16,0},{24,8},{1,17},{9,25},{17,1},{25,9},{2,18},{10... | collective-permute-start | bytes 1920008 | tf_op jit(solution)/shard_map/ppermute | solution.py:10
  3.0 18.1 %collective-permute-start.2 = (bf16[800,400]{0,1:T(8,128)(2,1)}, bf16[800,400]{0,1:T(8,128)(2,1)S(1)}, u32[]{:S(2)}, u32[]{:S(2)}) collective-permute-start(bf16[800,400]{0,1:T(8,128)(2,1)} %param.6), channel_id=1, source_target_pairs={{0,8},{8,0},{16,24},{24,16},{1,9},{9,1},{17,25},{25,17},{2,10},{10... | collective-permute-start | bytes 1920008 | tf_op jit(solution)/shard_map/ppermute | solution.py:10
  4.5 4.7 %copy-start.2 = (s32[400]{0:T(512)S(1)}, s32[400]{0:T(512)}, u32[]{:S(2)}) copy-start(s32[400]{0:T(512)} %param.8) | copy-start | bytes 4804
  6.2 16.6 %copy-start = (bf16[1536,3200]{1,0:T(8,128)(2,1)S(1)}, bf16[1536,3200]{1,0:T(8,128)(2,1)}, u32[]{:S(2)}) copy-start(bf16[1536,3200]{1,0:T(8,128)(2,1)} %param.5) | copy-start | bytes 29491204
  19.3 10.7 %collective-permute-start.1 = (bf16[400,400]{0,1:T(8,128)(2,1)S(1)}, bf16[400,400]{0,1:T(8,128)(2,1)S(1)}, u32[]{:S(2)}, u32[]{:S(2)}) collective-permute-start(bf16[400,400]{0,1:T(8,128)(2,1)S(1)} %slice.28), channel_id=1, source_target_pairs={{0,8},{8,0},{16,24},{24,16},{1,9},{9,1},{17,25},{25,17},{2,10},{10... | collective-permute-start | bytes 960008 | tf_op jit(solution)/shard_map/ppermute | solution.py:10
  21.2 10.1 %collective-permute-start.3 = (bf16[400,400]{0,1:T(8,128)(2,1)S(1)}, bf16[400,400]{0,1:T(8,128)(2,1)S(1)}, u32[]{:S(2)}, u32[]{:S(2)}) collective-permute-start(bf16[400,400]{0,1:T(8,128)(2,1)S(1)} %slice.29), channel_id=1, source_target_pairs={{0,16},{8,24},{16,0},{24,8},{1,17},{9,25},{17,1},{25,9},{2,18},{10... | collective-permute-start | bytes 960008 | tf_op jit(solution)/shard_map/ppermute | solution.py:10
  34.0 6.1 %collective-permute-start.6 = (f32[768,272]{0,1:T(8,128)}, f32[768,272]{0,1:T(8,128)}, u32[]{:S(2)}, u32[]{:S(2)}) collective-permute-start(f32[768,272]{0,1:T(8,128)} %slice.33), channel_id=1, source_target_pairs={{0,1},{1,0},{2,3},{3,2},{4,5},{5,4},{6,7},{7,6},{8,9},{9,8},{10,11... | collective-permute-start | bytes 2506760 | tf_op jit(solution)/shard_map/ppermute | solution.py:10
  35.5 2.5 %copy-start.1 = (f32[768,400]{0,1:T(8,128)S(1)}, f32[768,400]{0,1:T(8,128)}, u32[]{:S(2)}) copy-start(f32[768,400]{0,1:T(8,128)} %convolution_add_fusion) | copy-start | bytes 3686404
  35.5 13.3 %collective-permute-start.4 = (f32[768,128]{0,1:T(8,128)}, f32[768,128]{0,1:T(8,128)}, u32[]{:S(2)}, u32[]{:S(2)}) collective-permute-start(f32[768,128]{0,1:T(8,128)} %slice.31), channel_id=1, source_target_pairs={{0,1},{1,0},{2,3},{3,2},{4,5},{5,4},{6,7},{7,6},{8,9},{9,8},{10,11... | collective-permute-start | bytes 1179656 | tf_op jit(solution)/shard_map/ppermute | solution.py:10
  47.2 31.2 %collective-permute-start.7 = (f32[768,272]{0,1:T(8,128)}, f32[768,272]{0,1:T(8,128)}, u32[]{:S(2)}, u32[]{:S(2)}) collective-permute-start(f32[768,272]{0,1:T(8,128)} %copy.9), channel_id=1, source_target_pairs={{0,16},{8,24},{16,0},{24,8},{1,17},{9,25},{17,1},{25,9},{2,18},{10... | collective-permute-start | bytes 2506760 | tf_op jit(solution)/shard_map/ppermute | solution.py:10
  49.8 26.6 %collective-permute-start.5 = (f32[768,128]{0,1:T(8,128)S(1)}, f32[768,128]{0,1:T(8,128)S(1)}, u32[]{:S(2)}, u32[]{:S(2)}) collective-permute-start(f32[768,128]{0,1:T(8,128)S(1)} %slice_add_fusion.1), channel_id=1, source_target_pairs={{0,16},{8,24},{16,0},{24,8},{1,17},{9,25},{17,1},{25,9},{2,18},{10... | collective-permute-start | bytes 1179656 | tf_op jit(solution)/shard_map/ppermute | solution.py:10

commit v24 on v18

--- a/solution.py
+++ b/solution.py
@@ -13,7 +13,7 @@
 def gather_prow(own, prow_idx, prow_count):
     count = own.shape[0]
     if prow_count == 4 and count % 32 == 0:
-        half = count // 2
+        half = count // 2 + count // 16 // 16 * 16
         from_x = swap(own, "prow", 1)
         from_y = swap(own, "prow", 2)
         diag_a = swap(from_y[:half], "prow", 1)

time: 67 us -> 65.6 us (0.979)
  waiting for transfers between devices: 29.9 us -> 27.1 us
    ppermute x8, waiting for transfers between devices: 29.9 us -> 27.1 us  [swap(): lax.ppermute(value, axis, [(i, i ^ mask) for i in range(lax.axis_size(axi...]
    dynamic_slice x2 -> x3, local copies, waits for them, and re-layouts: 1.73 us -> 2.42 us  [contract(): lax.dynamic_slice_in_dim(labels, o, b.shape[0])[:, None]]
  transfers between devices with their start and end apart: 8 -> 8, of which waited for: 6 -> 5; matrix products, arithmetic and copies ran while one was open for 35% -> 37% of each run, Pallas kernels for 0% -> 0%
where the time goes in v24:
time: 65.6 us; the launch traced here: 65 us
  waiting for transfers between devices  27.1 us (41%)
  matrix products  15.2 us (23%)
  starting transfers between devices  10.5 us (16%)
  local copies, waits for them, and re-layouts  9.84 us (15%)
  other arithmetic  2.24 us (3%)
    ppermute x8, waiting for transfers between devices, swap(): lax.ppermute(value, axis, [(i, i ^ mask) for i in range(lax.axis_size(axi...  27.1 us
    dot_general x10, matrix products, contract(): product = jnp.dot(window, blocked, preferred_element_type=jnp.float32)  15.2 us
    ppermute x8, starting transfers between devices, swap(): lax.ppermute(value, axis, [(i, i ^ mask) for i in range(lax.axis_size(axi...  10.5 us
    gather x2, local copies, waits for them, and re-layouts, shards(): fetched = swap(jnp.take(piece, wanted, axis=0, mode='clip'), 'prow', half)  3.19 us
    dynamic_slice x3, local copies, waits for them, and re-layouts, contract(): lax.dynamic_slice_in_dim(labels, o, b.shape[0])[:, None]  2.42 us
    gather x2, local copies, waits for them, and re-layouts, shards(): results.append(piece - jnp.take(fetched, local, axis=0, mode='clip'))  2.36 us
    ppermute x1, local copies, waits for them, and re-layouts, swap(): lax.ppermute(value, axis, [(i, i ^ mask) for i in range(lax.axis_size(axi...  1.34 us
  transfers between devices with their start and end apart: 8, of which 5 were waited for; matrix products, arithmetic and copies ran while one was open for 37% of the time, Pallas kernels for 0%

profile of v24, /device:TPU:0, one launch (start us, length us, event | category | flops | bytes accessed | tf_op | source)
XLA Modules:
  0.0 65.0 jit_solution(2956334117852992177)
XLA Ops:
  0.0 3.0 %collective-permute-start = (bf16[800,400]{0,1:T(8,128)(2,1)}, bf16[800,400]{0,1:T(8,128)(2,1)S(1)}, u32[]{:S(2)}, u32[]{:S(2)}) collective-permute-start(bf16[800,400]{0,1:T(8,128)(2,1)} %param.6), channel_id=1, source_target_pairs={{0,16},{8,24},{16,0},{24,8},{1,17},{9,25},{17,1},{25,9},{2,18},{10... | collective-permute-start | bytes 1920008 | tf_op jit(solution)/shard_map/ppermute | solution.py:10
  3.0 1.5 %collective-permute-start.2 = (bf16[800,400]{0,1:T(8,128)(2,1)}, bf16[800,400]{0,1:T(8,128)(2,1)S(1)}, u32[]{:S(2)}, u32[]{:S(2)}) collective-permute-start(bf16[800,400]{0,1:T(8,128)(2,1)} %param.6), channel_id=1, source_target_pairs={{0,8},{8,0},{16,24},{24,16},{1,9},{9,1},{17,25},{25,17},{2,10},{10... | collective-permute-start | bytes 1920008 | tf_op jit(solution)/shard_map/ppermute | solution.py:10
  4.5 0.8 %dynamic_slice.83 = s32[448]{0:T(512)S(1)} dynamic-slice(s32[6400]{0:T(1024)} %param.7, s32[]{:T(128)S(6)} %dynamic_slice.82), dynamic_slice_sizes={448} | dynamic-slice | bytes 3588 | tf_op jit(solution)/shard_map/dynamic_slice | solution.py:41
  5.2 0.8 %dynamic_slice.86 = s32[352]{0:T(512)S(1)} dynamic-slice(s32[6400]{0:T(1024)} %param.7, s32[]{:T(128)S(6)} %dynamic_slice.85), dynamic_slice_sizes={352} | dynamic-slice | bytes 2820 | tf_op jit(solution)/shard_map/dynamic_slice | solution.py:41
  6.0 0.9 %fusion.31 = (s32[800]{0:T(1024)S(1)}, s32[800]{0:T(1024)S(1)}, s32[800]{0:T(1024)S(1)}) fusion(s32[6400]{0:T(1024)} %param.7, s32[]{:T(128)S(6)} %dynamic_slice.76, s32[]{:T(128)S(6)} %dynamic_slice.73, s32[]{:T(128)S(6)} %dynamic_slice.70), kind=kLoop, calls=%fused_computation.47 | loop fusion | bytes 19212 | tf_op jit(solution)/shard_map/dynamic_slice | solution.py:41
  6.9 0.8 %dynamic-slice_subtract_fusion.1 = (s32[768]{0:T(1024)S(1)}, s32[768]{0:T(1024)S(1)}) fusion(s32[6144]{0:T(1024)} %param.9, s32[]{:T(128)S(6)} %select_n.105, s32[]{:T(128)S(6)} %mul.45, s32[]{:T(128)S(6)} %mul.43, s32[]{:T(128)S(6)} %select_n.106), kind=kLoop, calls=%fused_computation.35 | loop fusion | flops 1536 | bytes 12304 | tf_op jit(solution)/shard_map/sub | solution.py:66
  7.7 2.9 %fusion.6 = f32[768,400]{0,1:T(8,128)S(1)} fusion(bf16[1536,3200]{1,0:T(8,128)(2,1)} %param.5, s32[]{:T(128)S(6)} %select_n.85, s32[]{:T(128)S(6)} %select_n.87, bf16[800,400]{0,1:T(8,128)(2,1)} %param.6, s32[800]{0:T(1024)S(1)} %get-tuple-element.19, s32[400]{0:T(512)} %param.8), kind=kOutput, calls=%fused_computation.15 | convolution fusion | flops 492160000 | bytes 3327112 | tf_op jit(solution)/shard_map/dot_general | solution.py:43
  10.6 2.8 %fusion.2 = f32[768,400]{0,1:T(8,128)S(1)} fusion(bf16[1536,3200]{1,0:T(8,128)(2,1)} %param.5, s32[]{:T(128)S(6)} %select_n.98, s32[]{:T(128)S(6)} %select_n.87, bf16[800,400]{0,1:T(8,128)(2,1)S(1)} %copy-done.2, s32[800]{0:T(1024)S(1)} %get-tuple-element.19, s32[400]{0:T(512)S(1)} %copy-done.1), kind=kOutput, calls=%fused_computation.11 | convolution fusion | flops 492160000 | bytes 3249864 | tf_op jit(solution)/shard_map/dot_general | solution.py:43
  13.4 5.8 %collective-permute-done = bf16[800,400]{0,1:T(8,128)(2,1)S(1)} collective-permute-done((bf16[800,400]{0,1:T(8,128)(2,1)}, bf16[800,400]{0,1:T(8,128)(2,1)S(1)}, u32[]{:S(2)}, u32[]{:S(2)}) %collective-permute-start) | collective-permute-done | bytes 640032 | tf_op jit(solution)/shard_map/ppermute | solution.py:10
  19.3 1.8 %collective-permute-start.1 = (bf16[448,400]{0,1:T(8,128)(2,1)S(1)}, bf16[448,400]{0,1:T(8,128)(2,1)S(1)}, u32[]{:S(2)}, u32[]{:S(2)}) collective-permute-start(bf16[448,400]{0,1:T(8,128)(2,1)S(1)} %slice.28), channel_id=1, source_target_pairs={{0,8},{8,0},{16,24},{24,16},{1,9},{9,1},{17,25},{25,17},{2,10},{10... | collective-permute-start | bytes 1075208 | tf_op jit(solution)/shard_map/ppermute | solution.py:10
  21.2 1.6 %collective-permute-start.3 = (bf16[352,400]{0,1:T(8,128)(2,1)S(1)}, bf16[352,400]{0,1:T(8,128)(2,1)S(1)}, u32[]{:S(2)}, u32[]{:S(2)}) collective-permute-start(bf16[352,400]{0,1:T(8,128)(2,1)S(1)} %slice.29), channel_id=1, source_target_pairs={{0,16},{8,24},{16,0},{24,8},{1,17},{9,25},{17,1},{25,9},{2,18},{10... | collective-permute-start | bytes 844808 | tf_op jit(solution)/shard_map/ppermute | solution.py:10
  22.8 2.7 %convolution_add_fusion.3 = f32[768,400]{0,1:T(8,128)S(1)} fusion(f32[768,400]{0,1:T(8,128)S(1)} %fusion.6, bf16[1536,3200]{1,0:T(8,128)(2,1)} %param.5, s32[]{:T(128)S(6)} %select_n.85, s32[]{:T(128)S(6)} %select_n.92, bf16[800,400]{0,1:T(8,128)(2,1)S(1)} %collective-permute-done, s32[800]{0:T(1024)S(1)} %get-tuple-element.18, s32[400]{0:T(512)S(1)} %copy-done.1), kind=kOutput, calls=%fused_computation.8 | convolution fusion | flops 492467200 | bytes 4478664 | tf_op jit(solution)/shard_map/dot_general | solution.py:43
  25.5 1.3 %convolution_add_fusion.1 = f32[768,400]{0,1:T(8,128)S(1)} fusion(f32[768,400]{0,1:T(8,128)S(1)} %fusion.2, bf16[1536,3200]{1,0:T(8,128)(2,1)S(1)} %copy-done, s32[]{:T(128)S(6)} %select_n.98, s32[]{:T(128)S(6)} %select_n.92, bf16[800,400]{0,1:T(8,128)(2,1)S(1)} %collective-permute-done, s32[800]{0:T(1024)S(1)} %get-tuple-element.18, s32[400]{0:T(512)S(1)} %copy-done.1), kind=kOutput, calls=%fused_computation.6 | convolution fusion | flops 492467200 | bytes 4556808 | tf_op jit(solution)/shard_map/dot_general | solution.py:43
  26.7 1.3 %convolution_add_fusion.2 = f32[768,400]{0,1:T(8,128)S(1)} fusion(f32[768,400]{0,1:T(8,128)S(1)} %convolution_add_fusion.3, bf16[1536,3200]{1,0:T(8,128)(2,1)S(1)} %copy-done, s32[]{:T(128)S(6)} %select_n.85, s32[]{:T(128)S(6)} %select_n.95, bf16[800,400]{0,1:T(8,128)(2,1)S(1)} %collective-permute-done.2, s32[800]{0:T(1024)S(1)} %get-tuple-element.17, ...), kind=kOutput, calls=%fused_computation.7 | convolution fusion | flops 492467200 | bytes 4556808 | tf_op jit(solution)/shard_map/dot_general | solution.py:43
  28.0 1.3 %convolution_add_fusion = f32[768,400]{0,1:T(8,128)S(1)} fusion(f32[768,400]{0,1:T(8,128)S(1)} %convolution_add_fusion.1, bf16[1536,3200]{1,0:T(8,128)(2,1)S(1)} %copy-done, s32[]{:T(128)S(6)} %select_n.98, s32[]{:T(128)S(6)} %select_n.95, bf16[800,400]{0,1:T(8,128)(2,1)S(1)} %collective-permute-done.2, s32[800]{0:T(1024)S(1)} %get-tuple-element.17, ...), kind=kOutput, calls=%fused_computation.5 | convolution fusion | flops 492467200 | bytes 4556808 | tf_op jit(solution)/shard_map/dot_general | solution.py:43
  29.3 0.7 %collective-permute-done.1 = bf16[448,400]{0,1:T(8,128)(2,1)S(1)} collective-permute-done((bf16[448,400]{0,1:T(8,128)(2,1)S(1)}, bf16[448,400]{0,1:T(8,128)(2,1)S(1)}, u32[]{:S(2)}, u32[]{:S(2)}) %collective-permute-start.1) | collective-permute-done | bytes 358432 | tf_op jit(solution)/shard_map/ppermute | solution.py:10
  30.0 0.8 %fusion.8 = f32[768,400]{0,1:T(8,128)S(1)} fusion(bf16[1536,3200]{1,0:T(8,128)(2,1)S(1)} %copy-done, s32[]{:T(128)S(6)} %select_n.85, s32[]{:T(128)S(6)} %select_n.100, bf16[448,400]{0,1:T(8,128)(2,1)S(1)} %collective-permute-done.1, s32[448]{0:T(512)S(1)} %dynamic_slice.83, s32[400]{0:T(512)S(1)} %copy-done.1), kind=kOutput, calls=%fused_computation.21 | convolution fusion | flops 275609600 | bytes 2428936 | tf_op jit(solution)/shard_map/dot_general | solution.py:43
  30.8 0.7 %add_add_fusion = f32[768,400]{0,1:T(8,128)S(1)} fusion(f32[768,400]{0,1:T(8,128)S(1)} %convolution_add_fusion.2, f32[768,400]{0,1:T(8,128)S(1)} %fusion.8, bf16[1536,3200]{1,0:T(8,128)(2,1)S(1)} %copy-done, s32[]{:T(128)S(6)} %select_n.85, s32[]{:T(128)S(6)} %select_n.103, bf16[352,400]{0,1:T(8,128)(2,1)S(1)} %collective-permute-done.3, ...), kind=kOutput, calls=%fused_computation.18 | convolution fusion | flops 217164800 | bytes 4587528 | tf_op jit(solution)/shard_map/dot_general | solution.py:43
  31.6 0.5 collective-permute-start.6
  32.1 0.8 %fusion.10 = f32[768,400]{0,1:T(8,128)S(1)} fusion(bf16[1536,3200]{1,0:T(8,128)(2,1)S(1)} %copy-done, s32[]{:T(128)S(6)} %select_n.98, s32[]{:T(128)S(6)} %select_n.100, bf16[448,400]{0,1:T(8,128)(2,1)S(1)} %collective-permute-done.1, s32[448]{0:T(512)S(1)} %dynamic_slice.83, s32[400]{0:T(512)S(1)} %copy-done.1), kind=kOutput, calls=%fused_computation.23 | convolution fusion | flops 275609600 | bytes 2428936 | tf_op jit(solution)/shard_map/dot_general | solution.py:43
  32.9 0.7 %add_add_fusion.1 = f32[768,400]{0,1:T(8,128)S(1)} fusion(f32[768,400]{0,1:T(8,128)S(1)} %convolution_add_fusion, f32[768,400]{0,1:T(8,128)S(1)} %fusion.10, bf16[1536,3200]{1,0:T(8,128)(2,1)S(1)} %copy-done, s32[]{:T(128)S(6)} %select_n.98, s32[]{:T(128)S(6)} %select_n.103, bf16[352,400]{0,1:T(8,128)(2,1)S(1)} %collective-permute-done.3, ...), kind=kOutput, calls=%fused_computation.19 | convolution fusion | flops 217164800 | bytes 4587528 | tf_op jit(solution)/shard_map/dot_general | solution.py:43
  33.7 0.8 %collective-permute-done.6 = f32[768,200]{0,1:T(8,128)S(1)} collective-permute-done((f32[768,200]{0,1:T(8,128)S(1)}, f32[768,200]{0,1:T(8,128)S(1)}, u32[]{:S(2)}, u32[]{:S(2)}) %collective-permute-start.6) | collective-permute-done | bytes 614432 | tf_op jit(solution)/shard_map/ppermute | solution.py:10
  34.7 1.5 %collective-permute-start.5 = (f32[768,200]{0,1:T(8,128)S(1)}, f32[768,200]{0,1:T(8,128)}, u32[]{:S(2)}, u32[]{:S(2)}) collective-permute-start(f32[768,200]{0,1:T(8,128)S(1)} %get-tuple-element.13), channel_id=1, source_target_pairs={{0,16},{8,24},{16,0},{24,8},{1,17},{9,25},{17,1},{25,9},{2,18},{10... | collective-permute-start | bytes 1843208 | tf_op jit(solution)/shard_map/ppermute | solution.py:10
  36.2 0.3 copy.8
  36.5 2.1 %gather_fusion.1 = f32[768,200]{1,0:T(8,128)S(1)} fusion(f32[768,200]{1,0:T(8,128)S(1)} %copy.8, s32[1024]{0:T(1024)S(1)} %pad_clamp_fusion), kind=kCustom, calls=%fused_computation.1 | custom fusion | bytes 1231872 | tf_op jit(solution)/shard_map/jit(_take)/gather | solution.py:78
  38.6 1.1 %copy.9 = f32[768,200]{0,1:T(8,128)} copy(f32[768,200]{1,0:T(8,128)S(1)} %gather_fusion.1) | data formatting | bytes 1228800 | tf_op jit(solution)/shard_map/jit(_take)/gather | solution.py:78
  39.7 0.6 collective-permute-start.7
  40.3 11.3 %collective-permute-done.5 = f32[768,200]{0,1:T(8,128)} collective-permute-done((f32[768,200]{0,1:T(8,128)S(1)}, f32[768,200]{0,1:T(8,128)}, u32[]{:S(2)}, u32[]{:S(2)}) %collective-permute-start.5) | collective-permute-done | bytes 614432 | tf_op jit(solution)/shard_map/ppermute | solution.py:10
  51.6 1.3 %copy.6 = f32[768,200]{1,0:T(8,128)S(1)} copy(f32[768,200]{0,1:T(8,128)} %collective-permute-done.5) | data formatting | bytes 1228800 | tf_op jit(solution)/shard_map/ppermute | solution.py:10
  52.9 2.1 %gather_fusion = f32[768,200]{1,0:T(8,128)S(1)} fusion(f32[768,200]{1,0:T(8,128)S(1)} %copy.6, s32[1024]{0:T(1024)S(1)} %pad_clamp_fusion.1), kind=kCustom, calls=%fused_computation | custom fusion | bytes 1231872 | tf_op jit(solution)/shard_map/jit(_take)/gather | solution.py:82
  55.4 8.4 %collective-permute-done.7 = f32[768,200]{0,1:T(8,128)S(1)} collective-permute-done((f32[768,200]{0,1:T(8,128)}, f32[768,200]{0,1:T(8,128)S(1)}, u32[]{:S(2)}, u32[]{:S(2)}) %collective-permute-start.7) | collective-permute-done | bytes 614432 | tf_op jit(solution)/shard_map/ppermute | solution.py:10
  63.9 1.1 %pad_maximum_fusion = f32[768,400]{0,1:T(8,128)} fusion(f32[768,200]{0,1:T(8,128)S(1)} %sub.23, f32[768,200]{0,1:T(8,128)S(1)} %sub.20), kind=kLoop, calls=%fused_computation.17 | loop fusion | flops 307200 | bytes 2457600 | tf_op jit(solution)/shard_map/concatenate | solution.py:83
  (19 shorter events, 0.9 us)
Async XLA Ops:
  0.0 19.2 %collective-permute-start = (bf16[800,400]{0,1:T(8,128)(2,1)}, bf16[800,400]{0,1:T(8,128)(2,1)S(1)}, u32[]{:S(2)}, u32[]{:S(2)}) collective-permute-start(bf16[800,400]{0,1:T(8,128)(2,1)} %param.6), channel_id=1, source_target_pairs={{0,16},{8,24},{16,0},{24,8},{1,17},{9,25},{17,1},{25,9},{2,18},{10... | collective-permute-start | bytes 1920008 | tf_op jit(solution)/shard_map/ppermute | solution.py:10
  3.0 18.1 %collective-permute-start.2 = (bf16[800,400]{0,1:T(8,128)(2,1)}, bf16[800,400]{0,1:T(8,128)(2,1)S(1)}, u32[]{:S(2)}, u32[]{:S(2)}) collective-permute-start(bf16[800,400]{0,1:T(8,128)(2,1)} %param.6), channel_id=1, source_target_pairs={{0,8},{8,0},{16,24},{24,16},{1,9},{9,1},{17,25},{25,17},{2,10},{10... | collective-permute-start | bytes 1920008 | tf_op jit(solution)/shard_map/ppermute | solution.py:10
  7.7 2.9 %copy-start.1 = (s32[400]{0:T(512)S(1)}, s32[400]{0:T(512)}, u32[]{:S(2)}) copy-start(s32[400]{0:T(512)} %param.8) | copy-start | bytes 4804
  7.7 2.9 %copy-start.2 = (bf16[800,400]{0,1:T(8,128)(2,1)S(1)}, bf16[800,400]{0,1:T(8,128)(2,1)}, u32[]{:S(2)}) copy-start(bf16[800,400]{0,1:T(8,128)(2,1)} %param.6) | copy-start | bytes 1920004
  10.6 14.9 %copy-start = (bf16[1536,3200]{1,0:T(8,128)(2,1)S(1)}, bf16[1536,3200]{1,0:T(8,128)(2,1)}, u32[]{:S(2)}) copy-start(bf16[1536,3200]{1,0:T(8,128)(2,1)} %param.5) | copy-start | bytes 29491204
  19.3 10.7 %collective-permute-start.1 = (bf16[448,400]{0,1:T(8,128)(2,1)S(1)}, bf16[448,400]{0,1:T(8,128)(2,1)S(1)}, u32[]{:S(2)}, u32[]{:S(2)}) collective-permute-start(bf16[448,400]{0,1:T(8,128)(2,1)S(1)} %slice.28), channel_id=1, source_target_pairs={{0,8},{8,0},{16,24},{24,16},{1,9},{9,1},{17,25},{25,17},{2,10},{10... | collective-permute-start | bytes 1075208 | tf_op jit(solution)/shard_map/ppermute | solution.py:10
  21.2 8.1 %collective-permute-start.3 = (bf16[352,400]{0,1:T(8,128)(2,1)S(1)}, bf16[352,400]{0,1:T(8,128)(2,1)S(1)}, u32[]{:S(2)}, u32[]{:S(2)}) collective-permute-start(bf16[352,400]{0,1:T(8,128)(2,1)S(1)} %slice.29), channel_id=1, source_target_pairs={{0,16},{8,24},{16,0},{24,8},{1,17},{9,25},{17,1},{25,9},{2,18},{10... | collective-permute-start | bytes 844808 | tf_op jit(solution)/shard_map/ppermute | solution.py:10
  31.6 2.1 %collective-permute-start.4 = (f32[768,200]{0,1:T(8,128)S(1)}, f32[768,200]{0,1:T(8,128)S(1)}, u32[]{:S(2)}, u32[]{:S(2)}) collective-permute-start(f32[768,200]{0,1:T(8,128)S(1)} %get-tuple-element.15), channel_id=1, source_target_pairs={{0,1},{1,0},{2,3},{3,2},{4,5},{5,4},{6,7},{7,6},{8,9},{9,8},{10,11... | collective-permute-start | bytes 1843208 | tf_op jit(solution)/shard_map/ppermute | solution.py:10
  31.6 2.9 %collective-permute-start.6 = (f32[768,200]{0,1:T(8,128)S(1)}, f32[768,200]{0,1:T(8,128)S(1)}, u32[]{:S(2)}, u32[]{:S(2)}) collective-permute-start(f32[768,200]{0,1:T(8,128)S(1)} %get-tuple-element.16), channel_id=1, source_target_pairs={{0,1},{1,0},{2,3},{3,2},{4,5},{5,4},{6,7},{7,6},{8,9},{9,8},{10,11... | collective-permute-start | bytes 1843208 | tf_op jit(solution)/shard_map/ppermute | solution.py:10
  34.7 16.9 %collective-permute-start.5 = (f32[768,200]{0,1:T(8,128)S(1)}, f32[768,200]{0,1:T(8,128)}, u32[]{:S(2)}, u32[]{:S(2)}) collective-permute-start(f32[768,200]{0,1:T(8,128)S(1)} %get-tuple-element.13), channel_id=1, source_target_pairs={{0,16},{8,24},{16,0},{24,8},{1,17},{9,25},{17,1},{25,9},{2,18},{10... | collective-permute-start | bytes 1843208 | tf_op jit(solution)/shard_map/ppermute | solution.py:10
  39.7 24.2 %collective-permute-start.7 = (f32[768,200]{0,1:T(8,128)}, f32[768,200]{0,1:T(8,128)S(1)}, u32[]{:S(2)}, u32[]{:S(2)}) collective-permute-start(f32[768,200]{0,1:T(8,128)} %copy.9), channel_id=1, source_target_pairs={{0,16},{8,24},{16,0},{24,8},{1,17},{9,25},{17,1},{25,9},{2,18},{10... | collective-permute-start | bytes 1843208 | tf_op jit(solution)/shard_map/ppermute | solution.py:10

commit v25 on v24

--- a/solution.py
+++ b/solution.py
@@ -20,7 +20,7 @@
         diag_b = swap(from_x[half:], "prow", 2)
         base = jnp.bitwise_xor(prow_idx, 3) * count
         return [[(own, prow_idx * count)], [(from_y, jnp.bitwise_xor(prow_idx, 2) * count)],
-                [(from_x, jnp.bitwise_xor(prow_idx, 1) * count)], [(diag_a, base), (diag_b, base + half)]]
+                [(from_x, jnp.bitwise_xor(prow_idx, 1) * count)], [(diag_b, base + half)], [(diag_a, base)]]
     groups = [[(own, prow_idx * count)]]
     for s in range(1, prow_count):
         groups.append([(swap(own, "prow", s), jnp.bitwise_xor(prow_idx, s) * count)])
@@ -31,7 +31,7 @@
     bands = [lax.dynamic_slice_in_dim(amplitudes, first, rows, axis=0) for first in firsts]
     terms = [None] * len(bands)
     for g, group in enumerate(groups):
-        if g == len(groups) - 1 and g > 0:
+        if g > 0 and (g == len(groups) - 1 or (len(groups) == 5 and g == 3)):
             blocks, held = lax.optimization_barrier((tuple(b for b, _ in group), tuple(terms)))
             group = [(b, o) for b, (_, o) in zip(blocks, group)]
             terms = list(held)

time: 65.6 us -> 68.3 us (1.041)
  other arithmetic: 2.24 us -> 3.91 us
  matrix products: 15.2 us -> 16.3 us
  waiting for transfers between devices: 27.1 us -> 26.2 us
  local copies, waits for them, and re-layouts: 9.84 us -> 10.7 us
    dot_general x10, matrix products: 15.2 us -> 16.3 us  [contract(): product = jnp.dot(window, blocked, preferred_element_type=jnp.float32)]
    add x1, other arithmetic: 0.16 us -> 1.23 us  [shards(): piece = piece + swap(part[:, j * step:(j + 1) * step], 'cuts', s)]
    ppermute x8, waiting for transfers between devices: 27.1 us -> 26.2 us  [swap(): lax.ppermute(value, axis, [(i, i ^ mask) for i in range(lax.axis_size(axi...]
    slice x1, local copies, waits for them, and re-layouts: 0.08 us -> 0.9 us  [shards(): piece = piece + swap(part[:, j * step:(j + 1) * step], 'cuts', s)]
  transfers between devices with their start and end apart: 8 -> 8, of which waited for: 5 -> 3; matrix products, arithmetic and copies ran while one was open for 37% -> 39% of each run, Pallas kernels for 0% -> 0%
where the time goes in v25:
time: 68.3 us; the launch traced here: 67.8 us
  waiting for transfers between devices  26.2 us (38%)
  matrix products  16.3 us (24%)
  local copies, waits for them, and re-layouts  10.7 us (16%)
  starting transfers between devices  10.4 us (15%)
  other arithmetic  3.91 us (6%)
    ppermute x8, waiting for transfers between devices, swap(): lax.ppermute(value, axis, [(i, i ^ mask) for i in range(lax.axis_size(axi...  26.2 us
    dot_general x10, matrix products, contract(): product = jnp.dot(window, blocked, preferred_element_type=jnp.float32)  16.3 us
    ppermute x8, starting transfers between devices, swap(): lax.ppermute(value, axis, [(i, i ^ mask) for i in range(lax.axis_size(axi...  10.4 us
    gather x2, local copies, waits for them, and re-layouts, shards(): fetched = swap(jnp.take(piece, wanted, axis=0, mode='clip'), 'prow', half)  3.19 us
    dynamic_slice x3, local copies, waits for them, and re-layouts, contract(): lax.dynamic_slice_in_dim(labels, o, b.shape[0])[:, None]  2.42 us
    gather x2, local copies, waits for them, and re-layouts, shards(): results.append(piece - jnp.take(fetched, local, axis=0, mode='clip'))  2.36 us
  transfers between devices with their start and end apart: 8, of which 3 were waited for; matrix products, arithmetic and copies ran while one was open for 39% of the time, Pallas kernels for 0%

profile of v25, /device:TPU:0, one launch (start us, length us, event | category | flops | bytes accessed | tf_op | source)
XLA Modules:
  0.0 67.8 jit_solution(1715861181179097074)
XLA Ops:
  0.0 3.0 %collective-permute-start = (bf16[800,400]{0,1:T(8,128)(2,1)}, bf16[800,400]{0,1:T(8,128)(2,1)S(1)}, u32[]{:S(2)}, u32[]{:S(2)}) collective-permute-start(bf16[800,400]{0,1:T(8,128)(2,1)} %param.6), channel_id=1, source_target_pairs={{0,16},{8,24},{16,0},{24,8},{1,17},{9,25},{17,1},{25,9},{2,18},{10... | collective-permute-start | bytes 1920008 | tf_op jit(solution)/shard_map/ppermute | solution.py:10
  3.0 1.5 %collective-permute-start.2 = (bf16[800,400]{0,1:T(8,128)(2,1)}, bf16[800,400]{0,1:T(8,128)(2,1)S(1)}, u32[]{:S(2)}, u32[]{:S(2)}) collective-permute-start(bf16[800,400]{0,1:T(8,128)(2,1)} %param.6), channel_id=1, source_target_pairs={{0,8},{8,0},{16,24},{24,16},{1,9},{9,1},{17,25},{25,17},{2,10},{10... | collective-permute-start | bytes 1920008 | tf_op jit(solution)/shard_map/ppermute | solution.py:10
  4.5 0.8 %dynamic_slice.83 = s32[352]{0:T(512)S(1)} dynamic-slice(s32[6400]{0:T(1024)} %param.7, s32[]{:T(128)S(6)} %dynamic_slice.82), dynamic_slice_sizes={352} | dynamic-slice | bytes 2820 | tf_op jit(solution)/shard_map/dynamic_slice | solution.py:41
  5.2 0.8 %dynamic_slice.87 = s32[448]{0:T(512)S(1)} dynamic-slice(s32[6400]{0:T(1024)} %param.7, s32[]{:T(128)S(6)} %dynamic_slice.86), dynamic_slice_sizes={448} | dynamic-slice | bytes 3588 | tf_op jit(solution)/shard_map/dynamic_slice | solution.py:41
  6.0 0.9 %fusion.27 = (s32[800]{0:T(1024)S(1)}, s32[800]{0:T(1024)S(1)}, s32[800]{0:T(1024)S(1)}) fusion(s32[6400]{0:T(1024)} %param.7, s32[]{:T(128)S(6)} %dynamic_slice.76, s32[]{:T(128)S(6)} %dynamic_slice.73, s32[]{:T(128)S(6)} %dynamic_slice.70), kind=kLoop, calls=%fused_computation.45 | loop fusion | bytes 19212 | tf_op jit(solution)/shard_map/dynamic_slice | solution.py:41
  6.9 2.9 %fusion.6 = f32[768,400]{0,1:T(8,128)S(1)} fusion(bf16[1536,3200]{1,0:T(8,128)(2,1)} %param.5, s32[]{:T(128)S(6)} %select_n.85, s32[]{:T(128)S(6)} %select_n.87, bf16[800,400]{0,1:T(8,128)(2,1)} %param.6, s32[800]{0:T(1024)S(1)} %get-tuple-element.23, s32[400]{0:T(512)} %param.8), kind=kOutput, calls=%fused_computation.15 | convolution fusion | flops 492160000 | bytes 3327112 | tf_op jit(solution)/shard_map/dot_general | solution.py:43
  9.8 2.8 %fusion.2 = f32[768,400]{0,1:T(8,128)S(1)} fusion(bf16[1536,3200]{1,0:T(8,128)(2,1)} %param.5, s32[]{:T(128)S(6)} %select_n.98, s32[]{:T(128)S(6)} %select_n.87, bf16[800,400]{0,1:T(8,128)(2,1)S(1)} %copy-done.2, s32[800]{0:T(1024)S(1)} %get-tuple-element.23, s32[400]{0:T(512)S(1)} %copy-done.1), kind=kOutput, calls=%fused_computation.11 | convolution fusion | flops 492160000 | bytes 3249864 | tf_op jit(solution)/shard_map/dot_general | solution.py:43
  12.6 6.6 %collective-permute-done = bf16[800,400]{0,1:T(8,128)(2,1)S(1)} collective-permute-done((bf16[800,400]{0,1:T(8,128)(2,1)}, bf16[800,400]{0,1:T(8,128)(2,1)S(1)}, u32[]{:S(2)}, u32[]{:S(2)}) %collective-permute-start) | collective-permute-done | bytes 640032 | tf_op jit(solution)/shard_map/ppermute | solution.py:10
  19.3 1.8 %collective-permute-start.1 = (bf16[448,400]{0,1:T(8,128)(2,1)S(1)}, bf16[448,400]{0,1:T(8,128)(2,1)S(1)}, u32[]{:S(2)}, u32[]{:S(2)}) collective-permute-start(bf16[448,400]{0,1:T(8,128)(2,1)S(1)} %slice.28), channel_id=1, source_target_pairs={{0,8},{8,0},{16,24},{24,16},{1,9},{9,1},{17,25},{25,17},{2,10},{10... | collective-permute-start | bytes 1075208 | tf_op jit(solution)/shard_map/ppermute | solution.py:10
  21.2 1.6 %collective-permute-start.3 = (bf16[352,400]{0,1:T(8,128)(2,1)S(1)}, bf16[352,400]{0,1:T(8,128)(2,1)S(1)}, u32[]{:S(2)}, u32[]{:S(2)}) collective-permute-start(bf16[352,400]{0,1:T(8,128)(2,1)S(1)} %slice.29), channel_id=1, source_target_pairs={{0,16},{8,24},{16,0},{24,8},{1,17},{9,25},{17,1},{25,9},{2,18},{10... | collective-permute-start | bytes 844808 | tf_op jit(solution)/shard_map/ppermute | solution.py:10
  22.8 2.7 %convolution_add_fusion.3 = f32[768,400]{0,1:T(8,128)S(1)} fusion(f32[768,400]{0,1:T(8,128)S(1)} %fusion.6, bf16[1536,3200]{1,0:T(8,128)(2,1)} %param.5, s32[]{:T(128)S(6)} %select_n.85, s32[]{:T(128)S(6)} %select_n.92, bf16[800,400]{0,1:T(8,128)(2,1)S(1)} %collective-permute-done, s32[800]{0:T(1024)S(1)} %get-tuple-element.22, s32[400]{0:T(512)S(1)} %copy-done.1), kind=kOutput, calls=%fused_computation.8 | convolution fusion | flops 492467200 | bytes 4478664 | tf_op jit(solution)/shard_map/dot_general | solution.py:43
  25.5 1.3 %convolution_add_fusion.1 = f32[768,400]{0,1:T(8,128)S(1)} fusion(f32[768,400]{0,1:T(8,128)S(1)} %fusion.2, bf16[1536,3200]{1,0:T(8,128)(2,1)S(1)} %copy-done, s32[]{:T(128)S(6)} %select_n.98, s32[]{:T(128)S(6)} %select_n.92, bf16[800,400]{0,1:T(8,128)(2,1)S(1)} %collective-permute-done, s32[800]{0:T(1024)S(1)} %get-tuple-element.22, s32[400]{0:T(512)S(1)} %copy-done.1), kind=kOutput, calls=%fused_computation.6 | convolution fusion | flops 492467200 | bytes 4556808 | tf_op jit(solution)/shard_map/dot_general | solution.py:43
  26.7 1.3 %convolution_add_fusion.2 = f32[768,400]{0,1:T(8,128)S(1)} fusion(f32[768,400]{0,1:T(8,128)S(1)} %convolution_add_fusion.3, bf16[1536,3200]{1,0:T(8,128)(2,1)S(1)} %copy-done, s32[]{:T(128)S(6)} %select_n.85, s32[]{:T(128)S(6)} %select_n.95, bf16[800,400]{0,1:T(8,128)(2,1)S(1)} %collective-permute-done.2, s32[800]{0:T(1024)S(1)} %get-tuple-element.21, ...), kind=kOutput, calls=%fused_computation.7 | convolution fusion | flops 492467200 | bytes 4556808 | tf_op jit(solution)/shard_map/dot_general | solution.py:43
  28.0 1.3 %convolution_add_fusion = f32[768,400]{0,1:T(8,128)S(1)} fusion(f32[768,400]{0,1:T(8,128)S(1)} %convolution_add_fusion.1, bf16[1536,3200]{1,0:T(8,128)(2,1)S(1)} %copy-done, s32[]{:T(128)S(6)} %select_n.98, s32[]{:T(128)S(6)} %select_n.95, bf16[800,400]{0,1:T(8,128)(2,1)S(1)} %collective-permute-done.2, s32[800]{0:T(1024)S(1)} %get-tuple-element.21, ...), kind=kOutput, calls=%fused_computation.5 | convolution fusion | flops 492467200 | bytes 4556808 | tf_op jit(solution)/shard_map/dot_general | solution.py:43
  29.3 0.7 %fusion.14 = f32[768,400]{0,1:T(8,128)S(1)} fusion(bf16[1536,3200]{1,0:T(8,128)(2,1)S(1)} %copy-done, s32[]{:T(128)S(6)} %select_n.85, s32[]{:T(128)S(6)} %select_n.100, bf16[352,400]{0,1:T(8,128)(2,1)S(1)} %collective-permute-done.3, s32[352]{0:T(512)S(1)} %dynamic_slice.83, s32[400]{0:T(512)S(1)} %copy-done.1), kind=kOutput, calls=%fused_computation.28 | convolution fusion | flops 216550400 | bytes 2129928 | tf_op jit(solution)/shard_map/dot_general | solution.py:43
  30.2 0.7 %fusion.12 = f32[768,400]{0,1:T(8,128)S(1)} fusion(bf16[1536,3200]{1,0:T(8,128)(2,1)S(1)} %copy-done, s32[]{:T(128)S(6)} %select_n.98, s32[]{:T(128)S(6)} %select_n.100, bf16[352,400]{0,1:T(8,128)(2,1)S(1)} %collective-permute-done.3, s32[352]{0:T(512)S(1)} %dynamic_slice.83, s32[400]{0:T(512)S(1)} %copy-done.1), kind=kOutput, calls=%fused_computation.26 | convolution fusion | flops 216550400 | bytes 2129928 | tf_op jit(solution)/shard_map/dot_general | solution.py:43
  31.0 0.8 %fusion.8 = f32[768,400]{0,1:T(8,128)S(1)} fusion(bf16[1536,3200]{1,0:T(8,128)(2,1)S(1)} %copy-done, s32[]{:T(128)S(6)} %select_n.85, s32[]{:T(128)S(6)} %select_n.103, bf16[448,400]{0,1:T(8,128)(2,1)S(1)} %collective-permute-done.1, s32[448]{0:T(512)S(1)} %dynamic_slice.87, s32[400]{0:T(512)S(1)} %copy-done.1), kind=kOutput, calls=%fused_computation.19 | convolution fusion | flops 275609600 | bytes 2428936 | tf_op jit(solution)/shard_map/dot_general | solution.py:43
  32.0 0.9 %fusion.26 = (f32[768,200]{0,1:T(8,128)}, f32[768,200]{0,1:T(8,128)S(1)}) fusion(f32[768,400]{0,1:T(8,128)S(1)} %add.127), kind=kLoop, calls=%fused_computation.44 | loop fusion | bytes 2457600 | tf_op jit(solution)/shard_map/slice | solution.py:76
  32.9 0.5 collective-permute-start.6
  33.4 0.8 %dynamic-slice_subtract_fusion.1 = (s32[768]{0:T(1024)S(1)}, s32[768]{0:T(1024)S(1)}) fusion(s32[6144]{0:T(1024)} %param.9, s32[]{:T(128)S(6)} %select_n.105, s32[]{:T(128)S(6)} %mul.45, s32[]{:T(128)S(6)} %mul.43, s32[]{:T(128)S(6)} %select_n.106), kind=kLoop, calls=%fused_computation.33 | loop fusion | flops 1536 | bytes 12304 | tf_op jit(solution)/shard_map/sub | solution.py:66
  34.2 2.0 %fusion.10 = f32[768,400]{0,1:T(8,128)S(1)} fusion(bf16[1536,3200]{1,0:T(8,128)(2,1)} %param.5, s32[]{:T(128)S(6)} %select_n.98, s32[]{:T(128)S(6)} %select_n.103, bf16[448,400]{0,1:T(8,128)(2,1)S(1)} %collective-permute-done.1, s32[448]{0:T(512)S(1)} %dynamic_slice.87, s32[400]{0:T(512)S(1)} %copy-done.1), kind=kOutput, calls=%fused_computation.21 | convolution fusion | flops 275609600 | bytes 2377032 | tf_op jit(solution)/shard_map/dot_general | solution.py:43
  36.4 1.2 %slice_add_fusion.1 = (f32[768,200]{0,1:T(8,128)S(1)}, f32[768,200]{0,1:T(8,128)S(1)}) fusion(f32[768,200]{0,1:T(8,128)S(1)} %collective-permute-done.4, f32[768,400]{0,1:T(8,128)S(1)} %add.126, f32[768,200]{0,1:T(8,128)} %collective-permute-done.6), kind=kLoop, calls=%fused_computation.24 | loop fusion | flops 307200 | bytes 3686400 | tf_op jit(solution)/shard_map/add | solution.py:76
  37.6 1.4 %collective-permute-start.5 = (f32[768,200]{0,1:T(8,128)S(1)}, f32[768,200]{0,1:T(8,128)}, u32[]{:S(2)}, u32[]{:S(2)}) collective-permute-start(f32[768,200]{0,1:T(8,128)S(1)} %get-tuple-element.17), channel_id=1, source_target_pairs={{0,16},{8,24},{16,0},{24,8},{1,17},{9,25},{17,1},{25,9},{2,18},{10... | collective-permute-start | bytes 1843208 | tf_op jit(solution)/shard_map/ppermute | solution.py:10
  39.0 0.3 copy.8
  39.3 2.1 %gather_fusion.1 = f32[768,200]{1,0:T(8,128)S(1)} fusion(f32[768,200]{1,0:T(8,128)S(1)} %copy.8, s32[1024]{0:T(1024)S(1)} %pad_clamp_fusion), kind=kCustom, calls=%fused_computation.1 | custom fusion | bytes 1231872 | tf_op jit(solution)/shard_map/jit(_take)/gather | solution.py:78
  41.4 1.1 %copy.9 = f32[768,200]{0,1:T(8,128)} copy(f32[768,200]{1,0:T(8,128)S(1)} %gather_fusion.1) | data formatting | bytes 1228800 | tf_op jit(solution)/shard_map/jit(_take)/gather | solution.py:78
  42.5 0.7 %collective-permute-start.7 = (f32[768,200]{0,1:T(8,128)}, f32[768,200]{0,1:T(8,128)S(1)}, u32[]{:S(2)}, u32[]{:S(2)}) collective-permute-start(f32[768,200]{0,1:T(8,128)} %copy.9), channel_id=1, source_target_pairs={{0,16},{8,24},{16,0},{24,8},{1,17},{9,25},{17,1},{25,9},{2,18},{10... | collective-permute-start | bytes 1843208 | tf_op jit(solution)/shard_map/ppermute | solution.py:10
  43.2 11.3 %collective-permute-done.5 = f32[768,200]{0,1:T(8,128)} collective-permute-done((f32[768,200]{0,1:T(8,128)S(1)}, f32[768,200]{0,1:T(8,128)}, u32[]{:S(2)}, u32[]{:S(2)}) %collective-permute-start.5) | collective-permute-done | bytes 614432 | tf_op jit(solution)/shard_map/ppermute | solution.py:10
  54.5 1.3 %copy.6 = f32[768,200]{1,0:T(8,128)S(1)} copy(f32[768,200]{0,1:T(8,128)} %collective-permute-done.5) | data formatting | bytes 1228800 | tf_op jit(solution)/shard_map/ppermute | solution.py:10
  55.8 2.1 %gather_fusion = f32[768,200]{1,0:T(8,128)S(1)} fusion(f32[768,200]{1,0:T(8,128)S(1)} %copy.6, s32[1024]{0:T(1024)S(1)} %pad_clamp_fusion.1), kind=kCustom, calls=%fused_computation | custom fusion | bytes 1231872 | tf_op jit(solution)/shard_map/jit(_take)/gather | solution.py:82
  58.3 8.3 %collective-permute-done.7 = f32[768,200]{0,1:T(8,128)S(1)} collective-permute-done((f32[768,200]{0,1:T(8,128)}, f32[768,200]{0,1:T(8,128)S(1)}, u32[]{:S(2)}, u32[]{:S(2)}) %collective-permute-start.7) | collective-permute-done | bytes 614432 | tf_op jit(solution)/shard_map/ppermute | solution.py:10
  66.7 1.1 %pad_maximum_fusion = f32[768,400]{0,1:T(8,128)} fusion(f32[768,200]{0,1:T(8,128)S(1)} %sub.23, f32[768,200]{0,1:T(8,128)S(1)} %sub.20), kind=kLoop, calls=%fused_computation.17 | loop fusion | flops 307200 | bytes 2457600 | tf_op jit(solution)/shard_map/concatenate | solution.py:83
  (23 shorter events, 1.2 us)
Async XLA Ops:
  0.0 19.2 %collective-permute-start = (bf16[800,400]{0,1:T(8,128)(2,1)}, bf16[800,400]{0,1:T(8,128)(2,1)S(1)}, u32[]{:S(2)}, u32[]{:S(2)}) collective-permute-start(bf16[800,400]{0,1:T(8,128)(2,1)} %param.6), channel_id=1, source_target_pairs={{0,16},{8,24},{16,0},{24,8},{1,17},{9,25},{17,1},{25,9},{2,18},{10... | collective-permute-start | bytes 1920008 | tf_op jit(solution)/shard_map/ppermute | solution.py:10
  3.0 18.1 %collective-permute-start.2 = (bf16[800,400]{0,1:T(8,128)(2,1)}, bf16[800,400]{0,1:T(8,128)(2,1)S(1)}, u32[]{:S(2)}, u32[]{:S(2)}) collective-permute-start(bf16[800,400]{0,1:T(8,128)(2,1)} %param.6), channel_id=1, source_target_pairs={{0,8},{8,0},{16,24},{24,16},{1,9},{9,1},{17,25},{25,17},{2,10},{10... | collective-permute-start | bytes 1920008 | tf_op jit(solution)/shard_map/ppermute | solution.py:10
  6.9 2.9 %copy-start.1 = (s32[400]{0:T(512)S(1)}, s32[400]{0:T(512)}, u32[]{:S(2)}) copy-start(s32[400]{0:T(512)} %param.8) | copy-start | bytes 4804
  6.9 2.9 %copy-start.2 = (bf16[800,400]{0,1:T(8,128)(2,1)S(1)}, bf16[800,400]{0,1:T(8,128)(2,1)}, u32[]{:S(2)}) copy-start(bf16[800,400]{0,1:T(8,128)(2,1)} %param.6) | copy-start | bytes 1920004
  9.8 15.6 %copy-start = (bf16[1536,3200]{1,0:T(8,128)(2,1)S(1)}, bf16[1536,3200]{1,0:T(8,128)(2,1)}, u32[]{:S(2)}) copy-start(bf16[1536,3200]{1,0:T(8,128)(2,1)} %param.5) | copy-start | bytes 29491204
  19.3 11.8 %collective-permute-start.1 = (bf16[448,400]{0,1:T(8,128)(2,1)S(1)}, bf16[448,400]{0,1:T(8,128)(2,1)S(1)}, u32[]{:S(2)}, u32[]{:S(2)}) collective-permute-start(bf16[448,400]{0,1:T(8,128)(2,1)S(1)} %slice.28), channel_id=1, source_target_pairs={{0,8},{8,0},{16,24},{24,16},{1,9},{9,1},{17,25},{25,17},{2,10},{10... | collective-permute-start | bytes 1075208 | tf_op jit(solution)/shard_map/ppermute | solution.py:10
  21.2 8.1 %collective-permute-start.3 = (bf16[352,400]{0,1:T(8,128)(2,1)S(1)}, bf16[352,400]{0,1:T(8,128)(2,1)S(1)}, u32[]{:S(2)}, u32[]{:S(2)}) collective-permute-start(bf16[352,400]{0,1:T(8,128)(2,1)S(1)} %slice.29), channel_id=1, source_target_pairs={{0,16},{8,24},{16,0},{24,8},{1,17},{9,25},{17,1},{25,9},{2,18},{10... | collective-permute-start | bytes 844808 | tf_op jit(solution)/shard_map/ppermute | solution.py:10
  32.9 3.5 %collective-permute-start.4 = (f32[768,200]{0,1:T(8,128)}, f32[768,200]{0,1:T(8,128)S(1)}, u32[]{:S(2)}, u32[]{:S(2)}) collective-permute-start(f32[768,200]{0,1:T(8,128)} %get-tuple-element.19), channel_id=1, source_target_pairs={{0,1},{1,0},{2,3},{3,2},{4,5},{5,4},{6,7},{7,6},{8,9},{9,8},{10,11... | collective-permute-start | bytes 1843208 | tf_op jit(solution)/shard_map/ppermute | solution.py:10
  32.9 3.5 %collective-permute-start.6 = (f32[768,200]{0,1:T(8,128)S(1)}, f32[768,200]{0,1:T(8,128)}, u32[]{:S(2)}, u32[]{:S(2)}) collective-permute-start(f32[768,200]{0,1:T(8,128)S(1)} %get-tuple-element.20), channel_id=1, source_target_pairs={{0,1},{1,0},{2,3},{3,2},{4,5},{5,4},{6,7},{7,6},{8,9},{9,8},{10,11... | collective-permute-start | bytes 1843208 | tf_op jit(solution)/shard_map/ppermute | solution.py:10
  37.6 16.9 %collective-permute-start.5 = (f32[768,200]{0,1:T(8,128)S(1)}, f32[768,200]{0,1:T(8,128)}, u32[]{:S(2)}, u32[]{:S(2)}) collective-permute-start(f32[768,200]{0,1:T(8,128)S(1)} %get-tuple-element.17), channel_id=1, source_target_pairs={{0,16},{8,24},{16,0},{24,8},{1,17},{9,25},{17,1},{25,9},{2,18},{10... | collective-permute-start | bytes 1843208 | tf_op jit(solution)/shard_map/ppermute | solution.py:10
  42.5 24.1 %collective-permute-start.7 = (f32[768,200]{0,1:T(8,128)}, f32[768,200]{0,1:T(8,128)S(1)}, u32[]{:S(2)}, u32[]{:S(2)}) collective-permute-start(f32[768,200]{0,1:T(8,128)} %copy.9), channel_id=1, source_target_pairs={{0,16},{8,24},{16,0},{24,8},{1,17},{9,25},{17,1},{25,9},{2,18},{10... | collective-permute-start | bytes 1843208 | tf_op jit(solution)/shard_map/ppermute | solution.py:10

commit v26 on v24

--- a/solution.py
+++ b/solution.py
@@ -13,7 +13,7 @@
 def gather_prow(own, prow_idx, prow_count):
     count = own.shape[0]
     if prow_count == 4 and count % 32 == 0:
-        half = count // 2 + count // 16 // 16 * 16
+        half = count // 2 + count // 24 // 16 * 16
         from_x = swap(own, "prow", 1)
         from_y = swap(own, "prow", 2)
         diag_a = swap(from_y[:half], "prow", 1)

time: 65.6 us -> 65.6 us (level)
  no operation moved by 1% of the time
where the time goes in v26:
time: 65.6 us; the launch traced here: 65 us
  waiting for transfers between devices  27.1 us (41%)
  matrix products  15.2 us (23%)
  starting transfers between devices  10.5 us (16%)
  local copies, waits for them, and re-layouts  9.84 us (15%)
  other arithmetic  2.24 us (3%)
    ppermute x8, waiting for transfers between devices, swap(): lax.ppermute(value, axis, [(i, i ^ mask) for i in range(lax.axis_size(axi...  27.1 us
    dot_general x10, matrix products, contract(): product = jnp.dot(window, blocked, preferred_element_type=jnp.float32)  15.2 us
    ppermute x8, starting transfers between devices, swap(): lax.ppermute(value, axis, [(i, i ^ mask) for i in range(lax.axis_size(axi...  10.5 us
    gather x2, local copies, waits for them, and re-layouts, shards(): fetched = swap(jnp.take(piece, wanted, axis=0, mode='clip'), 'prow', half)  3.19 us
    dynamic_slice x3, local copies, waits for them, and re-layouts, contract(): lax.dynamic_slice_in_dim(labels, o, b.shape[0])[:, None]  2.42 us
    gather x2, local copies, waits for them, and re-layouts, shards(): results.append(piece - jnp.take(fetched, local, axis=0, mode='clip'))  2.36 us
    ppermute x1, local copies, waits for them, and re-layouts, swap(): lax.ppermute(value, axis, [(i, i ^ mask) for i in range(lax.axis_size(axi...  1.34 us
  transfers between devices with their start and end apart: 8, of which 5 were waited for; matrix products, arithmetic and copies ran while one was open for 37% of the time, Pallas kernels for 0%

profile of v26, /device:TPU:0, one launch (start us, length us, event | category | flops | bytes accessed | tf_op | source)
XLA Modules:
  0.0 65.0 jit_solution(623895602021626658)
XLA Ops:
  0.0 3.0 %collective-permute-start = (bf16[800,400]{0,1:T(8,128)(2,1)}, bf16[800,400]{0,1:T(8,128)(2,1)S(1)}, u32[]{:S(2)}, u32[]{:S(2)}) collective-permute-start(bf16[800,400]{0,1:T(8,128)(2,1)} %param.6), channel_id=1, source_target_pairs={{0,16},{8,24},{16,0},{24,8},{1,17},{9,25},{17,1},{25,9},{2,18},{10... | collective-permute-start | bytes 1920008 | tf_op jit(solution)/shard_map/ppermute | solution.py:10
  3.0 1.5 %collective-permute-start.2 = (bf16[800,400]{0,1:T(8,128)(2,1)}, bf16[800,400]{0,1:T(8,128)(2,1)S(1)}, u32[]{:S(2)}, u32[]{:S(2)}) collective-permute-start(bf16[800,400]{0,1:T(8,128)(2,1)} %param.6), channel_id=1, source_target_pairs={{0,8},{8,0},{16,24},{24,16},{1,9},{9,1},{17,25},{25,17},{2,10},{10... | collective-permute-start | bytes 1920008 | tf_op jit(solution)/shard_map/ppermute | solution.py:10
  4.5 0.8 %dynamic_slice.83 = s32[432]{0:T(512)S(1)} dynamic-slice(s32[6400]{0:T(1024)} %param.7, s32[]{:T(128)S(6)} %dynamic_slice.82), dynamic_slice_sizes={432} | dynamic-slice | bytes 3460 | tf_op jit(solution)/shard_map/dynamic_slice | solution.py:41
  5.2 0.8 %dynamic_slice.86 = s32[368]{0:T(512)S(1)} dynamic-slice(s32[6400]{0:T(1024)} %param.7, s32[]{:T(128)S(6)} %dynamic_slice.85), dynamic_slice_sizes={368} | dynamic-slice | bytes 2948 | tf_op jit(solution)/shard_map/dynamic_slice | solution.py:41
  6.0 0.9 %fusion.31 = (s32[800]{0:T(1024)S(1)}, s32[800]{0:T(1024)S(1)}, s32[800]{0:T(1024)S(1)}) fusion(s32[6400]{0:T(1024)} %param.7, s32[]{:T(128)S(6)} %dynamic_slice.76, s32[]{:T(128)S(6)} %dynamic_slice.73, s32[]{:T(128)S(6)} %dynamic_slice.70), kind=kLoop, calls=%fused_computation.47 | loop fusion | bytes 19212 | tf_op jit(solution)/shard_map/dynamic_slice | solution.py:41
  6.9 0.8 %dynamic-slice_subtract_fusion.1 = (s32[768]{0:T(1024)S(1)}, s32[768]{0:T(1024)S(1)}) fusion(s32[6144]{0:T(1024)} %param.9, s32[]{:T(128)S(6)} %select_n.105, s32[]{:T(128)S(6)} %mul.45, s32[]{:T(128)S(6)} %mul.43, s32[]{:T(128)S(6)} %select_n.106), kind=kLoop, calls=%fused_computation.35 | loop fusion | flops 1536 | bytes 12304 | tf_op jit(solution)/shard_map/sub | solution.py:66
  7.7 2.9 %fusion.6 = f32[768,400]{0,1:T(8,128)S(1)} fusion(bf16[1536,3200]{1,0:T(8,128)(2,1)} %param.5, s32[]{:T(128)S(6)} %select_n.85, s32[]{:T(128)S(6)} %select_n.87, bf16[800,400]{0,1:T(8,128)(2,1)} %param.6, s32[800]{0:T(1024)S(1)} %get-tuple-element.19, s32[400]{0:T(512)} %param.8), kind=kOutput, calls=%fused_computation.15 | convolution fusion | flops 492160000 | bytes 3327112 | tf_op jit(solution)/shard_map/dot_general | solution.py:43
  10.6 2.8 %fusion.2 = f32[768,400]{0,1:T(8,128)S(1)} fusion(bf16[1536,3200]{1,0:T(8,128)(2,1)} %param.5, s32[]{:T(128)S(6)} %select_n.98, s32[]{:T(128)S(6)} %select_n.87, bf16[800,400]{0,1:T(8,128)(2,1)S(1)} %copy-done.2, s32[800]{0:T(1024)S(1)} %get-tuple-element.19, s32[400]{0:T(512)S(1)} %copy-done.1), kind=kOutput, calls=%fused_computation.11 | convolution fusion | flops 492160000 | bytes 3249864 | tf_op jit(solution)/shard_map/dot_general | solution.py:43
  13.4 5.8 %collective-permute-done = bf16[800,400]{0,1:T(8,128)(2,1)S(1)} collective-permute-done((bf16[800,400]{0,1:T(8,128)(2,1)}, bf16[800,400]{0,1:T(8,128)(2,1)S(1)}, u32[]{:S(2)}, u32[]{:S(2)}) %collective-permute-start) | collective-permute-done | bytes 640032 | tf_op jit(solution)/shard_map/ppermute | solution.py:10
  19.3 1.8 %collective-permute-start.1 = (bf16[432,400]{0,1:T(8,128)(2,1)S(1)}, bf16[432,400]{0,1:T(8,128)(2,1)S(1)}, u32[]{:S(2)}, u32[]{:S(2)}) collective-permute-start(bf16[432,400]{0,1:T(8,128)(2,1)S(1)} %slice.28), channel_id=1, source_target_pairs={{0,8},{8,0},{16,24},{24,16},{1,9},{9,1},{17,25},{25,17},{2,10},{10... | collective-permute-start | bytes 1036808 | tf_op jit(solution)/shard_map/ppermute | solution.py:10
  21.2 1.6 %collective-permute-start.3 = (bf16[368,400]{0,1:T(8,128)(2,1)S(1)}, bf16[368,400]{0,1:T(8,128)(2,1)S(1)}, u32[]{:S(2)}, u32[]{:S(2)}) collective-permute-start(bf16[368,400]{0,1:T(8,128)(2,1)S(1)} %slice.29), channel_id=1, source_target_pairs={{0,16},{8,24},{16,0},{24,8},{1,17},{9,25},{17,1},{25,9},{2,18},{10... | collective-permute-start | bytes 883208 | tf_op jit(solution)/shard_map/ppermute | solution.py:10
  22.8 2.7 %convolution_add_fusion.3 = f32[768,400]{0,1:T(8,128)S(1)} fusion(f32[768,400]{0,1:T(8,128)S(1)} %fusion.6, bf16[1536,3200]{1,0:T(8,128)(2,1)} %param.5, s32[]{:T(128)S(6)} %select_n.85, s32[]{:T(128)S(6)} %select_n.92, bf16[800,400]{0,1:T(8,128)(2,1)S(1)} %collective-permute-done, s32[800]{0:T(1024)S(1)} %get-tuple-element.18, s32[400]{0:T(512)S(1)} %copy-done.1), kind=kOutput, calls=%fused_computation.8 | convolution fusion | flops 492467200 | bytes 4478664 | tf_op jit(solution)/shard_map/dot_general | solution.py:43
  25.5 1.3 %convolution_add_fusion.1 = f32[768,400]{0,1:T(8,128)S(1)} fusion(f32[768,400]{0,1:T(8,128)S(1)} %fusion.2, bf16[1536,3200]{1,0:T(8,128)(2,1)S(1)} %copy-done, s32[]{:T(128)S(6)} %select_n.98, s32[]{:T(128)S(6)} %select_n.92, bf16[800,400]{0,1:T(8,128)(2,1)S(1)} %collective-permute-done, s32[800]{0:T(1024)S(1)} %get-tuple-element.18, s32[400]{0:T(512)S(1)} %copy-done.1), kind=kOutput, calls=%fused_computation.6 | convolution fusion | flops 492467200 | bytes 4556808 | tf_op jit(solution)/shard_map/dot_general | solution.py:43
  26.7 1.3 %convolution_add_fusion.2 = f32[768,400]{0,1:T(8,128)S(1)} fusion(f32[768,400]{0,1:T(8,128)S(1)} %convolution_add_fusion.3, bf16[1536,3200]{1,0:T(8,128)(2,1)S(1)} %copy-done, s32[]{:T(128)S(6)} %select_n.85, s32[]{:T(128)S(6)} %select_n.95, bf16[800,400]{0,1:T(8,128)(2,1)S(1)} %collective-permute-done.2, s32[800]{0:T(1024)S(1)} %get-tuple-element.17, ...), kind=kOutput, calls=%fused_computation.7 | convolution fusion | flops 492467200 | bytes 4556808 | tf_op jit(solution)/shard_map/dot_general | solution.py:43
  28.0 1.3 %convolution_add_fusion = f32[768,400]{0,1:T(8,128)S(1)} fusion(f32[768,400]{0,1:T(8,128)S(1)} %convolution_add_fusion.1, bf16[1536,3200]{1,0:T(8,128)(2,1)S(1)} %copy-done, s32[]{:T(128)S(6)} %select_n.98, s32[]{:T(128)S(6)} %select_n.95, bf16[800,400]{0,1:T(8,128)(2,1)S(1)} %collective-permute-done.2, s32[800]{0:T(1024)S(1)} %get-tuple-element.17, ...), kind=kOutput, calls=%fused_computation.5 | convolution fusion | flops 492467200 | bytes 4556808 | tf_op jit(solution)/shard_map/dot_general | solution.py:43
  29.3 0.7 %collective-permute-done.1 = bf16[432,400]{0,1:T(8,128)(2,1)S(1)} collective-permute-done((bf16[432,400]{0,1:T(8,128)(2,1)S(1)}, bf16[432,400]{0,1:T(8,128)(2,1)S(1)}, u32[]{:S(2)}, u32[]{:S(2)}) %collective-permute-start.1) | collective-permute-done | bytes 345632 | tf_op jit(solution)/shard_map/ppermute | solution.py:10
  30.0 0.8 %fusion.8 = f32[768,400]{0,1:T(8,128)S(1)} fusion(bf16[1536,3200]{1,0:T(8,128)(2,1)S(1)} %copy-done, s32[]{:T(128)S(6)} %select_n.85, s32[]{:T(128)S(6)} %select_n.100, bf16[432,400]{0,1:T(8,128)(2,1)S(1)} %collective-permute-done.1, s32[432]{0:T(512)S(1)} %dynamic_slice.83, s32[400]{0:T(512)S(1)} %copy-done.1), kind=kOutput, calls=%fused_computation.21 | convolution fusion | flops 265766400 | bytes 2428936 | tf_op jit(solution)/shard_map/dot_general | solution.py:43
  30.8 0.7 %add_add_fusion = f32[768,400]{0,1:T(8,128)S(1)} fusion(f32[768,400]{0,1:T(8,128)S(1)} %convolution_add_fusion.2, f32[768,400]{0,1:T(8,128)S(1)} %fusion.8, bf16[1536,3200]{1,0:T(8,128)(2,1)S(1)} %copy-done, s32[]{:T(128)S(6)} %select_n.85, s32[]{:T(128)S(6)} %select_n.103, bf16[368,400]{0,1:T(8,128)(2,1)S(1)} %collective-permute-done.3, ...), kind=kOutput, calls=%fused_computation.18 | convolution fusion | flops 227008000 | bytes 4587528 | tf_op jit(solution)/shard_map/dot_general | solution.py:43
  31.6 0.5 collective-permute-start.6
  32.1 0.8 %fusion.10 = f32[768,400]{0,1:T(8,128)S(1)} fusion(bf16[1536,3200]{1,0:T(8,128)(2,1)S(1)} %copy-done, s32[]{:T(128)S(6)} %select_n.98, s32[]{:T(128)S(6)} %select_n.100, bf16[432,400]{0,1:T(8,128)(2,1)S(1)} %collective-permute-done.1, s32[432]{0:T(512)S(1)} %dynamic_slice.83, s32[400]{0:T(512)S(1)} %copy-done.1), kind=kOutput, calls=%fused_computation.23 | convolution fusion | flops 265766400 | bytes 2428936 | tf_op jit(solution)/shard_map/dot_general | solution.py:43
  32.9 0.7 %add_add_fusion.1 = f32[768,400]{0,1:T(8,128)S(1)} fusion(f32[768,400]{0,1:T(8,128)S(1)} %convolution_add_fusion, f32[768,400]{0,1:T(8,128)S(1)} %fusion.10, bf16[1536,3200]{1,0:T(8,128)(2,1)S(1)} %copy-done, s32[]{:T(128)S(6)} %select_n.98, s32[]{:T(128)S(6)} %select_n.103, bf16[368,400]{0,1:T(8,128)(2,1)S(1)} %collective-permute-done.3, ...), kind=kOutput, calls=%fused_computation.19 | convolution fusion | flops 227008000 | bytes 4587528 | tf_op jit(solution)/shard_map/dot_general | solution.py:43
  33.7 0.8 %collective-permute-done.6 = f32[768,200]{0,1:T(8,128)S(1)} collective-permute-done((f32[768,200]{0,1:T(8,128)S(1)}, f32[768,200]{0,1:T(8,128)S(1)}, u32[]{:S(2)}, u32[]{:S(2)}) %collective-permute-start.6) | collective-permute-done | bytes 614432 | tf_op jit(solution)/shard_map/ppermute | solution.py:10
  34.7 1.5 %collective-permute-start.5 = (f32[768,200]{0,1:T(8,128)S(1)}, f32[768,200]{0,1:T(8,128)}, u32[]{:S(2)}, u32[]{:S(2)}) collective-permute-start(f32[768,200]{0,1:T(8,128)S(1)} %get-tuple-element.13), channel_id=1, source_target_pairs={{0,16},{8,24},{16,0},{24,8},{1,17},{9,25},{17,1},{25,9},{2,18},{10... | collective-permute-start | bytes 1843208 | tf_op jit(solution)/shard_map/ppermute | solution.py:10
  36.2 0.3 copy.8
  36.5 2.1 %gather_fusion.1 = f32[768,200]{1,0:T(8,128)S(1)} fusion(f32[768,200]{1,0:T(8,128)S(1)} %copy.8, s32[1024]{0:T(1024)S(1)} %pad_clamp_fusion), kind=kCustom, calls=%fused_computation.1 | custom fusion | bytes 1231872 | tf_op jit(solution)/shard_map/jit(_take)/gather | solution.py:78
  38.6 1.1 %copy.9 = f32[768,200]{0,1:T(8,128)} copy(f32[768,200]{1,0:T(8,128)S(1)} %gather_fusion.1) | data formatting | bytes 1228800 | tf_op jit(solution)/shard_map/jit(_take)/gather | solution.py:78
  39.7 0.6 collective-permute-start.7
  40.3 11.3 %collective-permute-done.5 = f32[768,200]{0,1:T(8,128)} collective-permute-done((f32[768,200]{0,1:T(8,128)S(1)}, f32[768,200]{0,1:T(8,128)}, u32[]{:S(2)}, u32[]{:S(2)}) %collective-permute-start.5) | collective-permute-done | bytes 614432 | tf_op jit(solution)/shard_map/ppermute | solution.py:10
  51.6 1.3 %copy.6 = f32[768,200]{1,0:T(8,128)S(1)} copy(f32[768,200]{0,1:T(8,128)} %collective-permute-done.5) | data formatting | bytes 1228800 | tf_op jit(solution)/shard_map/ppermute | solution.py:10
  52.9 2.1 %gather_fusion = f32[768,200]{1,0:T(8,128)S(1)} fusion(f32[768,200]{1,0:T(8,128)S(1)} %copy.6, s32[1024]{0:T(1024)S(1)} %pad_clamp_fusion.1), kind=kCustom, calls=%fused_computation | custom fusion | bytes 1231872 | tf_op jit(solution)/shard_map/jit(_take)/gather | solution.py:82
  55.4 8.4 %collective-permute-done.7 = f32[768,200]{0,1:T(8,128)S(1)} collective-permute-done((f32[768,200]{0,1:T(8,128)}, f32[768,200]{0,1:T(8,128)S(1)}, u32[]{:S(2)}, u32[]{:S(2)}) %collective-permute-start.7) | collective-permute-done | bytes 614432 | tf_op jit(solution)/shard_map/ppermute | solution.py:10
  63.9 1.1 %pad_maximum_fusion = f32[768,400]{0,1:T(8,128)} fusion(f32[768,200]{0,1:T(8,128)S(1)} %sub.23, f32[768,200]{0,1:T(8,128)S(1)} %sub.20), kind=kLoop, calls=%fused_computation.17 | loop fusion | flops 307200 | bytes 2457600 | tf_op jit(solution)/shard_map/concatenate | solution.py:83
  (19 shorter events, 0.9 us)
Async XLA Ops:
  0.0 19.2 %collective-permute-start = (bf16[800,400]{0,1:T(8,128)(2,1)}, bf16[800,400]{0,1:T(8,128)(2,1)S(1)}, u32[]{:S(2)}, u32[]{:S(2)}) collective-permute-start(bf16[800,400]{0,1:T(8,128)(2,1)} %param.6), channel_id=1, source_target_pairs={{0,16},{8,24},{16,0},{24,8},{1,17},{9,25},{17,1},{25,9},{2,18},{10... | collective-permute-start | bytes 1920008 | tf_op jit(solution)/shard_map/ppermute | solution.py:10
  3.0 18.1 %collective-permute-start.2 = (bf16[800,400]{0,1:T(8,128)(2,1)}, bf16[800,400]{0,1:T(8,128)(2,1)S(1)}, u32[]{:S(2)}, u32[]{:S(2)}) collective-permute-start(bf16[800,400]{0,1:T(8,128)(2,1)} %param.6), channel_id=1, source_target_pairs={{0,8},{8,0},{16,24},{24,16},{1,9},{9,1},{17,25},{25,17},{2,10},{10... | collective-permute-start | bytes 1920008 | tf_op jit(solution)/shard_map/ppermute | solution.py:10
  7.7 2.9 %copy-start.1 = (s32[400]{0:T(512)S(1)}, s32[400]{0:T(512)}, u32[]{:S(2)}) copy-start(s32[400]{0:T(512)} %param.8) | copy-start | bytes 4804
  7.7 2.9 %copy-start.2 = (bf16[800,400]{0,1:T(8,128)(2,1)S(1)}, bf16[800,400]{0,1:T(8,128)(2,1)}, u32[]{:S(2)}) copy-start(bf16[800,400]{0,1:T(8,128)(2,1)} %param.6) | copy-start | bytes 1920004
  10.6 14.9 %copy-start = (bf16[1536,3200]{1,0:T(8,128)(2,1)S(1)}, bf16[1536,3200]{1,0:T(8,128)(2,1)}, u32[]{:S(2)}) copy-start(bf16[1536,3200]{1,0:T(8,128)(2,1)} %param.5) | copy-start | bytes 29491204
  19.3 10.7 %collective-permute-start.1 = (bf16[432,400]{0,1:T(8,128)(2,1)S(1)}, bf16[432,400]{0,1:T(8,128)(2,1)S(1)}, u32[]{:S(2)}, u32[]{:S(2)}) collective-permute-start(bf16[432,400]{0,1:T(8,128)(2,1)S(1)} %slice.28), channel_id=1, source_target_pairs={{0,8},{8,0},{16,24},{24,16},{1,9},{9,1},{17,25},{25,17},{2,10},{10... | collective-permute-start | bytes 1036808 | tf_op jit(solution)/shard_map/ppermute | solution.py:10
  21.2 8.1 %collective-permute-start.3 = (bf16[368,400]{0,1:T(8,128)(2,1)S(1)}, bf16[368,400]{0,1:T(8,128)(2,1)S(1)}, u32[]{:S(2)}, u32[]{:S(2)}) collective-permute-start(bf16[368,400]{0,1:T(8,128)(2,1)S(1)} %slice.29), channel_id=1, source_target_pairs={{0,16},{8,24},{16,0},{24,8},{1,17},{9,25},{17,1},{25,9},{2,18},{10... | collective-permute-start | bytes 883208 | tf_op jit(solution)/shard_map/ppermute | solution.py:10
  31.6 2.1 %collective-permute-start.4 = (f32[768,200]{0,1:T(8,128)S(1)}, f32[768,200]{0,1:T(8,128)S(1)}, u32[]{:S(2)}, u32[]{:S(2)}) collective-permute-start(f32[768,200]{0,1:T(8,128)S(1)} %get-tuple-element.15), channel_id=1, source_target_pairs={{0,1},{1,0},{2,3},{3,2},{4,5},{5,4},{6,7},{7,6},{8,9},{9,8},{10,11... | collective-permute-start | bytes 1843208 | tf_op jit(solution)/shard_map/ppermute | solution.py:10
  31.6 2.9 %collective-permute-start.6 = (f32[768,200]{0,1:T(8,128)S(1)}, f32[768,200]{0,1:T(8,128)S(1)}, u32[]{:S(2)}, u32[]{:S(2)}) collective-permute-start(f32[768,200]{0,1:T(8,128)S(1)} %get-tuple-element.16), channel_id=1, source_target_pairs={{0,1},{1,0},{2,3},{3,2},{4,5},{5,4},{6,7},{7,6},{8,9},{9,8},{10,11... | collective-permute-start | bytes 1843208 | tf_op jit(solution)/shard_map/ppermute | solution.py:10
  34.7 16.9 %collective-permute-start.5 = (f32[768,200]{0,1:T(8,128)S(1)}, f32[768,200]{0,1:T(8,128)}, u32[]{:S(2)}, u32[]{:S(2)}) collective-permute-start(f32[768,200]{0,1:T(8,128)S(1)} %get-tuple-element.13), channel_id=1, source_target_pairs={{0,16},{8,24},{16,0},{24,8},{1,17},{9,25},{17,1},{25,9},{2,18},{10... | collective-permute-start | bytes 1843208 | tf_op jit(solution)/shard_map/ppermute | solution.py:10
  39.7 24.2 %collective-permute-start.7 = (f32[768,200]{0,1:T(8,128)}, f32[768,200]{0,1:T(8,128)S(1)}, u32[]{:S(2)}, u32[]{:S(2)}) collective-permute-start(f32[768,200]{0,1:T(8,128)} %copy.9), channel_id=1, source_target_pairs={{0,16},{8,24},{16,0},{24,8},{1,17},{9,25},{17,1},{25,9},{2,18},{10... | collective-permute-start | bytes 1843208 | tf_op jit(solution)/shard_map/ppermute | solution.py:10
